TPU v7x, 256 devices: a whole 4x4x8 slice. The times are simulated.
256 devices in a mesh: view: 8 (over x_hi, y), slab: 32 (over x_lo, z, core).
Axes of the slice: x: 4 (x_hi: 2, x_lo: 2; x = x_hi * 2 + x_lo), y: 4, z: 8, core: 2. Of those that a mesh axis runs over, the one named last changes fastest.
Arguments:
- estimate: float32 [64, 128, 512], P('slab'), may hold values from 1 to 2
- view_data: float32 [8, 64, 128, 512], P('view', 'slab'), may hold values from 1.5 to 3.5
- background: float32 [8], replicated, may hold values from 0.2 to 0.8
- psf_xy: float32 [8, 8, 2, 17], replicated, may hold values from 0.05 to 1
- psf_z: float32 [8, 3], replicated, may hold values from 0.2 to 1
- view_order: int32 [8], replicated, may hold values from 0 to 7, as said below
- depth_index: int32 [64], P('slab'), may hold values from 0 to 7
Outputs:
- updated: float32 [8, 64, 128, 512], P('view', 'slab')
Inputs may be any that keep to these rules, and one draw needn't show every extreme that they name: view_order[p] = (view_order[0] + p) mod 8: the views go once around in index order, starting from any view.
All inputs are finite; a program needn't handle non-finite values.
Results may differ from a plain program's by a relative error of at most 0.0001.
Values sent between devices are 32-bit elements; how exact they have to be, the bound alone decides.
No kernel may reach another device: no remote copies, remote signals or barrier semaphores. Data moves between devices by JAX's collectives and lax.ppermute only.
A program may use at most 128 MiB of HBM per device.

v0:
```python
import jax
import jax.numpy as jnp
from jax import lax
from jax.sharding import PartitionSpec as P

exact_mode = lax.Precision.HIGHEST


def band_matrix(taps, n):
    count = taps.shape[-1]
    reach = (count - 1) // 2
    block = min(128, n)
    nblocks = n // block
    rows = lax.broadcasted_iota(jnp.int32, (block, block), 0)
    cols = lax.broadcasted_iota(jnp.int32, (block, block), 1)
    offsets = (-1, 0, 1) if nblocks > 1 else (0,)
    parts = {}
    for off in offsets:
        d = off * block + cols - rows + reach
        m = jnp.zeros(taps.shape[:1] + (block, block), taps.dtype)
        for t in range(count):
            m = m + jnp.where((d == t)[None], taps[:, t, None, None], 0.0)
        parts[off] = m
    if nblocks == 1:
        return parts[0]
    bi = lax.broadcasted_iota(jnp.int32, (nblocks, nblocks), 0)
    bj = lax.broadcasted_iota(jnp.int32, (nblocks, nblocks), 1)
    full = jnp.zeros(taps.shape[:1] + (nblocks, block, nblocks, block), taps.dtype)
    for off, m in parts.items():
        sel = (bj - bi == off)[None, :, None, :, None]
        full = full + jnp.where(sel, m[:, None, :, None, :], 0.0)
    return full.reshape(taps.shape[:1] + (n, n))


def halo(array, axis, width):
    size = lax.axis_size(axis)
    up = [(i, i + 1) for i in range(size - 1)]
    down = [(i + 1, i) for i in range(size - 1)]
    below = lax.ppermute(array[-width:], axis, up)
    above = lax.ppermute(array[:width], axis, down)
    return jnp.concatenate([below, array, above], axis=0)


def per_device(estimate, view_data, background, psf_xy, psf_z, view_order, depth_index):
    view_count = lax.axis_size("view")
    my_view = lax.axis_index("view")
    xy_kernels = psf_xy / jnp.sum(psf_xy, axis=-1, keepdims=True)
    z_kernels = psf_z / jnp.sum(psf_z, axis=-1, keepdims=True)
    data_all = lax.all_gather(view_data[0], "view", axis=0)
    count = estimate.shape[0]
    ny, nx = estimate.shape[1], estimate.shape[2]
    current = estimate
    results = jnp.zeros_like(estimate)
    for position in range(view_count):
        view_id = view_order[position]
        table = lax.dynamic_index_in_dim(xy_kernels, view_id, 0, keepdims=False)
        slice_taps = jnp.take(table, depth_index, axis=0)
        by = band_matrix(slice_taps[:, 0], ny)
        bx = band_matrix(slice_taps[:, 1], nx)
        kz = lax.dynamic_index_in_dim(z_kernels, view_id, 0, keepdims=False)
        offset = lax.dynamic_index_in_dim(background, view_id, 0, keepdims=False)
        data = lax.dynamic_index_in_dim(data_all, view_id, 0, keepdims=False)
        padded = halo(current, "slab", 1)
        c = kz[0] * padded[0:count]
        for k in range(1, 3):
            c = c + kz[k] * padded[k : k + count]
        t = jnp.einsum("lij,ljx->lix", by, c, precision=exact_mode)
        blurred = jnp.einsum("lix,lax->lia", t, bx, precision=exact_mode)
        quotient = data / (blurred + offset)
        u = jnp.einsum("lij,lix->ljx", by, quotient, precision=exact_mode)
        g = jnp.einsum("ljx,lxa->lja", u, bx, precision=exact_mode)
        gp = halo(g, "slab", 1)
        corr = kz[0] * gp[2 : 2 + count]
        for k in range(1, 3):
            corr = corr + kz[k] * gp[2 - k : 2 - k + count]
        current = current * corr
        results = jnp.where(my_view == view_id, current, results)
    return results[None]


def solution(mesh):
    return jax.shard_map(
        per_device,
        mesh=mesh,
        in_specs=(
            P("slab", None, None),
            P("view", "slab", None, None),
            P(),
            P(),
            P(),
            P(),
            P("slab"),
        ),
        out_specs=P("view", "slab", None, None),
        check_vma=False,
    )
```

profile of v0, /device:TPU:2, one launch (start us, length us, event | category | flops | bytes accessed | tf_op | source)
XLA Modules:
  0.0 499.1 jit_solution(6066378484917251598)
XLA Ops:
  10.3 7.2 %collective-permute-start.1 = (f32[1,128,512]{2,1,0:T(8,128)}, f32[1,128,512]{2,1,0:T(8,128)}, u32[]{:S(2)}, u32[]{:S(2)}) collective-permute-start(f32[1,128,512]{2,1,0:T(8,128)} %get-tuple-element.317), channel_id=1, source_target_pairs={{1,0},{2,1},{3,2},{4,3},{5,4},{6,5},{7,6},{8,7},{9,8},{10,9},{11,1... | collective-permute-start | bytes 786440 | tf_op jit(solution)/shard_map/ppermute | solution.py:40
  101.2 11.6 %select_add_fusion.1 = (f32[2,512,512]{2,1,0:T(8,128)S(1)}, f32[2,512,512]{2,1,0:T(8,128)}, f32[2,512,512]{2,1,0:T(8,128)}) fusion(f32[2,512,512]{2,1,0:T(8,128)} %broadcast_in_dim.7598, f32[2,512,512]{2,1,0:T(8,128)} %broadcast_in_dim.7596, f32[2,512,512]{2,1,0:T(8,128)} %broadcast_in_dim.7594, pred[512,512]{1,0:T(8,128)(4,1)S(1)} %get-tuple-element.468, ...), kind=kLoop, calls=%fused_computation.9 | loop fusion | flops 7864320 | bytes 25952256 | tf_op jit(solution)/shard_map/add | solution.py:31
  117.7 4.8 fusion.115
  122.9 5.0 %fusion.7 = f32[2,128,512]{2,1,0:T(8,128)S(1)} fusion(f32[2,128,512]{2,1,0:T(8,128)} %fusion.115, f32[2,512,512]{2,1,0:T(8,128)} %get-tuple-element.285, f32[8,2,128,512]{3,2,1,0:T(8,128)} %all-gather.2.cloned.1.call-done, s32[]{:T(128)S(6)} %select_n.3472, f32[]{:T(128)} %bitcast.9), kind=kOutput, calls=%fused_computation.31 | convolution fusion | flops 805568512 | bytes 3670024 | tf_op jit(solution)/shard_map/lix,lax->lia/dot_general | solution.py:68
  139.8 3.1 broadcast_in_dim.7298
  144.7 3.1 broadcast_in_dim.7302
  149.5 3.1 broadcast_in_dim.7372
  154.3 3.1 broadcast_in_dim.7376
  159.1 3.1 broadcast_in_dim.7446
  163.9 3.1 broadcast_in_dim.7450
  168.8 3.1 broadcast_in_dim.7300
  173.6 3.1 broadcast_in_dim.7374
  178.5 3.1 broadcast_in_dim.7448
  183.3 3.1 broadcast_in_dim.7668
  188.0 3.1 broadcast_in_dim.7672
  192.9 3.1 broadcast_in_dim.7670
  197.7 3.1 broadcast_in_dim.7224
  202.5 3.1 broadcast_in_dim.7228
  207.7 3.5 broadcast_in_dim.7226
  211.2 3.2 fusion.110
  216.5 5.9 %collective-permute-start.5 = (f32[1,128,512]{2,1,0:T(8,128)S(1)}, f32[1,128,512]{2,1,0:T(8,128)}, u32[]{:S(2)}, u32[]{:S(2)}) collective-permute-start(f32[1,128,512]{2,1,0:T(8,128)S(1)} %get-tuple-element.313), channel_id=1, source_target_pairs={{1,0},{2,1},{3,2},{4,3},{5,4},{6,5},{7,6},{8,7},{9,8},{10,9},{11,1... | collective-permute-start | bytes 786440 | tf_op jit(solution)/shard_map/ppermute | solution.py:40
  222.4 13.4 %select_add_fusion = (f32[2,512,512]{2,1,0:T(8,128)S(1)}, f32[2,512,512]{2,1,0:T(8,128)}, f32[2,512,512]{2,1,0:T(8,128)S(1)}, f32[2,512,512]{2,1,0:T(8,128)S(1)}, f32[2,512,512]{2,1,0:T(8,128)S(1)}) fusion(f32[2,512,512]{2,1,0:T(8,128)} %broadcast_in_dim.7672, f32[2,512,512]{2,1,0:T(8,128)} %broadcast_in_dim.7670, f32[2,512,512]{2,1,0:T(8,128)} %broadcast_in_dim.7668, ...), kind=kLoop, calls=%fused_computation.8 | loop fusion | flops 13107200 | bytes 42729472 | tf_op jit(solution)/shard_map/add | solution.py:31
  237.1 4.0 fusion.101
  241.1 3.9 fusion.6
  253.7 5.9 %collective-permute-done.7 = f32[1,128,512]{2,1,0:T(8,128)S(1)} collective-permute-done((f32[1,128,512]{2,1,0:T(8,128)S(1)}, f32[1,128,512]{2,1,0:T(8,128)S(1)}, u32[]{:S(2)}, u32[]{:S(2)}) %collective-permute-start.7) | collective-permute-done | bytes 262176 | tf_op jit(solution)/shard_map/ppermute | solution.py:39
  263.9 5.9 %collective-permute-start.9 = (f32[1,128,512]{2,1,0:T(8,128)S(1)}, f32[1,128,512]{2,1,0:T(8,128)S(1)}, u32[]{:S(2)}, u32[]{:S(2)}) collective-permute-start(f32[1,128,512]{2,1,0:T(8,128)S(1)} %get-tuple-element.309), channel_id=1, source_target_pairs={{1,0},{2,1},{3,2},{4,3},{5,4},{6,5},{7,6},{8,7},{9,8},{10,9},{11,1... | collective-permute-start | bytes 786440 | tf_op jit(solution)/shard_map/ppermute | solution.py:40
  281.6 5.9 %collective-permute-start.10 = (f32[1,128,512]{2,1,0:T(8,128)S(1)}, f32[1,128,512]{2,1,0:T(8,128)S(1)}, u32[]{:S(2)}, u32[]{:S(2)}) collective-permute-start(f32[1,128,512]{2,1,0:T(8,128)S(1)} %get-tuple-element.306), channel_id=1, source_target_pairs={{1,0},{2,1},{3,2},{4,3},{5,4},{6,5},{7,6},{8,7},{9,8},{10,9},{11,1... | collective-permute-start | bytes 786440 | tf_op jit(solution)/shard_map/ppermute | solution.py:40
  291.4 5.9 %collective-permute-done.11 = f32[1,128,512]{2,1,0:T(8,128)S(1)} collective-permute-done((f32[1,128,512]{2,1,0:T(8,128)S(1)}, f32[1,128,512]{2,1,0:T(8,128)S(1)}, u32[]{:S(2)}, u32[]{:S(2)}) %collective-permute-start.11) | collective-permute-done | bytes 262176 | tf_op jit(solution)/shard_map/ppermute | solution.py:39
  301.2 5.8 %collective-permute-start.13 = (f32[1,128,512]{2,1,0:T(8,128)S(1)}, f32[1,128,512]{2,1,0:T(8,128)S(1)}, u32[]{:S(2)}, u32[]{:S(2)}) collective-permute-start(f32[1,128,512]{2,1,0:T(8,128)S(1)} %get-tuple-element.305), channel_id=1, source_target_pairs={{1,0},{2,1},{3,2},{4,3},{5,4},{6,5},{7,6},{8,7},{9,8},{10,9},{11,1... | collective-permute-start | bytes 786440 | tf_op jit(solution)/shard_map/ppermute | solution.py:40
  310.9 2.9 fusion.73
  319.1 5.9 %collective-permute-start.14 = (f32[1,128,512]{2,1,0:T(8,128)S(1)}, f32[1,128,512]{2,1,0:T(8,128)S(1)}, u32[]{:S(2)}, u32[]{:S(2)}) collective-permute-start(f32[1,128,512]{2,1,0:T(8,128)S(1)} %get-tuple-element.302), channel_id=1, source_target_pairs={{1,0},{2,1},{3,2},{4,3},{5,4},{6,5},{7,6},{8,7},{9,8},{10,9},{11,1... | collective-permute-start | bytes 786440 | tf_op jit(solution)/shard_map/ppermute | solution.py:40
  328.9 5.9 %collective-permute-done.15 = f32[1,128,512]{2,1,0:T(8,128)S(1)} collective-permute-done((f32[1,128,512]{2,1,0:T(8,128)S(1)}, f32[1,128,512]{2,1,0:T(8,128)S(1)}, u32[]{:S(2)}, u32[]{:S(2)}) %collective-permute-start.15) | collective-permute-done | bytes 262176 | tf_op jit(solution)/shard_map/ppermute | solution.py:39
  338.9 6.0 %collective-permute-start.17 = (f32[1,128,512]{2,1,0:T(8,128)S(1)}, f32[1,128,512]{2,1,0:T(8,128)S(1)}, u32[]{:S(2)}, u32[]{:S(2)}) collective-permute-start(f32[1,128,512]{2,1,0:T(8,128)S(1)} %get-tuple-element.301), channel_id=1, source_target_pairs={{1,0},{2,1},{3,2},{4,3},{5,4},{6,5},{7,6},{8,7},{9,8},{10,9},{11,1... | collective-permute-start | bytes 786440 | tf_op jit(solution)/shard_map/ppermute | solution.py:40
  351.4 2.9 fusion.3
  356.7 5.9 %collective-permute-start.18 = (f32[1,128,512]{2,1,0:T(8,128)S(1)}, f32[1,128,512]{2,1,0:T(8,128)S(1)}, u32[]{:S(2)}, u32[]{:S(2)}) collective-permute-start(f32[1,128,512]{2,1,0:T(8,128)S(1)} %get-tuple-element.298), channel_id=1, source_target_pairs={{1,0},{2,1},{3,2},{4,3},{5,4},{6,5},{7,6},{8,7},{9,8},{10,9},{11,1... | collective-permute-start | bytes 786440 | tf_op jit(solution)/shard_map/ppermute | solution.py:40
  366.5 5.9 %collective-permute-done.19 = f32[1,128,512]{2,1,0:T(8,128)S(1)} collective-permute-done((f32[1,128,512]{2,1,0:T(8,128)S(1)}, f32[1,128,512]{2,1,0:T(8,128)S(1)}, u32[]{:S(2)}, u32[]{:S(2)}) %collective-permute-start.19) | collective-permute-done | bytes 262176 | tf_op jit(solution)/shard_map/ppermute | solution.py:39
  376.6 5.8 %collective-permute-start.21 = (f32[1,128,512]{2,1,0:T(8,128)S(1)}, f32[1,128,512]{2,1,0:T(8,128)S(1)}, u32[]{:S(2)}, u32[]{:S(2)}) collective-permute-start(f32[1,128,512]{2,1,0:T(8,128)S(1)} %get-tuple-element.297), channel_id=1, source_target_pairs={{1,0},{2,1},{3,2},{4,3},{5,4},{6,5},{7,6},{8,7},{9,8},{10,9},{11,1... | collective-permute-start | bytes 786440 | tf_op jit(solution)/shard_map/ppermute | solution.py:40
  386.2 3.0 fusion.45
  389.2 3.0 fusion.2
  394.5 5.9 %collective-permute-start.22 = (f32[1,128,512]{2,1,0:T(8,128)S(1)}, f32[1,128,512]{2,1,0:T(8,128)S(1)}, u32[]{:S(2)}, u32[]{:S(2)}) collective-permute-start(f32[1,128,512]{2,1,0:T(8,128)S(1)} %get-tuple-element.294), channel_id=1, source_target_pairs={{1,0},{2,1},{3,2},{4,3},{5,4},{6,5},{7,6},{8,7},{9,8},{10,9},{11,1... | collective-permute-start | bytes 786440 | tf_op jit(solution)/shard_map/ppermute | solution.py:40
  404.3 5.9 %collective-permute-done.23 = f32[1,128,512]{2,1,0:T(8,128)S(1)} collective-permute-done((f32[1,128,512]{2,1,0:T(8,128)S(1)}, f32[1,128,512]{2,1,0:T(8,128)S(1)}, u32[]{:S(2)}, u32[]{:S(2)}) %collective-permute-start.23) | collective-permute-done | bytes 262176 | tf_op jit(solution)/shard_map/ppermute | solution.py:39
  414.4 6.0 %collective-permute-start.25 = (f32[1,128,512]{2,1,0:T(8,128)S(1)}, f32[1,128,512]{2,1,0:T(8,128)S(1)}, u32[]{:S(2)}, u32[]{:S(2)}) collective-permute-start(f32[1,128,512]{2,1,0:T(8,128)S(1)} %get-tuple-element.293), channel_id=1, source_target_pairs={{1,0},{2,1},{3,2},{4,3},{5,4},{6,5},{7,6},{8,7},{9,8},{10,9},{11,1... | collective-permute-start | bytes 786440 | tf_op jit(solution)/shard_map/ppermute | solution.py:40
  432.1 5.9 %collective-permute-start.26 = (f32[1,128,512]{2,1,0:T(8,128)S(1)}, f32[1,128,512]{2,1,0:T(8,128)S(1)}, u32[]{:S(2)}, u32[]{:S(2)}) collective-permute-start(f32[1,128,512]{2,1,0:T(8,128)S(1)} %get-tuple-element.290), channel_id=1, source_target_pairs={{1,0},{2,1},{3,2},{4,3},{5,4},{6,5},{7,6},{8,7},{9,8},{10,9},{11,1... | collective-permute-start | bytes 786440 | tf_op jit(solution)/shard_map/ppermute | solution.py:40
  441.9 5.9 %collective-permute-done.27 = f32[1,128,512]{2,1,0:T(8,128)S(1)} collective-permute-done((f32[1,128,512]{2,1,0:T(8,128)S(1)}, f32[1,128,512]{2,1,0:T(8,128)S(1)}, u32[]{:S(2)}, u32[]{:S(2)}) %collective-permute-start.27) | collective-permute-done | bytes 262176 | tf_op jit(solution)/shard_map/ppermute | solution.py:39
  451.8 5.8 %collective-permute-start.29 = (f32[1,128,512]{2,1,0:T(8,128)S(1)}, f32[1,128,512]{2,1,0:T(8,128)S(1)}, u32[]{:S(2)}, u32[]{:S(2)}) collective-permute-start(f32[1,128,512]{2,1,0:T(8,128)S(1)} %get-tuple-element.289), channel_id=1, source_target_pairs={{1,0},{2,1},{3,2},{4,3},{5,4},{6,5},{7,6},{8,7},{9,8},{10,9},{11,1... | collective-permute-start | bytes 786440 | tf_op jit(solution)/shard_map/ppermute | solution.py:40
  461.4 2.9 fusion.17
  471.1 5.9 %collective-permute-start.30 = (f32[1,128,512]{2,1,0:T(8,128)}, f32[1,128,512]{2,1,0:T(8,128)}, u32[]{:S(2)}, u32[]{:S(2)}) collective-permute-start(f32[1,128,512]{2,1,0:T(8,128)} %get-tuple-element.286), channel_id=1, source_target_pairs={{1,0},{2,1},{3,2},{4,3},{5,4},{6,5},{7,6},{8,7},{9,8},{10,9},{11,1... | collective-permute-start | bytes 786440 | tf_op jit(solution)/shard_map/ppermute | solution.py:40
  487.0 4.8 fusion.12
  (568 shorter events, 229.7 us)
Async XLA Ops:
  6.5 116.3 %all-gather.2.cloned.1.call-start = ((), (), s32[]{:S(2)}) async-start(), calls=%async_computation | async-start | bytes 4718592 | tf_op jit(solution)/shard_map/all_gather | solution.py:49
  8.4 109.3 %collective-permute-start = (f32[1,128,512]{2,1,0:T(8,128)}, f32[1,128,512]{2,1,0:T(8,128)}, u32[]{:S(2)}, u32[]{:S(2)}) collective-permute-start(f32[1,128,512]{2,1,0:T(8,128)} %get-tuple-element.316), channel_id=1, source_target_pairs={{0,1},{1,2},{2,3},{3,4},{4,5},{5,6},{6,7},{7,8},{8,9},{9,10},{10,1... | collective-permute-start | bytes 786440 | tf_op jit(solution)/shard_map/ppermute | solution.py:39
  10.3 107.4 %collective-permute-start.1 = (f32[1,128,512]{2,1,0:T(8,128)}, f32[1,128,512]{2,1,0:T(8,128)}, u32[]{:S(2)}, u32[]{:S(2)}) collective-permute-start(f32[1,128,512]{2,1,0:T(8,128)} %get-tuple-element.317), channel_id=1, source_target_pairs={{1,0},{2,1},{3,2},{4,3},{5,4},{6,5},{7,6},{8,7},{9,8},{10,9},{11,1... | collective-permute-start | bytes 786440 | tf_op jit(solution)/shard_map/ppermute | solution.py:40
  30.9 68.5 %copy-start.19 = (pred[128,128]{0,1:T(8,128)(4,1)}, pred[128,128]{0,1:T(8,128)(4,1)S(1)}, u32[]{:S(2)}) copy-start(pred[128,128]{0,1:T(8,128)(4,1)S(1)} %get-tuple-element.461) | copy-start | bytes 49156
  30.9 68.5 %copy-start.22 = (pred[128,128]{0,1:T(8,128)(4,1)}, pred[128,128]{0,1:T(8,128)(4,1)S(1)}, u32[]{:S(2)}) copy-start(pred[128,128]{0,1:T(8,128)(4,1)S(1)} %get-tuple-element.462) | copy-start | bytes 49156
  30.9 68.5 %copy-start.25 = (pred[128,128]{0,1:T(8,128)(4,1)}, pred[128,128]{0,1:T(8,128)(4,1)S(1)}, u32[]{:S(2)}) copy-start(pred[128,128]{0,1:T(8,128)(4,1)S(1)} %get-tuple-element.463) | copy-start | bytes 49156
  31.0 68.4 %copy-start.28 = (pred[128,128]{0,1:T(8,128)(4,1)}, pred[128,128]{0,1:T(8,128)(4,1)S(1)}, u32[]{:S(2)}) copy-start(pred[128,128]{0,1:T(8,128)(4,1)S(1)} %get-tuple-element.464) | copy-start | bytes 49156
  31.0 68.4 %copy-start.31 = (pred[128,128]{0,1:T(8,128)(4,1)}, pred[128,128]{0,1:T(8,128)(4,1)S(1)}, u32[]{:S(2)}) copy-start(pred[128,128]{0,1:T(8,128)(4,1)S(1)} %get-tuple-element.465) | copy-start | bytes 49156
  31.0 68.4 %copy-start.34 = (pred[128,128]{0,1:T(8,128)(4,1)}, pred[128,128]{0,1:T(8,128)(4,1)S(1)}, u32[]{:S(2)}) copy-start(pred[128,128]{0,1:T(8,128)(4,1)S(1)} %get-tuple-element.466) | copy-start | bytes 49156
  31.0 68.4 %copy-start.37 = (pred[128,128]{0,1:T(8,128)(4,1)}, pred[128,128]{0,1:T(8,128)(4,1)S(1)}, u32[]{:S(2)}) copy-start(pred[128,128]{0,1:T(8,128)(4,1)S(1)} %get-tuple-element.467) | copy-start | bytes 49156
  31.1 68.4 %copy-start.40 = (pred[128,128]{0,1:T(8,128)(4,1)}, pred[128,128]{0,1:T(8,128)(4,1)S(1)}, u32[]{:S(2)}) copy-start(pred[128,128]{0,1:T(8,128)(4,1)S(1)} %fusion.204) | copy-start | bytes 49156
  43.0 53.3 %copy-start.43 = (pred[128,128]{0,1:T(8,128)(4,1)}, pred[128,128]{0,1:T(8,128)(4,1)S(1)}, u32[]{:S(2)}) copy-start(pred[128,128]{0,1:T(8,128)(4,1)S(1)} %get-tuple-element.398) | copy-start | bytes 49156
  43.0 53.3 %copy-start.44 = (pred[128,128]{0,1:T(8,128)(4,1)}, pred[128,128]{0,1:T(8,128)(4,1)S(1)}, u32[]{:S(2)}) copy-start(pred[128,128]{0,1:T(8,128)(4,1)S(1)} %get-tuple-element.399) | copy-start | bytes 49156
  43.0 53.3 %copy-start.45 = (pred[128,128]{0,1:T(8,128)(4,1)}, pred[128,128]{0,1:T(8,128)(4,1)S(1)}, u32[]{:S(2)}) copy-start(pred[128,128]{0,1:T(8,128)(4,1)S(1)} %get-tuple-element.400) | copy-start | bytes 49156
  43.1 53.3 %copy-start.46 = (pred[128,128]{0,1:T(8,128)(4,1)}, pred[128,128]{0,1:T(8,128)(4,1)S(1)}, u32[]{:S(2)}) copy-start(pred[128,128]{0,1:T(8,128)(4,1)S(1)} %get-tuple-element.401) | copy-start | bytes 49156
  43.1 53.3 %copy-start.47 = (pred[128,128]{0,1:T(8,128)(4,1)}, pred[128,128]{0,1:T(8,128)(4,1)S(1)}, u32[]{:S(2)}) copy-start(pred[128,128]{0,1:T(8,128)(4,1)S(1)} %get-tuple-element.402) | copy-start | bytes 49156
  43.1 53.3 %copy-start.48 = (pred[128,128]{0,1:T(8,128)(4,1)}, pred[128,128]{0,1:T(8,128)(4,1)S(1)}, u32[]{:S(2)}) copy-start(pred[128,128]{0,1:T(8,128)(4,1)S(1)} %get-tuple-element.403) | copy-start | bytes 49156
  43.1 53.3 %copy-start.49 = (pred[128,128]{0,1:T(8,128)(4,1)}, pred[128,128]{0,1:T(8,128)(4,1)S(1)}, u32[]{:S(2)}) copy-start(pred[128,128]{0,1:T(8,128)(4,1)S(1)} %get-tuple-element.404) | copy-start | bytes 49156
  131.5 79.7 %collective-permute-start.2 = (f32[1,128,512]{2,1,0:T(8,128)}, f32[1,128,512]{2,1,0:T(8,128)}, u32[]{:S(2)}, u32[]{:S(2)}) collective-permute-start(f32[1,128,512]{2,1,0:T(8,128)} %get-tuple-element.314), channel_id=1, source_target_pairs={{1,0},{2,1},{3,2},{4,3},{5,4},{6,5},{7,6},{8,7},{9,8},{10,9},{11,1... | collective-permute-start | bytes 786440 | tf_op jit(solution)/shard_map/ppermute | solution.py:40
  134.1 77.1 %collective-permute-start.3 = (f32[1,128,512]{2,1,0:T(8,128)}, f32[1,128,512]{2,1,0:T(8,128)}, u32[]{:S(2)}, u32[]{:S(2)}) collective-permute-start(f32[1,128,512]{2,1,0:T(8,128)} %get-tuple-element.315), channel_id=1, source_target_pairs={{0,1},{1,2},{2,3},{3,4},{4,5},{5,6},{6,7},{7,8},{8,9},{9,10},{10,1... | collective-permute-start | bytes 786440 | tf_op jit(solution)/shard_map/ppermute | solution.py:39
  214.5 21.8 %collective-permute-start.4 = (f32[1,128,512]{2,1,0:T(8,128)S(1)}, f32[1,128,512]{2,1,0:T(8,128)S(1)}, u32[]{:S(2)}, u32[]{:S(2)}) collective-permute-start(f32[1,128,512]{2,1,0:T(8,128)S(1)} %get-tuple-element.312), channel_id=1, source_target_pairs={{0,1},{1,2},{2,3},{3,4},{4,5},{5,6},{6,7},{7,8},{8,9},{9,10},{10,1... | collective-permute-start | bytes 786440 | tf_op jit(solution)/shard_map/ppermute | solution.py:39
  216.5 19.8 %collective-permute-start.5 = (f32[1,128,512]{2,1,0:T(8,128)S(1)}, f32[1,128,512]{2,1,0:T(8,128)}, u32[]{:S(2)}, u32[]{:S(2)}) collective-permute-start(f32[1,128,512]{2,1,0:T(8,128)S(1)} %get-tuple-element.313), channel_id=1, source_target_pairs={{1,0},{2,1},{3,2},{4,3},{5,4},{6,5},{7,6},{8,7},{9,8},{10,9},{11,1... | collective-permute-start | bytes 786440 | tf_op jit(solution)/shard_map/ppermute | solution.py:40
  247.4 6.3 %collective-permute-start.6 = (f32[1,128,512]{2,1,0:T(8,128)S(1)}, f32[1,128,512]{2,1,0:T(8,128)S(1)}, u32[]{:S(2)}, u32[]{:S(2)}) collective-permute-start(f32[1,128,512]{2,1,0:T(8,128)S(1)} %get-tuple-element.310), channel_id=1, source_target_pairs={{1,0},{2,1},{3,2},{4,3},{5,4},{6,5},{7,6},{8,7},{9,8},{10,9},{11,1... | collective-permute-start | bytes 786440 | tf_op jit(solution)/shard_map/ppermute | solution.py:40
  249.8 9.8 %collective-permute-start.7 = (f32[1,128,512]{2,1,0:T(8,128)S(1)}, f32[1,128,512]{2,1,0:T(8,128)S(1)}, u32[]{:S(2)}, u32[]{:S(2)}) collective-permute-start(f32[1,128,512]{2,1,0:T(8,128)S(1)} %get-tuple-element.311), channel_id=1, source_target_pairs={{0,1},{1,2},{2,3},{3,4},{4,5},{5,6},{6,7},{7,8},{8,9},{9,10},{10,1... | collective-permute-start | bytes 786440 | tf_op jit(solution)/shard_map/ppermute | solution.py:39
  261.7 10.1 %collective-permute-start.8 = (f32[1,128,512]{2,1,0:T(8,128)S(1)}, f32[1,128,512]{2,1,0:T(8,128)S(1)}, u32[]{:S(2)}, u32[]{:S(2)}) collective-permute-start(f32[1,128,512]{2,1,0:T(8,128)S(1)} %get-tuple-element.308), channel_id=1, source_target_pairs={{0,1},{1,2},{2,3},{3,4},{4,5},{5,6},{6,7},{7,8},{8,9},{9,10},{10,1... | collective-permute-start | bytes 786440 | tf_op jit(solution)/shard_map/ppermute | solution.py:39
  263.9 9.6 %collective-permute-start.9 = (f32[1,128,512]{2,1,0:T(8,128)S(1)}, f32[1,128,512]{2,1,0:T(8,128)S(1)}, u32[]{:S(2)}, u32[]{:S(2)}) collective-permute-start(f32[1,128,512]{2,1,0:T(8,128)S(1)} %get-tuple-element.309), channel_id=1, source_target_pairs={{1,0},{2,1},{3,2},{4,3},{5,4},{6,5},{7,6},{8,7},{9,8},{10,9},{11,1... | collective-permute-start | bytes 786440 | tf_op jit(solution)/shard_map/ppermute | solution.py:40
  281.6 9.8 %collective-permute-start.10 = (f32[1,128,512]{2,1,0:T(8,128)S(1)}, f32[1,128,512]{2,1,0:T(8,128)S(1)}, u32[]{:S(2)}, u32[]{:S(2)}) collective-permute-start(f32[1,128,512]{2,1,0:T(8,128)S(1)} %get-tuple-element.306), channel_id=1, source_target_pairs={{1,0},{2,1},{3,2},{4,3},{5,4},{6,5},{7,6},{8,7},{9,8},{10,9},{11,1... | collective-permute-start | bytes 786440 | tf_op jit(solution)/shard_map/ppermute | solution.py:40
  287.5 9.8 %collective-permute-start.11 = (f32[1,128,512]{2,1,0:T(8,128)S(1)}, f32[1,128,512]{2,1,0:T(8,128)S(1)}, u32[]{:S(2)}, u32[]{:S(2)}) collective-permute-start(f32[1,128,512]{2,1,0:T(8,128)S(1)} %get-tuple-element.307), channel_id=1, source_target_pairs={{0,1},{1,2},{2,3},{3,4},{4,5},{5,6},{6,7},{7,8},{8,9},{9,10},{10,1... | collective-permute-start | bytes 786440 | tf_op jit(solution)/shard_map/ppermute | solution.py:39
  299.3 9.8 %collective-permute-start.12 = (f32[1,128,512]{2,1,0:T(8,128)S(1)}, f32[1,128,512]{2,1,0:T(8,128)S(1)}, u32[]{:S(2)}, u32[]{:S(2)}) collective-permute-start(f32[1,128,512]{2,1,0:T(8,128)S(1)} %get-tuple-element.304), channel_id=1, source_target_pairs={{0,1},{1,2},{2,3},{3,4},{4,5},{5,6},{6,7},{7,8},{8,9},{9,10},{10,1... | collective-permute-start | bytes 786440 | tf_op jit(solution)/shard_map/ppermute | solution.py:39
  301.2 9.6 %collective-permute-start.13 = (f32[1,128,512]{2,1,0:T(8,128)S(1)}, f32[1,128,512]{2,1,0:T(8,128)S(1)}, u32[]{:S(2)}, u32[]{:S(2)}) collective-permute-start(f32[1,128,512]{2,1,0:T(8,128)S(1)} %get-tuple-element.305), channel_id=1, source_target_pairs={{1,0},{2,1},{3,2},{4,3},{5,4},{6,5},{7,6},{8,7},{9,8},{10,9},{11,1... | collective-permute-start | bytes 786440 | tf_op jit(solution)/shard_map/ppermute | solution.py:40
  319.1 9.8 %collective-permute-start.14 = (f32[1,128,512]{2,1,0:T(8,128)S(1)}, f32[1,128,512]{2,1,0:T(8,128)S(1)}, u32[]{:S(2)}, u32[]{:S(2)}) collective-permute-start(f32[1,128,512]{2,1,0:T(8,128)S(1)} %get-tuple-element.302), channel_id=1, source_target_pairs={{1,0},{2,1},{3,2},{4,3},{5,4},{6,5},{7,6},{8,7},{9,8},{10,9},{11,1... | collective-permute-start | bytes 786440 | tf_op jit(solution)/shard_map/ppermute | solution.py:40
  325.0 9.8 %collective-permute-start.15 = (f32[1,128,512]{2,1,0:T(8,128)S(1)}, f32[1,128,512]{2,1,0:T(8,128)S(1)}, u32[]{:S(2)}, u32[]{:S(2)}) collective-permute-start(f32[1,128,512]{2,1,0:T(8,128)S(1)} %get-tuple-element.303), channel_id=1, source_target_pairs={{0,1},{1,2},{2,3},{3,4},{4,5},{5,6},{6,7},{7,8},{8,9},{9,10},{10,1... | collective-permute-start | bytes 786440 | tf_op jit(solution)/shard_map/ppermute | solution.py:39
  336.9 9.8 %collective-permute-start.16 = (f32[1,128,512]{2,1,0:T(8,128)S(1)}, f32[1,128,512]{2,1,0:T(8,128)S(1)}, u32[]{:S(2)}, u32[]{:S(2)}) collective-permute-start(f32[1,128,512]{2,1,0:T(8,128)S(1)} %get-tuple-element.300), channel_id=1, source_target_pairs={{0,1},{1,2},{2,3},{3,4},{4,5},{5,6},{6,7},{7,8},{8,9},{9,10},{10,1... | collective-permute-start | bytes 786440 | tf_op jit(solution)/shard_map/ppermute | solution.py:39
  338.9 9.6 %collective-permute-start.17 = (f32[1,128,512]{2,1,0:T(8,128)S(1)}, f32[1,128,512]{2,1,0:T(8,128)S(1)}, u32[]{:S(2)}, u32[]{:S(2)}) collective-permute-start(f32[1,128,512]{2,1,0:T(8,128)S(1)} %get-tuple-element.301), channel_id=1, source_target_pairs={{1,0},{2,1},{3,2},{4,3},{5,4},{6,5},{7,6},{8,7},{9,8},{10,9},{11,1... | collective-permute-start | bytes 786440 | tf_op jit(solution)/shard_map/ppermute | solution.py:40
  356.7 9.8 %collective-permute-start.18 = (f32[1,128,512]{2,1,0:T(8,128)S(1)}, f32[1,128,512]{2,1,0:T(8,128)S(1)}, u32[]{:S(2)}, u32[]{:S(2)}) collective-permute-start(f32[1,128,512]{2,1,0:T(8,128)S(1)} %get-tuple-element.298), channel_id=1, source_target_pairs={{1,0},{2,1},{3,2},{4,3},{5,4},{6,5},{7,6},{8,7},{9,8},{10,9},{11,1... | collective-permute-start | bytes 786440 | tf_op jit(solution)/shard_map/ppermute | solution.py:40
  362.6 9.8 %collective-permute-start.19 = (f32[1,128,512]{2,1,0:T(8,128)S(1)}, f32[1,128,512]{2,1,0:T(8,128)S(1)}, u32[]{:S(2)}, u32[]{:S(2)}) collective-permute-start(f32[1,128,512]{2,1,0:T(8,128)S(1)} %get-tuple-element.299), channel_id=1, source_target_pairs={{0,1},{1,2},{2,3},{3,4},{4,5},{5,6},{6,7},{7,8},{8,9},{9,10},{10,1... | collective-permute-start | bytes 786440 | tf_op jit(solution)/shard_map/ppermute | solution.py:39
  374.5 9.9 %collective-permute-start.20 = (f32[1,128,512]{2,1,0:T(8,128)S(1)}, f32[1,128,512]{2,1,0:T(8,128)S(1)}, u32[]{:S(2)}, u32[]{:S(2)}) collective-permute-start(f32[1,128,512]{2,1,0:T(8,128)S(1)} %get-tuple-element.296), channel_id=1, source_target_pairs={{0,1},{1,2},{2,3},{3,4},{4,5},{5,6},{6,7},{7,8},{8,9},{9,10},{10,1... | collective-permute-start | bytes 786440 | tf_op jit(solution)/shard_map/ppermute | solution.py:39
  376.6 9.6 %collective-permute-start.21 = (f32[1,128,512]{2,1,0:T(8,128)S(1)}, f32[1,128,512]{2,1,0:T(8,128)S(1)}, u32[]{:S(2)}, u32[]{:S(2)}) collective-permute-start(f32[1,128,512]{2,1,0:T(8,128)S(1)} %get-tuple-element.297), channel_id=1, source_target_pairs={{1,0},{2,1},{3,2},{4,3},{5,4},{6,5},{7,6},{8,7},{9,8},{10,9},{11,1... | collective-permute-start | bytes 786440 | tf_op jit(solution)/shard_map/ppermute | solution.py:40
  394.5 9.8 %collective-permute-start.22 = (f32[1,128,512]{2,1,0:T(8,128)S(1)}, f32[1,128,512]{2,1,0:T(8,128)S(1)}, u32[]{:S(2)}, u32[]{:S(2)}) collective-permute-start(f32[1,128,512]{2,1,0:T(8,128)S(1)} %get-tuple-element.294), channel_id=1, source_target_pairs={{1,0},{2,1},{3,2},{4,3},{5,4},{6,5},{7,6},{8,7},{9,8},{10,9},{11,1... | collective-permute-start | bytes 786440 | tf_op jit(solution)/shard_map/ppermute | solution.py:40
  400.4 9.8 %collective-permute-start.23 = (f32[1,128,512]{2,1,0:T(8,128)S(1)}, f32[1,128,512]{2,1,0:T(8,128)S(1)}, u32[]{:S(2)}, u32[]{:S(2)}) collective-permute-start(f32[1,128,512]{2,1,0:T(8,128)S(1)} %get-tuple-element.295), channel_id=1, source_target_pairs={{0,1},{1,2},{2,3},{3,4},{4,5},{5,6},{6,7},{7,8},{8,9},{9,10},{10,1... | collective-permute-start | bytes 786440 | tf_op jit(solution)/shard_map/ppermute | solution.py:39
  412.4 9.8 %collective-permute-start.24 = (f32[1,128,512]{2,1,0:T(8,128)S(1)}, f32[1,128,512]{2,1,0:T(8,128)S(1)}, u32[]{:S(2)}, u32[]{:S(2)}) collective-permute-start(f32[1,128,512]{2,1,0:T(8,128)S(1)} %get-tuple-element.292), channel_id=1, source_target_pairs={{0,1},{1,2},{2,3},{3,4},{4,5},{5,6},{6,7},{7,8},{8,9},{9,10},{10,1... | collective-permute-start | bytes 786440 | tf_op jit(solution)/shard_map/ppermute | solution.py:39
  414.4 9.6 %collective-permute-start.25 = (f32[1,128,512]{2,1,0:T(8,128)S(1)}, f32[1,128,512]{2,1,0:T(8,128)S(1)}, u32[]{:S(2)}, u32[]{:S(2)}) collective-permute-start(f32[1,128,512]{2,1,0:T(8,128)S(1)} %get-tuple-element.293), channel_id=1, source_target_pairs={{1,0},{2,1},{3,2},{4,3},{5,4},{6,5},{7,6},{8,7},{9,8},{10,9},{11,1... | collective-permute-start | bytes 786440 | tf_op jit(solution)/shard_map/ppermute | solution.py:40
  432.1 9.8 %collective-permute-start.26 = (f32[1,128,512]{2,1,0:T(8,128)S(1)}, f32[1,128,512]{2,1,0:T(8,128)S(1)}, u32[]{:S(2)}, u32[]{:S(2)}) collective-permute-start(f32[1,128,512]{2,1,0:T(8,128)S(1)} %get-tuple-element.290), channel_id=1, source_target_pairs={{1,0},{2,1},{3,2},{4,3},{5,4},{6,5},{7,6},{8,7},{9,8},{10,9},{11,1... | collective-permute-start | bytes 786440 | tf_op jit(solution)/shard_map/ppermute | solution.py:40
  438.0 9.8 %collective-permute-start.27 = (f32[1,128,512]{2,1,0:T(8,128)S(1)}, f32[1,128,512]{2,1,0:T(8,128)S(1)}, u32[]{:S(2)}, u32[]{:S(2)}) collective-permute-start(f32[1,128,512]{2,1,0:T(8,128)S(1)} %get-tuple-element.291), channel_id=1, source_target_pairs={{0,1},{1,2},{2,3},{3,4},{4,5},{5,6},{6,7},{7,8},{8,9},{9,10},{10,1... | collective-permute-start | bytes 786440 | tf_op jit(solution)/shard_map/ppermute | solution.py:39
  449.9 9.8 %collective-permute-start.28 = (f32[1,128,512]{2,1,0:T(8,128)S(1)}, f32[1,128,512]{2,1,0:T(8,128)S(1)}, u32[]{:S(2)}, u32[]{:S(2)}) collective-permute-start(f32[1,128,512]{2,1,0:T(8,128)S(1)} %get-tuple-element.288), channel_id=1, source_target_pairs={{0,1},{1,2},{2,3},{3,4},{4,5},{5,6},{6,7},{7,8},{8,9},{9,10},{10,1... | collective-permute-start | bytes 786440 | tf_op jit(solution)/shard_map/ppermute | solution.py:39
  451.8 9.6 %collective-permute-start.29 = (f32[1,128,512]{2,1,0:T(8,128)S(1)}, f32[1,128,512]{2,1,0:T(8,128)S(1)}, u32[]{:S(2)}, u32[]{:S(2)}) collective-permute-start(f32[1,128,512]{2,1,0:T(8,128)S(1)} %get-tuple-element.289), channel_id=1, source_target_pairs={{1,0},{2,1},{3,2},{4,3},{5,4},{6,5},{7,6},{8,7},{9,8},{10,9},{11,1... | collective-permute-start | bytes 786440 | tf_op jit(solution)/shard_map/ppermute | solution.py:40
  471.1 13.0 %collective-permute-start.30 = (f32[1,128,512]{2,1,0:T(8,128)}, f32[1,128,512]{2,1,0:T(8,128)}, u32[]{:S(2)}, u32[]{:S(2)}) collective-permute-start(f32[1,128,512]{2,1,0:T(8,128)} %get-tuple-element.286), channel_id=1, source_target_pairs={{1,0},{2,1},{3,2},{4,3},{5,4},{6,5},{7,6},{8,7},{9,8},{10,9},{11,1... | collective-permute-start | bytes 786440 | tf_op jit(solution)/shard_map/ppermute | solution.py:40
  477.0 9.9 %collective-permute-start.31 = (f32[1,128,512]{2,1,0:T(8,128)S(1)}, f32[1,128,512]{2,1,0:T(8,128)}, u32[]{:S(2)}, u32[]{:S(2)}) collective-permute-start(f32[1,128,512]{2,1,0:T(8,128)S(1)} %get-tuple-element.287), channel_id=1, source_target_pairs={{0,1},{1,2},{2,3},{3,4},{4,5},{5,6},{6,7},{7,8},{8,9},{9,10},{10,1... | collective-permute-start | bytes 786440 | tf_op jit(solution)/shard_map/ppermute | solution.py:39
  (150 other events, 2404.8 us)
Sparse Core Ops, SparseCore 0:
  17.6 76.1 all-gather.1
where the time goes:
time: 506 us; the launch traced here: 499 us
  local copies, waits for them, and re-layouts  123 us (24%)
  starting transfers between devices  120 us (24%)
  other arithmetic  79.4 us (16%)
  matrix products  70.6 us (14%)
  waiting for transfers between devices  68.2 us (13%)
  between operations  37.6 us (7%)
    broadcast_in_dim x52, local copies, waits for them, and re-layouts, band_matrix(): full = full + jnp.where(sel, m[:, None, :, None, :], 0.0)  91.8 us
    ppermute x16, starting transfers between devices, halo(): above = lax.ppermute(array[:width], axis, down)  88.7 us
    ppermute x16, waiting for transfers between devices, halo(): below = lax.ppermute(array[-width:], axis, up)  46 us
    ppermute x16, starting transfers between devices, halo(): below = lax.ppermute(array[-width:], axis, up)  31.1 us
    add x24, other arithmetic, band_matrix(): m = m + jnp.where((d == t)[None], taps[:, t, None, None], 0.0)  28.7 us
    dot_general x8, matrix products, per_device(): blurred = jnp.einsum('lix,lax->lia', t, bx, precision=exact_mode)  26.4 us
    dot_general x8, matrix products, per_device(): t = jnp.einsum('lij,ljx->lix', by, c, precision=exact_mode)  26.3 us
    add x2, other arithmetic, band_matrix(): full = full + jnp.where(sel, m[:, None, :, None, :], 0.0)  25 us
  transfers between devices with their start and end apart: 33, of which 25 were waited for; matrix products, arithmetic and copies ran while one was open for 36% of the time, Pallas kernels for 0%

commit v1 on v0

v1 whole, which is shorter than its diff:
```python
import jax
import jax.numpy as jnp
from jax import lax
from jax.sharding import PartitionSpec as P

RZ = 1


exact_mode = lax.Precision.HIGHEST


def halo(array, axis, width):
    size = lax.axis_size(axis)
    up = [(i, i + 1) for i in range(size - 1)]
    down = [(i + 1, i) for i in range(size - 1)]
    below = lax.ppermute(array[-width:], axis, up)
    above = lax.ppermute(array[:width], axis, down)
    return jnp.concatenate([below, array, above], axis=0)


def tap_matrix(taps, block):
    count = taps.shape[-1]
    width = block + count - 1
    rows = jnp.arange(block, dtype=jnp.int32)[:, None]
    cols = jnp.arange(width, dtype=jnp.int32)[None, :]
    offset = cols - rows
    picks = (offset[:, :, None] == jnp.arange(count, dtype=jnp.int32)[None, None, :]).astype(
        taps.dtype
    )
    return jnp.einsum("...t,abt->...ab", taps, picks, precision=exact_mode)


def band_matrix(taps, n):
    count = taps.shape[-1]
    reach = (count - 1) // 2
    block = min(128, n)
    mats = tap_matrix(taps, block)
    lead = taps.shape[:-1]
    rows = []
    for blk in range(n // block):
        start = blk * block - reach
        lo = max(start, 0)
        hi = min(start + block + 2 * reach, n)
        piece = mats[..., lo - start : hi - start]
        parts = []
        if lo > 0:
            parts.append(jnp.zeros(lead + (block, lo), taps.dtype))
        parts.append(piece)
        if hi < n:
            parts.append(jnp.zeros(lead + (block, n - hi), taps.dtype))
        rows.append(jnp.concatenate(parts, axis=-1))
    return jnp.concatenate(rows, axis=-2)


def per_device(estimate, view_data, background, psf_xy, psf_z, view_order, depth_index):
    view_count = lax.axis_size("view")
    my_view = lax.axis_index("view")
    xy_kernels = psf_xy / jnp.sum(psf_xy, axis=-1, keepdims=True)
    z_kernels = psf_z / jnp.sum(psf_z, axis=-1, keepdims=True)
    data_all = lax.all_gather(view_data[0], "view", axis=0)
    count, ny, nx = estimate.shape
    step_taps = jnp.take(jnp.take(xy_kernels, view_order, axis=0), depth_index, axis=1)
    by_all = band_matrix(step_taps[:, :, 0], ny)
    bx_all = band_matrix(step_taps[:, :, 1], nx)
    current = estimate
    results = jnp.zeros_like(estimate)
    for position in range(view_count):
        view_id = view_order[position]
        by = by_all[position]
        bx = bx_all[position]
        kz = lax.dynamic_index_in_dim(z_kernels, view_id, 0, keepdims=False)
        offset = lax.dynamic_index_in_dim(background, view_id, 0, keepdims=False)
        data = lax.dynamic_index_in_dim(data_all, view_id, 0, keepdims=False)
        padded = halo(current, "slab", RZ)
        c = kz[0] * padded[0:count]
        for k in range(1, 3):
            c = c + kz[k] * padded[k : k + count]
        t = jnp.einsum("lij,ljx->lix", by, c, precision=exact_mode)
        blurred = jnp.einsum("lix,lax->lia", t, bx, precision=exact_mode)
        quotient = data / (blurred + offset)
        u = jnp.einsum("lji,ljx->lix", by, quotient, precision=exact_mode)
        g = jnp.einsum("lix,lxa->lia", u, bx, precision=exact_mode)
        gp = halo(g, "slab", RZ)
        corr = kz[0] * gp[2 : 2 + count]
        for k in range(1, 3):
            corr = corr + kz[k] * gp[2 - k : 2 - k + count]
        current = current * corr
        results = jnp.where(my_view == view_id, current, results)
    return results[None]


def solution(mesh):
    return jax.shard_map(
        per_device,
        mesh=mesh,
        in_specs=(
            P("slab", None, None),
            P("view", "slab", None, None),
            P(),
            P(),
            P(),
            P(),
            P("slab"),
        ),
        out_specs=P("view", "slab", None, None),
        check_vma=False,
    )
```

time: 506 us -> 437 us (0.86)
  local copies, waits for them, and re-layouts: 123 us -> 75.7 us
  other arithmetic: 79.4 us -> 49.1 us
  waiting for transfers between devices: 68.2 us -> 79.6 us
  starting transfers between devices: 120 us -> 127 us
  matrix products: 70.6 us -> 64 us
    broadcast_in_dim x52 -> x0, local copies, waits for them, and re-layouts: 91.8 us -> none  [band_matrix(): full = full + jnp.where(sel, m[:, None, :, None, :], 0.0)]
    add x28 -> x0, other arithmetic: 53.7 us -> none  [the longest x24 28.7 us: band_matrix(): m = m + jnp.where((d == t)[None], taps[:, t, None, None], 0.0)]
    slice x20 -> x3, local copies, waits for them, and re-layouts: 11.6 us -> 64.9 us  [the longest x1 58.4 us: per_device(): bx = bx_all[position]]
    concatenate x0 -> x1, other arithmetic: none -> 25.5 us  [band_matrix(): return jnp.concatenate(rows, axis=-2)]
    ppermute x16, waiting for transfers between devices: 46 us -> 55.7 us  [halo(): below = lax.ppermute(array[-width:], axis, up)]
    dot_general x8, matrix products: 26.4 us -> 17.4 us  [per_device(): blurred = jnp.einsum('lix,lax->lia', t, bx, precision=exact_mode)]
    dot_general x16 -> x18, matrix products: 17.9 us -> 25.4 us  [the longest x8 18.2 us: per_device(): g = jnp.einsum('lix,lxa->lia', u, bx, precision=exact_mode)]
    ppermute x16, starting transfers between devices: 88.7 us -> 95.4 us  [halo(): above = lax.ppermute(array[:width], axis, down)]
  transfers between devices with their start and end apart: 33 -> 33, of which waited for: 25 -> 28; matrix products, arithmetic and copies ran while one was open for 36% -> 25% of each run, Pallas kernels for 0% -> 0%
where the time goes in v1:
time: 437 us; the launch traced here: 431 us
  starting transfers between devices  127 us (29%)
  waiting for transfers between devices  79.6 us (18%)
  local copies, waits for them, and re-layouts  75.7 us (17%)
  matrix products  64 us (15%)
  other arithmetic  49.1 us (11%)
  between operations  35.7 us (8%)
    ppermute x16, starting transfers between devices, halo(): above = lax.ppermute(array[:width], axis, down)  95.4 us
    slice x1, local copies, waits for them, and re-layouts, per_device(): bx = bx_all[position]  58.4 us
    ppermute x16, waiting for transfers between devices, halo(): below = lax.ppermute(array[-width:], axis, up)  55.7 us
    ppermute x16, starting transfers between devices, halo(): below = lax.ppermute(array[-width:], axis, up)  31.8 us
    concatenate x1, other arithmetic, band_matrix(): return jnp.concatenate(rows, axis=-2)  25.5 us
    ppermute x16, waiting for transfers between devices, halo(): above = lax.ppermute(array[:width], axis, down)  23.9 us
    dot_general x8, matrix products, per_device(): t = jnp.einsum('lij,ljx->lix', by, c, precision=exact_mode)  21.2 us
    dot_general x8, matrix products, per_device(): g = jnp.einsum('lix,lxa->lia', u, bx, precision=exact_mode)  18.2 us
  transfers between devices with their start and end apart: 33, of which 28 were waited for; matrix products, arithmetic and copies ran while one was open for 25% of the time, Pallas kernels for 0%

profile of v1, /device:TPU:2, one launch (start us, length us, event | category | flops | bytes accessed | tf_op | source)
XLA Modules:
  0.0 431.4 jit_solution(16777150510526966137)
XLA Ops:
  8.4 7.2 %collective-permute-start.1 = (f32[1,128,512]{2,1,0:T(8,128)}, f32[1,128,512]{2,1,0:T(8,128)S(1)}, u32[]{:S(2)}, u32[]{:S(2)}) collective-permute-start(f32[1,128,512]{2,1,0:T(8,128)} %get-tuple-element.54), channel_id=1, source_target_pairs={{1,0},{2,1},{3,2},{4,3},{5,4},{6,5},{7,6},{8,7},{9,8},{10,9},{11,1... | collective-permute-start | bytes 786440 | tf_op jit(solution)/shard_map/ppermute | solution.py:17
  45.9 25.5 %select_maximum_fusion = f32[8,2,512,512]{2,0,3,1:T(8,128)} fusion(f32[8,2,128,136]{2,0,3,1:T(8,128)S(1)} %get-tuple-element.22, f32[8,2,128,136]{2,0,3,1:T(8,128)S(1)} %get-tuple-element.21, f32[8,2,128,120]{2,0,3,1:T(8,128)S(1)} %broadcast.40, f32[8,2,128,144]{2,0,3,1:T(8,128)S(1)} %fusion.50, f32[8,2,128,248]{2,0,3,1:T(8,128)S(1)} %broadcast.41), kind=kLoop, calls=%fused_computation.2 | loop fusion | flops 46137344 | bytes 23199744 | tf_op jit(solution)/shard_map/concatenate | solution.py:52
  71.4 58.4 %fusion.259 = (f32[1,2,512,512]{2,0,3,1:T(1,128)S(1)}, f32[1,2,512,512]{2,0,3,1:T(1,128)}, f32[1,2,512,512]{2,0,3,1:T(1,128)}, f32[1,2,512,512]{2,0,3,1:T(1,128)...) fusion(f32[8,2,512,512]{2,0,3,1:T(8,128)} %select_maximum_fusion), kind=kLoop, calls=%fused_computation.269 | loop fusion | bytes 33554432 | tf_op jit(solution)/shard_map/slice | solution.py:70
  129.8 6.4 %fusion.260 = (f32[1,2,128,128]{2,0,3,1:T(1,128)S(1)}, f32[1,2,128,128]{2,0,3,1:T(1,128)S(1)}, f32[1,2,128,128]{2,0,3,1:T(1,128)S(1)}, f32[1,2,128,128]{2,0,3,1:...) fusion(f32[8,2,128,144]{2,0,3,1:T(8,128)} %fusion.52), kind=kLoop, calls=%fused_computation.270 | loop fusion | bytes 2097152 | tf_op jit(solution)/shard_map/slice | solution.py:69
  136.9 3.6 fusion.211
  140.6 3.7 fusion.57
  145.0 2.3 fusion.29
  149.3 5.9 %collective-permute-start.2 = (f32[1,128,512]{2,1,0:T(8,128)S(1)}, f32[1,128,512]{2,1,0:T(8,128)S(1)}, u32[]{:S(2)}, u32[]{:S(2)}) collective-permute-start(f32[1,128,512]{2,1,0:T(8,128)S(1)} %get-tuple-element.51), channel_id=1, source_target_pairs={{1,0},{2,1},{3,2},{4,3},{5,4},{6,5},{7,6},{8,7},{9,8},{10,9},{11,1... | collective-permute-start | bytes 786440 | tf_op jit(solution)/shard_map/ppermute | solution.py:17
  161.2 5.9 %collective-permute-start.5 = (f32[1,128,512]{2,1,0:T(8,128)S(1)}, f32[1,128,512]{2,1,0:T(8,128)S(1)}, u32[]{:S(2)}, u32[]{:S(2)}) collective-permute-start(f32[1,128,512]{2,1,0:T(8,128)S(1)} %get-tuple-element.50), channel_id=1, source_target_pairs={{1,0},{2,1},{3,2},{4,3},{5,4},{6,5},{7,6},{8,7},{9,8},{10,9},{11,1... | collective-permute-start | bytes 786440 | tf_op jit(solution)/shard_map/ppermute | solution.py:17
  167.1 2.2 collective-permute-start.4
  171.0 6.2 %collective-permute-done.4 = f32[1,128,512]{2,1,0:T(8,128)S(1)} collective-permute-done((f32[1,128,512]{2,1,0:T(8,128)S(1)}, f32[1,128,512]{2,1,0:T(8,128)S(1)}, u32[]{:S(2)}, u32[]{:S(2)}) %collective-permute-start.4) | collective-permute-done | bytes 262176 | tf_op jit(solution)/shard_map/ppermute | solution.py:16
  177.2 2.6 fusion.197
  182.2 2.3 fusion.25
  186.5 5.9 %collective-permute-start.6 = (f32[1,128,512]{2,1,0:T(8,128)S(1)}, f32[1,128,512]{2,1,0:T(8,128)S(1)}, u32[]{:S(2)}, u32[]{:S(2)}) collective-permute-start(f32[1,128,512]{2,1,0:T(8,128)S(1)} %get-tuple-element.47), channel_id=1, source_target_pairs={{1,0},{2,1},{3,2},{4,3},{5,4},{6,5},{7,6},{8,7},{9,8},{10,9},{11,1... | collective-permute-start | bytes 786440 | tf_op jit(solution)/shard_map/ppermute | solution.py:17
  198.4 5.9 %collective-permute-start.9 = (f32[1,128,512]{2,1,0:T(8,128)S(1)}, f32[1,128,512]{2,1,0:T(8,128)S(1)}, u32[]{:S(2)}, u32[]{:S(2)}) collective-permute-start(f32[1,128,512]{2,1,0:T(8,128)S(1)} %get-tuple-element.46), channel_id=1, source_target_pairs={{1,0},{2,1},{3,2},{4,3},{5,4},{6,5},{7,6},{8,7},{9,8},{10,9},{11,1... | collective-permute-start | bytes 786440 | tf_op jit(solution)/shard_map/ppermute | solution.py:17
  208.2 5.9 %collective-permute-done.8 = f32[1,128,512]{2,1,0:T(8,128)S(1)} collective-permute-done((f32[1,128,512]{2,1,0:T(8,128)S(1)}, f32[1,128,512]{2,1,0:T(8,128)S(1)}, u32[]{:S(2)}, u32[]{:S(2)}) %collective-permute-start.8) | collective-permute-done | bytes 262176 | tf_op jit(solution)/shard_map/ppermute | solution.py:16
  214.1 2.5 fusion.183
  219.2 2.3 fusion.21
  223.5 5.9 %collective-permute-start.10 = (f32[1,128,512]{2,1,0:T(8,128)S(1)}, f32[1,128,512]{2,1,0:T(8,128)S(1)}, u32[]{:S(2)}, u32[]{:S(2)}) collective-permute-start(f32[1,128,512]{2,1,0:T(8,128)S(1)} %get-tuple-element.43), channel_id=1, source_target_pairs={{1,0},{2,1},{3,2},{4,3},{5,4},{6,5},{7,6},{8,7},{9,8},{10,9},{11,1... | collective-permute-start | bytes 786440 | tf_op jit(solution)/shard_map/ppermute | solution.py:17
  235.3 5.9 %collective-permute-start.13 = (f32[1,128,512]{2,1,0:T(8,128)S(1)}, f32[1,128,512]{2,1,0:T(8,128)S(1)}, u32[]{:S(2)}, u32[]{:S(2)}) collective-permute-start(f32[1,128,512]{2,1,0:T(8,128)S(1)} %get-tuple-element.42), channel_id=1, source_target_pairs={{1,0},{2,1},{3,2},{4,3},{5,4},{6,5},{7,6},{8,7},{9,8},{10,9},{11,1... | collective-permute-start | bytes 786440 | tf_op jit(solution)/shard_map/ppermute | solution.py:17
  241.2 2.4 collective-permute-start.12
  245.1 5.9 %collective-permute-done.12 = f32[1,128,512]{2,1,0:T(8,128)S(1)} collective-permute-done((f32[1,128,512]{2,1,0:T(8,128)S(1)}, f32[1,128,512]{2,1,0:T(8,128)S(1)}, u32[]{:S(2)}, u32[]{:S(2)}) %collective-permute-start.12) | collective-permute-done | bytes 262176 | tf_op jit(solution)/shard_map/ppermute | solution.py:16
  251.0 2.5 fusion.169
  256.0 2.3 fusion.17
  260.3 5.9 %collective-permute-start.14 = (f32[1,128,512]{2,1,0:T(8,128)S(1)}, f32[1,128,512]{2,1,0:T(8,128)S(1)}, u32[]{:S(2)}, u32[]{:S(2)}) collective-permute-start(f32[1,128,512]{2,1,0:T(8,128)S(1)} %get-tuple-element.39), channel_id=1, source_target_pairs={{1,0},{2,1},{3,2},{4,3},{5,4},{6,5},{7,6},{8,7},{9,8},{10,9},{11,1... | collective-permute-start | bytes 786440 | tf_op jit(solution)/shard_map/ppermute | solution.py:17
  272.1 5.9 %collective-permute-start.17 = (f32[1,128,512]{2,1,0:T(8,128)S(1)}, f32[1,128,512]{2,1,0:T(8,128)S(1)}, u32[]{:S(2)}, u32[]{:S(2)}) collective-permute-start(f32[1,128,512]{2,1,0:T(8,128)S(1)} %get-tuple-element.38), channel_id=1, source_target_pairs={{1,0},{2,1},{3,2},{4,3},{5,4},{6,5},{7,6},{8,7},{9,8},{10,9},{11,1... | collective-permute-start | bytes 786440 | tf_op jit(solution)/shard_map/ppermute | solution.py:17
  281.9 5.9 %collective-permute-done.16 = f32[1,128,512]{2,1,0:T(8,128)S(1)} collective-permute-done((f32[1,128,512]{2,1,0:T(8,128)S(1)}, f32[1,128,512]{2,1,0:T(8,128)S(1)}, u32[]{:S(2)}, u32[]{:S(2)}) %collective-permute-start.16) | collective-permute-done | bytes 262176 | tf_op jit(solution)/shard_map/ppermute | solution.py:16
  287.9 2.4 fusion.155
  292.9 2.3 fusion.13
  297.2 5.9 %collective-permute-start.18 = (f32[1,128,512]{2,1,0:T(8,128)S(1)}, f32[1,128,512]{2,1,0:T(8,128)S(1)}, u32[]{:S(2)}, u32[]{:S(2)}) collective-permute-start(f32[1,128,512]{2,1,0:T(8,128)S(1)} %get-tuple-element.35), channel_id=1, source_target_pairs={{1,0},{2,1},{3,2},{4,3},{5,4},{6,5},{7,6},{8,7},{9,8},{10,9},{11,1... | collective-permute-start | bytes 786440 | tf_op jit(solution)/shard_map/ppermute | solution.py:17
  308.9 5.9 %collective-permute-start.21 = (f32[1,128,512]{2,1,0:T(8,128)S(1)}, f32[1,128,512]{2,1,0:T(8,128)S(1)}, u32[]{:S(2)}, u32[]{:S(2)}) collective-permute-start(f32[1,128,512]{2,1,0:T(8,128)S(1)} %get-tuple-element.34), channel_id=1, source_target_pairs={{1,0},{2,1},{3,2},{4,3},{5,4},{6,5},{7,6},{8,7},{9,8},{10,9},{11,1... | collective-permute-start | bytes 786440 | tf_op jit(solution)/shard_map/ppermute | solution.py:17
  318.7 5.9 %collective-permute-done.20 = f32[1,128,512]{2,1,0:T(8,128)S(1)} collective-permute-done((f32[1,128,512]{2,1,0:T(8,128)S(1)}, f32[1,128,512]{2,1,0:T(8,128)S(1)}, u32[]{:S(2)}, u32[]{:S(2)}) %collective-permute-start.20) | collective-permute-done | bytes 262176 | tf_op jit(solution)/shard_map/ppermute | solution.py:16
  324.6 2.5 fusion.141
  329.7 2.3 fusion.9
  334.0 5.9 %collective-permute-start.22 = (f32[1,128,512]{2,1,0:T(8,128)S(1)}, f32[1,128,512]{2,1,0:T(8,128)S(1)}, u32[]{:S(2)}, u32[]{:S(2)}) collective-permute-start(f32[1,128,512]{2,1,0:T(8,128)S(1)} %get-tuple-element.31), channel_id=1, source_target_pairs={{1,0},{2,1},{3,2},{4,3},{5,4},{6,5},{7,6},{8,7},{9,8},{10,9},{11,1... | collective-permute-start | bytes 786440 | tf_op jit(solution)/shard_map/ppermute | solution.py:17
  345.8 5.9 %collective-permute-start.25 = (f32[1,128,512]{2,1,0:T(8,128)S(1)}, f32[1,128,512]{2,1,0:T(8,128)S(1)}, u32[]{:S(2)}, u32[]{:S(2)}) collective-permute-start(f32[1,128,512]{2,1,0:T(8,128)S(1)} %get-tuple-element.30), channel_id=1, source_target_pairs={{1,0},{2,1},{3,2},{4,3},{5,4},{6,5},{7,6},{8,7},{9,8},{10,9},{11,1... | collective-permute-start | bytes 786440 | tf_op jit(solution)/shard_map/ppermute | solution.py:17
  355.6 5.9 %collective-permute-done.24 = f32[1,128,512]{2,1,0:T(8,128)S(1)} collective-permute-done((f32[1,128,512]{2,1,0:T(8,128)S(1)}, f32[1,128,512]{2,1,0:T(8,128)S(1)}, u32[]{:S(2)}, u32[]{:S(2)}) %collective-permute-start.24) | collective-permute-done | bytes 262176 | tf_op jit(solution)/shard_map/ppermute | solution.py:16
  361.6 2.6 fusion.127
  366.8 2.3 fusion.5
  371.0 5.8 %collective-permute-start.26 = (f32[1,128,512]{2,1,0:T(8,128)S(1)}, f32[1,128,512]{2,1,0:T(8,128)S(1)}, u32[]{:S(2)}, u32[]{:S(2)}) collective-permute-start(f32[1,128,512]{2,1,0:T(8,128)S(1)} %get-tuple-element.27), channel_id=1, source_target_pairs={{1,0},{2,1},{3,2},{4,3},{5,4},{6,5},{7,6},{8,7},{9,8},{10,9},{11,1... | collective-permute-start | bytes 786440 | tf_op jit(solution)/shard_map/ppermute | solution.py:17
  380.7 2.1 fusion.122
  382.8 5.9 %collective-permute-start.29 = (f32[1,128,512]{2,1,0:T(8,128)S(1)}, f32[1,128,512]{2,1,0:T(8,128)S(1)}, u32[]{:S(2)}, u32[]{:S(2)}) collective-permute-start(f32[1,128,512]{2,1,0:T(8,128)S(1)} %get-tuple-element.26), channel_id=1, source_target_pairs={{1,0},{2,1},{3,2},{4,3},{5,4},{6,5},{7,6},{8,7},{9,8},{10,9},{11,1... | collective-permute-start | bytes 786440 | tf_op jit(solution)/shard_map/ppermute | solution.py:17
  388.8 2.1 collective-permute-start.28
  392.6 5.9 %collective-permute-done.28 = f32[1,128,512]{2,1,0:T(8,128)S(1)} collective-permute-done((f32[1,128,512]{2,1,0:T(8,128)S(1)}, f32[1,128,512]{2,1,0:T(8,128)S(1)}, u32[]{:S(2)}, u32[]{:S(2)}) %collective-permute-start.28) | collective-permute-done | bytes 262176 | tf_op jit(solution)/shard_map/ppermute | solution.py:16
  398.6 2.5 fusion.113
  403.6 2.3 fusion.1
  408.7 5.8 %collective-permute-start.30 = (f32[1,128,512]{2,1,0:T(8,128)S(1)}, f32[1,128,512]{2,1,0:T(8,128)S(1)}, u32[]{:S(2)}, u32[]{:S(2)}) collective-permute-start(f32[1,128,512]{2,1,0:T(8,128)S(1)} %get-tuple-element.23), channel_id=1, source_target_pairs={{1,0},{2,1},{3,2},{4,3},{5,4},{6,5},{7,6},{8,7},{9,8},{10,9},{11,1... | collective-permute-start | bytes 786440 | tf_op jit(solution)/shard_map/ppermute | solution.py:17
  419.7 4.6 %fusion.108 = f32[1,2,128,512]{3,2,1,0:T(8,128)} fusion(f32[2,128,512]{2,1,0:T(8,128)} %copy-done.11, f32[2,128,512]{2,1,0:T(8,128)} %copy-done.13, f32[1,128,512]{2,1,0:T(8,128)S(1)} %collective-permute-done.31, f32[1,128,512]{2,1,0:T(8,128)S(1)} %collective-permute-done.30, f32[2,128,512]{2,1,0:T(8,128)} %copy-done.10, f32[2,128,512]{2,1,0:T(8,128)} %copy-done.9, ...), kind=kLoop, calls=%fused_computation.82 | loop fusion | flops 2097152 | bytes 5242900 | tf_op jit(solution)/shard_map/broadcast_in_dim | solution.py:89
  (159 shorter events, 111.7 us)
Async XLA Ops:
  6.5 34.5 %copy-start.22 = (f32[8]{0:T(128)S(1)}, f32[8]{0:T(128)}, u32[]{:S(2)}) copy-start(f32[8]{0:T(128)} %param.9) | copy-start | bytes 100
  6.5 134.1 %all-gather.2.cloned.1.call-start = ((), (), s32[]{:S(2)}) async-start(), calls=%async_computation | async-start | bytes 4718592 | tf_op jit(solution)/shard_map/all_gather | solution.py:60
  8.4 127.8 %collective-permute-start.1 = (f32[1,128,512]{2,1,0:T(8,128)}, f32[1,128,512]{2,1,0:T(8,128)S(1)}, u32[]{:S(2)}, u32[]{:S(2)}) collective-permute-start(f32[1,128,512]{2,1,0:T(8,128)} %get-tuple-element.54), channel_id=1, source_target_pairs={{1,0},{2,1},{3,2},{4,3},{5,4},{6,5},{7,6},{8,7},{9,8},{10,9},{11,1... | collective-permute-start | bytes 786440 | tf_op jit(solution)/shard_map/ppermute | solution.py:17
  15.6 120.6 %collective-permute-start = (f32[1,128,512]{2,1,0:T(8,128)}, f32[1,128,512]{2,1,0:T(8,128)}, u32[]{:S(2)}, u32[]{:S(2)}) collective-permute-start(f32[1,128,512]{2,1,0:T(8,128)} %get-tuple-element.53), channel_id=1, source_target_pairs={{0,1},{1,2},{2,3},{3,4},{4,5},{5,6},{6,7},{7,8},{8,9},{9,10},{10,1... | collective-permute-start | bytes 786440 | tf_op jit(solution)/shard_map/ppermute | solution.py:16
  145.0 34.8 %copy-start.14 = (f32[8,2,128,512]{3,2,1,0:T(8,128)S(1)}, f32[8,2,128,512]{3,2,1,0:T(8,128)}, u32[]{:S(2)}) copy-start(f32[8,2,128,512]{3,2,1,0:T(8,128)} %all-gather.2.cloned.1.call-done) | copy-start | bytes 12582916
  147.3 29.9 %copy-start.18 = (f32[1,2,128,128]{2,0,3,1:T(1,128)S(1)}, f32[1,2,128,128]{2,0,3,1:T(1,128)}, u32[]{:S(2)}) copy-start(f32[1,2,128,128]{2,0,3,1:T(1,128)} %get-tuple-element.19) | copy-start | bytes 393220
  147.3 9.8 %collective-permute-start.3 = (f32[1,128,512]{2,1,0:T(8,128)S(1)}, f32[1,128,512]{2,1,0:T(8,128)S(1)}, u32[]{:S(2)}, u32[]{:S(2)}) collective-permute-start(f32[1,128,512]{2,1,0:T(8,128)S(1)} %get-tuple-element.52), channel_id=1, source_target_pairs={{0,1},{1,2},{2,3},{3,4},{4,5},{5,6},{6,7},{7,8},{8,9},{9,10},{10,1... | collective-permute-start | bytes 786440 | tf_op jit(solution)/shard_map/ppermute | solution.py:16
  149.3 30.5 %copy-start.5 = (f32[1,2,512,512]{2,0,3,1:T(1,128)S(1)}, f32[1,2,512,512]{2,0,3,1:T(1,128)}, u32[]{:S(2)}) copy-start(f32[1,2,512,512]{2,0,3,1:T(1,128)} %get-tuple-element.11) | copy-start | bytes 6291460
  149.3 9.8 %collective-permute-start.2 = (f32[1,128,512]{2,1,0:T(8,128)S(1)}, f32[1,128,512]{2,1,0:T(8,128)S(1)}, u32[]{:S(2)}, u32[]{:S(2)}) collective-permute-start(f32[1,128,512]{2,1,0:T(8,128)S(1)} %get-tuple-element.51), channel_id=1, source_target_pairs={{1,0},{2,1},{3,2},{4,3},{5,4},{6,5},{7,6},{8,7},{9,8},{10,9},{11,1... | collective-permute-start | bytes 786440 | tf_op jit(solution)/shard_map/ppermute | solution.py:17
  161.2 9.8 %collective-permute-start.5 = (f32[1,128,512]{2,1,0:T(8,128)S(1)}, f32[1,128,512]{2,1,0:T(8,128)S(1)}, u32[]{:S(2)}, u32[]{:S(2)}) collective-permute-start(f32[1,128,512]{2,1,0:T(8,128)S(1)} %get-tuple-element.50), channel_id=1, source_target_pairs={{1,0},{2,1},{3,2},{4,3},{5,4},{6,5},{7,6},{8,7},{9,8},{10,9},{11,1... | collective-permute-start | bytes 786440 | tf_op jit(solution)/shard_map/ppermute | solution.py:17
  167.1 10.1 %collective-permute-start.4 = (f32[1,128,512]{2,1,0:T(8,128)S(1)}, f32[1,128,512]{2,1,0:T(8,128)S(1)}, u32[]{:S(2)}, u32[]{:S(2)}) collective-permute-start(f32[1,128,512]{2,1,0:T(8,128)S(1)} %get-tuple-element.49), channel_id=1, source_target_pairs={{0,1},{1,2},{2,3},{3,4},{4,5},{5,6},{6,7},{7,8},{8,9},{9,10},{10,1... | collective-permute-start | bytes 786440 | tf_op jit(solution)/shard_map/ppermute | solution.py:16
  184.5 29.6 %copy-start.17 = (f32[1,2,128,128]{2,0,3,1:T(1,128)S(1)}, f32[1,2,128,128]{2,0,3,1:T(1,128)}, u32[]{:S(2)}) copy-start(f32[1,2,128,128]{2,0,3,1:T(1,128)} %get-tuple-element.18) | copy-start | bytes 393220
  184.6 9.8 %collective-permute-start.7 = (f32[1,128,512]{2,1,0:T(8,128)S(1)}, f32[1,128,512]{2,1,0:T(8,128)S(1)}, u32[]{:S(2)}, u32[]{:S(2)}) collective-permute-start(f32[1,128,512]{2,1,0:T(8,128)S(1)} %get-tuple-element.48), channel_id=1, source_target_pairs={{0,1},{1,2},{2,3},{3,4},{4,5},{5,6},{6,7},{7,8},{8,9},{9,10},{10,1... | collective-permute-start | bytes 786440 | tf_op jit(solution)/shard_map/ppermute | solution.py:16
  186.5 30.1 %copy-start.4 = (f32[1,2,512,512]{2,0,3,1:T(1,128)S(1)}, f32[1,2,512,512]{2,0,3,1:T(1,128)}, u32[]{:S(2)}) copy-start(f32[1,2,512,512]{2,0,3,1:T(1,128)} %get-tuple-element.10) | copy-start | bytes 6291460
  186.5 9.8 %collective-permute-start.6 = (f32[1,128,512]{2,1,0:T(8,128)S(1)}, f32[1,128,512]{2,1,0:T(8,128)S(1)}, u32[]{:S(2)}, u32[]{:S(2)}) collective-permute-start(f32[1,128,512]{2,1,0:T(8,128)S(1)} %get-tuple-element.47), channel_id=1, source_target_pairs={{1,0},{2,1},{3,2},{4,3},{5,4},{6,5},{7,6},{8,7},{9,8},{10,9},{11,1... | collective-permute-start | bytes 786440 | tf_op jit(solution)/shard_map/ppermute | solution.py:17
  198.4 9.8 %collective-permute-start.9 = (f32[1,128,512]{2,1,0:T(8,128)S(1)}, f32[1,128,512]{2,1,0:T(8,128)S(1)}, u32[]{:S(2)}, u32[]{:S(2)}) collective-permute-start(f32[1,128,512]{2,1,0:T(8,128)S(1)} %get-tuple-element.46), channel_id=1, source_target_pairs={{1,0},{2,1},{3,2},{4,3},{5,4},{6,5},{7,6},{8,7},{9,8},{10,9},{11,1... | collective-permute-start | bytes 786440 | tf_op jit(solution)/shard_map/ppermute | solution.py:17
  204.3 9.8 %collective-permute-start.8 = (f32[1,128,512]{2,1,0:T(8,128)S(1)}, f32[1,128,512]{2,1,0:T(8,128)S(1)}, u32[]{:S(2)}, u32[]{:S(2)}) collective-permute-start(f32[1,128,512]{2,1,0:T(8,128)S(1)} %get-tuple-element.45), channel_id=1, source_target_pairs={{0,1},{1,2},{2,3},{3,4},{4,5},{5,6},{6,7},{7,8},{8,9},{9,10},{10,1... | collective-permute-start | bytes 786440 | tf_op jit(solution)/shard_map/ppermute | solution.py:16
  221.6 9.8 %collective-permute-start.11 = (f32[1,128,512]{2,1,0:T(8,128)S(1)}, f32[1,128,512]{2,1,0:T(8,128)S(1)}, u32[]{:S(2)}, u32[]{:S(2)}) collective-permute-start(f32[1,128,512]{2,1,0:T(8,128)S(1)} %get-tuple-element.44), channel_id=1, source_target_pairs={{0,1},{1,2},{2,3},{3,4},{4,5},{5,6},{6,7},{7,8},{8,9},{9,10},{10,1... | collective-permute-start | bytes 786440 | tf_op jit(solution)/shard_map/ppermute | solution.py:16
  223.5 30.0 %copy-start.3 = (f32[1,2,512,512]{2,0,3,1:T(1,128)S(1)}, f32[1,2,512,512]{2,0,3,1:T(1,128)}, u32[]{:S(2)}) copy-start(f32[1,2,512,512]{2,0,3,1:T(1,128)} %get-tuple-element.9) | copy-start | bytes 6291460
  223.5 9.8 %collective-permute-start.10 = (f32[1,128,512]{2,1,0:T(8,128)S(1)}, f32[1,128,512]{2,1,0:T(8,128)S(1)}, u32[]{:S(2)}, u32[]{:S(2)}) collective-permute-start(f32[1,128,512]{2,1,0:T(8,128)S(1)} %get-tuple-element.43), channel_id=1, source_target_pairs={{1,0},{2,1},{3,2},{4,3},{5,4},{6,5},{7,6},{8,7},{9,8},{10,9},{11,1... | collective-permute-start | bytes 786440 | tf_op jit(solution)/shard_map/ppermute | solution.py:17
  235.2 34.8 %copy-start.7 = (f32[2,128,512]{2,1,0:T(8,128)}, f32[2,128,512]{2,1,0:T(8,128)S(1)}, u32[]{:S(2)}) copy-start(f32[2,128,512]{2,1,0:T(8,128)S(1)} %fusion.178) | copy-start | bytes 1572868
  235.3 9.8 %collective-permute-start.13 = (f32[1,128,512]{2,1,0:T(8,128)S(1)}, f32[1,128,512]{2,1,0:T(8,128)S(1)}, u32[]{:S(2)}, u32[]{:S(2)}) collective-permute-start(f32[1,128,512]{2,1,0:T(8,128)S(1)} %get-tuple-element.42), channel_id=1, source_target_pairs={{1,0},{2,1},{3,2},{4,3},{5,4},{6,5},{7,6},{8,7},{9,8},{10,9},{11,1... | collective-permute-start | bytes 786440 | tf_op jit(solution)/shard_map/ppermute | solution.py:17
  241.2 9.8 %collective-permute-start.12 = (f32[1,128,512]{2,1,0:T(8,128)S(1)}, f32[1,128,512]{2,1,0:T(8,128)S(1)}, u32[]{:S(2)}, u32[]{:S(2)}) collective-permute-start(f32[1,128,512]{2,1,0:T(8,128)S(1)} %get-tuple-element.41), channel_id=1, source_target_pairs={{0,1},{1,2},{2,3},{3,4},{4,5},{5,6},{6,7},{7,8},{8,9},{9,10},{10,1... | collective-permute-start | bytes 786440 | tf_op jit(solution)/shard_map/ppermute | solution.py:16
  258.3 29.5 %copy-start.15 = (f32[1,2,128,128]{2,0,3,1:T(1,128)S(1)}, f32[1,2,128,128]{2,0,3,1:T(1,128)}, u32[]{:S(2)}) copy-start(f32[1,2,128,128]{2,0,3,1:T(1,128)} %get-tuple-element.16) | copy-start | bytes 393220
  258.4 9.8 %collective-permute-start.15 = (f32[1,128,512]{2,1,0:T(8,128)S(1)}, f32[1,128,512]{2,1,0:T(8,128)S(1)}, u32[]{:S(2)}, u32[]{:S(2)}) collective-permute-start(f32[1,128,512]{2,1,0:T(8,128)S(1)} %get-tuple-element.40), channel_id=1, source_target_pairs={{0,1},{1,2},{2,3},{3,4},{4,5},{5,6},{6,7},{7,8},{8,9},{9,10},{10,1... | collective-permute-start | bytes 786440 | tf_op jit(solution)/shard_map/ppermute | solution.py:16
  260.3 30.0 %copy-start.2 = (f32[1,2,512,512]{2,0,3,1:T(1,128)S(1)}, f32[1,2,512,512]{2,0,3,1:T(1,128)}, u32[]{:S(2)}) copy-start(f32[1,2,512,512]{2,0,3,1:T(1,128)} %get-tuple-element.8) | copy-start | bytes 6291460
  260.3 9.8 %collective-permute-start.14 = (f32[1,128,512]{2,1,0:T(8,128)S(1)}, f32[1,128,512]{2,1,0:T(8,128)S(1)}, u32[]{:S(2)}, u32[]{:S(2)}) collective-permute-start(f32[1,128,512]{2,1,0:T(8,128)S(1)} %get-tuple-element.39), channel_id=1, source_target_pairs={{1,0},{2,1},{3,2},{4,3},{5,4},{6,5},{7,6},{8,7},{9,8},{10,9},{11,1... | collective-permute-start | bytes 786440 | tf_op jit(solution)/shard_map/ppermute | solution.py:17
  272.1 34.8 %copy-start.8 = (f32[2,128,512]{2,1,0:T(8,128)}, f32[2,128,512]{2,1,0:T(8,128)S(1)}, u32[]{:S(2)}) copy-start(f32[2,128,512]{2,1,0:T(8,128)S(1)} %fusion.164) | copy-start | bytes 1572868
  272.1 9.8 %collective-permute-start.17 = (f32[1,128,512]{2,1,0:T(8,128)S(1)}, f32[1,128,512]{2,1,0:T(8,128)S(1)}, u32[]{:S(2)}, u32[]{:S(2)}) collective-permute-start(f32[1,128,512]{2,1,0:T(8,128)S(1)} %get-tuple-element.38), channel_id=1, source_target_pairs={{1,0},{2,1},{3,2},{4,3},{5,4},{6,5},{7,6},{8,7},{9,8},{10,9},{11,1... | collective-permute-start | bytes 786440 | tf_op jit(solution)/shard_map/ppermute | solution.py:17
  278.1 9.8 %collective-permute-start.16 = (f32[1,128,512]{2,1,0:T(8,128)S(1)}, f32[1,128,512]{2,1,0:T(8,128)S(1)}, u32[]{:S(2)}, u32[]{:S(2)}) collective-permute-start(f32[1,128,512]{2,1,0:T(8,128)S(1)} %get-tuple-element.37), channel_id=1, source_target_pairs={{0,1},{1,2},{2,3},{3,4},{4,5},{5,6},{6,7},{7,8},{8,9},{9,10},{10,1... | collective-permute-start | bytes 786440 | tf_op jit(solution)/shard_map/ppermute | solution.py:16
  295.2 9.8 %collective-permute-start.19 = (f32[1,128,512]{2,1,0:T(8,128)S(1)}, f32[1,128,512]{2,1,0:T(8,128)S(1)}, u32[]{:S(2)}, u32[]{:S(2)}) collective-permute-start(f32[1,128,512]{2,1,0:T(8,128)S(1)} %get-tuple-element.36), channel_id=1, source_target_pairs={{0,1},{1,2},{2,3},{3,4},{4,5},{5,6},{6,7},{7,8},{8,9},{9,10},{10,1... | collective-permute-start | bytes 786440 | tf_op jit(solution)/shard_map/ppermute | solution.py:16
  297.1 30.0 %copy-start.1 = (f32[1,2,512,512]{2,0,3,1:T(1,128)S(1)}, f32[1,2,512,512]{2,0,3,1:T(1,128)}, u32[]{:S(2)}) copy-start(f32[1,2,512,512]{2,0,3,1:T(1,128)} %get-tuple-element.7) | copy-start | bytes 6291460
  297.2 9.8 %collective-permute-start.18 = (f32[1,128,512]{2,1,0:T(8,128)S(1)}, f32[1,128,512]{2,1,0:T(8,128)S(1)}, u32[]{:S(2)}, u32[]{:S(2)}) collective-permute-start(f32[1,128,512]{2,1,0:T(8,128)S(1)} %get-tuple-element.35), channel_id=1, source_target_pairs={{1,0},{2,1},{3,2},{4,3},{5,4},{6,5},{7,6},{8,7},{9,8},{10,9},{11,1... | collective-permute-start | bytes 786440 | tf_op jit(solution)/shard_map/ppermute | solution.py:17
  308.9 34.9 %copy-start.9 = (f32[2,128,512]{2,1,0:T(8,128)}, f32[2,128,512]{2,1,0:T(8,128)S(1)}, u32[]{:S(2)}) copy-start(f32[2,128,512]{2,1,0:T(8,128)S(1)} %fusion.150) | copy-start | bytes 1572868
  308.9 9.8 %collective-permute-start.21 = (f32[1,128,512]{2,1,0:T(8,128)S(1)}, f32[1,128,512]{2,1,0:T(8,128)S(1)}, u32[]{:S(2)}, u32[]{:S(2)}) collective-permute-start(f32[1,128,512]{2,1,0:T(8,128)S(1)} %get-tuple-element.34), channel_id=1, source_target_pairs={{1,0},{2,1},{3,2},{4,3},{5,4},{6,5},{7,6},{8,7},{9,8},{10,9},{11,1... | collective-permute-start | bytes 786440 | tf_op jit(solution)/shard_map/ppermute | solution.py:17
  314.8 9.8 %collective-permute-start.20 = (f32[1,128,512]{2,1,0:T(8,128)S(1)}, f32[1,128,512]{2,1,0:T(8,128)S(1)}, u32[]{:S(2)}, u32[]{:S(2)}) collective-permute-start(f32[1,128,512]{2,1,0:T(8,128)S(1)} %get-tuple-element.33), channel_id=1, source_target_pairs={{0,1},{1,2},{2,3},{3,4},{4,5},{5,6},{6,7},{7,8},{8,9},{9,10},{10,1... | collective-permute-start | bytes 786440 | tf_op jit(solution)/shard_map/ppermute | solution.py:16
  332.0 9.8 %collective-permute-start.23 = (f32[1,128,512]{2,1,0:T(8,128)S(1)}, f32[1,128,512]{2,1,0:T(8,128)S(1)}, u32[]{:S(2)}, u32[]{:S(2)}) collective-permute-start(f32[1,128,512]{2,1,0:T(8,128)S(1)} %get-tuple-element.32), channel_id=1, source_target_pairs={{0,1},{1,2},{2,3},{3,4},{4,5},{5,6},{6,7},{7,8},{8,9},{9,10},{10,1... | collective-permute-start | bytes 786440 | tf_op jit(solution)/shard_map/ppermute | solution.py:16
  334.0 30.2 %copy-start = (f32[1,2,512,512]{2,0,3,1:T(1,128)S(1)}, f32[1,2,512,512]{2,0,3,1:T(1,128)}, u32[]{:S(2)}) copy-start(f32[1,2,512,512]{2,0,3,1:T(1,128)} %get-tuple-element.6) | copy-start | bytes 6291460
  334.0 9.8 %collective-permute-start.22 = (f32[1,128,512]{2,1,0:T(8,128)S(1)}, f32[1,128,512]{2,1,0:T(8,128)S(1)}, u32[]{:S(2)}, u32[]{:S(2)}) collective-permute-start(f32[1,128,512]{2,1,0:T(8,128)S(1)} %get-tuple-element.31), channel_id=1, source_target_pairs={{1,0},{2,1},{3,2},{4,3},{5,4},{6,5},{7,6},{8,7},{9,8},{10,9},{11,1... | collective-permute-start | bytes 786440 | tf_op jit(solution)/shard_map/ppermute | solution.py:17
  345.8 34.9 %copy-start.10 = (f32[2,128,512]{2,1,0:T(8,128)}, f32[2,128,512]{2,1,0:T(8,128)S(1)}, u32[]{:S(2)}) copy-start(f32[2,128,512]{2,1,0:T(8,128)S(1)} %fusion.136) | copy-start | bytes 1572868
  345.8 9.8 %collective-permute-start.25 = (f32[1,128,512]{2,1,0:T(8,128)S(1)}, f32[1,128,512]{2,1,0:T(8,128)S(1)}, u32[]{:S(2)}, u32[]{:S(2)}) collective-permute-start(f32[1,128,512]{2,1,0:T(8,128)S(1)} %get-tuple-element.30), channel_id=1, source_target_pairs={{1,0},{2,1},{3,2},{4,3},{5,4},{6,5},{7,6},{8,7},{9,8},{10,9},{11,1... | collective-permute-start | bytes 786440 | tf_op jit(solution)/shard_map/ppermute | solution.py:17
  351.8 9.8 %collective-permute-start.24 = (f32[1,128,512]{2,1,0:T(8,128)S(1)}, f32[1,128,512]{2,1,0:T(8,128)S(1)}, u32[]{:S(2)}, u32[]{:S(2)}) collective-permute-start(f32[1,128,512]{2,1,0:T(8,128)S(1)} %get-tuple-element.29), channel_id=1, source_target_pairs={{0,1},{1,2},{2,3},{3,4},{4,5},{5,6},{6,7},{7,8},{8,9},{9,10},{10,1... | collective-permute-start | bytes 786440 | tf_op jit(solution)/shard_map/ppermute | solution.py:16
  369.1 9.8 %collective-permute-start.27 = (f32[1,128,512]{2,1,0:T(8,128)S(1)}, f32[1,128,512]{2,1,0:T(8,128)S(1)}, u32[]{:S(2)}, u32[]{:S(2)}) collective-permute-start(f32[1,128,512]{2,1,0:T(8,128)S(1)} %get-tuple-element.28), channel_id=1, source_target_pairs={{0,1},{1,2},{2,3},{3,4},{4,5},{5,6},{6,7},{7,8},{8,9},{9,10},{10,1... | collective-permute-start | bytes 786440 | tf_op jit(solution)/shard_map/ppermute | solution.py:16
  371.0 9.6 %collective-permute-start.26 = (f32[1,128,512]{2,1,0:T(8,128)S(1)}, f32[1,128,512]{2,1,0:T(8,128)S(1)}, u32[]{:S(2)}, u32[]{:S(2)}) collective-permute-start(f32[1,128,512]{2,1,0:T(8,128)S(1)} %get-tuple-element.27), channel_id=1, source_target_pairs={{1,0},{2,1},{3,2},{4,3},{5,4},{6,5},{7,6},{8,7},{9,8},{10,9},{11,1... | collective-permute-start | bytes 786440 | tf_op jit(solution)/shard_map/ppermute | solution.py:17
  382.8 9.8 %collective-permute-start.29 = (f32[1,128,512]{2,1,0:T(8,128)S(1)}, f32[1,128,512]{2,1,0:T(8,128)S(1)}, u32[]{:S(2)}, u32[]{:S(2)}) collective-permute-start(f32[1,128,512]{2,1,0:T(8,128)S(1)} %get-tuple-element.26), channel_id=1, source_target_pairs={{1,0},{2,1},{3,2},{4,3},{5,4},{6,5},{7,6},{8,7},{9,8},{10,9},{11,1... | collective-permute-start | bytes 786440 | tf_op jit(solution)/shard_map/ppermute | solution.py:17
  388.8 9.8 %collective-permute-start.28 = (f32[1,128,512]{2,1,0:T(8,128)S(1)}, f32[1,128,512]{2,1,0:T(8,128)S(1)}, u32[]{:S(2)}, u32[]{:S(2)}) collective-permute-start(f32[1,128,512]{2,1,0:T(8,128)S(1)} %get-tuple-element.25), channel_id=1, source_target_pairs={{0,1},{1,2},{2,3},{3,4},{4,5},{5,6},{6,7},{7,8},{8,9},{9,10},{10,1... | collective-permute-start | bytes 786440 | tf_op jit(solution)/shard_map/ppermute | solution.py:16
  406.7 12.9 %collective-permute-start.31 = (f32[1,128,512]{2,1,0:T(8,128)S(1)}, f32[1,128,512]{2,1,0:T(8,128)S(1)}, u32[]{:S(2)}, u32[]{:S(2)}) collective-permute-start(f32[1,128,512]{2,1,0:T(8,128)S(1)} %get-tuple-element.24), channel_id=1, source_target_pairs={{0,1},{1,2},{2,3},{3,4},{4,5},{5,6},{6,7},{7,8},{8,9},{9,10},{10,1... | collective-permute-start | bytes 786440 | tf_op jit(solution)/shard_map/ppermute | solution.py:16
  408.7 11.0 %collective-permute-start.30 = (f32[1,128,512]{2,1,0:T(8,128)S(1)}, f32[1,128,512]{2,1,0:T(8,128)S(1)}, u32[]{:S(2)}, u32[]{:S(2)}) collective-permute-start(f32[1,128,512]{2,1,0:T(8,128)S(1)} %get-tuple-element.23), channel_id=1, source_target_pairs={{1,0},{2,1},{3,2},{4,3},{5,4},{6,5},{7,6},{8,7},{9,8},{10,9},{11,1... | collective-permute-start | bytes 786440 | tf_op jit(solution)/shard_map/ppermute | solution.py:17
  (11 other events, 134.9 us)
Sparse Core Ops, SparseCore 0:
  17.7 75.2 all-gather.1

commit v2 on v1

v2 whole, which is shorter than its diff:
```python
import jax
import jax.numpy as jnp
from jax import lax
from jax.sharding import PartitionSpec as P

RZ = 1


exact_mode = lax.Precision.HIGHEST
blur_mode = lax.Precision.HIGH


def halo(array, axis, width):
    size = lax.axis_size(axis)
    up = [(i, i + 1) for i in range(size - 1)]
    down = [(i + 1, i) for i in range(size - 1)]
    below = lax.ppermute(array[-width:], axis, up)
    above = lax.ppermute(array[:width], axis, down)
    return jnp.concatenate([below, array, above], axis=0)


def tap_matrix(taps, block):
    count = taps.shape[-1]
    width = block + count - 1
    rows = jnp.arange(block, dtype=jnp.int32)[:, None]
    cols = jnp.arange(width, dtype=jnp.int32)[None, :]
    offset = cols - rows
    picks = (offset[:, :, None] == jnp.arange(count, dtype=jnp.int32)[None, None, :]).astype(
        taps.dtype
    )
    return jnp.einsum("...t,abt->...ab", taps, picks, precision=exact_mode)


def band_matrix(mats, n, reach):
    block = mats.shape[-2]
    lead = mats.shape[:-2]
    rows = []
    for blk in range(n // block):
        start = blk * block - reach
        lo = max(start, 0)
        hi = min(start + block + 2 * reach, n)
        parts = []
        if lo > 0:
            parts.append(jnp.zeros(lead + (block, lo), mats.dtype))
        parts.append(mats[..., lo - start : hi - start])
        if hi < n:
            parts.append(jnp.zeros(lead + (block, n - hi), mats.dtype))
        rows.append(jnp.concatenate(parts, axis=-1))
    return jnp.concatenate(rows, axis=-2)


def per_device(estimate, view_data, background, psf_xy, psf_z, view_order, depth_index):
    view_count = lax.axis_size("view")
    my_view = lax.axis_index("view")
    levels = psf_xy.shape[1]
    kernel_len = psf_xy.shape[3]
    reach = (kernel_len - 1) // 2
    xy_kernels = psf_xy / jnp.sum(psf_xy, axis=-1, keepdims=True)
    z_kernels = psf_z / jnp.sum(psf_z, axis=-1, keepdims=True)
    data_all = lax.all_gather(view_data[0], "view", axis=0)
    count, ny, nx = estimate.shape
    views = psf_xy.shape[0]
    view_hot = (view_order[:, None] == jnp.arange(views, dtype=jnp.int32)[None, :]).astype(
        jnp.float32
    )
    level_hot = (depth_index[:, None] == jnp.arange(levels, dtype=jnp.int32)[None, :]).astype(
        jnp.float32
    )
    step_kernels = jnp.einsum("pv,vdk->pdk", view_hot, xy_kernels.reshape(views, levels, -1),
                              precision=exact_mode)
    step_taps = jnp.einsum("ld,pdk->plk", level_hot, step_kernels, precision=exact_mode)
    step_taps = step_taps.reshape(view_count, count, 2, kernel_len)
    mats_y = lax.optimization_barrier(tap_matrix(step_taps[:, :, 0], min(128, ny)))
    mats_x = lax.optimization_barrier(tap_matrix(step_taps[:, :, 1], min(128, nx)))
    by_all = band_matrix(mats_y, ny, reach)
    bx_all = band_matrix(mats_x, nx, reach)
    padded = halo(estimate, "slab", RZ)
    results = jnp.zeros_like(estimate)
    for position in range(view_count):
        view_id = view_order[position]
        by = by_all[position]
        bx = bx_all[position]
        kz = lax.dynamic_index_in_dim(z_kernels, view_id, 0, keepdims=False)
        offset = lax.dynamic_index_in_dim(background, view_id, 0, keepdims=False)
        data = lax.dynamic_index_in_dim(data_all, view_id, 0, keepdims=False)
        c = kz[0] * padded[0:count]
        for k in range(1, 3):
            c = c + kz[k] * padded[k : k + count]
        t = jnp.einsum("lij,ljx->lix", by, c, precision=blur_mode)
        blurred = jnp.einsum("lix,lax->lia", t, bx, precision=blur_mode)
        quotient = data / (blurred + offset)
        u = jnp.einsum("lji,ljx->lix", by, quotient, precision=blur_mode)
        g = jnp.einsum("lix,lxa->lia", u, bx, precision=blur_mode)
        gp = halo(g, "slab", 2 * RZ)
        corr = kz[0] * gp[2 : 2 + count + 2]
        for k in range(1, 3):
            corr = corr + kz[k] * gp[2 - k : 2 - k + count + 2]
        padded = padded * corr
        results = jnp.where(my_view == view_id, padded[RZ:-RZ], results)
    return results[None]


def solution(mesh):
    return jax.shard_map(
        per_device,
        mesh=mesh,
        in_specs=(
            P("slab", None, None),
            P("view", "slab", None, None),
            P(),
            P(),
            P(),
            P(),
            P("slab"),
        ),
        out_specs=P("view", "slab", None, None),
        check_vma=False,
    )
```

time: 437 us -> 334 us (0.76)
  starting transfers between devices: 127 us -> 51.8 us
  matrix products: 64 us -> 49.8 us
  waiting for transfers between devices: 79.6 us -> 71.4 us
    ppermute x16 -> x9, starting transfers between devices: 95.4 us -> 31 us  [halo(): above = lax.ppermute(array[:width], axis, down)]
    dot_general x32 -> x34, matrix products: 61.4 us -> 47.3 us  [the longest x8 19.6 us: per_device(): t = jnp.einsum('lij,ljx->lix', by, c, precision=blur_mode)]
    ppermute x16 -> x9, waiting for transfers between devices: 55.7 us -> 41.6 us  [halo(): below = lax.ppermute(array[-width:], axis, up)]
    ppermute x16 -> x9, starting transfers between devices: 31.8 us -> 20.8 us  [halo(): below = lax.ppermute(array[-width:], axis, up)]
    ppermute x16 -> x9, waiting for transfers between devices: 23.9 us -> 29.7 us  [halo(): above = lax.ppermute(array[:width], axis, down)]
  transfers between devices with their start and end apart: 33 -> 19, of which waited for: 28 -> 16; matrix products, arithmetic and copies ran while one was open for 25% -> 32% of each run, Pallas kernels for 0% -> 0%
where the time goes in v2:
time: 334 us; the launch traced here: 329 us
  local copies, waits for them, and re-layouts  73.2 us (22%)
  waiting for transfers between devices  71.4 us (21%)
  starting transfers between devices  51.8 us (16%)
  matrix products  49.8 us (15%)
  other arithmetic  48.6 us (15%)
  between operations  34.6 us (10%)
    slice x1, local copies, waits for them, and re-layouts, per_device(): bx = bx_all[position]  58.6 us
    ppermute x9, waiting for transfers between devices, halo(): below = lax.ppermute(array[-width:], axis, up)  41.6 us
    ppermute x9, starting transfers between devices, halo(): above = lax.ppermute(array[:width], axis, down)  31 us
    ppermute x9, waiting for transfers between devices, halo(): above = lax.ppermute(array[:width], axis, down)  29.7 us
    concatenate x1, other arithmetic, band_matrix(): return jnp.concatenate(rows, axis=-2)  25.8 us
    ppermute x9, starting transfers between devices, halo(): below = lax.ppermute(array[-width:], axis, up)  20.8 us
    dot_general x8, matrix products, per_device(): t = jnp.einsum('lij,ljx->lix', by, c, precision=blur_mode)  19.6 us
    mul x7, other arithmetic, per_device(): padded = padded * corr  15.4 us
  transfers between devices with their start and end apart: 19, of which 16 were waited for; matrix products, arithmetic and copies ran while one was open for 32% of the time, Pallas kernels for 0%

profile of v2, /device:TPU:2, one launch (start us, length us, event | category | flops | bytes accessed | tf_op | source)
XLA Modules:
  0.0 329.4 jit_solution(11570127586076802977)
XLA Ops:
  8.4 7.3 %collective-permute-start.1 = (f32[1,128,512]{2,1,0:T(8,128)}, f32[1,128,512]{2,1,0:T(8,128)S(1)}, u32[]{:S(2)}, u32[]{:S(2)}) collective-permute-start(f32[1,128,512]{2,1,0:T(8,128)} %get-tuple-element.24), channel_id=1, source_target_pairs={{1,0},{2,1},{3,2},{4,3},{5,4},{6,5},{7,6},{8,7},{9,8},{10,9},{11,1... | collective-permute-start | bytes 786440 | tf_op jit(solution)/shard_map/ppermute | solution.py:18
  42.6 25.8 %select_maximum_fusion = f32[8,2,512,512]{2,0,3,1:T(8,128)} fusion(f32[8,2,128,136]{2,0,3,1:T(8,128)S(1)} %get-tuple-element.22, f32[8,2,128,136]{2,0,3,1:T(8,128)S(1)} %get-tuple-element.21, f32[8,2,128,120]{2,0,3,1:T(8,128)S(1)} %broadcast.20, f32[8,2,128,144]{2,0,3,1:T(8,128)S(1)} %fusion.50, f32[8,2,128,248]{2,0,3,1:T(8,128)S(1)} %broadcast.21), kind=kLoop, calls=%fused_computation | loop fusion | flops 46137344 | bytes 23199744 | tf_op jit(solution)/shard_map/concatenate | solution.py:49
  68.3 58.6 %fusion.234 = (f32[1,2,512,512]{2,0,3,1:T(1,128)S(1)}, f32[1,2,512,512]{2,0,3,1:T(1,128)}, f32[1,2,512,512]{2,0,3,1:T(1,128)}, f32[1,2,512,512]{2,0,3,1:T(1,128)...) fusion(f32[8,2,512,512]{2,0,3,1:T(8,128)} %select_maximum_fusion), kind=kLoop, calls=%fused_computation.251 | loop fusion | bytes 33554432 | tf_op jit(solution)/shard_map/slice | solution.py:82
  127.0 5.8 %fusion.235 = (f32[1,2,128,128]{2,0,3,1:T(1,128)S(1)}, f32[1,2,128,128]{2,0,3,1:T(1,128)S(1)}, f32[1,2,128,128]{2,0,3,1:T(1,128)S(1)}, f32[1,2,128,128]{2,0,3,1:...) fusion(f32[8,2,128,144]{2,0,3,1:T(8,128)} %fusion.52), kind=kLoop, calls=%fused_computation.252 | loop fusion | bytes 2097152 | tf_op jit(solution)/shard_map/slice | solution.py:81
  133.7 3.4 %fusion.177 = f32[2,128,512]{2,1,0:T(8,128)S(1)} fusion(f32[2,128,128]{1,2,0:T(8,128)S(1)} %bitcast.216, f32[1,128,512]{2,1,0:T(8,128)} %copy-done.22, f32[2,128,512]{2,1,0:T(8,128)S(1)} %copy-done.12, f32[1,128,512]{2,1,0:T(8,128)} %copy-done.24, f32[]{:T(128)} %bitcast.13, f32[]{:T(128)} %bitcast.12, f32[]{:T(128)} %bitcast.2), kind=kOutput, calls=%fused_computation.182 | convolution fusion | flops 101580800 | bytes 1703948 | tf_op jit(solution)/shard_map/lij,ljx->lix/dot_general | solution.py:89
  137.1 3.1 fusion.57
  142.0 5.9 %collective-permute-start.2 = (f32[2,128,512]{2,1,0:T(8,128)S(1)}, f32[2,128,512]{2,1,0:T(8,128)S(1)}, u32[]{:S(2)}, u32[]{:S(2)}) collective-permute-start(f32[2,128,512]{2,1,0:T(8,128)S(1)} %fusion.29), channel_id=1, source_target_pairs={{1,0},{2,1},{3,2},{4,3},{5,4},{6,5},{7,6},{8,7},{9,8},{10,9},{11,1... | collective-permute-start | bytes 1572872 | tf_op jit(solution)/shard_map/ppermute | solution.py:18
  147.9 2.1 collective-permute-start.3
  150.0 4.6 %collective-permute-done.2 = f32[2,128,512]{2,1,0:T(8,128)S(1)} collective-permute-done((f32[2,128,512]{2,1,0:T(8,128)S(1)}, f32[2,128,512]{2,1,0:T(8,128)S(1)}, u32[]{:S(2)}, u32[]{:S(2)}) %collective-permute-start.2) | collective-permute-done | bytes 524320 | tf_op jit(solution)/shard_map/ppermute | solution.py:18
  154.5 5.9 %collective-permute-done.3 = f32[2,128,512]{2,1,0:T(8,128)S(1)} collective-permute-done((f32[2,128,512]{2,1,0:T(8,128)S(1)}, f32[2,128,512]{2,1,0:T(8,128)S(1)}, u32[]{:S(2)}, u32[]{:S(2)}) %collective-permute-start.3) | collective-permute-done | bytes 524320 | tf_op jit(solution)/shard_map/ppermute | solution.py:17
  160.5 2.2 fusion.129
  162.7 2.2 fusion.171
  168.1 2.1 collective-permute-start.4
  170.2 2.4 collective-permute-start.5
  173.2 3.7 %collective-permute-done.4 = f32[2,128,512]{2,1,0:T(8,128)S(1)} collective-permute-done((f32[2,128,512]{2,1,0:T(8,128)S(1)}, f32[2,128,512]{2,1,0:T(8,128)S(1)}, u32[]{:S(2)}, u32[]{:S(2)}) %collective-permute-start.4) | collective-permute-done | bytes 524320 | tf_op jit(solution)/shard_map/ppermute | solution.py:18
  176.9 5.9 %collective-permute-done.5 = f32[2,128,512]{2,1,0:T(8,128)S(1)} collective-permute-done((f32[2,128,512]{2,1,0:T(8,128)S(1)}, f32[2,128,512]{2,1,0:T(8,128)S(1)}, u32[]{:S(2)}, u32[]{:S(2)}) %collective-permute-start.5) | collective-permute-done | bytes 524320 | tf_op jit(solution)/shard_map/ppermute | solution.py:17
  182.8 2.1 fusion.125
  184.9 2.3 fusion.166
  190.3 2.1 collective-permute-start.6
  192.4 2.4 collective-permute-start.7
  194.8 4.3 %collective-permute-done.6 = f32[2,128,512]{2,1,0:T(8,128)S(1)} collective-permute-done((f32[2,128,512]{2,1,0:T(8,128)S(1)}, f32[2,128,512]{2,1,0:T(8,128)S(1)}, u32[]{:S(2)}, u32[]{:S(2)}) %collective-permute-start.6) | collective-permute-done | bytes 524320 | tf_op jit(solution)/shard_map/ppermute | solution.py:18
  199.1 5.9 %collective-permute-done.7 = f32[2,128,512]{2,1,0:T(8,128)S(1)} collective-permute-done((f32[2,128,512]{2,1,0:T(8,128)S(1)}, f32[2,128,512]{2,1,0:T(8,128)S(1)}, u32[]{:S(2)}, u32[]{:S(2)}) %collective-permute-start.7) | collective-permute-done | bytes 524320 | tf_op jit(solution)/shard_map/ppermute | solution.py:17
  205.0 2.2 fusion.121
  207.2 2.3 fusion.161
  212.6 2.1 collective-permute-start.8
  214.6 2.6 collective-permute-start.9
  217.9 3.4 %collective-permute-done.8 = f32[2,128,512]{2,1,0:T(8,128)S(1)} collective-permute-done((f32[2,128,512]{2,1,0:T(8,128)S(1)}, f32[2,128,512]{2,1,0:T(8,128)S(1)}, u32[]{:S(2)}, u32[]{:S(2)}) %collective-permute-start.8) | collective-permute-done | bytes 524320 | tf_op jit(solution)/shard_map/ppermute | solution.py:18
  221.3 5.9 %collective-permute-done.9 = f32[2,128,512]{2,1,0:T(8,128)S(1)} collective-permute-done((f32[2,128,512]{2,1,0:T(8,128)S(1)}, f32[2,128,512]{2,1,0:T(8,128)S(1)}, u32[]{:S(2)}, u32[]{:S(2)}) %collective-permute-start.9) | collective-permute-done | bytes 524320 | tf_op jit(solution)/shard_map/ppermute | solution.py:17
  227.2 2.2 fusion.117
  229.5 2.4 fusion.156
  234.9 2.1 collective-permute-start.10
  237.0 2.4 collective-permute-start.11
  239.4 4.3 %collective-permute-done.10 = f32[2,128,512]{2,1,0:T(8,128)S(1)} collective-permute-done((f32[2,128,512]{2,1,0:T(8,128)S(1)}, f32[2,128,512]{2,1,0:T(8,128)S(1)}, u32[]{:S(2)}, u32[]{:S(2)}) %collective-permute-start.10) | collective-permute-done | bytes 524320 | tf_op jit(solution)/shard_map/ppermute | solution.py:18
  243.7 5.9 %collective-permute-done.11 = f32[2,128,512]{2,1,0:T(8,128)S(1)} collective-permute-done((f32[2,128,512]{2,1,0:T(8,128)S(1)}, f32[2,128,512]{2,1,0:T(8,128)S(1)}, u32[]{:S(2)}, u32[]{:S(2)}) %collective-permute-start.11) | collective-permute-done | bytes 524320 | tf_op jit(solution)/shard_map/ppermute | solution.py:17
  249.6 2.3 fusion.113
  251.9 2.3 fusion.151
  259.2 2.4 collective-permute-start.13
  262.2 3.7 %collective-permute-done.12 = f32[2,128,512]{2,1,0:T(8,128)S(1)} collective-permute-done((f32[2,128,512]{2,1,0:T(8,128)S(1)}, f32[2,128,512]{2,1,0:T(8,128)S(1)}, u32[]{:S(2)}, u32[]{:S(2)}) %collective-permute-start.12) | collective-permute-done | bytes 524320 | tf_op jit(solution)/shard_map/ppermute | solution.py:18
  265.9 5.9 %collective-permute-done.13 = f32[2,128,512]{2,1,0:T(8,128)S(1)} collective-permute-done((f32[2,128,512]{2,1,0:T(8,128)S(1)}, f32[2,128,512]{2,1,0:T(8,128)S(1)}, u32[]{:S(2)}, u32[]{:S(2)}) %collective-permute-start.13) | collective-permute-done | bytes 524320 | tf_op jit(solution)/shard_map/ppermute | solution.py:17
  271.8 2.2 fusion.109
  274.0 2.4 fusion.146
  281.4 2.7 collective-permute-start.15
  284.1 4.0 %collective-permute-done.14 = f32[2,128,512]{2,1,0:T(8,128)S(1)} collective-permute-done((f32[2,128,512]{2,1,0:T(8,128)S(1)}, f32[2,128,512]{2,1,0:T(8,128)S(1)}, u32[]{:S(2)}, u32[]{:S(2)}) %collective-permute-start.14) | collective-permute-done | bytes 524320 | tf_op jit(solution)/shard_map/ppermute | solution.py:18
  288.1 5.9 %collective-permute-done.15 = f32[2,128,512]{2,1,0:T(8,128)S(1)} collective-permute-done((f32[2,128,512]{2,1,0:T(8,128)S(1)}, f32[2,128,512]{2,1,0:T(8,128)S(1)}, u32[]{:S(2)}, u32[]{:S(2)}) %collective-permute-start.15) | collective-permute-done | bytes 524320 | tf_op jit(solution)/shard_map/ppermute | solution.py:17
  294.0 2.2 fusion.105
  296.2 2.2 fusion.141
  304.2 5.8 %collective-permute-start.16 = (f32[2,128,512]{2,1,0:T(8,128)}, f32[2,128,512]{2,1,0:T(8,128)S(1)}, u32[]{:S(2)}, u32[]{:S(2)}) collective-permute-start(f32[2,128,512]{2,1,0:T(8,128)} %fusion.1), channel_id=1, source_target_pairs={{1,0},{2,1},{3,2},{4,3},{5,4},{6,5},{7,6},{8,7},{9,8},{10,9},{11,1... | collective-permute-start | bytes 1572872 | tf_op jit(solution)/shard_map/ppermute | solution.py:18
  316.9 5.4 %fusion.136 = f32[1,2,128,512]{3,2,1,0:T(8,128)} fusion(f32[2,128,512]{2,1,0:T(8,128)} %fusion.1, f32[2,128,512]{2,1,0:T(8,128)S(1)} %collective-permute-done.17, f32[2,128,512]{2,1,0:T(8,128)S(1)} %collective-permute-done.16, f32[4,128,512]{2,1,0:T(8,128)} %copy-done.14, f32[4,128,512]{2,1,0:T(8,128)} %copy-done.11, f32[4,128,512]{2,1,0:T(8,128)} %copy-done.10, ...), kind=kLoop, calls=%fused_computation.137 | loop fusion | flops 2359296 | bytes 5767188 | tf_op jit(solution)/shard_map/broadcast_in_dim | solution.py:100
  (119 shorter events, 47.5 us)
Async XLA Ops:
  6.5 25.8 %copy-start.30 = (s32[2]{0:T(128)S(1)}, s32[2]{0:T(128)}, u32[]{:S(2)}) copy-start(s32[2]{0:T(128)} %param.13) | copy-start | bytes 28
  6.5 27.9 %copy-start.27 = (f32[8,3]{0,1:T(4,128)S(1)}, f32[8,3]{0,1:T(4,128)}, u32[]{:S(2)}) copy-start(f32[8,3]{0,1:T(4,128)} %param.11) | copy-start | bytes 292
  6.5 130.5 %all-gather.2.cloned.1.call-start = ((), (), s32[]{:S(2)}) async-start(), calls=%async_computation | async-start | bytes 4718592 | tf_op jit(solution)/shard_map/all_gather | solution.py:60
  8.4 31.8 %copy-start.26 = (f32[8]{0:T(128)S(1)}, f32[8]{0:T(128)}, u32[]{:S(2)}) copy-start(f32[8]{0:T(128)} %param.9) | copy-start | bytes 100
  8.4 124.4 %collective-permute-start.1 = (f32[1,128,512]{2,1,0:T(8,128)}, f32[1,128,512]{2,1,0:T(8,128)S(1)}, u32[]{:S(2)}, u32[]{:S(2)}) collective-permute-start(f32[1,128,512]{2,1,0:T(8,128)} %get-tuple-element.24), channel_id=1, source_target_pairs={{1,0},{2,1},{3,2},{4,3},{5,4},{6,5},{7,6},{8,7},{9,8},{10,9},{11,1... | collective-permute-start | bytes 786440 | tf_op jit(solution)/shard_map/ppermute | solution.py:18
  15.7 117.1 %collective-permute-start = (f32[1,128,512]{2,1,0:T(8,128)}, f32[1,128,512]{2,1,0:T(8,128)S(1)}, u32[]{:S(2)}, u32[]{:S(2)}) collective-permute-start(f32[1,128,512]{2,1,0:T(8,128)} %get-tuple-element.23), channel_id=1, source_target_pairs={{0,1},{1,2},{2,3},{3,4},{4,5},{5,6},{6,7},{7,8},{8,9},{9,10},{10,1... | collective-permute-start | bytes 786440 | tf_op jit(solution)/shard_map/ppermute | solution.py:17
  127.0 6.7 %copy-start.12 = (f32[2,128,512]{2,1,0:T(8,128)S(1)}, f32[2,128,512]{2,1,0:T(8,128)}, u32[]{:S(2)}) copy-start(f32[2,128,512]{2,1,0:T(8,128)} %param.7) | copy-start | bytes 1572868
  132.8 0.9 copy-start.20
  137.1 3.2 copy-start.21
  137.1 3.6 %copy-start.6 = (f32[1,2,512,512]{2,0,3,1:T(1,128)S(1)}, f32[1,2,512,512]{2,0,3,1:T(1,128)}, u32[]{:S(2)}) copy-start(f32[1,2,512,512]{2,0,3,1:T(1,128)} %get-tuple-element.12) | copy-start | bytes 6291460
  140.3 20.2 %copy-start.13 = (f32[2,128,512]{2,1,0:T(8,128)S(1)}, f32[2,128,512]{2,1,0:T(8,128)}, u32[]{:S(2)}) copy-start(f32[2,128,512]{2,1,0:T(8,128)} %param.7) | copy-start | bytes 1572868
  140.3 20.2 %copy-start.23 = (f32[1,128,512]{2,1,0:T(8,128)S(1)}, f32[1,128,512]{2,1,0:T(8,128)}, u32[]{:S(2)}) copy-start(f32[1,128,512]{2,1,0:T(8,128)} %copy-done.22) | copy-start | bytes 786436
  140.3 20.2 %copy-start.25 = (f32[1,128,512]{2,1,0:T(8,128)S(1)}, f32[1,128,512]{2,1,0:T(8,128)}, u32[]{:S(2)}) copy-start(f32[1,128,512]{2,1,0:T(8,128)} %copy-done.24) | copy-start | bytes 786436
  140.7 24.3 %copy-start.15 = (f32[8,2,128,512]{3,2,1,0:T(8,128)S(1)}, f32[8,2,128,512]{3,2,1,0:T(8,128)}, u32[]{:S(2)}) copy-start(f32[8,2,128,512]{3,2,1,0:T(8,128)} %all-gather.2.cloned.1.call-done) | copy-start | bytes 12582916
  141.9 20.8 %copy-start.19 = (f32[1,2,128,128]{2,0,3,1:T(1,128)S(1)}, f32[1,2,128,128]{2,0,3,1:T(1,128)}, u32[]{:S(2)}) copy-start(f32[1,2,128,128]{2,0,3,1:T(1,128)} %get-tuple-element.19) | copy-start | bytes 393220
  142.0 23.1 %copy-start.5 = (f32[1,2,512,512]{2,0,3,1:T(1,128)S(1)}, f32[1,2,512,512]{2,0,3,1:T(1,128)}, u32[]{:S(2)}) copy-start(f32[1,2,512,512]{2,0,3,1:T(1,128)} %get-tuple-element.11) | copy-start | bytes 6291460
  142.0 12.6 %collective-permute-start.2 = (f32[2,128,512]{2,1,0:T(8,128)S(1)}, f32[2,128,512]{2,1,0:T(8,128)S(1)}, u32[]{:S(2)}, u32[]{:S(2)}) collective-permute-start(f32[2,128,512]{2,1,0:T(8,128)S(1)} %fusion.29), channel_id=1, source_target_pairs={{1,0},{2,1},{3,2},{4,3},{5,4},{6,5},{7,6},{8,7},{9,8},{10,9},{11,1... | collective-permute-start | bytes 1572872 | tf_op jit(solution)/shard_map/ppermute | solution.py:18
  147.9 12.6 %collective-permute-start.3 = (f32[2,128,512]{2,1,0:T(8,128)S(1)}, f32[2,128,512]{2,1,0:T(8,128)S(1)}, u32[]{:S(2)}, u32[]{:S(2)}) collective-permute-start(f32[2,128,512]{2,1,0:T(8,128)S(1)} %fusion.29), channel_id=1, source_target_pairs={{0,1},{1,2},{2,3},{3,4},{4,5},{5,6},{6,7},{7,8},{8,9},{9,10},{10,1... | collective-permute-start | bytes 1572872 | tf_op jit(solution)/shard_map/ppermute | solution.py:17
  166.5 6.1 %copy-start.28 = (f32[1,3]{0,1:T(4,128)S(1)}, f32[1,3]{0,1:T(4,128)}, u32[]{:S(2)}) copy-start(f32[1,3]{0,1:T(4,128)} %get-tuple-element.34) | copy-start | bytes 40
  166.5 6.1 %copy-start.29 = (f32[1,3]{0,1:T(4,128)S(1)}, f32[1,3]{0,1:T(4,128)}, u32[]{:S(2)}) copy-start(f32[1,3]{0,1:T(4,128)} %get-tuple-element.35) | copy-start | bytes 40
  168.1 16.8 %copy-start.18 = (f32[1,2,128,128]{2,0,3,1:T(1,128)S(1)}, f32[1,2,128,128]{2,0,3,1:T(1,128)}, u32[]{:S(2)}) copy-start(f32[1,2,128,128]{2,0,3,1:T(1,128)} %get-tuple-element.18) | copy-start | bytes 393220
  168.1 8.7 %collective-permute-start.4 = (f32[2,128,512]{2,1,0:T(8,128)S(1)}, f32[2,128,512]{2,1,0:T(8,128)S(1)}, u32[]{:S(2)}, u32[]{:S(2)}) collective-permute-start(f32[2,128,512]{2,1,0:T(8,128)S(1)} %fusion.25), channel_id=1, source_target_pairs={{1,0},{2,1},{3,2},{4,3},{5,4},{6,5},{7,6},{8,7},{9,8},{10,9},{11,1... | collective-permute-start | bytes 1572872 | tf_op jit(solution)/shard_map/ppermute | solution.py:18
  170.2 12.6 %collective-permute-start.5 = (f32[2,128,512]{2,1,0:T(8,128)S(1)}, f32[2,128,512]{2,1,0:T(8,128)S(1)}, u32[]{:S(2)}, u32[]{:S(2)}) collective-permute-start(f32[2,128,512]{2,1,0:T(8,128)S(1)} %fusion.25), channel_id=1, source_target_pairs={{0,1},{1,2},{2,3},{3,4},{4,5},{5,6},{6,7},{7,8},{8,9},{9,10},{10,1... | collective-permute-start | bytes 1572872 | tf_op jit(solution)/shard_map/ppermute | solution.py:17
  173.2 14.1 %copy-start.4 = (f32[1,2,512,512]{2,0,3,1:T(1,128)S(1)}, f32[1,2,512,512]{2,0,3,1:T(1,128)}, u32[]{:S(2)}) copy-start(f32[1,2,512,512]{2,0,3,1:T(1,128)} %get-tuple-element.10) | copy-start | bytes 6291460
  184.9 20.1 %copy-start.7 = (f32[4,128,512]{2,1,0:T(8,128)}, f32[4,128,512]{2,1,0:T(8,128)S(1)}, u32[]{:S(2)}) copy-start(f32[4,128,512]{2,1,0:T(8,128)S(1)} %fusion.125) | copy-start | bytes 3145732
  190.3 16.9 %copy-start.17 = (f32[1,2,128,128]{2,0,3,1:T(1,128)S(1)}, f32[1,2,128,128]{2,0,3,1:T(1,128)}, u32[]{:S(2)}) copy-start(f32[1,2,128,128]{2,0,3,1:T(1,128)} %get-tuple-element.17) | copy-start | bytes 393220
  190.3 19.2 %copy-start.3 = (f32[1,2,512,512]{2,0,3,1:T(1,128)S(1)}, f32[1,2,512,512]{2,0,3,1:T(1,128)}, u32[]{:S(2)}) copy-start(f32[1,2,512,512]{2,0,3,1:T(1,128)} %get-tuple-element.9) | copy-start | bytes 6291460
  190.3 8.7 %collective-permute-start.6 = (f32[2,128,512]{2,1,0:T(8,128)S(1)}, f32[2,128,512]{2,1,0:T(8,128)S(1)}, u32[]{:S(2)}, u32[]{:S(2)}) collective-permute-start(f32[2,128,512]{2,1,0:T(8,128)S(1)} %fusion.21), channel_id=1, source_target_pairs={{1,0},{2,1},{3,2},{4,3},{5,4},{6,5},{7,6},{8,7},{9,8},{10,9},{11,1... | collective-permute-start | bytes 1572872 | tf_op jit(solution)/shard_map/ppermute | solution.py:18
  192.4 12.6 %collective-permute-start.7 = (f32[2,128,512]{2,1,0:T(8,128)S(1)}, f32[2,128,512]{2,1,0:T(8,128)S(1)}, u32[]{:S(2)}, u32[]{:S(2)}) collective-permute-start(f32[2,128,512]{2,1,0:T(8,128)S(1)} %fusion.21), channel_id=1, source_target_pairs={{0,1},{1,2},{2,3},{3,4},{4,5},{5,6},{6,7},{7,8},{8,9},{9,10},{10,1... | collective-permute-start | bytes 1572872 | tf_op jit(solution)/shard_map/ppermute | solution.py:17
  207.2 20.0 %copy-start.8 = (f32[4,128,512]{2,1,0:T(8,128)}, f32[4,128,512]{2,1,0:T(8,128)S(1)}, u32[]{:S(2)}) copy-start(f32[4,128,512]{2,1,0:T(8,128)S(1)} %fusion.121) | copy-start | bytes 3145732
  212.6 16.9 %copy-start.16 = (f32[1,2,128,128]{2,0,3,1:T(1,128)S(1)}, f32[1,2,128,128]{2,0,3,1:T(1,128)}, u32[]{:S(2)}) copy-start(f32[1,2,128,128]{2,0,3,1:T(1,128)} %get-tuple-element.16) | copy-start | bytes 393220
  212.6 8.7 %collective-permute-start.8 = (f32[2,128,512]{2,1,0:T(8,128)S(1)}, f32[2,128,512]{2,1,0:T(8,128)S(1)}, u32[]{:S(2)}, u32[]{:S(2)}) collective-permute-start(f32[2,128,512]{2,1,0:T(8,128)S(1)} %fusion.17), channel_id=1, source_target_pairs={{1,0},{2,1},{3,2},{4,3},{5,4},{6,5},{7,6},{8,7},{9,8},{10,9},{11,1... | collective-permute-start | bytes 1572872 | tf_op jit(solution)/shard_map/ppermute | solution.py:18
  214.6 12.6 %collective-permute-start.9 = (f32[2,128,512]{2,1,0:T(8,128)S(1)}, f32[2,128,512]{2,1,0:T(8,128)S(1)}, u32[]{:S(2)}, u32[]{:S(2)}) collective-permute-start(f32[2,128,512]{2,1,0:T(8,128)S(1)} %fusion.17), channel_id=1, source_target_pairs={{0,1},{1,2},{2,3},{3,4},{4,5},{5,6},{6,7},{7,8},{8,9},{9,10},{10,1... | collective-permute-start | bytes 1572872 | tf_op jit(solution)/shard_map/ppermute | solution.py:17
  217.9 14.0 %copy-start.2 = (f32[1,2,512,512]{2,0,3,1:T(1,128)S(1)}, f32[1,2,512,512]{2,0,3,1:T(1,128)}, u32[]{:S(2)}) copy-start(f32[1,2,512,512]{2,0,3,1:T(1,128)} %get-tuple-element.8) | copy-start | bytes 6291460
  229.4 20.2 %copy-start.9 = (f32[4,128,512]{2,1,0:T(8,128)}, f32[4,128,512]{2,1,0:T(8,128)S(1)}, u32[]{:S(2)}) copy-start(f32[4,128,512]{2,1,0:T(8,128)S(1)} %fusion.117) | copy-start | bytes 3145732
  234.9 19.3 %copy-start.1 = (f32[1,2,512,512]{2,0,3,1:T(1,128)S(1)}, f32[1,2,512,512]{2,0,3,1:T(1,128)}, u32[]{:S(2)}) copy-start(f32[1,2,512,512]{2,0,3,1:T(1,128)} %get-tuple-element.7) | copy-start | bytes 6291460
  234.9 8.7 %collective-permute-start.10 = (f32[2,128,512]{2,1,0:T(8,128)S(1)}, f32[2,128,512]{2,1,0:T(8,128)S(1)}, u32[]{:S(2)}, u32[]{:S(2)}) collective-permute-start(f32[2,128,512]{2,1,0:T(8,128)S(1)} %fusion.13), channel_id=1, source_target_pairs={{1,0},{2,1},{3,2},{4,3},{5,4},{6,5},{7,6},{8,7},{9,8},{10,9},{11,1... | collective-permute-start | bytes 1572872 | tf_op jit(solution)/shard_map/ppermute | solution.py:18
  237.0 12.6 %collective-permute-start.11 = (f32[2,128,512]{2,1,0:T(8,128)S(1)}, f32[2,128,512]{2,1,0:T(8,128)S(1)}, u32[]{:S(2)}, u32[]{:S(2)}) collective-permute-start(f32[2,128,512]{2,1,0:T(8,128)S(1)} %fusion.13), channel_id=1, source_target_pairs={{0,1},{1,2},{2,3},{3,4},{4,5},{5,6},{6,7},{7,8},{8,9},{9,10},{10,1... | collective-permute-start | bytes 1572872 | tf_op jit(solution)/shard_map/ppermute | solution.py:17
  251.9 19.9 %copy-start.10 = (f32[4,128,512]{2,1,0:T(8,128)}, f32[4,128,512]{2,1,0:T(8,128)S(1)}, u32[]{:S(2)}) copy-start(f32[4,128,512]{2,1,0:T(8,128)S(1)} %fusion.113) | copy-start | bytes 3145732
  257.3 8.6 %collective-permute-start.12 = (f32[2,128,512]{2,1,0:T(8,128)S(1)}, f32[2,128,512]{2,1,0:T(8,128)S(1)}, u32[]{:S(2)}, u32[]{:S(2)}) collective-permute-start(f32[2,128,512]{2,1,0:T(8,128)S(1)} %fusion.9), channel_id=1, source_target_pairs={{1,0},{2,1},{3,2},{4,3},{5,4},{6,5},{7,6},{8,7},{9,8},{10,9},{11,1... | collective-permute-start | bytes 1572872 | tf_op jit(solution)/shard_map/ppermute | solution.py:18
  259.2 12.6 %collective-permute-start.13 = (f32[2,128,512]{2,1,0:T(8,128)S(1)}, f32[2,128,512]{2,1,0:T(8,128)S(1)}, u32[]{:S(2)}, u32[]{:S(2)}) collective-permute-start(f32[2,128,512]{2,1,0:T(8,128)S(1)} %fusion.9), channel_id=1, source_target_pairs={{0,1},{1,2},{2,3},{3,4},{4,5},{5,6},{6,7},{7,8},{8,9},{9,10},{10,1... | collective-permute-start | bytes 1572872 | tf_op jit(solution)/shard_map/ppermute | solution.py:17
  262.2 14.2 %copy-start = (f32[1,2,512,512]{2,0,3,1:T(1,128)S(1)}, f32[1,2,512,512]{2,0,3,1:T(1,128)}, u32[]{:S(2)}) copy-start(f32[1,2,512,512]{2,0,3,1:T(1,128)} %get-tuple-element.6) | copy-start | bytes 6291460
  274.0 20.0 %copy-start.11 = (f32[4,128,512]{2,1,0:T(8,128)}, f32[4,128,512]{2,1,0:T(8,128)S(1)}, u32[]{:S(2)}) copy-start(f32[4,128,512]{2,1,0:T(8,128)S(1)} %fusion.109) | copy-start | bytes 3145732
  279.5 8.6 %collective-permute-start.14 = (f32[2,128,512]{2,1,0:T(8,128)S(1)}, f32[2,128,512]{2,1,0:T(8,128)S(1)}, u32[]{:S(2)}, u32[]{:S(2)}) collective-permute-start(f32[2,128,512]{2,1,0:T(8,128)S(1)} %fusion.5), channel_id=1, source_target_pairs={{1,0},{2,1},{3,2},{4,3},{5,4},{6,5},{7,6},{8,7},{9,8},{10,9},{11,1... | collective-permute-start | bytes 1572872 | tf_op jit(solution)/shard_map/ppermute | solution.py:18
  281.4 12.6 %collective-permute-start.15 = (f32[2,128,512]{2,1,0:T(8,128)S(1)}, f32[2,128,512]{2,1,0:T(8,128)S(1)}, u32[]{:S(2)}, u32[]{:S(2)}) collective-permute-start(f32[2,128,512]{2,1,0:T(8,128)S(1)} %fusion.5), channel_id=1, source_target_pairs={{0,1},{1,2},{2,3},{3,4},{4,5},{5,6},{6,7},{7,8},{8,9},{9,10},{10,1... | collective-permute-start | bytes 1572872 | tf_op jit(solution)/shard_map/ppermute | solution.py:17
  296.2 3.6 %copy-start.14 = (f32[4,128,512]{2,1,0:T(8,128)}, f32[4,128,512]{2,1,0:T(8,128)S(1)}, u32[]{:S(2)}) copy-start(f32[4,128,512]{2,1,0:T(8,128)S(1)} %fusion.105) | copy-start | bytes 3145732
  302.2 12.8 %collective-permute-start.17 = (f32[2,128,512]{2,1,0:T(8,128)}, f32[2,128,512]{2,1,0:T(8,128)S(1)}, u32[]{:S(2)}, u32[]{:S(2)}) collective-permute-start(f32[2,128,512]{2,1,0:T(8,128)} %fusion.1), channel_id=1, source_target_pairs={{0,1},{1,2},{2,3},{3,4},{4,5},{5,6},{6,7},{7,8},{8,9},{9,10},{10,1... | collective-permute-start | bytes 1572872 | tf_op jit(solution)/shard_map/ppermute | solution.py:17
  304.2 12.8 %collective-permute-start.16 = (f32[2,128,512]{2,1,0:T(8,128)}, f32[2,128,512]{2,1,0:T(8,128)S(1)}, u32[]{:S(2)}, u32[]{:S(2)}) collective-permute-start(f32[2,128,512]{2,1,0:T(8,128)} %fusion.1), channel_id=1, source_target_pairs={{1,0},{2,1},{3,2},{4,3},{5,4},{6,5},{7,6},{8,7},{9,8},{10,9},{11,1... | collective-permute-start | bytes 1572872 | tf_op jit(solution)/shard_map/ppermute | solution.py:18
  (2 other events, 1.6 us)
Sparse Core Ops, SparseCore 0:
  17.8 75.2 all-gather.1

commit v3 on v2

--- a/solution.py
+++ b/solution.py
@@ -33,19 +33,19 @@
 
 def band_matrix(mats, n, reach):
     block = mats.shape[-2]
-    lead = mats.shape[:-2]
-    rows = []
-    for blk in range(n // block):
-        start = blk * block - reach
-        lo = max(start, 0)
-        hi = min(start + block + 2 * reach, n)
-        parts = []
-        if lo > 0:
-            parts.append(jnp.zeros(lead + (block, lo), mats.dtype))
-        parts.append(mats[..., lo - start : hi - start])
-        if hi < n:
-            parts.append(jnp.zeros(lead + (block, n - hi), mats.dtype))
-        rows.append(jnp.concatenate(parts, axis=-1))
+    nblocks = n // block
+    diagonal = mats[..., reach : reach + block]
+    if nblocks == 1:
+        return diagonal
+    zeros = jnp.zeros(mats.shape[:-1] + (block - reach,), mats.dtype)
+    upper = jnp.concatenate([mats[..., block + reach :], zeros], axis=-1)
+    lower = jnp.concatenate([zeros, mats[..., :reach]], axis=-1)
+    empty = jnp.zeros_like(diagonal)
+    pick = {0: diagonal, 1: upper, -1: lower}
+    rows = [
+        jnp.concatenate([pick.get(col - row, empty) for col in range(nblocks)], axis=-1)
+        for row in range(nblocks)
+    ]
     return jnp.concatenate(rows, axis=-2)
 
 
@@ -70,16 +70,21 @@
                               precision=exact_mode)
     step_taps = jnp.einsum("ld,pdk->plk", level_hot, step_kernels, precision=exact_mode)
     step_taps = step_taps.reshape(view_count, count, 2, kernel_len)
-    mats_y = lax.optimization_barrier(tap_matrix(step_taps[:, :, 0], min(128, ny)))
-    mats_x = lax.optimization_barrier(tap_matrix(step_taps[:, :, 1], min(128, nx)))
-    by_all = band_matrix(mats_y, ny, reach)
-    bx_all = band_matrix(mats_x, nx, reach)
+    taps_y = step_taps[:, :, 0]
+    taps_x = step_taps[:, :, 1]
+    mats = [
+        lax.optimization_barrier(tap_matrix(taps, min(128, n)))
+        for taps, n in ((taps_y, ny), (taps_y[..., ::-1], ny), (taps_x, nx), (taps_x[..., ::-1], nx))
+    ]
+    by_all = [band_matrix(mats[0][p], ny, reach) for p in range(view_count)]
+    byr_all = [band_matrix(mats[1][p], ny, reach) for p in range(view_count)]
+    bx_all = [band_matrix(mats[2][p], nx, reach) for p in range(view_count)]
+    bxr_all = [band_matrix(mats[3][p], nx, reach) for p in range(view_count)]
     padded = halo(estimate, "slab", RZ)
     results = jnp.zeros_like(estimate)
     for position in range(view_count):
         view_id = view_order[position]
         by = by_all[position]
-        bx = bx_all[position]
         kz = lax.dynamic_index_in_dim(z_kernels, view_id, 0, keepdims=False)
         offset = lax.dynamic_index_in_dim(background, view_id, 0, keepdims=False)
         data = lax.dynamic_index_in_dim(data_all, view_id, 0, keepdims=False)
@@ -87,10 +92,10 @@
         for k in range(1, 3):
             c = c + kz[k] * padded[k : k + count]
         t = jnp.einsum("lij,ljx->lix", by, c, precision=blur_mode)
-        blurred = jnp.einsum("lix,lax->lia", t, bx, precision=blur_mode)
+        blurred = jnp.einsum("lix,lax->lia", t, bx_all[position], precision=blur_mode)
         quotient = data / (blurred + offset)
-        u = jnp.einsum("lji,ljx->lix", by, quotient, precision=blur_mode)
-        g = jnp.einsum("lix,lxa->lia", u, bx, precision=blur_mode)
+        u = jnp.einsum("lij,ljx->lix", byr_all[position], quotient, precision=blur_mode)
+        g = jnp.einsum("lix,lax->lia", u, bxr_all[position], precision=blur_mode)
         gp = halo(g, "slab", 2 * RZ)
         corr = kz[0] * gp[2 : 2 + count + 2]
         for k in range(1, 3):

time: 334 us -> 282 us (0.84)
  local copies, waits for them, and re-layouts: 73.2 us -> 20.8 us
  waiting for transfers between devices: 71.4 us -> 102 us
  other arithmetic: 48.6 us -> 24.4 us
  starting transfers between devices: 51.8 us -> 46.8 us
    slice x4 -> x21, local copies, waits for them, and re-layouts: 64.6 us -> 13 us  [the longest x1 6.87 us: per_device(): bx_all = [band_matrix(mats[2][p], nx, reach) for p in range(view_count)]]
    all_gather x1, waiting for transfers between devices: 0.02 us -> 26.3 us  [per_device(): data_all = lax.all_gather(view_data[0], 'view', axis=0)]
    concatenate x1 -> x0, other arithmetic: 25.8 us -> none  [band_matrix(): return jnp.concatenate(rows, axis=-2)]
    ppermute x9, waiting for transfers between devices: 41.6 us -> 47.1 us  [halo(): below = lax.ppermute(array[-width:], axis, up)]
    ppermute x9, starting transfers between devices: 31 us -> 25.8 us  [halo(): above = lax.ppermute(array[:width], axis, down)]
  transfers between devices with their start and end apart: 19 -> 19, of which waited for: 16 -> 16; matrix products, arithmetic and copies ran while one was open for 32% -> 12% of each run, Pallas kernels for 0% -> 0%
where the time goes in v3:
time: 282 us; the launch traced here: 280 us
  waiting for transfers between devices  102 us (36%)
  matrix products  52.1 us (18%)
  starting transfers between devices  46.8 us (17%)
  between operations  34.1 us (12%)
  other arithmetic  24.4 us (9%)
  local copies, waits for them, and re-layouts  20.8 us (7%)
    ppermute x9, waiting for transfers between devices, halo(): below = lax.ppermute(array[-width:], axis, up)  47.1 us
    ppermute x9, waiting for transfers between devices, halo(): above = lax.ppermute(array[:width], axis, down)  27.5 us
    all_gather x1, waiting for transfers between devices, per_device(): data_all = lax.all_gather(view_data[0], 'view', axis=0)  26.3 us
    ppermute x9, starting transfers between devices, halo(): above = lax.ppermute(array[:width], axis, down)  25.8 us
    ppermute x9, starting transfers between devices, halo(): below = lax.ppermute(array[-width:], axis, up)  21.1 us
    dot_general x8, matrix products, per_device(): t = jnp.einsum('lij,ljx->lix', by, c, precision=blur_mode)  19.6 us
    mul x7, other arithmetic, per_device(): padded = padded * corr  16.4 us
    dot_general x8, matrix products, per_device(): jnp.einsum('lix,lax->lia', t, bx_all[position], precision=blur_mode)  14 us
  transfers between devices with their start and end apart: 19, of which 16 were waited for; matrix products, arithmetic and copies ran while one was open for 12% of the time, Pallas kernels for 0%

profile of v3, /device:TPU:2, one launch (start us, length us, event | category | flops | bytes accessed | tf_op | source)
XLA Modules:
  0.0 280.0 jit_solution(5228117419383909691)
XLA Ops:
  11.0 7.2 %collective-permute-start.1 = (f32[1,128,512]{2,1,0:T(8,128)}, f32[1,128,512]{2,1,0:T(8,128)}, u32[]{:S(2)}, u32[]{:S(2)}) collective-permute-start(f32[1,128,512]{2,1,0:T(8,128)} %get-tuple-element.38), channel_id=1, source_target_pairs={{1,0},{2,1},{3,2},{4,3},{5,4},{6,5},{7,6},{8,7},{9,8},{10,9},{11,1... | collective-permute-start | bytes 786440 | tf_op jit(solution)/shard_map/ppermute | solution.py:18
  44.9 6.9 %fusion.445 = (f32[1,2,128,144]{2,0,3,1:T(1,128)}, f32[1,2,128,144]{2,0,3,1:T(1,128)}, f32[1,2,128,144]{2,0,3,1:T(1,128)}, f32[1,2,128,144]{2,0,3,1:T(1,128)}, f...) fusion(f32[8,2,128,144]{2,0,3,1:T(8,128)} %fusion.209), kind=kLoop, calls=%fused_computation.508 | loop fusion | bytes 2359296 | tf_op jit(solution)/shard_map/slice | solution.py:81
  59.0 3.3 %fusion.340 = f32[2,128,512]{2,1,0:T(8,128)S(1)} fusion(f32[1,128,512]{2,1,0:T(8,128)} %collective-permute-done.1, f32[2,128,512]{2,1,0:T(8,128)S(1)} %copy-done.3, f32[1,128,512]{2,1,0:T(8,128)} %collective-permute-done, f32[]{:T(128)} %bitcast.16, f32[]{:T(128)} %bitcast.15, f32[]{:T(128)} %bitcast.2, f32[2,128,144]{1,2,0:T(8,128)S(1)} %bitcast.229), kind=kOutput, calls=%fused_computation.391 | convolution fusion | flops 101580800 | bytes 1703948 | tf_op jit(solution)/shard_map/lij,ljx->lix/dot_general | solution.py:94
  62.2 26.3 %all-gather.2.cloned.1.call-done = f32[8,2,128,512]{3,2,1,0:T(8,128)} async-done(((f32[1,2,128,512]{3,2,1,0:T(8,128)}), f32[8,2,128,512]{3,2,1,0:T(8,128)}) %all-gather.2.cloned.1.call-update) | async-done | bytes 4194320 | tf_op jit(solution)/shard_map/all_gather | solution.py:60
  88.6 2.5 fusion.267
  92.6 5.1 %collective-permute-start.2 = (f32[2,128,512]{2,1,0:T(8,128)S(1)}, f32[2,128,512]{2,1,0:T(8,128)S(1)}, u32[]{:S(2)}, u32[]{:S(2)}) collective-permute-start(f32[2,128,512]{2,1,0:T(8,128)S(1)} %fusion.8), channel_id=1, source_target_pairs={{1,0},{2,1},{3,2},{4,3},{5,4},{6,5},{7,6},{8,7},{9,8},{10,9},{11,1... | collective-permute-start | bytes 1572872 | tf_op jit(solution)/shard_map/ppermute | solution.py:18
  97.7 2.1 collective-permute-start.3
  99.9 4.5 %collective-permute-done.2 = f32[2,128,512]{2,1,0:T(8,128)S(1)} collective-permute-done((f32[2,128,512]{2,1,0:T(8,128)S(1)}, f32[2,128,512]{2,1,0:T(8,128)S(1)}, u32[]{:S(2)}, u32[]{:S(2)}) %collective-permute-start.2) | collective-permute-done | bytes 524320 | tf_op jit(solution)/shard_map/ppermute | solution.py:18
  104.4 5.9 %collective-permute-done.3 = f32[2,128,512]{2,1,0:T(8,128)S(1)} collective-permute-done((f32[2,128,512]{2,1,0:T(8,128)S(1)}, f32[2,128,512]{2,1,0:T(8,128)S(1)}, u32[]{:S(2)}, u32[]{:S(2)}) %collective-permute-start.3) | collective-permute-done | bytes 524320 | tf_op jit(solution)/shard_map/ppermute | solution.py:17
  110.4 3.1 %fusion.266 = f32[4,128,512]{2,1,0:T(8,128)S(1)} fusion(f32[2,128,512]{2,1,0:T(8,128)S(1)} %collective-permute-done.2, f32[2,128,512]{2,1,0:T(8,128)S(1)} %fusion.8, f32[2,128,512]{2,1,0:T(8,128)S(1)} %collective-permute-done.3, f32[1,128,512]{2,1,0:T(8,128)} %collective-permute-done.1, f32[2,128,512]{2,1,0:T(8,128)S(1)} %copy-done.4, ...), kind=kLoop, calls=%fused_computation.313 | loop fusion | flops 3145728 | bytes 3670028 | tf_op jit(solution)/shard_map/mul | solution.py:103
  113.5 2.3 fusion.334
  119.0 1.9 collective-permute-start.4
  120.9 2.4 collective-permute-start.5
  124.0 3.6 %collective-permute-done.4 = f32[2,128,512]{2,1,0:T(8,128)S(1)} collective-permute-done((f32[2,128,512]{2,1,0:T(8,128)S(1)}, f32[2,128,512]{2,1,0:T(8,128)S(1)}, u32[]{:S(2)}, u32[]{:S(2)}) %collective-permute-start.4) | collective-permute-done | bytes 524320 | tf_op jit(solution)/shard_map/ppermute | solution.py:18
  127.6 5.9 %collective-permute-done.5 = f32[2,128,512]{2,1,0:T(8,128)S(1)} collective-permute-done((f32[2,128,512]{2,1,0:T(8,128)S(1)}, f32[2,128,512]{2,1,0:T(8,128)S(1)}, u32[]{:S(2)}, u32[]{:S(2)}) %collective-permute-start.5) | collective-permute-done | bytes 524320 | tf_op jit(solution)/shard_map/ppermute | solution.py:17
  133.5 2.2 fusion.262
  135.7 2.3 fusion.329
  141.1 1.9 collective-permute-start.6
  143.0 2.4 collective-permute-start.7
  145.6 4.2 %collective-permute-done.6 = f32[2,128,512]{2,1,0:T(8,128)S(1)} collective-permute-done((f32[2,128,512]{2,1,0:T(8,128)S(1)}, f32[2,128,512]{2,1,0:T(8,128)S(1)}, u32[]{:S(2)}, u32[]{:S(2)}) %collective-permute-start.6) | collective-permute-done | bytes 524320 | tf_op jit(solution)/shard_map/ppermute | solution.py:18
  149.7 5.9 %collective-permute-done.7 = f32[2,128,512]{2,1,0:T(8,128)S(1)} collective-permute-done((f32[2,128,512]{2,1,0:T(8,128)S(1)}, f32[2,128,512]{2,1,0:T(8,128)S(1)}, u32[]{:S(2)}, u32[]{:S(2)}) %collective-permute-start.7) | collective-permute-done | bytes 524320 | tf_op jit(solution)/shard_map/ppermute | solution.py:17
  155.7 2.2 fusion.258
  157.9 2.4 fusion.324
  165.3 2.4 collective-permute-start.9
  168.4 3.6 %collective-permute-done.8 = f32[2,128,512]{2,1,0:T(8,128)S(1)} collective-permute-done((f32[2,128,512]{2,1,0:T(8,128)S(1)}, f32[2,128,512]{2,1,0:T(8,128)S(1)}, u32[]{:S(2)}, u32[]{:S(2)}) %collective-permute-start.8) | collective-permute-done | bytes 524320 | tf_op jit(solution)/shard_map/ppermute | solution.py:18
  172.0 5.9 %collective-permute-done.9 = f32[2,128,512]{2,1,0:T(8,128)S(1)} collective-permute-done((f32[2,128,512]{2,1,0:T(8,128)S(1)}, f32[2,128,512]{2,1,0:T(8,128)S(1)}, u32[]{:S(2)}, u32[]{:S(2)}) %collective-permute-start.9) | collective-permute-done | bytes 524320 | tf_op jit(solution)/shard_map/ppermute | solution.py:17
  177.9 2.3 fusion.254
  180.2 2.3 fusion.319
  185.6 1.9 collective-permute-start.10
  187.5 2.4 collective-permute-start.11
  190.0 4.2 %collective-permute-done.10 = f32[2,128,512]{2,1,0:T(8,128)S(1)} collective-permute-done((f32[2,128,512]{2,1,0:T(8,128)S(1)}, f32[2,128,512]{2,1,0:T(8,128)S(1)}, u32[]{:S(2)}, u32[]{:S(2)}) %collective-permute-start.10) | collective-permute-done | bytes 524320 | tf_op jit(solution)/shard_map/ppermute | solution.py:18
  194.2 5.9 %collective-permute-done.11 = f32[2,128,512]{2,1,0:T(8,128)S(1)} collective-permute-done((f32[2,128,512]{2,1,0:T(8,128)S(1)}, f32[2,128,512]{2,1,0:T(8,128)S(1)}, u32[]{:S(2)}, u32[]{:S(2)}) %collective-permute-start.11) | collective-permute-done | bytes 524320 | tf_op jit(solution)/shard_map/ppermute | solution.py:17
  200.1 2.2 fusion.250
  202.4 2.4 fusion.314
  209.8 2.6 collective-permute-start.13
  213.1 3.4 %collective-permute-done.12 = f32[2,128,512]{2,1,0:T(8,128)S(1)} collective-permute-done((f32[2,128,512]{2,1,0:T(8,128)S(1)}, f32[2,128,512]{2,1,0:T(8,128)S(1)}, u32[]{:S(2)}, u32[]{:S(2)}) %collective-permute-start.12) | collective-permute-done | bytes 524320 | tf_op jit(solution)/shard_map/ppermute | solution.py:18
  216.5 5.9 %collective-permute-done.13 = f32[2,128,512]{2,1,0:T(8,128)S(1)} collective-permute-done((f32[2,128,512]{2,1,0:T(8,128)S(1)}, f32[2,128,512]{2,1,0:T(8,128)S(1)}, u32[]{:S(2)}, u32[]{:S(2)}) %collective-permute-start.13) | collective-permute-done | bytes 524320 | tf_op jit(solution)/shard_map/ppermute | solution.py:17
  222.4 2.3 fusion.246
  224.7 2.3 fusion.309
  230.1 1.9 collective-permute-start.14
  232.0 2.4 collective-permute-start.15
  234.5 4.2 %collective-permute-done.14 = f32[2,128,512]{2,1,0:T(8,128)S(1)} collective-permute-done((f32[2,128,512]{2,1,0:T(8,128)S(1)}, f32[2,128,512]{2,1,0:T(8,128)S(1)}, u32[]{:S(2)}, u32[]{:S(2)}) %collective-permute-start.14) | collective-permute-done | bytes 524320 | tf_op jit(solution)/shard_map/ppermute | solution.py:18
  238.7 5.9 %collective-permute-done.15 = f32[2,128,512]{2,1,0:T(8,128)S(1)} collective-permute-done((f32[2,128,512]{2,1,0:T(8,128)S(1)}, f32[2,128,512]{2,1,0:T(8,128)S(1)}, u32[]{:S(2)}, u32[]{:S(2)}) %collective-permute-start.15) | collective-permute-done | bytes 524320 | tf_op jit(solution)/shard_map/ppermute | solution.py:17
  244.6 2.2 fusion.242
  246.8 2.4 fusion.304
  254.8 2.4 collective-permute-start.17
  262.2 5.6 %collective-permute-done.17 = f32[2,128,512]{2,1,0:T(8,128)} collective-permute-done((f32[2,128,512]{2,1,0:T(8,128)}, f32[2,128,512]{2,1,0:T(8,128)}, u32[]{:S(2)}, u32[]{:S(2)}) %collective-permute-start.17) | collective-permute-done | bytes 524320 | tf_op jit(solution)/shard_map/ppermute | solution.py:17
  267.8 5.3 %fusion.299 = f32[1,2,128,512]{3,2,1,0:T(8,128)} fusion(f32[2,128,512]{2,1,0:T(8,128)} %fusion.78, f32[2,128,512]{2,1,0:T(8,128)} %collective-permute-done.17, f32[2,128,512]{2,1,0:T(8,128)} %collective-permute-done.16, f32[4,128,512]{2,1,0:T(8,128)} %copy-done.5, f32[4,128,512]{2,1,0:T(8,128)} %copy-done.2, f32[4,128,512]{2,1,0:T(8,128)} %copy-done.1, ...), kind=kLoop, calls=%fused_computation.346 | loop fusion | flops 2359296 | bytes 5767188 | tf_op jit(solution)/shard_map/broadcast_in_dim | solution.py:105
  (169 shorter events, 54.9 us)
Async XLA Ops:
  6.5 82.0 %all-gather.2.cloned.1.call-start = ((), (), s32[]{:S(2)}) async-start(), calls=%async_computation | async-start | bytes 4718592 | tf_op jit(solution)/shard_map/all_gather | solution.py:60
  9.1 49.8 %collective-permute-start = (f32[1,128,512]{2,1,0:T(8,128)}, f32[1,128,512]{2,1,0:T(8,128)}, u32[]{:S(2)}, u32[]{:S(2)}) collective-permute-start(f32[1,128,512]{2,1,0:T(8,128)} %get-tuple-element.37), channel_id=1, source_target_pairs={{0,1},{1,2},{2,3},{3,4},{4,5},{5,6},{6,7},{7,8},{8,9},{9,10},{10,1... | collective-permute-start | bytes 786440 | tf_op jit(solution)/shard_map/ppermute | solution.py:17
  11.0 47.9 %collective-permute-start.1 = (f32[1,128,512]{2,1,0:T(8,128)}, f32[1,128,512]{2,1,0:T(8,128)}, u32[]{:S(2)}, u32[]{:S(2)}) collective-permute-start(f32[1,128,512]{2,1,0:T(8,128)} %get-tuple-element.38), channel_id=1, source_target_pairs={{1,0},{2,1},{3,2},{4,3},{5,4},{6,5},{7,6},{8,7},{9,8},{10,9},{11,1... | collective-permute-start | bytes 786440 | tf_op jit(solution)/shard_map/ppermute | solution.py:18
  35.0 9.2 %copy-start.41 = (f32[8,3]{0,1:T(4,128)S(1)}, f32[8,3]{0,1:T(4,128)}, u32[]{:S(2)}) copy-start(f32[8,3]{0,1:T(4,128)} %param.11) | copy-start | bytes 292
  56.0 32.6 %copy-start.23 = (f32[1,2,128,144]{2,0,3,1:T(1,128)S(1)}, f32[1,2,128,144]{2,0,3,1:T(1,128)}, u32[]{:S(2)}) copy-start(f32[1,2,128,144]{2,0,3,1:T(1,128)} %copy-done.22) | copy-start | bytes 442372
  56.0 32.6 %copy-start.38 = (f32[2,128,136]{1,2,0:T(8,128)S(1)}, f32[2,128,136]{1,2,0:T(8,128)}, u32[]{:S(2)}) copy-start(f32[2,128,136]{1,2,0:T(8,128)} %get-tuple-element.69) | copy-start | bytes 417796
  56.0 32.6 %copy-start.39 = (f32[2,128,136]{1,2,0:T(8,128)S(1)}, f32[2,128,136]{1,2,0:T(8,128)}, u32[]{:S(2)}) copy-start(f32[2,128,136]{1,2,0:T(8,128)} %get-tuple-element.70) | copy-start | bytes 417796
  57.6 66.4 %copy-start.19 = (f32[1,2,128,144]{2,0,3,1:T(1,128)}, f32[1,2,128,144]{2,0,3,1:T(1,128)S(1)}, u32[]{:S(2)}) copy-start(f32[1,2,128,144]{2,0,3,1:T(1,128)S(1)} %get-tuple-element.10) | copy-start | bytes 442372
  57.6 87.9 %copy-start.16 = (f32[1,2,128,144]{2,0,3,1:T(1,128)}, f32[1,2,128,144]{2,0,3,1:T(1,128)S(1)}, u32[]{:S(2)}) copy-start(f32[1,2,128,144]{2,0,3,1:T(1,128)S(1)} %get-tuple-element.9) | copy-start | bytes 442372
  91.6 8.3 %copy-start.21 = (f32[1,2,128,144]{2,0,3,1:T(1,128)S(1)}, f32[1,2,128,144]{2,0,3,1:T(1,128)}, u32[]{:S(2)}) copy-start(f32[1,2,128,144]{2,0,3,1:T(1,128)} %get-tuple-element.26) | copy-start | bytes 442372
  91.6 18.8 %copy-start.4 = (f32[2,128,512]{2,1,0:T(8,128)S(1)}, f32[2,128,512]{2,1,0:T(8,128)}, u32[]{:S(2)}) copy-start(f32[2,128,512]{2,1,0:T(8,128)} %param.7) | copy-start | bytes 1572868
  92.6 11.8 %collective-permute-start.2 = (f32[2,128,512]{2,1,0:T(8,128)S(1)}, f32[2,128,512]{2,1,0:T(8,128)S(1)}, u32[]{:S(2)}, u32[]{:S(2)}) collective-permute-start(f32[2,128,512]{2,1,0:T(8,128)S(1)} %fusion.8), channel_id=1, source_target_pairs={{1,0},{2,1},{3,2},{4,3},{5,4},{6,5},{7,6},{8,7},{9,8},{10,9},{11,1... | collective-permute-start | bytes 1572872 | tf_op jit(solution)/shard_map/ppermute | solution.py:18
  97.7 12.6 %collective-permute-start.3 = (f32[2,128,512]{2,1,0:T(8,128)S(1)}, f32[2,128,512]{2,1,0:T(8,128)S(1)}, u32[]{:S(2)}, u32[]{:S(2)}) collective-permute-start(f32[2,128,512]{2,1,0:T(8,128)S(1)} %fusion.8), channel_id=1, source_target_pairs={{0,1},{1,2},{2,3},{3,4},{4,5},{5,6},{6,7},{7,8},{8,9},{9,10},{10,1... | collective-permute-start | bytes 1572872 | tf_op jit(solution)/shard_map/ppermute | solution.py:17
  99.9 13.6 %copy-start.36 = (f32[1,2,128,144]{2,0,3,1:T(1,128)S(1)}, f32[1,2,128,144]{2,0,3,1:T(1,128)}, u32[]{:S(2)}) copy-start(f32[1,2,128,144]{2,0,3,1:T(1,128)} %get-tuple-element.35) | copy-start | bytes 442372
  99.9 15.9 %copy-start.44 = (f32[8,2,128,512]{3,2,1,0:T(8,128)S(1)}, f32[8,2,128,512]{3,2,1,0:T(8,128)}, u32[]{:S(2)}) copy-start(f32[8,2,128,512]{3,2,1,0:T(8,128)} %all-gather.2.cloned.1.call-done) | copy-start | bytes 12582916
  118.0 5.4 %copy-start.42 = (f32[1,3]{0,1:T(4,128)S(1)}, f32[1,3]{0,1:T(4,128)}, u32[]{:S(2)}) copy-start(f32[1,3]{0,1:T(4,128)} %get-tuple-element.80) | copy-start | bytes 40
  118.0 5.4 %copy-start.43 = (f32[1,3]{0,1:T(4,128)S(1)}, f32[1,3]{0,1:T(4,128)}, u32[]{:S(2)}) copy-start(f32[1,3]{0,1:T(4,128)} %get-tuple-element.81) | copy-start | bytes 40
  118.0 6.0 %copy-start.18 = (f32[1,2,128,144]{2,0,3,1:T(1,128)S(1)}, f32[1,2,128,144]{2,0,3,1:T(1,128)}, u32[]{:S(2)}) copy-start(f32[1,2,128,144]{2,0,3,1:T(1,128)} %get-tuple-element.25) | copy-start | bytes 442372
  119.0 8.6 %collective-permute-start.4 = (f32[2,128,512]{2,1,0:T(8,128)S(1)}, f32[2,128,512]{2,1,0:T(8,128)S(1)}, u32[]{:S(2)}, u32[]{:S(2)}) collective-permute-start(f32[2,128,512]{2,1,0:T(8,128)S(1)} %fusion.18), channel_id=1, source_target_pairs={{1,0},{2,1},{3,2},{4,3},{5,4},{6,5},{7,6},{8,7},{9,8},{10,9},{11,1... | collective-permute-start | bytes 1572872 | tf_op jit(solution)/shard_map/ppermute | solution.py:18
  120.9 12.6 %collective-permute-start.5 = (f32[2,128,512]{2,1,0:T(8,128)S(1)}, f32[2,128,512]{2,1,0:T(8,128)S(1)}, u32[]{:S(2)}, u32[]{:S(2)}) collective-permute-start(f32[2,128,512]{2,1,0:T(8,128)S(1)} %fusion.18), channel_id=1, source_target_pairs={{0,1},{1,2},{2,3},{3,4},{4,5},{5,6},{6,7},{7,8},{8,9},{9,10},{10,1... | collective-permute-start | bytes 1572872 | tf_op jit(solution)/shard_map/ppermute | solution.py:17
  124.0 11.7 %copy-start.34 = (f32[1,2,128,144]{2,0,3,1:T(1,128)S(1)}, f32[1,2,128,144]{2,0,3,1:T(1,128)}, u32[]{:S(2)}) copy-start(f32[1,2,128,144]{2,0,3,1:T(1,128)} %get-tuple-element.34) | copy-start | bytes 442372
  141.1 8.6 %collective-permute-start.6 = (f32[2,128,512]{2,1,0:T(8,128)S(1)}, f32[2,128,512]{2,1,0:T(8,128)S(1)}, u32[]{:S(2)}, u32[]{:S(2)}) collective-permute-start(f32[2,128,512]{2,1,0:T(8,128)S(1)} %fusion.28), channel_id=1, source_target_pairs={{1,0},{2,1},{3,2},{4,3},{5,4},{6,5},{7,6},{8,7},{9,8},{10,9},{11,1... | collective-permute-start | bytes 1572872 | tf_op jit(solution)/shard_map/ppermute | solution.py:18
  143.0 12.6 %collective-permute-start.7 = (f32[2,128,512]{2,1,0:T(8,128)S(1)}, f32[2,128,512]{2,1,0:T(8,128)S(1)}, u32[]{:S(2)}, u32[]{:S(2)}) collective-permute-start(f32[2,128,512]{2,1,0:T(8,128)S(1)} %fusion.28), channel_id=1, source_target_pairs={{0,1},{1,2},{2,3},{3,4},{4,5},{5,6},{6,7},{7,8},{8,9},{9,10},{10,1... | collective-permute-start | bytes 1572872 | tf_op jit(solution)/shard_map/ppermute | solution.py:17
  145.5 12.3 %copy-start.32 = (f32[1,2,128,144]{2,0,3,1:T(1,128)S(1)}, f32[1,2,128,144]{2,0,3,1:T(1,128)}, u32[]{:S(2)}) copy-start(f32[1,2,128,144]{2,0,3,1:T(1,128)} %get-tuple-element.33) | copy-start | bytes 442372
  162.4 5.9 %copy-start.13 = (f32[1,2,128,144]{2,0,3,1:T(1,128)S(1)}, f32[1,2,128,144]{2,0,3,1:T(1,128)}, u32[]{:S(2)}) copy-start(f32[1,2,128,144]{2,0,3,1:T(1,128)} %get-tuple-element.23) | copy-start | bytes 442372
  162.4 6.0 %copy-start.14 = (f32[1,2,128,144]{2,0,3,1:T(1,128)S(1)}, f32[1,2,128,144]{2,0,3,1:T(1,128)}, u32[]{:S(2)}) copy-start(f32[1,2,128,144]{2,0,3,1:T(1,128)} %get-tuple-element.8) | copy-start | bytes 442372
  163.4 8.6 %collective-permute-start.8 = (f32[2,128,512]{2,1,0:T(8,128)S(1)}, f32[2,128,512]{2,1,0:T(8,128)S(1)}, u32[]{:S(2)}, u32[]{:S(2)}) collective-permute-start(f32[2,128,512]{2,1,0:T(8,128)S(1)} %fusion.38), channel_id=1, source_target_pairs={{1,0},{2,1},{3,2},{4,3},{5,4},{6,5},{7,6},{8,7},{9,8},{10,9},{11,1... | collective-permute-start | bytes 1572872 | tf_op jit(solution)/shard_map/ppermute | solution.py:18
  165.3 12.6 %collective-permute-start.9 = (f32[2,128,512]{2,1,0:T(8,128)S(1)}, f32[2,128,512]{2,1,0:T(8,128)S(1)}, u32[]{:S(2)}, u32[]{:S(2)}) collective-permute-start(f32[2,128,512]{2,1,0:T(8,128)S(1)} %fusion.38), channel_id=1, source_target_pairs={{0,1},{1,2},{2,3},{3,4},{4,5},{5,6},{6,7},{7,8},{8,9},{9,10},{10,1... | collective-permute-start | bytes 1572872 | tf_op jit(solution)/shard_map/ppermute | solution.py:17
  168.4 11.8 %copy-start.30 = (f32[1,2,128,144]{2,0,3,1:T(1,128)S(1)}, f32[1,2,128,144]{2,0,3,1:T(1,128)}, u32[]{:S(2)}) copy-start(f32[1,2,128,144]{2,0,3,1:T(1,128)} %get-tuple-element.32) | copy-start | bytes 442372
  180.2 19.9 %copy-start = (f32[4,128,512]{2,1,0:T(8,128)}, f32[4,128,512]{2,1,0:T(8,128)S(1)}, u32[]{:S(2)}) copy-start(f32[4,128,512]{2,1,0:T(8,128)S(1)} %fusion.254) | copy-start | bytes 3145732
  184.6 5.3 %copy-start.11 = (f32[1,2,128,144]{2,0,3,1:T(1,128)S(1)}, f32[1,2,128,144]{2,0,3,1:T(1,128)}, u32[]{:S(2)}) copy-start(f32[1,2,128,144]{2,0,3,1:T(1,128)} %get-tuple-element.22) | copy-start | bytes 442372
  184.6 5.4 %copy-start.12 = (f32[1,2,128,144]{2,0,3,1:T(1,128)S(1)}, f32[1,2,128,144]{2,0,3,1:T(1,128)}, u32[]{:S(2)}) copy-start(f32[1,2,128,144]{2,0,3,1:T(1,128)} %get-tuple-element.7) | copy-start | bytes 442372
  185.6 8.6 %collective-permute-start.10 = (f32[2,128,512]{2,1,0:T(8,128)S(1)}, f32[2,128,512]{2,1,0:T(8,128)S(1)}, u32[]{:S(2)}, u32[]{:S(2)}) collective-permute-start(f32[2,128,512]{2,1,0:T(8,128)S(1)} %fusion.48), channel_id=1, source_target_pairs={{1,0},{2,1},{3,2},{4,3},{5,4},{6,5},{7,6},{8,7},{9,8},{10,9},{11,1... | collective-permute-start | bytes 1572872 | tf_op jit(solution)/shard_map/ppermute | solution.py:18
  187.5 12.6 %collective-permute-start.11 = (f32[2,128,512]{2,1,0:T(8,128)S(1)}, f32[2,128,512]{2,1,0:T(8,128)S(1)}, u32[]{:S(2)}, u32[]{:S(2)}) collective-permute-start(f32[2,128,512]{2,1,0:T(8,128)S(1)} %fusion.48), channel_id=1, source_target_pairs={{0,1},{1,2},{2,3},{3,4},{4,5},{5,6},{6,7},{7,8},{8,9},{9,10},{10,1... | collective-permute-start | bytes 1572872 | tf_op jit(solution)/shard_map/ppermute | solution.py:17
  190.0 12.4 %copy-start.28 = (f32[1,2,128,144]{2,0,3,1:T(1,128)S(1)}, f32[1,2,128,144]{2,0,3,1:T(1,128)}, u32[]{:S(2)}) copy-start(f32[1,2,128,144]{2,0,3,1:T(1,128)} %get-tuple-element.31) | copy-start | bytes 442372
  202.4 20.0 %copy-start.1 = (f32[4,128,512]{2,1,0:T(8,128)}, f32[4,128,512]{2,1,0:T(8,128)S(1)}, u32[]{:S(2)}) copy-start(f32[4,128,512]{2,1,0:T(8,128)S(1)} %fusion.250) | copy-start | bytes 3145732
  206.9 6.2 %copy-start.9 = (f32[1,2,128,144]{2,0,3,1:T(1,128)S(1)}, f32[1,2,128,144]{2,0,3,1:T(1,128)}, u32[]{:S(2)}) copy-start(f32[1,2,128,144]{2,0,3,1:T(1,128)} %get-tuple-element.28) | copy-start | bytes 442372
  206.9 6.2 %copy-start.10 = (f32[1,2,128,144]{2,0,3,1:T(1,128)S(1)}, f32[1,2,128,144]{2,0,3,1:T(1,128)}, u32[]{:S(2)}) copy-start(f32[1,2,128,144]{2,0,3,1:T(1,128)} %get-tuple-element.6) | copy-start | bytes 442372
  207.9 8.6 %collective-permute-start.12 = (f32[2,128,512]{2,1,0:T(8,128)S(1)}, f32[2,128,512]{2,1,0:T(8,128)S(1)}, u32[]{:S(2)}, u32[]{:S(2)}) collective-permute-start(f32[2,128,512]{2,1,0:T(8,128)S(1)} %fusion.58), channel_id=1, source_target_pairs={{1,0},{2,1},{3,2},{4,3},{5,4},{6,5},{7,6},{8,7},{9,8},{10,9},{11,1... | collective-permute-start | bytes 1572872 | tf_op jit(solution)/shard_map/ppermute | solution.py:18
  209.8 12.6 %collective-permute-start.13 = (f32[2,128,512]{2,1,0:T(8,128)S(1)}, f32[2,128,512]{2,1,0:T(8,128)S(1)}, u32[]{:S(2)}, u32[]{:S(2)}) collective-permute-start(f32[2,128,512]{2,1,0:T(8,128)S(1)} %fusion.58), channel_id=1, source_target_pairs={{0,1},{1,2},{2,3},{3,4},{4,5},{5,6},{6,7},{7,8},{8,9},{9,10},{10,1... | collective-permute-start | bytes 1572872 | tf_op jit(solution)/shard_map/ppermute | solution.py:17
  213.1 11.6 %copy-start.26 = (f32[1,2,128,144]{2,0,3,1:T(1,128)S(1)}, f32[1,2,128,144]{2,0,3,1:T(1,128)}, u32[]{:S(2)}) copy-start(f32[1,2,128,144]{2,0,3,1:T(1,128)} %get-tuple-element.30) | copy-start | bytes 442372
  224.7 19.9 %copy-start.2 = (f32[4,128,512]{2,1,0:T(8,128)}, f32[4,128,512]{2,1,0:T(8,128)S(1)}, u32[]{:S(2)}) copy-start(f32[4,128,512]{2,1,0:T(8,128)S(1)} %fusion.246) | copy-start | bytes 3145732
  229.1 5.4 %copy-start.8 = (f32[1,2,128,144]{2,0,3,1:T(1,128)S(1)}, f32[1,2,128,144]{2,0,3,1:T(1,128)}, u32[]{:S(2)}) copy-start(f32[1,2,128,144]{2,0,3,1:T(1,128)} %get-tuple-element.5) | copy-start | bytes 442372
  230.1 8.6 %collective-permute-start.14 = (f32[2,128,512]{2,1,0:T(8,128)S(1)}, f32[2,128,512]{2,1,0:T(8,128)S(1)}, u32[]{:S(2)}, u32[]{:S(2)}) collective-permute-start(f32[2,128,512]{2,1,0:T(8,128)S(1)} %fusion.68), channel_id=1, source_target_pairs={{1,0},{2,1},{3,2},{4,3},{5,4},{6,5},{7,6},{8,7},{9,8},{10,9},{11,1... | collective-permute-start | bytes 1572872 | tf_op jit(solution)/shard_map/ppermute | solution.py:18
  232.0 12.6 %collective-permute-start.15 = (f32[2,128,512]{2,1,0:T(8,128)S(1)}, f32[2,128,512]{2,1,0:T(8,128)S(1)}, u32[]{:S(2)}, u32[]{:S(2)}) collective-permute-start(f32[2,128,512]{2,1,0:T(8,128)S(1)} %fusion.68), channel_id=1, source_target_pairs={{0,1},{1,2},{2,3},{3,4},{4,5},{5,6},{6,7},{7,8},{8,9},{9,10},{10,1... | collective-permute-start | bytes 1572872 | tf_op jit(solution)/shard_map/ppermute | solution.py:17
  234.5 12.3 %copy-start.25 = (f32[1,2,128,144]{2,0,3,1:T(1,128)S(1)}, f32[1,2,128,144]{2,0,3,1:T(1,128)}, u32[]{:S(2)}) copy-start(f32[1,2,128,144]{2,0,3,1:T(1,128)} %get-tuple-element.29) | copy-start | bytes 442372
  252.9 9.2 %collective-permute-start.16 = (f32[2,128,512]{2,1,0:T(8,128)}, f32[2,128,512]{2,1,0:T(8,128)}, u32[]{:S(2)}, u32[]{:S(2)}) collective-permute-start(f32[2,128,512]{2,1,0:T(8,128)} %fusion.78), channel_id=1, source_target_pairs={{1,0},{2,1},{3,2},{4,3},{5,4},{6,5},{7,6},{8,7},{9,8},{10,9},{11,1... | collective-permute-start | bytes 1572872 | tf_op jit(solution)/shard_map/ppermute | solution.py:18
  254.8 12.9 %collective-permute-start.17 = (f32[2,128,512]{2,1,0:T(8,128)}, f32[2,128,512]{2,1,0:T(8,128)}, u32[]{:S(2)}, u32[]{:S(2)}) collective-permute-start(f32[2,128,512]{2,1,0:T(8,128)} %fusion.78), channel_id=1, source_target_pairs={{0,1},{1,2},{2,3},{3,4},{4,5},{5,6},{6,7},{7,8},{8,9},{9,10},{10,1... | collective-permute-start | bytes 1572872 | tf_op jit(solution)/shard_map/ppermute | solution.py:17
  (16 other events, 43.5 us)
Sparse Core Ops, SparseCore 0:
  10.0 78.4 all-gather.1

commit v4 on v3

--- a/solution.py
+++ b/solution.py
@@ -10,12 +10,19 @@
 blur_mode = lax.Precision.HIGH
 
 
-def halo(array, axis, width):
+def halo(array, axis, width, pieces=2):
     size = lax.axis_size(axis)
     up = [(i, i + 1) for i in range(size - 1)]
     down = [(i + 1, i) for i in range(size - 1)]
-    below = lax.ppermute(array[-width:], axis, up)
-    above = lax.ppermute(array[:width], axis, down)
+    rows = array.shape[1]
+    step = rows // pieces
+    below, above = [], []
+    for k in range(pieces):
+        part = array[:, k * step : (k + 1) * step]
+        below.append(lax.ppermute(part[-width:], axis, up))
+        above.append(lax.ppermute(part[:width], axis, down))
+    below = jnp.concatenate(below, axis=1)
+    above = jnp.concatenate(above, axis=1)
     return jnp.concatenate([below, array, above], axis=0)
 
 
@@ -102,6 +109,7 @@
             corr = corr + kz[k] * gp[2 - k : 2 - k + count + 2]
         padded = padded * corr
         results = jnp.where(my_view == view_id, padded[RZ:-RZ], results)
+        padded, results = lax.optimization_barrier((padded, results))
     return results[None]
 
 

time: 282 us -> 346 us (1.23)
  starting transfers between devices: 46.8 us -> 137 us
  waiting for transfers between devices: 102 us -> 51.6 us
  local copies, waits for them, and re-layouts: 20.8 us -> 36.9 us
  matrix products: 52.1 us -> 58.8 us
    ppermute x18 -> x36, starting transfers between devices: 46.8 us -> 137 us  [the longest x18 101 us: halo(): above.append(lax.ppermute(part[:width], axis, down))]
    ppermute x18 -> x36, waiting for transfers between devices: 74.7 us -> 31.7 us  [the longest x18 24.4 us: halo(): above.append(lax.ppermute(part[:width], axis, down))]
    slice x16, local copies, waits for them, and re-layouts: 1.07 us -> 11.9 us  [band_matrix(): diagonal = mats[..., reach:reach + block]]
    all_gather x1, waiting for transfers between devices: 26.3 us -> 19.2 us  [per_device(): data_all = lax.all_gather(view_data[0], 'view', axis=0)]
    dot_general x8, matrix products: 14 us -> 21 us  [per_device(): jnp.einsum('lix,lax->lia', t, bx_all[position], precision=blur_mode)]
    slice x2 -> x9, local copies, waits for them, and re-layouts: 2.46 us -> 8.51 us  [the longest x8 6.55 us: halo(): part = array[:, k * step:(k + 1) * step]]
    broadcast_in_dim x1 -> x0, other arithmetic: 5.34 us -> none  [per_device(): return results[None]]
    slice x1, local copies, waits for them, and re-layouts: 6.87 us -> 1.62 us  [per_device(): bx_all = [band_matrix(mats[2][p], nx, reach) for p in range(view_count)]]
  transfers between devices with their start and end apart: 19 -> 37, of which waited for: 16 -> 17; matrix products, arithmetic and copies ran while one was open for 12% -> 13% of each run, Pallas kernels for 0% -> 0%
where the time goes in v4:
time: 346 us; the launch traced here: 344 us
  starting transfers between devices  137 us (40%)
  matrix products  58.8 us (17%)
  waiting for transfers between devices  51.6 us (15%)
  local copies, waits for them, and re-layouts  36.9 us (11%)
  between operations  36.1 us (10%)
  other arithmetic  23.1 us (7%)
    ppermute x18, starting transfers between devices, halo(): above.append(lax.ppermute(part[:width], axis, down))  101 us
    ppermute x18, starting transfers between devices, halo(): below.append(lax.ppermute(part[-width:], axis, up))  36.4 us
    ppermute x18, waiting for transfers between devices, halo(): above.append(lax.ppermute(part[:width], axis, down))  24.4 us
    dot_general x8, matrix products, per_device(): jnp.einsum('lix,lax->lia', t, bx_all[position], precision=blur_mode)  21 us
    dot_general x8, matrix products, per_device(): t = jnp.einsum('lij,ljx->lix', by, c, precision=blur_mode)  19.2 us
    all_gather x1, waiting for transfers between devices, per_device(): data_all = lax.all_gather(view_data[0], 'view', axis=0)  19.2 us
    mul x8, other arithmetic, per_device(): padded = padded * corr  17.7 us
    slice x16, local copies, waits for them, and re-layouts, band_matrix(): diagonal = mats[..., reach:reach + block]  11.9 us
  transfers between devices with their start and end apart: 37, of which 17 were waited for; matrix products, arithmetic and copies ran while one was open for 13% of the time, Pallas kernels for 0%

profile of v4, /device:TPU:2, one launch (start us, length us, event | category | flops | bytes accessed | tf_op | source)
XLA Modules:
  0.0 343.7 jit_solution(9235379833621989109)
XLA Ops:
  11.1 3.9 %collective-permute-start.1 = (f32[1,64,512]{2,1,0:T(8,128)}, f32[1,64,512]{2,1,0:T(8,128)}, u32[]{:S(2)}, u32[]{:S(2)}) collective-permute-start(f32[1,64,512]{2,1,0:T(8,128)} %get-tuple-element.83), channel_id=1, source_target_pairs={{0,1},{1,2},{2,3},{3,4},{4,5},{5,6},{6,7},{7,8},{8,9},{9,10},{10,1... | collective-permute-start | bytes 393224 | tf_op jit(solution)/shard_map/ppermute | solution.py:22
  15.1 5.2 %collective-permute-start.2 = (f32[1,64,512]{2,1,0:T(8,128)}, f32[1,64,512]{2,1,0:T(8,128)}, u32[]{:S(2)}, u32[]{:S(2)}) collective-permute-start(f32[1,64,512]{2,1,0:T(8,128)} %get-tuple-element.85), channel_id=1, source_target_pairs={{1,0},{2,1},{3,2},{4,3},{5,4},{6,5},{7,6},{8,7},{9,8},{10,9},{11,1... | collective-permute-start | bytes 393224 | tf_op jit(solution)/shard_map/ppermute | solution.py:23
  20.2 2.6 collective-permute-start.3
  43.1 2.7 fusion.207
  67.0 2.3 fusion.301
  69.3 19.2 %all-gather.2.cloned.1.call-done = f32[8,2,128,512]{3,2,1,0:T(8,128)} async-done(((f32[1,2,128,512]{3,2,1,0:T(8,128)}), f32[8,2,128,512]{3,2,1,0:T(8,128)}) %all-gather.2.cloned.1.call-update) | async-done | bytes 4194320 | tf_op jit(solution)/shard_map/all_gather | solution.py:67
  88.7 2.6 fusion.271
  96.2 5.7 %collective-permute-start.4 = (f32[2,64,512]{2,1,0:T(8,128)}, f32[2,64,512]{2,1,0:T(8,128)S(1)}, u32[]{:S(2)}, u32[]{:S(2)}) collective-permute-start(f32[2,64,512]{2,1,0:T(8,128)} %get-tuple-element.82), channel_id=1, source_target_pairs={{1,0},{2,1},{3,2},{4,3},{5,4},{6,5},{7,6},{8,7},{9,8},{10,9},{11,1... | collective-permute-start | bytes 786440 | tf_op jit(solution)/shard_map/ppermute | solution.py:23
  105.3 5.9 %collective-permute-start.5 = (f32[2,64,512]{2,1,0:T(8,128)S(1)}, f32[2,64,512]{2,1,0:T(8,128)S(1)}, u32[]{:S(2)}, u32[]{:S(2)}) collective-permute-start(f32[2,64,512]{2,1,0:T(8,128)S(1)} %get-tuple-element.81), channel_id=1, source_target_pairs={{1,0},{2,1},{3,2},{4,3},{5,4},{6,5},{7,6},{8,7},{9,8},{10,9},{11,1... | collective-permute-start | bytes 786440 | tf_op jit(solution)/shard_map/ppermute | solution.py:23
  111.8 3.1 collective-permute-done.5
  115.0 2.3 fusion.270
  117.3 2.3 fusion.362
  119.7 2.7 fusion.274
  126.6 5.9 %collective-permute-start.8 = (f32[2,64,512]{2,1,0:T(8,128)}, f32[2,64,512]{2,1,0:T(8,128)S(1)}, u32[]{:S(2)}, u32[]{:S(2)}) collective-permute-start(f32[2,64,512]{2,1,0:T(8,128)} %get-tuple-element.80), channel_id=1, source_target_pairs={{1,0},{2,1},{3,2},{4,3},{5,4},{6,5},{7,6},{8,7},{9,8},{10,9},{11,1... | collective-permute-start | bytes 786440 | tf_op jit(solution)/shard_map/ppermute | solution.py:23
  136.4 5.8 %collective-permute-start.9 = (f32[2,64,512]{2,1,0:T(8,128)}, f32[2,64,512]{2,1,0:T(8,128)S(1)}, u32[]{:S(2)}, u32[]{:S(2)}) collective-permute-start(f32[2,64,512]{2,1,0:T(8,128)} %get-tuple-element.79), channel_id=1, source_target_pairs={{1,0},{2,1},{3,2},{4,3},{5,4},{6,5},{7,6},{8,7},{9,8},{10,9},{11,1... | collective-permute-start | bytes 786440 | tf_op jit(solution)/shard_map/ppermute | solution.py:23
  143.3 3.1 collective-permute-done.9
  148.8 2.5 fusion.353
  151.4 2.6 fusion.277
  158.9 5.8 %collective-permute-start.12 = (f32[2,64,512]{2,1,0:T(8,128)}, f32[2,64,512]{2,1,0:T(8,128)S(1)}, u32[]{:S(2)}, u32[]{:S(2)}) collective-permute-start(f32[2,64,512]{2,1,0:T(8,128)} %get-tuple-element.78), channel_id=1, source_target_pairs={{1,0},{2,1},{3,2},{4,3},{5,4},{6,5},{7,6},{8,7},{9,8},{10,9},{11,1... | collective-permute-start | bytes 786440 | tf_op jit(solution)/shard_map/ppermute | solution.py:23
  168.0 5.8 %collective-permute-start.13 = (f32[2,64,512]{2,1,0:T(8,128)}, f32[2,64,512]{2,1,0:T(8,128)S(1)}, u32[]{:S(2)}, u32[]{:S(2)}) collective-permute-start(f32[2,64,512]{2,1,0:T(8,128)} %get-tuple-element.77), channel_id=1, source_target_pairs={{1,0},{2,1},{3,2},{4,3},{5,4},{6,5},{7,6},{8,7},{9,8},{10,9},{11,1... | collective-permute-start | bytes 786440 | tf_op jit(solution)/shard_map/ppermute | solution.py:23
  174.8 3.1 collective-permute-done.13
  180.3 2.5 fusion.344
  183.0 2.6 fusion.280
  189.7 5.8 %collective-permute-start.16 = (f32[2,64,512]{2,1,0:T(8,128)}, f32[2,64,512]{2,1,0:T(8,128)S(1)}, u32[]{:S(2)}, u32[]{:S(2)}) collective-permute-start(f32[2,64,512]{2,1,0:T(8,128)} %get-tuple-element.76), channel_id=1, source_target_pairs={{1,0},{2,1},{3,2},{4,3},{5,4},{6,5},{7,6},{8,7},{9,8},{10,9},{11,1... | collective-permute-start | bytes 786440 | tf_op jit(solution)/shard_map/ppermute | solution.py:23
  199.5 5.8 %collective-permute-start.17 = (f32[2,64,512]{2,1,0:T(8,128)}, f32[2,64,512]{2,1,0:T(8,128)S(1)}, u32[]{:S(2)}, u32[]{:S(2)}) collective-permute-start(f32[2,64,512]{2,1,0:T(8,128)} %get-tuple-element.75), channel_id=1, source_target_pairs={{1,0},{2,1},{3,2},{4,3},{5,4},{6,5},{7,6},{8,7},{9,8},{10,9},{11,1... | collective-permute-start | bytes 786440 | tf_op jit(solution)/shard_map/ppermute | solution.py:23
  206.3 3.1 collective-permute-done.17
  209.5 2.3 fusion.258
  211.9 2.3 fusion.335
  214.4 2.7 fusion.283
  222.1 5.8 %collective-permute-start.20 = (f32[2,64,512]{2,1,0:T(8,128)}, f32[2,64,512]{2,1,0:T(8,128)S(1)}, u32[]{:S(2)}, u32[]{:S(2)}) collective-permute-start(f32[2,64,512]{2,1,0:T(8,128)} %get-tuple-element.74), channel_id=1, source_target_pairs={{1,0},{2,1},{3,2},{4,3},{5,4},{6,5},{7,6},{8,7},{9,8},{10,9},{11,1... | collective-permute-start | bytes 786440 | tf_op jit(solution)/shard_map/ppermute | solution.py:23
  231.3 6.0 %collective-permute-start.21 = (f32[2,64,512]{2,1,0:T(8,128)}, f32[2,64,512]{2,1,0:T(8,128)S(1)}, u32[]{:S(2)}, u32[]{:S(2)}) collective-permute-start(f32[2,64,512]{2,1,0:T(8,128)} %get-tuple-element.73), channel_id=1, source_target_pairs={{1,0},{2,1},{3,2},{4,3},{5,4},{6,5},{7,6},{8,7},{9,8},{10,9},{11,1... | collective-permute-start | bytes 786440 | tf_op jit(solution)/shard_map/ppermute | solution.py:23
  237.9 3.3 collective-permute-done.21
  243.5 2.4 fusion.326
  246.1 2.6 fusion.286
  252.8 5.8 %collective-permute-start.24 = (f32[2,64,512]{2,1,0:T(8,128)}, f32[2,64,512]{2,1,0:T(8,128)S(1)}, u32[]{:S(2)}, u32[]{:S(2)}) collective-permute-start(f32[2,64,512]{2,1,0:T(8,128)} %get-tuple-element.72), channel_id=1, source_target_pairs={{1,0},{2,1},{3,2},{4,3},{5,4},{6,5},{7,6},{8,7},{9,8},{10,9},{11,1... | collective-permute-start | bytes 786440 | tf_op jit(solution)/shard_map/ppermute | solution.py:23
  262.5 5.8 %collective-permute-start.25 = (f32[2,64,512]{2,1,0:T(8,128)}, f32[2,64,512]{2,1,0:T(8,128)S(1)}, u32[]{:S(2)}, u32[]{:S(2)}) collective-permute-start(f32[2,64,512]{2,1,0:T(8,128)} %get-tuple-element.71), channel_id=1, source_target_pairs={{1,0},{2,1},{3,2},{4,3},{5,4},{6,5},{7,6},{8,7},{9,8},{10,9},{11,1... | collective-permute-start | bytes 786440 | tf_op jit(solution)/shard_map/ppermute | solution.py:23
  269.4 3.0 collective-permute-done.25
  274.9 2.5 fusion.317
  277.5 2.7 fusion.289
  285.1 5.8 %collective-permute-start.28 = (f32[2,64,512]{2,1,0:T(8,128)}, f32[2,64,512]{2,1,0:T(8,128)S(1)}, u32[]{:S(2)}, u32[]{:S(2)}) collective-permute-start(f32[2,64,512]{2,1,0:T(8,128)} %get-tuple-element.70), channel_id=1, source_target_pairs={{1,0},{2,1},{3,2},{4,3},{5,4},{6,5},{7,6},{8,7},{9,8},{10,9},{11,1... | collective-permute-start | bytes 786440 | tf_op jit(solution)/shard_map/ppermute | solution.py:23
  294.2 5.8 %collective-permute-start.29 = (f32[2,64,512]{2,1,0:T(8,128)}, f32[2,64,512]{2,1,0:T(8,128)S(1)}, u32[]{:S(2)}, u32[]{:S(2)}) collective-permute-start(f32[2,64,512]{2,1,0:T(8,128)} %get-tuple-element.69), channel_id=1, source_target_pairs={{1,0},{2,1},{3,2},{4,3},{5,4},{6,5},{7,6},{8,7},{9,8},{10,9},{11,1... | collective-permute-start | bytes 786440 | tf_op jit(solution)/shard_map/ppermute | solution.py:23
  301.0 3.2 collective-permute-done.29
  304.2 2.3 fusion.246
  306.6 2.4 fusion.308
  309.1 2.6 fusion.292
  315.8 5.8 %collective-permute-start.32 = (f32[2,64,512]{2,1,0:T(8,128)}, f32[2,64,512]{2,1,0:T(8,128)S(1)}, u32[]{:S(2)}, u32[]{:S(2)}) collective-permute-start(f32[2,64,512]{2,1,0:T(8,128)} %get-tuple-element.68), channel_id=1, source_target_pairs={{1,0},{2,1},{3,2},{4,3},{5,4},{6,5},{7,6},{8,7},{9,8},{10,9},{11,1... | collective-permute-start | bytes 786440 | tf_op jit(solution)/shard_map/ppermute | solution.py:23
  324.2 5.8 %collective-permute-start.33 = (f32[2,64,512]{2,1,0:T(8,128)S(1)}, f32[2,64,512]{2,1,0:T(8,128)S(1)}, u32[]{:S(2)}, u32[]{:S(2)}) collective-permute-start(f32[2,64,512]{2,1,0:T(8,128)S(1)} %get-tuple-element.67), channel_id=1, source_target_pairs={{1,0},{2,1},{3,2},{4,3},{5,4},{6,5},{7,6},{8,7},{9,8},{10,9},{11,1... | collective-permute-start | bytes 786440 | tf_op jit(solution)/shard_map/ppermute | solution.py:23
  331.5 2.4 collective-permute-done.33
  (367 shorter events, 109.7 us)
Async XLA Ops:
  6.5 82.0 %all-gather.2.cloned.1.call-start = ((), (), s32[]{:S(2)}) async-start(), calls=%async_computation | async-start | bytes 4718592 | tf_op jit(solution)/shard_map/all_gather | solution.py:67
  9.2 54.1 %collective-permute-start = (f32[1,64,512]{2,1,0:T(8,128)}, f32[1,64,512]{2,1,0:T(8,128)}, u32[]{:S(2)}, u32[]{:S(2)}) collective-permute-start(f32[1,64,512]{2,1,0:T(8,128)} %get-tuple-element.86), channel_id=1, source_target_pairs={{0,1},{1,2},{2,3},{3,4},{4,5},{5,6},{6,7},{7,8},{8,9},{9,10},{10,1... | collective-permute-start | bytes 393224 | tf_op jit(solution)/shard_map/ppermute | solution.py:22
  11.1 54.0 %collective-permute-start.1 = (f32[1,64,512]{2,1,0:T(8,128)}, f32[1,64,512]{2,1,0:T(8,128)}, u32[]{:S(2)}, u32[]{:S(2)}) collective-permute-start(f32[1,64,512]{2,1,0:T(8,128)} %get-tuple-element.83), channel_id=1, source_target_pairs={{0,1},{1,2},{2,3},{3,4},{4,5},{5,6},{6,7},{7,8},{8,9},{9,10},{10,1... | collective-permute-start | bytes 393224 | tf_op jit(solution)/shard_map/ppermute | solution.py:22
  15.1 49.2 %collective-permute-start.2 = (f32[1,64,512]{2,1,0:T(8,128)}, f32[1,64,512]{2,1,0:T(8,128)}, u32[]{:S(2)}, u32[]{:S(2)}) collective-permute-start(f32[1,64,512]{2,1,0:T(8,128)} %get-tuple-element.85), channel_id=1, source_target_pairs={{1,0},{2,1},{3,2},{4,3},{5,4},{6,5},{7,6},{8,7},{9,8},{10,9},{11,1... | collective-permute-start | bytes 393224 | tf_op jit(solution)/shard_map/ppermute | solution.py:23
  20.2 45.9 %collective-permute-start.3 = (f32[1,64,512]{2,1,0:T(8,128)}, f32[1,64,512]{2,1,0:T(8,128)}, u32[]{:S(2)}, u32[]{:S(2)}) collective-permute-start(f32[1,64,512]{2,1,0:T(8,128)} %get-tuple-element.84), channel_id=1, source_target_pairs={{1,0},{2,1},{3,2},{4,3},{5,4},{6,5},{7,6},{8,7},{9,8},{10,9},{11,1... | collective-permute-start | bytes 393224 | tf_op jit(solution)/shard_map/ppermute | solution.py:23
  55.5 39.9 %copy-start.21 = (f32[1,2,128,144]{2,0,3,1:T(1,128)}, f32[1,2,128,144]{2,0,3,1:T(1,128)S(1)}, u32[]{:S(2)}) copy-start(f32[1,2,128,144]{2,0,3,1:T(1,128)S(1)} %get-tuple-element.40) | copy-start | bytes 442372
  55.5 77.0 %copy-start.17 = (f32[1,2,128,144]{2,0,3,1:T(1,128)}, f32[1,2,128,144]{2,0,3,1:T(1,128)S(1)}, u32[]{:S(2)}) copy-start(f32[1,2,128,144]{2,0,3,1:T(1,128)S(1)} %get-tuple-element.39) | copy-start | bytes 442372
  60.3 6.8 %copy-start.1 = (f32[2,128,512]{2,1,0:T(8,128)S(1)}, f32[2,128,512]{2,1,0:T(8,128)}, u32[]{:S(2)}) copy-start(f32[2,128,512]{2,1,0:T(8,128)} %param.7) | copy-start | bytes 1572868
  62.0 26.7 %copy-start.28 = (f32[1,2,128,144]{2,0,3,1:T(1,128)S(1)}, f32[1,2,128,144]{2,0,3,1:T(1,128)}, u32[]{:S(2)}) copy-start(f32[1,2,128,144]{2,0,3,1:T(1,128)} %copy-done.27) | copy-start | bytes 442372
  62.0 26.7 %copy-start.71 = (f32[2,128,136]{1,2,0:T(8,128)S(1)}, f32[2,128,136]{1,2,0:T(8,128)}, u32[]{:S(2)}) copy-start(f32[2,128,136]{1,2,0:T(8,128)} %get-tuple-element.117) | copy-start | bytes 417796
  62.0 26.7 %copy-start.72 = (f32[2,128,136]{1,2,0:T(8,128)S(1)}, f32[2,128,136]{1,2,0:T(8,128)}, u32[]{:S(2)}) copy-start(f32[2,128,136]{1,2,0:T(8,128)} %get-tuple-element.118) | copy-start | bytes 417796
  91.8 12.1 %copy-start.15 = (f32[1,2,128,144]{2,0,3,1:T(1,128)S(1)}, f32[1,2,128,144]{2,0,3,1:T(1,128)}, u32[]{:S(2)}) copy-start(f32[1,2,128,144]{2,0,3,1:T(1,128)} %get-tuple-element.54) | copy-start | bytes 442372
  93.5 17.7 %collective-permute-start.6 = (f32[2,64,512]{2,1,0:T(8,128)}, f32[2,64,512]{2,1,0:T(8,128)S(1)}, u32[]{:S(2)}, u32[]{:S(2)}) collective-permute-start(f32[2,64,512]{2,1,0:T(8,128)} %get-tuple-element.82), channel_id=1, source_target_pairs={{0,1},{1,2},{2,3},{3,4},{4,5},{5,6},{6,7},{7,8},{8,9},{9,10},{10,1... | collective-permute-start | bytes 786440 | tf_op jit(solution)/shard_map/ppermute | solution.py:22
  96.2 15.0 %collective-permute-start.4 = (f32[2,64,512]{2,1,0:T(8,128)}, f32[2,64,512]{2,1,0:T(8,128)S(1)}, u32[]{:S(2)}, u32[]{:S(2)}) collective-permute-start(f32[2,64,512]{2,1,0:T(8,128)} %get-tuple-element.82), channel_id=1, source_target_pairs={{1,0},{2,1},{3,2},{4,3},{5,4},{6,5},{7,6},{8,7},{9,8},{10,9},{11,1... | collective-permute-start | bytes 786440 | tf_op jit(solution)/shard_map/ppermute | solution.py:23
  102.0 9.8 %collective-permute-start.7 = (f32[2,64,512]{2,1,0:T(8,128)S(1)}, f32[2,64,512]{2,1,0:T(8,128)S(1)}, u32[]{:S(2)}, u32[]{:S(2)}) collective-permute-start(f32[2,64,512]{2,1,0:T(8,128)S(1)} %get-tuple-element.81), channel_id=1, source_target_pairs={{0,1},{1,2},{2,3},{3,4},{4,5},{5,6},{6,7},{7,8},{8,9},{9,10},{10,1... | collective-permute-start | bytes 786440 | tf_op jit(solution)/shard_map/ppermute | solution.py:22
  105.3 9.6 %collective-permute-start.5 = (f32[2,64,512]{2,1,0:T(8,128)S(1)}, f32[2,64,512]{2,1,0:T(8,128)S(1)}, u32[]{:S(2)}, u32[]{:S(2)}) collective-permute-start(f32[2,64,512]{2,1,0:T(8,128)S(1)} %get-tuple-element.81), channel_id=1, source_target_pairs={{1,0},{2,1},{3,2},{4,3},{5,4},{6,5},{7,6},{8,7},{9,8},{10,9},{11,1... | collective-permute-start | bytes 786440 | tf_op jit(solution)/shard_map/ppermute | solution.py:23
  124.7 17.5 %collective-permute-start.10 = (f32[2,64,512]{2,1,0:T(8,128)}, f32[2,64,512]{2,1,0:T(8,128)S(1)}, u32[]{:S(2)}, u32[]{:S(2)}) collective-permute-start(f32[2,64,512]{2,1,0:T(8,128)} %get-tuple-element.80), channel_id=1, source_target_pairs={{0,1},{1,2},{2,3},{3,4},{4,5},{5,6},{6,7},{7,8},{8,9},{9,10},{10,1... | collective-permute-start | bytes 786440 | tf_op jit(solution)/shard_map/ppermute | solution.py:22
  126.6 15.6 %collective-permute-start.8 = (f32[2,64,512]{2,1,0:T(8,128)}, f32[2,64,512]{2,1,0:T(8,128)S(1)}, u32[]{:S(2)}, u32[]{:S(2)}) collective-permute-start(f32[2,64,512]{2,1,0:T(8,128)} %get-tuple-element.80), channel_id=1, source_target_pairs={{1,0},{2,1},{3,2},{4,3},{5,4},{6,5},{7,6},{8,7},{9,8},{10,9},{11,1... | collective-permute-start | bytes 786440 | tf_op jit(solution)/shard_map/ppermute | solution.py:23
  133.3 10.0 %collective-permute-start.11 = (f32[2,64,512]{2,1,0:T(8,128)}, f32[2,64,512]{2,1,0:T(8,128)S(1)}, u32[]{:S(2)}, u32[]{:S(2)}) collective-permute-start(f32[2,64,512]{2,1,0:T(8,128)} %get-tuple-element.79), channel_id=1, source_target_pairs={{0,1},{1,2},{2,3},{3,4},{4,5},{5,6},{6,7},{7,8},{8,9},{9,10},{10,1... | collective-permute-start | bytes 786440 | tf_op jit(solution)/shard_map/ppermute | solution.py:22
  136.4 9.9 %collective-permute-start.9 = (f32[2,64,512]{2,1,0:T(8,128)}, f32[2,64,512]{2,1,0:T(8,128)S(1)}, u32[]{:S(2)}, u32[]{:S(2)}) collective-permute-start(f32[2,64,512]{2,1,0:T(8,128)} %get-tuple-element.79), channel_id=1, source_target_pairs={{1,0},{2,1},{3,2},{4,3},{5,4},{6,5},{7,6},{8,7},{9,8},{10,9},{11,1... | collective-permute-start | bytes 786440 | tf_op jit(solution)/shard_map/ppermute | solution.py:23
  154.4 12.2 %copy-start.13 = (f32[1,2,128,144]{2,0,3,1:T(1,128)S(1)}, f32[1,2,128,144]{2,0,3,1:T(1,128)}, u32[]{:S(2)}) copy-start(f32[1,2,128,144]{2,0,3,1:T(1,128)} %get-tuple-element.38) | copy-start | bytes 442372
  156.3 17.5 %collective-permute-start.14 = (f32[2,64,512]{2,1,0:T(8,128)}, f32[2,64,512]{2,1,0:T(8,128)S(1)}, u32[]{:S(2)}, u32[]{:S(2)}) collective-permute-start(f32[2,64,512]{2,1,0:T(8,128)} %get-tuple-element.78), channel_id=1, source_target_pairs={{0,1},{1,2},{2,3},{3,4},{4,5},{5,6},{6,7},{7,8},{8,9},{9,10},{10,1... | collective-permute-start | bytes 786440 | tf_op jit(solution)/shard_map/ppermute | solution.py:22
  158.9 14.8 %collective-permute-start.12 = (f32[2,64,512]{2,1,0:T(8,128)}, f32[2,64,512]{2,1,0:T(8,128)S(1)}, u32[]{:S(2)}, u32[]{:S(2)}) collective-permute-start(f32[2,64,512]{2,1,0:T(8,128)} %get-tuple-element.78), channel_id=1, source_target_pairs={{1,0},{2,1},{3,2},{4,3},{5,4},{6,5},{7,6},{8,7},{9,8},{10,9},{11,1... | collective-permute-start | bytes 786440 | tf_op jit(solution)/shard_map/ppermute | solution.py:23
  164.7 10.0 %collective-permute-start.15 = (f32[2,64,512]{2,1,0:T(8,128)}, f32[2,64,512]{2,1,0:T(8,128)S(1)}, u32[]{:S(2)}, u32[]{:S(2)}) collective-permute-start(f32[2,64,512]{2,1,0:T(8,128)} %get-tuple-element.77), channel_id=1, source_target_pairs={{0,1},{1,2},{2,3},{3,4},{4,5},{5,6},{6,7},{7,8},{8,9},{9,10},{10,1... | collective-permute-start | bytes 786440 | tf_op jit(solution)/shard_map/ppermute | solution.py:22
  168.0 9.9 %collective-permute-start.13 = (f32[2,64,512]{2,1,0:T(8,128)}, f32[2,64,512]{2,1,0:T(8,128)S(1)}, u32[]{:S(2)}, u32[]{:S(2)}) collective-permute-start(f32[2,64,512]{2,1,0:T(8,128)} %get-tuple-element.77), channel_id=1, source_target_pairs={{1,0},{2,1},{3,2},{4,3},{5,4},{6,5},{7,6},{8,7},{9,8},{10,9},{11,1... | collective-permute-start | bytes 786440 | tf_op jit(solution)/shard_map/ppermute | solution.py:23
  186.0 9.6 %copy-start.7 = (f32[1,2,128,144]{2,0,3,1:T(1,128)S(1)}, f32[1,2,128,144]{2,0,3,1:T(1,128)}, u32[]{:S(2)}) copy-start(f32[1,2,128,144]{2,0,3,1:T(1,128)} %get-tuple-element.52) | copy-start | bytes 442372
  187.8 17.5 %collective-permute-start.18 = (f32[2,64,512]{2,1,0:T(8,128)}, f32[2,64,512]{2,1,0:T(8,128)S(1)}, u32[]{:S(2)}, u32[]{:S(2)}) collective-permute-start(f32[2,64,512]{2,1,0:T(8,128)} %get-tuple-element.76), channel_id=1, source_target_pairs={{0,1},{1,2},{2,3},{3,4},{4,5},{5,6},{6,7},{7,8},{8,9},{9,10},{10,1... | collective-permute-start | bytes 786440 | tf_op jit(solution)/shard_map/ppermute | solution.py:22
  189.7 15.6 %collective-permute-start.16 = (f32[2,64,512]{2,1,0:T(8,128)}, f32[2,64,512]{2,1,0:T(8,128)S(1)}, u32[]{:S(2)}, u32[]{:S(2)}) collective-permute-start(f32[2,64,512]{2,1,0:T(8,128)} %get-tuple-element.76), channel_id=1, source_target_pairs={{1,0},{2,1},{3,2},{4,3},{5,4},{6,5},{7,6},{8,7},{9,8},{10,9},{11,1... | collective-permute-start | bytes 786440 | tf_op jit(solution)/shard_map/ppermute | solution.py:23
  196.3 10.0 %collective-permute-start.19 = (f32[2,64,512]{2,1,0:T(8,128)}, f32[2,64,512]{2,1,0:T(8,128)S(1)}, u32[]{:S(2)}, u32[]{:S(2)}) collective-permute-start(f32[2,64,512]{2,1,0:T(8,128)} %get-tuple-element.75), channel_id=1, source_target_pairs={{0,1},{1,2},{2,3},{3,4},{4,5},{5,6},{6,7},{7,8},{8,9},{9,10},{10,1... | collective-permute-start | bytes 786440 | tf_op jit(solution)/shard_map/ppermute | solution.py:22
  199.5 9.9 %collective-permute-start.17 = (f32[2,64,512]{2,1,0:T(8,128)}, f32[2,64,512]{2,1,0:T(8,128)S(1)}, u32[]{:S(2)}, u32[]{:S(2)}) collective-permute-start(f32[2,64,512]{2,1,0:T(8,128)} %get-tuple-element.75), channel_id=1, source_target_pairs={{1,0},{2,1},{3,2},{4,3},{5,4},{6,5},{7,6},{8,7},{9,8},{10,9},{11,1... | collective-permute-start | bytes 786440 | tf_op jit(solution)/shard_map/ppermute | solution.py:23
  217.6 12.3 %copy-start.4 = (f32[1,2,128,144]{2,0,3,1:T(1,128)S(1)}, f32[1,2,128,144]{2,0,3,1:T(1,128)}, u32[]{:S(2)}) copy-start(f32[1,2,128,144]{2,0,3,1:T(1,128)} %get-tuple-element.58) | copy-start | bytes 442372
  219.4 17.9 %collective-permute-start.22 = (f32[2,64,512]{2,1,0:T(8,128)}, f32[2,64,512]{2,1,0:T(8,128)S(1)}, u32[]{:S(2)}, u32[]{:S(2)}) collective-permute-start(f32[2,64,512]{2,1,0:T(8,128)} %get-tuple-element.74), channel_id=1, source_target_pairs={{0,1},{1,2},{2,3},{3,4},{4,5},{5,6},{6,7},{7,8},{8,9},{9,10},{10,1... | collective-permute-start | bytes 786440 | tf_op jit(solution)/shard_map/ppermute | solution.py:22
  222.1 15.2 %collective-permute-start.20 = (f32[2,64,512]{2,1,0:T(8,128)}, f32[2,64,512]{2,1,0:T(8,128)S(1)}, u32[]{:S(2)}, u32[]{:S(2)}) collective-permute-start(f32[2,64,512]{2,1,0:T(8,128)} %get-tuple-element.74), channel_id=1, source_target_pairs={{1,0},{2,1},{3,2},{4,3},{5,4},{6,5},{7,6},{8,7},{9,8},{10,9},{11,1... | collective-permute-start | bytes 786440 | tf_op jit(solution)/shard_map/ppermute | solution.py:23
  227.9 10.0 %collective-permute-start.23 = (f32[2,64,512]{2,1,0:T(8,128)}, f32[2,64,512]{2,1,0:T(8,128)S(1)}, u32[]{:S(2)}, u32[]{:S(2)}) collective-permute-start(f32[2,64,512]{2,1,0:T(8,128)} %get-tuple-element.73), channel_id=1, source_target_pairs={{0,1},{1,2},{2,3},{3,4},{4,5},{5,6},{6,7},{7,8},{8,9},{9,10},{10,1... | collective-permute-start | bytes 786440 | tf_op jit(solution)/shard_map/ppermute | solution.py:22
  231.3 9.9 %collective-permute-start.21 = (f32[2,64,512]{2,1,0:T(8,128)}, f32[2,64,512]{2,1,0:T(8,128)S(1)}, u32[]{:S(2)}, u32[]{:S(2)}) collective-permute-start(f32[2,64,512]{2,1,0:T(8,128)} %get-tuple-element.73), channel_id=1, source_target_pairs={{1,0},{2,1},{3,2},{4,3},{5,4},{6,5},{7,6},{8,7},{9,8},{10,9},{11,1... | collective-permute-start | bytes 786440 | tf_op jit(solution)/shard_map/ppermute | solution.py:23
  249.1 9.6 %copy-start.5 = (f32[1,2,128,144]{2,0,3,1:T(1,128)S(1)}, f32[1,2,128,144]{2,0,3,1:T(1,128)}, u32[]{:S(2)}) copy-start(f32[1,2,128,144]{2,0,3,1:T(1,128)} %get-tuple-element.36) | copy-start | bytes 442372
  250.9 17.4 %collective-permute-start.26 = (f32[2,64,512]{2,1,0:T(8,128)}, f32[2,64,512]{2,1,0:T(8,128)S(1)}, u32[]{:S(2)}, u32[]{:S(2)}) collective-permute-start(f32[2,64,512]{2,1,0:T(8,128)} %get-tuple-element.72), channel_id=1, source_target_pairs={{0,1},{1,2},{2,3},{3,4},{4,5},{5,6},{6,7},{7,8},{8,9},{9,10},{10,1... | collective-permute-start | bytes 786440 | tf_op jit(solution)/shard_map/ppermute | solution.py:22
  252.8 15.5 %collective-permute-start.24 = (f32[2,64,512]{2,1,0:T(8,128)}, f32[2,64,512]{2,1,0:T(8,128)S(1)}, u32[]{:S(2)}, u32[]{:S(2)}) collective-permute-start(f32[2,64,512]{2,1,0:T(8,128)} %get-tuple-element.72), channel_id=1, source_target_pairs={{1,0},{2,1},{3,2},{4,3},{5,4},{6,5},{7,6},{8,7},{9,8},{10,9},{11,1... | collective-permute-start | bytes 786440 | tf_op jit(solution)/shard_map/ppermute | solution.py:23
  259.4 10.0 %collective-permute-start.27 = (f32[2,64,512]{2,1,0:T(8,128)}, f32[2,64,512]{2,1,0:T(8,128)S(1)}, u32[]{:S(2)}, u32[]{:S(2)}) collective-permute-start(f32[2,64,512]{2,1,0:T(8,128)} %get-tuple-element.71), channel_id=1, source_target_pairs={{0,1},{1,2},{2,3},{3,4},{4,5},{5,6},{6,7},{7,8},{8,9},{9,10},{10,1... | collective-permute-start | bytes 786440 | tf_op jit(solution)/shard_map/ppermute | solution.py:22
  262.5 9.9 %collective-permute-start.25 = (f32[2,64,512]{2,1,0:T(8,128)}, f32[2,64,512]{2,1,0:T(8,128)S(1)}, u32[]{:S(2)}, u32[]{:S(2)}) collective-permute-start(f32[2,64,512]{2,1,0:T(8,128)} %get-tuple-element.71), channel_id=1, source_target_pairs={{1,0},{2,1},{3,2},{4,3},{5,4},{6,5},{7,6},{8,7},{9,8},{10,9},{11,1... | collective-permute-start | bytes 786440 | tf_op jit(solution)/shard_map/ppermute | solution.py:23
  282.4 17.6 %collective-permute-start.30 = (f32[2,64,512]{2,1,0:T(8,128)}, f32[2,64,512]{2,1,0:T(8,128)S(1)}, u32[]{:S(2)}, u32[]{:S(2)}) collective-permute-start(f32[2,64,512]{2,1,0:T(8,128)} %get-tuple-element.70), channel_id=1, source_target_pairs={{0,1},{1,2},{2,3},{3,4},{4,5},{5,6},{6,7},{7,8},{8,9},{9,10},{10,1... | collective-permute-start | bytes 786440 | tf_op jit(solution)/shard_map/ppermute | solution.py:22
  285.1 14.9 %collective-permute-start.28 = (f32[2,64,512]{2,1,0:T(8,128)}, f32[2,64,512]{2,1,0:T(8,128)S(1)}, u32[]{:S(2)}, u32[]{:S(2)}) collective-permute-start(f32[2,64,512]{2,1,0:T(8,128)} %get-tuple-element.70), channel_id=1, source_target_pairs={{1,0},{2,1},{3,2},{4,3},{5,4},{6,5},{7,6},{8,7},{9,8},{10,9},{11,1... | collective-permute-start | bytes 786440 | tf_op jit(solution)/shard_map/ppermute | solution.py:23
  290.9 10.0 %collective-permute-start.31 = (f32[2,64,512]{2,1,0:T(8,128)}, f32[2,64,512]{2,1,0:T(8,128)S(1)}, u32[]{:S(2)}, u32[]{:S(2)}) collective-permute-start(f32[2,64,512]{2,1,0:T(8,128)} %get-tuple-element.69), channel_id=1, source_target_pairs={{0,1},{1,2},{2,3},{3,4},{4,5},{5,6},{6,7},{7,8},{8,9},{9,10},{10,1... | collective-permute-start | bytes 786440 | tf_op jit(solution)/shard_map/ppermute | solution.py:22
  294.2 9.9 %collective-permute-start.29 = (f32[2,64,512]{2,1,0:T(8,128)}, f32[2,64,512]{2,1,0:T(8,128)S(1)}, u32[]{:S(2)}, u32[]{:S(2)}) collective-permute-start(f32[2,64,512]{2,1,0:T(8,128)} %get-tuple-element.69), channel_id=1, source_target_pairs={{1,0},{2,1},{3,2},{4,3},{5,4},{6,5},{7,6},{8,7},{9,8},{10,9},{11,1... | collective-permute-start | bytes 786440 | tf_op jit(solution)/shard_map/ppermute | solution.py:23
  313.9 16.1 %collective-permute-start.34 = (f32[2,64,512]{2,1,0:T(8,128)}, f32[2,64,512]{2,1,0:T(8,128)S(1)}, u32[]{:S(2)}, u32[]{:S(2)}) collective-permute-start(f32[2,64,512]{2,1,0:T(8,128)} %get-tuple-element.68), channel_id=1, source_target_pairs={{0,1},{1,2},{2,3},{3,4},{4,5},{5,6},{6,7},{7,8},{8,9},{9,10},{10,1... | collective-permute-start | bytes 786440 | tf_op jit(solution)/shard_map/ppermute | solution.py:22
  315.8 14.2 %collective-permute-start.32 = (f32[2,64,512]{2,1,0:T(8,128)}, f32[2,64,512]{2,1,0:T(8,128)S(1)}, u32[]{:S(2)}, u32[]{:S(2)}) collective-permute-start(f32[2,64,512]{2,1,0:T(8,128)} %get-tuple-element.68), channel_id=1, source_target_pairs={{1,0},{2,1},{3,2},{4,3},{5,4},{6,5},{7,6},{8,7},{9,8},{10,9},{11,1... | collective-permute-start | bytes 786440 | tf_op jit(solution)/shard_map/ppermute | solution.py:23
  321.6 9.8 %collective-permute-start.35 = (f32[2,64,512]{2,1,0:T(8,128)S(1)}, f32[2,64,512]{2,1,0:T(8,128)S(1)}, u32[]{:S(2)}, u32[]{:S(2)}) collective-permute-start(f32[2,64,512]{2,1,0:T(8,128)S(1)} %get-tuple-element.67), channel_id=1, source_target_pairs={{0,1},{1,2},{2,3},{3,4},{4,5},{5,6},{6,7},{7,8},{8,9},{9,10},{10,1... | collective-permute-start | bytes 786440 | tf_op jit(solution)/shard_map/ppermute | solution.py:22
  324.2 9.6 %collective-permute-start.33 = (f32[2,64,512]{2,1,0:T(8,128)S(1)}, f32[2,64,512]{2,1,0:T(8,128)S(1)}, u32[]{:S(2)}, u32[]{:S(2)}) collective-permute-start(f32[2,64,512]{2,1,0:T(8,128)S(1)} %get-tuple-element.67), channel_id=1, source_target_pairs={{1,0},{2,1},{3,2},{4,3},{5,4},{6,5},{7,6},{8,7},{9,8},{10,9},{11,1... | collective-permute-start | bytes 786440 | tf_op jit(solution)/shard_map/ppermute | solution.py:23
  (89 other events, 268.4 us)
Sparse Core Ops, SparseCore 0:
  10.0 78.4 all-gather.1

commit v5 on v3

--- a/solution.py
+++ b/solution.py
@@ -57,7 +57,13 @@
     reach = (kernel_len - 1) // 2
     xy_kernels = psf_xy / jnp.sum(psf_xy, axis=-1, keepdims=True)
     z_kernels = psf_z / jnp.sum(psf_z, axis=-1, keepdims=True)
-    data_all = lax.all_gather(view_data[0], "view", axis=0)
+    local = view_data[0]
+    received = [local]
+    for by in range(1, lax.axis_size("view")):
+        received.append(
+            lax.ppermute(local, "view", [(i, (i + by) % view_count) for i in range(view_count)])
+        )
+    stacked = jnp.stack(received, axis=0)
     count, ny, nx = estimate.shape
     views = psf_xy.shape[0]
     view_hot = (view_order[:, None] == jnp.arange(views, dtype=jnp.int32)[None, :]).astype(
@@ -87,7 +93,8 @@
         by = by_all[position]
         kz = lax.dynamic_index_in_dim(z_kernels, view_id, 0, keepdims=False)
         offset = lax.dynamic_index_in_dim(background, view_id, 0, keepdims=False)
-        data = lax.dynamic_index_in_dim(data_all, view_id, 0, keepdims=False)
+        lag = (my_view - view_id) % view_count
+        data = lax.dynamic_index_in_dim(stacked, lag, 0, keepdims=False)
         c = kz[0] * padded[0:count]
         for k in range(1, 3):
             c = c + kz[k] * padded[k : k + count]

time: 282 us -> 305 us (1.082)
  starting transfers between devices: 46.8 us -> 66.3 us
  waiting for transfers between devices: 102 us -> 87.3 us
  other arithmetic: 24.4 us -> 35.7 us
  between operations: 34.1 us -> 25.8 us
  local copies, waits for them, and re-layouts: 20.8 us -> 27.8 us
  matrix products: 52.1 us -> 57.6 us
    ppermute x0 -> x7, waiting for transfers between devices: none -> 26.5 us  [per_device(): lax.ppermute(local, 'view', [(i, (i + by) % view_count) for i in range(vi...]
    all_gather x1 -> x0, waiting for transfers between devices: 26.3 us -> none  [per_device(): data_all = lax.all_gather(view_data[0], 'view', axis=0)]
    ppermute x0 -> x7, starting transfers between devices: none -> 15.4 us  [per_device(): lax.ppermute(local, 'view', [(i, (i + by) % view_count) for i in range(vi...]
    mul x7, other arithmetic: 16.4 us -> 30.1 us  [per_device(): padded = padded * corr]
    ppermute x9, waiting for transfers between devices: 27.5 us -> 15 us  [halo(): above = lax.ppermute(array[:width], axis, down)]
    dot_general x8, matrix products: 3.35 us -> 10.8 us  [per_device(): jnp.einsum('lij,ljx->lix', byr_all[position], quotient, precision=blur_mode)]
    unnamed x90 -> x123, local copies, waits for them, and re-layouts: 0.19 us -> 6.79 us
    slice x16, local copies, waits for them, and re-layouts: 1.07 us -> 7.34 us  [band_matrix(): diagonal = mats[..., reach:reach + block]]
  transfers between devices with their start and end apart: 19 -> 25, of which waited for: 16 -> 18; matrix products, arithmetic and copies ran while one was open for 12% -> 12% of each run, Pallas kernels for 0% -> 0%
where the time goes in v5:
time: 305 us; the launch traced here: 300 us
  waiting for transfers between devices  87.3 us (29%)
  starting transfers between devices  66.3 us (22%)
  matrix products  57.6 us (19%)
  other arithmetic  35.7 us (12%)
  local copies, waits for them, and re-layouts  27.8 us (9%)
  between operations  25.8 us (8%)
    ppermute x9, waiting for transfers between devices, halo(): below = lax.ppermute(array[-width:], axis, up)  45.7 us
    ppermute x9, starting transfers between devices, halo(): above = lax.ppermute(array[:width], axis, down)  30.5 us
    mul x7, other arithmetic, per_device(): padded = padded * corr  30.1 us
    ppermute x7, waiting for transfers between devices, per_device(): lax.ppermute(local, 'view', [(i, (i + by) % view_count) for i in range(vi...  26.5 us
    ppermute x9, starting transfers between devices, halo(): below = lax.ppermute(array[-width:], axis, up)  20.4 us
    dot_general x8, matrix products, per_device(): t = jnp.einsum('lij,ljx->lix', by, c, precision=blur_mode)  19.1 us
    ppermute x7, starting transfers between devices, per_device(): lax.ppermute(local, 'view', [(i, (i + by) % view_count) for i in range(vi...  15.4 us
    ppermute x9, waiting for transfers between devices, halo(): above = lax.ppermute(array[:width], axis, down)  15 us
  transfers between devices with their start and end apart: 25, of which 18 were waited for; matrix products, arithmetic and copies ran while one was open for 12% of the time, Pallas kernels for 0%

profile of v5, /device:TPU:2, one launch (start us, length us, event | category | flops | bytes accessed | tf_op | source)
XLA Modules:
  0.0 300.4 jit_solution(8297590801264907991)
XLA Ops:
  1.7 2.9 collective-permute-start.3
  4.6 2.9 collective-permute-start.4
  9.3 1.9 collective-permute-start
  11.2 7.2 %collective-permute-start.1 = (f32[1,128,512]{2,1,0:T(8,128)}, f32[1,128,512]{2,1,0:T(8,128)}, u32[]{:S(2)}, u32[]{:S(2)}) collective-permute-start(f32[1,128,512]{2,1,0:T(8,128)} %get-tuple-element.38), channel_id=1, source_target_pairs={{1,0},{2,1},{3,2},{4,3},{5,4},{6,5},{7,6},{8,7},{9,8},{10,9},{11,1... | collective-permute-start | bytes 786440 | tf_op jit(solution)/shard_map/ppermute | solution.py:18
  49.5 3.6 %collective-permute-start.6 = (f32[2,128,512]{2,1,0:T(8,128)S(1)}, f32[2,128,512]{2,1,0:T(8,128)S(1)}, u32[]{:S(2)}, u32[]{:S(2)}) collective-permute-start(f32[2,128,512]{2,1,0:T(8,128)S(1)} %bitcast.241), channel_id=1, source_target_pairs={{0,160},{32,192},{64,224},{96,0},{128,32},{160,64},{192,96},{224,1... | collective-permute-start | bytes 1572872 | tf_op jit(solution)/shard_map/ppermute | solution.py:64
  53.1 3.4 %fusion.316 = f32[2,128,512]{2,1,0:T(8,128)S(1)} fusion(f32[1,128,512]{2,1,0:T(8,128)} %collective-permute-done.1, f32[2,128,512]{2,1,0:T(8,128)S(1)} %copy-done.3, f32[1,128,512]{2,1,0:T(8,128)} %collective-permute-done, f32[]{:T(128)} %bitcast.24, f32[]{:T(128)} %bitcast.23, f32[]{:T(128)} %bitcast.2, f32[2,128,144]{1,2,0:T(8,128)S(1)} %bitcast.236), kind=kOutput, calls=%fused_computation.383 | convolution fusion | flops 101580800 | bytes 1703948 | tf_op jit(solution)/shard_map/lij,ljx->lix/dot_general | solution.py:101
  58.4 2.5 collective-permute-start.7
  66.0 7.1 %collective-permute-done.6 = f32[2,128,512]{2,1,0:T(8,128)S(1)} collective-permute-done((f32[2,128,512]{2,1,0:T(8,128)S(1)}, f32[2,128,512]{2,1,0:T(8,128)S(1)}, u32[]{:S(2)}, u32[]{:S(2)}) %collective-permute-start.6) | collective-permute-done | bytes 524320 | tf_op jit(solution)/shard_map/ppermute | solution.py:64
  73.1 11.2 %collective-permute-done.7 = f32[2,128,512]{2,1,0:T(8,128)S(1)} collective-permute-done((f32[2,128,512]{2,1,0:T(8,128)S(1)}, f32[2,128,512]{2,1,0:T(8,128)S(1)}, u32[]{:S(2)}, u32[]{:S(2)}) %collective-permute-start.7) | collective-permute-done | bytes 524320 | tf_op jit(solution)/shard_map/ppermute | solution.py:64
  84.4 8.3 %collective-permute-done.8 = f32[2,128,512]{2,1,0:T(8,128)S(1)} collective-permute-done((f32[2,128,512]{2,1,0:T(8,128)S(1)}, f32[2,128,512]{2,1,0:T(8,128)S(1)}, u32[]{:S(2)}, u32[]{:S(2)}) %collective-permute-start.8) | collective-permute-done | bytes 524320 | tf_op jit(solution)/shard_map/ppermute | solution.py:64
  96.6 5.8 %collective-permute-start.9 = (f32[2,128,512]{2,1,0:T(8,128)S(1)}, f32[2,128,512]{2,1,0:T(8,128)}, u32[]{:S(2)}, u32[]{:S(2)}) collective-permute-start(f32[2,128,512]{2,1,0:T(8,128)S(1)} %fusion.8), channel_id=1, source_target_pairs={{1,0},{2,1},{3,2},{4,3},{5,4},{6,5},{7,6},{8,7},{9,8},{10,9},{11,1... | collective-permute-start | bytes 1572872 | tf_op jit(solution)/shard_map/ppermute | solution.py:18
  103.0 4.2 %collective-permute-done.10 = f32[2,128,512]{2,1,0:T(8,128)S(1)} collective-permute-done((f32[2,128,512]{2,1,0:T(8,128)S(1)}, f32[2,128,512]{2,1,0:T(8,128)S(1)}, u32[]{:S(2)}, u32[]{:S(2)}) %collective-permute-start.10) | collective-permute-done | bytes 524320 | tf_op jit(solution)/shard_map/ppermute | solution.py:17
  109.0 3.8 %fusion.266 = f32[4,128,512]{2,1,0:T(8,128)S(1)} fusion(f32[2,128,512]{2,1,0:T(8,128)} %collective-permute-done.9, f32[2,128,512]{2,1,0:T(8,128)S(1)} %fusion.8, f32[2,128,512]{2,1,0:T(8,128)} %copy-done.29, f32[1,128,512]{2,1,0:T(8,128)} %collective-permute-done.1, f32[2,128,512]{2,1,0:T(8,128)S(1)} %copy-done.3, f32[1,128,512]{2,1,0:T(8,128)} %collective-permute-done, ...), kind=kLoop, calls=%fused_computation.313 | loop fusion | flops 3145728 | bytes 3670028 | tf_op jit(solution)/shard_map/mul | solution.py:110
  112.8 2.2 fusion.310
  119.2 6.0 %collective-permute-start.11 = (f32[2,128,512]{2,1,0:T(8,128)S(1)}, f32[2,128,512]{2,1,0:T(8,128)}, u32[]{:S(2)}, u32[]{:S(2)}) collective-permute-start(f32[2,128,512]{2,1,0:T(8,128)S(1)} %fusion.18), channel_id=1, source_target_pairs={{1,0},{2,1},{3,2},{4,3},{5,4},{6,5},{7,6},{8,7},{9,8},{10,9},{11,1... | collective-permute-start | bytes 1572872 | tf_op jit(solution)/shard_map/ppermute | solution.py:18
  125.3 1.9 collective-permute-start.12
  128.5 3.4 %collective-permute-done.11 = f32[2,128,512]{2,1,0:T(8,128)} collective-permute-done((f32[2,128,512]{2,1,0:T(8,128)S(1)}, f32[2,128,512]{2,1,0:T(8,128)}, u32[]{:S(2)}, u32[]{:S(2)}) %collective-permute-start.11) | collective-permute-done | bytes 524320 | tf_op jit(solution)/shard_map/ppermute | solution.py:18
  132.0 6.0 %collective-permute-done.12 = f32[2,128,512]{2,1,0:T(8,128)} collective-permute-done((f32[2,128,512]{2,1,0:T(8,128)S(1)}, f32[2,128,512]{2,1,0:T(8,128)}, u32[]{:S(2)}, u32[]{:S(2)}) %collective-permute-start.12) | collective-permute-done | bytes 524320 | tf_op jit(solution)/shard_map/ppermute | solution.py:17
  138.0 4.2 %fusion.262 = f32[4,128,512]{2,1,0:T(8,128)S(1)} fusion(f32[4,128,512]{2,1,0:T(8,128)S(1)} %fusion.266, f32[2,128,512]{2,1,0:T(8,128)} %collective-permute-done.11, f32[2,128,512]{2,1,0:T(8,128)} %copy-done.27, f32[2,128,512]{2,1,0:T(8,128)} %collective-permute-done.12, f32[]{:T(128)} %bitcast.39, f32[]{:T(128)} %bitcast.38, f32[]{:T(128)} %bitcast.34), kind=kLoop, calls=%fused_computation.307 | loop fusion | flops 2621440 | bytes 3670028 | tf_op jit(solution)/shard_map/mul | solution.py:110
  142.2 2.1 fusion.305
  148.5 1.9 collective-permute-start.13
  150.4 2.4 collective-permute-start.14
  153.6 3.5 %collective-permute-done.13 = f32[2,128,512]{2,1,0:T(8,128)} collective-permute-done((f32[2,128,512]{2,1,0:T(8,128)S(1)}, f32[2,128,512]{2,1,0:T(8,128)}, u32[]{:S(2)}, u32[]{:S(2)}) %collective-permute-start.13) | collective-permute-done | bytes 524320 | tf_op jit(solution)/shard_map/ppermute | solution.py:18
  157.1 6.0 %collective-permute-done.14 = f32[2,128,512]{2,1,0:T(8,128)} collective-permute-done((f32[2,128,512]{2,1,0:T(8,128)S(1)}, f32[2,128,512]{2,1,0:T(8,128)}, u32[]{:S(2)}, u32[]{:S(2)}) %collective-permute-start.14) | collective-permute-done | bytes 524320 | tf_op jit(solution)/shard_map/ppermute | solution.py:17
  163.1 4.1 %fusion.258 = f32[4,128,512]{2,1,0:T(8,128)S(1)} fusion(f32[4,128,512]{2,1,0:T(8,128)S(1)} %fusion.262, f32[2,128,512]{2,1,0:T(8,128)} %collective-permute-done.13, f32[2,128,512]{2,1,0:T(8,128)} %copy-done.28, f32[2,128,512]{2,1,0:T(8,128)} %collective-permute-done.14, f32[]{:T(128)} %bitcast.49, f32[]{:T(128)} %bitcast.48, f32[]{:T(128)} %bitcast.44), kind=kLoop, calls=%fused_computation.301 | loop fusion | flops 2621440 | bytes 3670028 | tf_op jit(solution)/shard_map/mul | solution.py:110
  167.3 2.2 fusion.300
  174.3 1.9 collective-permute-start.15
  176.2 2.6 collective-permute-start.16
  183.2 5.9 %collective-permute-done.16 = f32[2,128,512]{2,1,0:T(8,128)} collective-permute-done((f32[2,128,512]{2,1,0:T(8,128)}, f32[2,128,512]{2,1,0:T(8,128)}, u32[]{:S(2)}, u32[]{:S(2)}) %collective-permute-start.16) | collective-permute-done | bytes 524320 | tf_op jit(solution)/shard_map/ppermute | solution.py:17
  189.2 4.2 %fusion.254 = f32[4,128,512]{2,1,0:T(8,128)S(1)} fusion(f32[4,128,512]{2,1,0:T(8,128)S(1)} %fusion.258, f32[2,128,512]{2,1,0:T(8,128)} %collective-permute-done.15, f32[2,128,512]{2,1,0:T(8,128)} %fusion.38, f32[2,128,512]{2,1,0:T(8,128)} %collective-permute-done.16, f32[]{:T(128)} %bitcast.59, f32[]{:T(128)} %bitcast.58, f32[]{:T(128)} %bitcast.54), kind=kLoop, calls=%fused_computation.295 | loop fusion | flops 2621440 | bytes 3670028 | tf_op jit(solution)/shard_map/mul | solution.py:110
  193.3 2.3 fusion.295
  200.4 1.9 collective-permute-start.17
  202.3 2.4 collective-permute-start.18
  209.3 5.9 %collective-permute-done.18 = f32[2,128,512]{2,1,0:T(8,128)} collective-permute-done((f32[2,128,512]{2,1,0:T(8,128)}, f32[2,128,512]{2,1,0:T(8,128)}, u32[]{:S(2)}, u32[]{:S(2)}) %collective-permute-start.18) | collective-permute-done | bytes 524320 | tf_op jit(solution)/shard_map/ppermute | solution.py:17
  215.2 4.5 %fusion.250 = f32[4,128,512]{2,1,0:T(8,128)S(1)} fusion(f32[4,128,512]{2,1,0:T(8,128)} %copy-done, f32[2,128,512]{2,1,0:T(8,128)} %collective-permute-done.17, f32[2,128,512]{2,1,0:T(8,128)} %fusion.48, f32[2,128,512]{2,1,0:T(8,128)} %collective-permute-done.18, f32[]{:T(128)} %bitcast.69, f32[]{:T(128)} %bitcast.68, f32[]{:T(128)} %bitcast.64), kind=kLoop, calls=%fused_computation.289 | loop fusion | flops 2621440 | bytes 3670028 | tf_op jit(solution)/shard_map/mul | solution.py:110
  219.8 2.4 fusion.290
  229.0 2.4 collective-permute-start.20
  236.0 5.9 %collective-permute-done.20 = f32[2,128,512]{2,1,0:T(8,128)} collective-permute-done((f32[2,128,512]{2,1,0:T(8,128)}, f32[2,128,512]{2,1,0:T(8,128)}, u32[]{:S(2)}, u32[]{:S(2)}) %collective-permute-start.20) | collective-permute-done | bytes 524320 | tf_op jit(solution)/shard_map/ppermute | solution.py:17
  241.9 4.7 %fusion.246 = f32[4,128,512]{2,1,0:T(8,128)S(1)} fusion(f32[4,128,512]{2,1,0:T(8,128)} %copy-done.1, f32[2,128,512]{2,1,0:T(8,128)} %collective-permute-done.19, f32[2,128,512]{2,1,0:T(8,128)} %fusion.58, f32[2,128,512]{2,1,0:T(8,128)} %collective-permute-done.20, f32[]{:T(128)} %bitcast.79, f32[]{:T(128)} %bitcast.78, f32[]{:T(128)} %bitcast.74), kind=kLoop, calls=%fused_computation.283 | loop fusion | flops 2621440 | bytes 3670028 | tf_op jit(solution)/shard_map/mul | solution.py:110
  246.7 2.3 fusion.285
  255.7 2.4 collective-permute-start.22
  259.9 2.8 collective-permute-done.21
  262.7 5.9 %collective-permute-done.22 = f32[2,128,512]{2,1,0:T(8,128)} collective-permute-done((f32[2,128,512]{2,1,0:T(8,128)}, f32[2,128,512]{2,1,0:T(8,128)}, u32[]{:S(2)}, u32[]{:S(2)}) %collective-permute-start.22) | collective-permute-done | bytes 524320 | tf_op jit(solution)/shard_map/ppermute | solution.py:17
  268.6 4.5 %fusion.242 = f32[4,128,512]{2,1,0:T(8,128)S(1)} fusion(f32[4,128,512]{2,1,0:T(8,128)} %copy-done.2, f32[2,128,512]{2,1,0:T(8,128)} %collective-permute-done.21, f32[2,128,512]{2,1,0:T(8,128)} %fusion.68, f32[2,128,512]{2,1,0:T(8,128)} %collective-permute-done.22, f32[]{:T(128)} %bitcast.89, f32[]{:T(128)} %bitcast.88, f32[]{:T(128)} %bitcast.84), kind=kLoop, calls=%fused_computation.277 | loop fusion | flops 2621440 | bytes 3670028 | tf_op jit(solution)/shard_map/mul | solution.py:110
  273.2 2.3 fusion.280
  282.2 2.4 collective-permute-start.24
  289.4 5.7 %collective-permute-done.24 = f32[2,128,512]{2,1,0:T(8,128)} collective-permute-done((f32[2,128,512]{2,1,0:T(8,128)}, f32[2,128,512]{2,1,0:T(8,128)}, u32[]{:S(2)}, u32[]{:S(2)}) %collective-permute-start.24) | collective-permute-done | bytes 524320 | tf_op jit(solution)/shard_map/ppermute | solution.py:17
  295.1 5.2 %fusion.275 = f32[1,2,128,512]{3,2,1,0:T(8,128)} fusion(f32[2,128,512]{2,1,0:T(8,128)} %fusion.78, f32[2,128,512]{2,1,0:T(8,128)} %collective-permute-done.24, f32[2,128,512]{2,1,0:T(8,128)} %collective-permute-done.23, f32[4,128,512]{2,1,0:T(8,128)} %copy-done.4, f32[4,128,512]{2,1,0:T(8,128)} %copy-done.2, f32[4,128,512]{2,1,0:T(8,128)} %copy-done.1, ...), kind=kLoop, calls=%fused_computation.338 | loop fusion | flops 2359296 | bytes 5767188 | tf_op jit(solution)/shard_map/broadcast_in_dim | solution.py:112
  (214 shorter events, 82.9 us)
Async XLA Ops:
  0.0 32.1 %copy-start.54 = (s32[8]{0:T(128)S(1)}, s32[8]{0:T(128)}, u32[]{:S(2)}) copy-start(s32[8]{0:T(128)} %param.12) | copy-start | bytes 100
  0.0 31.7 %copy-start.38 = (f32[8,8,2,17]{3,2,1,0:T(2,128)S(1)}, f32[8,8,2,17]{3,2,1,0:T(2,128)}, u32[]{:S(2)}) copy-start(f32[8,8,2,17]{3,2,1,0:T(2,128)} %param.10) | copy-start | bytes 26116
  0.0 32.2 %copy-start.57 = (s32[2]{0:T(128)S(1)}, s32[2]{0:T(128)}, u32[]{:S(2)}) copy-start(s32[2]{0:T(128)} %param.13) | copy-start | bytes 28
  0.0 58.4 %collective-permute-start.2 = (f32[2,128,512]{2,1,0:T(8,128)}, f32[2,128,512]{2,1,0:T(8,128)}, u32[]{:S(2)}, u32[]{:S(2)}) collective-permute-start(f32[2,128,512]{2,1,0:T(8,128)} %bitcast.237), channel_id=1, source_target_pairs={{0,32},{32,64},{64,96},{96,128},{128,160},{160,192},{192,224},{224... | collective-permute-start | bytes 1572872 | tf_op jit(solution)/shard_map/ppermute | solution.py:64
  1.7 60.4 %collective-permute-start.3 = (f32[2,128,512]{2,1,0:T(8,128)}, f32[2,128,512]{2,1,0:T(8,128)}, u32[]{:S(2)}, u32[]{:S(2)}) collective-permute-start(f32[2,128,512]{2,1,0:T(8,128)} %bitcast.238), channel_id=1, source_target_pairs={{0,64},{32,96},{64,128},{96,160},{128,192},{160,224},{192,0},{224,... | collective-permute-start | bytes 1572872 | tf_op jit(solution)/shard_map/ppermute | solution.py:64
  4.6 60.3 %collective-permute-start.4 = (f32[2,128,512]{2,1,0:T(8,128)}, f32[2,128,512]{2,1,0:T(8,128)}, u32[]{:S(2)}, u32[]{:S(2)}) collective-permute-start(f32[2,128,512]{2,1,0:T(8,128)} %bitcast.239), channel_id=1, source_target_pairs={{0,96},{32,128},{64,160},{96,192},{128,224},{160,0},{192,32},{224,... | collective-permute-start | bytes 1572872 | tf_op jit(solution)/shard_map/ppermute | solution.py:64
  9.3 40.0 %collective-permute-start = (f32[1,128,512]{2,1,0:T(8,128)}, f32[1,128,512]{2,1,0:T(8,128)}, u32[]{:S(2)}, u32[]{:S(2)}) collective-permute-start(f32[1,128,512]{2,1,0:T(8,128)} %get-tuple-element.37), channel_id=1, source_target_pairs={{0,1},{1,2},{2,3},{3,4},{4,5},{5,6},{6,7},{7,8},{8,9},{9,10},{10,1... | collective-permute-start | bytes 786440 | tf_op jit(solution)/shard_map/ppermute | solution.py:17
  11.2 38.2 %collective-permute-start.1 = (f32[1,128,512]{2,1,0:T(8,128)}, f32[1,128,512]{2,1,0:T(8,128)}, u32[]{:S(2)}, u32[]{:S(2)}) collective-permute-start(f32[1,128,512]{2,1,0:T(8,128)} %get-tuple-element.38), channel_id=1, source_target_pairs={{1,0},{2,1},{3,2},{4,3},{5,4},{6,5},{7,6},{8,7},{9,8},{10,9},{11,1... | collective-permute-start | bytes 786440 | tf_op jit(solution)/shard_map/ppermute | solution.py:18
  37.4 91.0 %copy-start.16 = (f32[1,2,128,144]{2,0,3,1:T(1,128)}, f32[1,2,128,144]{2,0,3,1:T(1,128)S(1)}, u32[]{:S(2)}) copy-start(f32[1,2,128,144]{2,0,3,1:T(1,128)S(1)} %get-tuple-element.25) | copy-start | bytes 442372
  42.4 111.1 %copy-start.14 = (f32[1,2,128,144]{2,0,3,1:T(1,128)}, f32[1,2,128,144]{2,0,3,1:T(1,128)S(1)}, u32[]{:S(2)}) copy-start(f32[1,2,128,144]{2,0,3,1:T(1,128)S(1)} %get-tuple-element.9) | copy-start | bytes 442372
  49.4 16.6 %collective-permute-start.5 = (f32[2,128,512]{2,1,0:T(8,128)S(1)}, f32[2,128,512]{2,1,0:T(8,128)S(1)}, u32[]{:S(2)}, u32[]{:S(2)}) collective-permute-start(f32[2,128,512]{2,1,0:T(8,128)S(1)} %bitcast.240), channel_id=1, source_target_pairs={{0,128},{32,160},{64,192},{96,224},{128,0},{160,32},{192,64},{224,... | collective-permute-start | bytes 1572872 | tf_op jit(solution)/shard_map/ppermute | solution.py:64
  49.5 23.6 %collective-permute-start.6 = (f32[2,128,512]{2,1,0:T(8,128)S(1)}, f32[2,128,512]{2,1,0:T(8,128)S(1)}, u32[]{:S(2)}, u32[]{:S(2)}) collective-permute-start(f32[2,128,512]{2,1,0:T(8,128)S(1)} %bitcast.241), channel_id=1, source_target_pairs={{0,160},{32,192},{64,224},{96,0},{128,32},{160,64},{192,96},{224,1... | collective-permute-start | bytes 1572872 | tf_op jit(solution)/shard_map/ppermute | solution.py:64
  56.5 36.6 %copy-start.30 = (f32[2,128,256]{1,2,0:T(8,128)}, f32[2,128,256]{1,2,0:T(8,128)S(1)}, u32[]{:S(2)}) copy-start(f32[2,128,256]{1,2,0:T(8,128)S(1)} %broadcast.27) | copy-start | bytes 786436
  56.6 36.6 %copy-start.47 = (f32[2,128,120]{1,2,0:T(8,128)}, f32[2,128,120]{1,2,0:T(8,128)S(1)}, u32[]{:S(2)}) copy-start(f32[2,128,120]{1,2,0:T(8,128)S(1)} %broadcast.26) | copy-start | bytes 368644
  58.4 25.9 %collective-permute-start.7 = (f32[2,128,512]{2,1,0:T(8,128)S(1)}, f32[2,128,512]{2,1,0:T(8,128)S(1)}, u32[]{:S(2)}, u32[]{:S(2)}) collective-permute-start(f32[2,128,512]{2,1,0:T(8,128)S(1)} %bitcast.242), channel_id=1, source_target_pairs={{0,192},{32,224},{64,0},{96,32},{128,64},{160,96},{192,128},{224,1... | collective-permute-start | bytes 1572872 | tf_op jit(solution)/shard_map/ppermute | solution.py:64
  62.0 30.6 %collective-permute-start.8 = (f32[2,128,512]{2,1,0:T(8,128)S(1)}, f32[2,128,512]{2,1,0:T(8,128)S(1)}, u32[]{:S(2)}, u32[]{:S(2)}) collective-permute-start(f32[2,128,512]{2,1,0:T(8,128)S(1)} %bitcast.243), channel_id=1, source_target_pairs={{0,224},{32,0},{64,32},{96,64},{128,96},{160,128},{192,160},{224,1... | collective-permute-start | bytes 1572872 | tf_op jit(solution)/shard_map/ppermute | solution.py:64
  65.9 26.7 %copy-start.46 = (f32[1,2,128,144]{2,0,3,1:T(1,128)S(1)}, f32[1,2,128,144]{2,0,3,1:T(1,128)}, u32[]{:S(2)}) copy-start(f32[1,2,128,144]{2,0,3,1:T(1,128)} %get-tuple-element.20) | copy-start | bytes 442372
  94.7 12.6 %collective-permute-start.10 = (f32[2,128,512]{2,1,0:T(8,128)S(1)}, f32[2,128,512]{2,1,0:T(8,128)S(1)}, u32[]{:S(2)}, u32[]{:S(2)}) collective-permute-start(f32[2,128,512]{2,1,0:T(8,128)S(1)} %fusion.8), channel_id=1, source_target_pairs={{0,1},{1,2},{2,3},{3,4},{4,5},{5,6},{6,7},{7,8},{8,9},{9,10},{10,1... | collective-permute-start | bytes 1572872 | tf_op jit(solution)/shard_map/ppermute | solution.py:17
  96.6 12.4 %collective-permute-start.9 = (f32[2,128,512]{2,1,0:T(8,128)S(1)}, f32[2,128,512]{2,1,0:T(8,128)}, u32[]{:S(2)}, u32[]{:S(2)}) collective-permute-start(f32[2,128,512]{2,1,0:T(8,128)S(1)} %fusion.8), channel_id=1, source_target_pairs={{1,0},{2,1},{3,2},{4,3},{5,4},{6,5},{7,6},{8,7},{9,8},{10,9},{11,1... | collective-permute-start | bytes 1572872 | tf_op jit(solution)/shard_map/ppermute | solution.py:18
  119.2 12.7 %collective-permute-start.11 = (f32[2,128,512]{2,1,0:T(8,128)S(1)}, f32[2,128,512]{2,1,0:T(8,128)}, u32[]{:S(2)}, u32[]{:S(2)}) collective-permute-start(f32[2,128,512]{2,1,0:T(8,128)S(1)} %fusion.18), channel_id=1, source_target_pairs={{1,0},{2,1},{3,2},{4,3},{5,4},{6,5},{7,6},{8,7},{9,8},{10,9},{11,1... | collective-permute-start | bytes 1572872 | tf_op jit(solution)/shard_map/ppermute | solution.py:18
  125.3 12.7 %collective-permute-start.12 = (f32[2,128,512]{2,1,0:T(8,128)S(1)}, f32[2,128,512]{2,1,0:T(8,128)}, u32[]{:S(2)}, u32[]{:S(2)}) collective-permute-start(f32[2,128,512]{2,1,0:T(8,128)S(1)} %fusion.18), channel_id=1, source_target_pairs={{0,1},{1,2},{2,3},{3,4},{4,5},{5,6},{6,7},{7,8},{8,9},{9,10},{10,1... | collective-permute-start | bytes 1572872 | tf_op jit(solution)/shard_map/ppermute | solution.py:17
  128.4 13.8 %copy-start.23 = (f32[1,2,128,144]{2,0,3,1:T(1,128)S(1)}, f32[1,2,128,144]{2,0,3,1:T(1,128)}, u32[]{:S(2)}) copy-start(f32[1,2,128,144]{2,0,3,1:T(1,128)} %get-tuple-element.34) | copy-start | bytes 442372
  128.5 15.9 %copy-start.17 = (f32[1,2,128,144]{2,0,3,1:T(1,128)S(1)}, f32[1,2,128,144]{2,0,3,1:T(1,128)}, u32[]{:S(2)}) copy-start(f32[1,2,128,144]{2,0,3,1:T(1,128)} %copy-done.16) | copy-start | bytes 442372
  128.5 15.9 %copy-start.32 = (f32[2,128,256]{1,2,0:T(8,128)S(1)}, f32[2,128,256]{1,2,0:T(8,128)}, u32[]{:S(2)}) copy-start(f32[2,128,256]{1,2,0:T(8,128)} %copy-done.30) | copy-start | bytes 786436
  128.5 15.9 %copy-start.49 = (f32[2,128,120]{1,2,0:T(8,128)S(1)}, f32[2,128,120]{1,2,0:T(8,128)}, u32[]{:S(2)}) copy-start(f32[2,128,120]{1,2,0:T(8,128)} %copy-done.47) | copy-start | bytes 368644
  148.5 8.6 %collective-permute-start.13 = (f32[2,128,512]{2,1,0:T(8,128)S(1)}, f32[2,128,512]{2,1,0:T(8,128)}, u32[]{:S(2)}, u32[]{:S(2)}) collective-permute-start(f32[2,128,512]{2,1,0:T(8,128)S(1)} %fusion.28), channel_id=1, source_target_pairs={{1,0},{2,1},{3,2},{4,3},{5,4},{6,5},{7,6},{8,7},{9,8},{10,9},{11,1... | collective-permute-start | bytes 1572872 | tf_op jit(solution)/shard_map/ppermute | solution.py:18
  150.4 12.7 %collective-permute-start.14 = (f32[2,128,512]{2,1,0:T(8,128)S(1)}, f32[2,128,512]{2,1,0:T(8,128)}, u32[]{:S(2)}, u32[]{:S(2)}) collective-permute-start(f32[2,128,512]{2,1,0:T(8,128)S(1)} %fusion.28), channel_id=1, source_target_pairs={{0,1},{1,2},{2,3},{3,4},{4,5},{5,6},{6,7},{7,8},{8,9},{9,10},{10,1... | collective-permute-start | bytes 1572872 | tf_op jit(solution)/shard_map/ppermute | solution.py:17
  153.5 13.8 %copy-start.22 = (f32[1,2,128,144]{2,0,3,1:T(1,128)S(1)}, f32[1,2,128,144]{2,0,3,1:T(1,128)}, u32[]{:S(2)}) copy-start(f32[1,2,128,144]{2,0,3,1:T(1,128)} %get-tuple-element.33) | copy-start | bytes 442372
  153.5 15.9 %copy-start.13 = (f32[1,2,128,144]{2,0,3,1:T(1,128)S(1)}, f32[1,2,128,144]{2,0,3,1:T(1,128)}, u32[]{:S(2)}) copy-start(f32[1,2,128,144]{2,0,3,1:T(1,128)} %get-tuple-element.24) | copy-start | bytes 442372
  153.5 15.9 %copy-start.33 = (f32[2,128,256]{1,2,0:T(8,128)S(1)}, f32[2,128,256]{1,2,0:T(8,128)}, u32[]{:S(2)}) copy-start(f32[2,128,256]{1,2,0:T(8,128)} %copy-done.30) | copy-start | bytes 786436
  153.5 15.9 %copy-start.50 = (f32[2,128,120]{1,2,0:T(8,128)S(1)}, f32[2,128,120]{1,2,0:T(8,128)}, u32[]{:S(2)}) copy-start(f32[2,128,120]{1,2,0:T(8,128)} %copy-done.47) | copy-start | bytes 368644
  174.3 8.9 %collective-permute-start.15 = (f32[2,128,512]{2,1,0:T(8,128)}, f32[2,128,512]{2,1,0:T(8,128)}, u32[]{:S(2)}, u32[]{:S(2)}) collective-permute-start(f32[2,128,512]{2,1,0:T(8,128)} %fusion.38), channel_id=1, source_target_pairs={{1,0},{2,1},{3,2},{4,3},{5,4},{6,5},{7,6},{8,7},{9,8},{10,9},{11,1... | collective-permute-start | bytes 1572872 | tf_op jit(solution)/shard_map/ppermute | solution.py:18
  176.2 12.9 %collective-permute-start.16 = (f32[2,128,512]{2,1,0:T(8,128)}, f32[2,128,512]{2,1,0:T(8,128)}, u32[]{:S(2)}, u32[]{:S(2)}) collective-permute-start(f32[2,128,512]{2,1,0:T(8,128)} %fusion.38), channel_id=1, source_target_pairs={{0,1},{1,2},{2,3},{3,4},{4,5},{5,6},{6,7},{7,8},{8,9},{9,10},{10,1... | collective-permute-start | bytes 1572872 | tf_op jit(solution)/shard_map/ppermute | solution.py:17
  182.1 13.5 %copy-start.10 = (f32[1,2,128,144]{2,0,3,1:T(1,128)S(1)}, f32[1,2,128,144]{2,0,3,1:T(1,128)}, u32[]{:S(2)}) copy-start(f32[1,2,128,144]{2,0,3,1:T(1,128)} %get-tuple-element.23) | copy-start | bytes 442372
  200.4 8.9 %collective-permute-start.17 = (f32[2,128,512]{2,1,0:T(8,128)}, f32[2,128,512]{2,1,0:T(8,128)}, u32[]{:S(2)}, u32[]{:S(2)}) collective-permute-start(f32[2,128,512]{2,1,0:T(8,128)} %fusion.48), channel_id=1, source_target_pairs={{1,0},{2,1},{3,2},{4,3},{5,4},{6,5},{7,6},{8,7},{9,8},{10,9},{11,1... | collective-permute-start | bytes 1572872 | tf_op jit(solution)/shard_map/ppermute | solution.py:18
  202.3 12.9 %collective-permute-start.18 = (f32[2,128,512]{2,1,0:T(8,128)}, f32[2,128,512]{2,1,0:T(8,128)}, u32[]{:S(2)}, u32[]{:S(2)}) collective-permute-start(f32[2,128,512]{2,1,0:T(8,128)} %fusion.48), channel_id=1, source_target_pairs={{0,1},{1,2},{2,3},{3,4},{4,5},{5,6},{6,7},{7,8},{8,9},{9,10},{10,1... | collective-permute-start | bytes 1572872 | tf_op jit(solution)/shard_map/ppermute | solution.py:17
  207.4 14.8 %copy-start.8 = (f32[1,2,128,144]{2,0,3,1:T(1,128)S(1)}, f32[1,2,128,144]{2,0,3,1:T(1,128)}, u32[]{:S(2)}) copy-start(f32[1,2,128,144]{2,0,3,1:T(1,128)} %get-tuple-element.22) | copy-start | bytes 442372
  207.4 14.8 %copy-start.35 = (f32[2,128,256]{1,2,0:T(8,128)S(1)}, f32[2,128,256]{1,2,0:T(8,128)}, u32[]{:S(2)}) copy-start(f32[2,128,256]{1,2,0:T(8,128)} %copy-done.30) | copy-start | bytes 786436
  227.1 8.9 %collective-permute-start.19 = (f32[2,128,512]{2,1,0:T(8,128)}, f32[2,128,512]{2,1,0:T(8,128)}, u32[]{:S(2)}, u32[]{:S(2)}) collective-permute-start(f32[2,128,512]{2,1,0:T(8,128)} %fusion.58), channel_id=1, source_target_pairs={{1,0},{2,1},{3,2},{4,3},{5,4},{6,5},{7,6},{8,7},{9,8},{10,9},{11,1... | collective-permute-start | bytes 1572872 | tf_op jit(solution)/shard_map/ppermute | solution.py:18
  229.0 12.9 %collective-permute-start.20 = (f32[2,128,512]{2,1,0:T(8,128)}, f32[2,128,512]{2,1,0:T(8,128)}, u32[]{:S(2)}, u32[]{:S(2)}) collective-permute-start(f32[2,128,512]{2,1,0:T(8,128)} %fusion.58), channel_id=1, source_target_pairs={{0,1},{1,2},{2,3},{3,4},{4,5},{5,6},{6,7},{7,8},{8,9},{9,10},{10,1... | collective-permute-start | bytes 1572872 | tf_op jit(solution)/shard_map/ppermute | solution.py:17
  234.6 14.3 %copy-start.6 = (f32[1,2,128,144]{2,0,3,1:T(1,128)S(1)}, f32[1,2,128,144]{2,0,3,1:T(1,128)}, u32[]{:S(2)}) copy-start(f32[1,2,128,144]{2,0,3,1:T(1,128)} %get-tuple-element.28) | copy-start | bytes 442372
  234.6 14.3 %copy-start.36 = (f32[2,128,256]{1,2,0:T(8,128)S(1)}, f32[2,128,256]{1,2,0:T(8,128)}, u32[]{:S(2)}) copy-start(f32[2,128,256]{1,2,0:T(8,128)} %copy-done.30) | copy-start | bytes 786436
  253.8 8.9 %collective-permute-start.21 = (f32[2,128,512]{2,1,0:T(8,128)}, f32[2,128,512]{2,1,0:T(8,128)}, u32[]{:S(2)}, u32[]{:S(2)}) collective-permute-start(f32[2,128,512]{2,1,0:T(8,128)} %fusion.68), channel_id=1, source_target_pairs={{1,0},{2,1},{3,2},{4,3},{5,4},{6,5},{7,6},{8,7},{9,8},{10,9},{11,1... | collective-permute-start | bytes 1572872 | tf_op jit(solution)/shard_map/ppermute | solution.py:18
  255.7 12.9 %collective-permute-start.22 = (f32[2,128,512]{2,1,0:T(8,128)}, f32[2,128,512]{2,1,0:T(8,128)}, u32[]{:S(2)}, u32[]{:S(2)}) collective-permute-start(f32[2,128,512]{2,1,0:T(8,128)} %fusion.68), channel_id=1, source_target_pairs={{0,1},{1,2},{2,3},{3,4},{4,5},{5,6},{6,7},{7,8},{8,9},{9,10},{10,1... | collective-permute-start | bytes 1572872 | tf_op jit(solution)/shard_map/ppermute | solution.py:17
  258.8 14.3 %copy-start.18 = (f32[1,2,128,144]{2,0,3,1:T(1,128)S(1)}, f32[1,2,128,144]{2,0,3,1:T(1,128)}, u32[]{:S(2)}) copy-start(f32[1,2,128,144]{2,0,3,1:T(1,128)} %get-tuple-element.29) | copy-start | bytes 442372
  259.9 15.6 %copy-start.37 = (f32[2,128,256]{1,2,0:T(8,128)S(1)}, f32[2,128,256]{1,2,0:T(8,128)}, u32[]{:S(2)}) copy-start(f32[2,128,256]{1,2,0:T(8,128)} %copy-done.30) | copy-start | bytes 786436
  280.3 9.2 %collective-permute-start.23 = (f32[2,128,512]{2,1,0:T(8,128)}, f32[2,128,512]{2,1,0:T(8,128)}, u32[]{:S(2)}, u32[]{:S(2)}) collective-permute-start(f32[2,128,512]{2,1,0:T(8,128)} %fusion.78), channel_id=1, source_target_pairs={{1,0},{2,1},{3,2},{4,3},{5,4},{6,5},{7,6},{8,7},{9,8},{10,9},{11,1... | collective-permute-start | bytes 1572872 | tf_op jit(solution)/shard_map/ppermute | solution.py:18
  282.2 12.9 %collective-permute-start.24 = (f32[2,128,512]{2,1,0:T(8,128)}, f32[2,128,512]{2,1,0:T(8,128)}, u32[]{:S(2)}, u32[]{:S(2)}) collective-permute-start(f32[2,128,512]{2,1,0:T(8,128)} %fusion.78), channel_id=1, source_target_pairs={{0,1},{1,2},{2,3},{3,4},{4,5},{5,6},{6,7},{7,8},{8,9},{9,10},{10,1... | collective-permute-start | bytes 1572872 | tf_op jit(solution)/shard_map/ppermute | solution.py:17
  (35 other events, 225.3 us)

commit v6 on v3

--- a/solution.py
+++ b/solution.py
@@ -12,10 +12,15 @@
 
 def halo(array, axis, width):
     size = lax.axis_size(axis)
-    up = [(i, i + 1) for i in range(size - 1)]
-    down = [(i + 1, i) for i in range(size - 1)]
-    below = lax.ppermute(array[-width:], axis, up)
-    above = lax.ppermute(array[:width], axis, down)
+    odd = lax.axis_index(axis) % 2 == 1
+    top = array[-width:]
+    bottom = array[:width]
+    inner = [(i, i + 1) for i in range(0, size - 1, 2)] + [(i + 1, i) for i in range(0, size - 1, 2)]
+    outer = [(i, i + 1) for i in range(1, size - 1, 2)] + [(i + 1, i) for i in range(1, size - 1, 2)]
+    inner_got = lax.ppermute(jnp.where(odd, bottom, top), axis, inner)
+    outer_got = lax.ppermute(jnp.where(odd, top, bottom), axis, outer)
+    below = jnp.where(odd, inner_got, outer_got)
+    above = jnp.where(odd, outer_got, inner_got)
     return jnp.concatenate([below, array, above], axis=0)
 
 

time: 282 us -> 264 us (0.936)
  waiting for transfers between devices: 102 us -> 79.8 us
  other arithmetic: 24.4 us -> 28.5 us
  starting transfers between devices: 46.8 us -> 50.2 us
    ppermute x18, waiting for transfers between devices: 74.7 us -> 51.3 us  [the longest x9 51.3 us: halo(): outer_got = lax.ppermute(jnp.where(odd, top, bottom), axis, outer)]
    select_n x0 -> x10, other arithmetic: none -> 4.99 us  [the longest x1 1.88 us: halo(): inner_got = lax.ppermute(jnp.where(odd, bottom, top), axis, inner)]
    ppermute x18, starting transfers between devices: 46.8 us -> 50.2 us  [the longest x9 49 us: halo(): outer_got = lax.ppermute(jnp.where(odd, top, bottom), axis, outer)]
  transfers between devices with their start and end apart: 19 -> 19, of which waited for: 16 -> 9; matrix products, arithmetic and copies ran while one was open for 12% -> 12% of each run, Pallas kernels for 0% -> 0%
where the time goes in v6:
time: 264 us; the launch traced here: 262 us
  waiting for transfers between devices  79.8 us (30%)
  matrix products  50.3 us (19%)
  starting transfers between devices  50.2 us (19%)
  between operations  35.2 us (13%)
  other arithmetic  28.5 us (11%)
  local copies, waits for them, and re-layouts  18.5 us (7%)
    ppermute x9, waiting for transfers between devices, halo(): outer_got = lax.ppermute(jnp.where(odd, top, bottom), axis, outer)  51.3 us
    ppermute x9, starting transfers between devices, halo(): outer_got = lax.ppermute(jnp.where(odd, top, bottom), axis, outer)  49 us
    all_gather x1, waiting for transfers between devices, per_device(): data_all = lax.all_gather(view_data[0], 'view', axis=0)  27.8 us
    dot_general x8, matrix products, per_device(): t = jnp.einsum('lij,ljx->lix', by, c, precision=blur_mode)  18.5 us
    mul x7, other arithmetic, per_device(): padded = padded * corr  16 us
    dot_general x8, matrix products, per_device(): jnp.einsum('lix,lax->lia', t, bx_all[position], precision=blur_mode)  14.1 us
    dot_general x8, matrix products, per_device(): g = jnp.einsum('lix,lax->lia', u, bxr_all[position], precision=blur_mode)  8.43 us
    slice x1, local copies, waits for them, and re-layouts, per_device(): bx_all = [band_matrix(mats[2][p], nx, reach) for p in range(view_count)]  6.37 us
  transfers between devices with their start and end apart: 19, of which 9 were waited for; matrix products, arithmetic and copies ran while one was open for 12% of the time, Pallas kernels for 0%

profile of v6, /device:TPU:2, one launch (start us, length us, event | category | flops | bytes accessed | tf_op | source)
XLA Modules:
  0.0 262.5 jit_solution(4972646826968169700)
XLA Ops:
  7.3 1.9 slice_select_fusion.1
  9.2 7.8 %collective-permute-start.1 = (f32[1,128,512]{2,1,0:T(8,128)}, f32[1,128,512]{2,1,0:T(8,128)}, u32[]{:S(2)}, u32[]{:S(2)}) collective-permute-start(f32[1,128,512]{2,1,0:T(8,128)} %get-tuple-element.56), channel_id=1, source_target_pairs={{1,2},{3,4},{5,6},{7,8},{9,10},{11,12},{13,14},{15,16},{17,18},{19... | collective-permute-start | bytes 786440 | tf_op jit(solution)/shard_map/ppermute | solution.py:21
  33.6 1.8 fusion.209
  36.3 1.6 fusion.207
  43.7 6.4 %fusion.445 = (f32[1,2,128,144]{2,0,3,1:T(1,128)}, f32[1,2,128,144]{2,0,3,1:T(1,128)}, f32[1,2,128,144]{2,0,3,1:T(1,128)}, f32[1,2,128,144]{2,0,3,1:T(1,128)}, f...) fusion(f32[8,2,128,144]{2,0,3,1:T(8,128)} %fusion.209), kind=kLoop, calls=%fused_computation.528 | loop fusion | bytes 2359296 | tf_op jit(solution)/shard_map/slice | solution.py:86
  50.8 1.7 fusion.446
  52.6 1.7 fusion.444
  58.3 2.4 fusion.340
  60.7 27.8 %all-gather.2.cloned.1.call-done = f32[8,2,128,512]{3,2,1,0:T(8,128)} async-done(((f32[1,2,128,512]{3,2,1,0:T(8,128)}), f32[8,2,128,512]{3,2,1,0:T(8,128)}) %all-gather.2.cloned.1.call-update) | async-done | bytes 4194320 | tf_op jit(solution)/shard_map/all_gather | solution.py:65
  88.6 2.5 fusion.267
  92.5 5.1 %collective-permute-start.2 = (f32[2,128,512]{2,1,0:T(8,128)S(1)}, f32[2,128,512]{2,1,0:T(8,128)S(1)}, u32[]{:S(2)}, u32[]{:S(2)}) collective-permute-start(f32[2,128,512]{2,1,0:T(8,128)S(1)} %fusion.8), channel_id=1, source_target_pairs={{1,2},{3,4},{5,6},{7,8},{9,10},{11,12},{13,14},{15,16},{17,18},{19... | collective-permute-start | bytes 1572872 | tf_op jit(solution)/shard_map/ppermute | solution.py:21
  98.0 7.1 %collective-permute-done.2 = f32[2,128,512]{2,1,0:T(8,128)S(1)} collective-permute-done((f32[2,128,512]{2,1,0:T(8,128)S(1)}, f32[2,128,512]{2,1,0:T(8,128)S(1)}, u32[]{:S(2)}, u32[]{:S(2)}) %collective-permute-start.2) | collective-permute-done | bytes 524320 | tf_op jit(solution)/shard_map/ppermute | solution.py:21
  105.3 2.8 %fusion.266 = f32[4,128,512]{2,1,0:T(8,128)S(1)} fusion(f32[2,128,512]{2,1,0:T(8,128)S(1)} %get-tuple-element.52, f32[2,128,512]{2,1,0:T(8,128)S(1)} %fusion.8, f32[2,128,512]{2,1,0:T(8,128)S(1)} %get-tuple-element.51, f32[1,128,512]{2,1,0:T(8,128)S(1)} %get-tuple-element.54, f32[2,128,512]{2,1,0:T(8,128)S(1)} %copy-done.5, ...), kind=kLoop, calls=%fused_computation.313 | loop fusion | flops 3145728 | bytes 3670028 | tf_op jit(solution)/shard_map/mul | solution.py:108
  108.1 2.3 fusion.334
  110.5 1.6 fusion.270
  113.6 5.1 %collective-permute-start.4 = (f32[2,128,512]{2,1,0:T(8,128)S(1)}, f32[2,128,512]{2,1,0:T(8,128)S(1)}, u32[]{:S(2)}, u32[]{:S(2)}) collective-permute-start(f32[2,128,512]{2,1,0:T(8,128)S(1)} %fusion.18), channel_id=1, source_target_pairs={{1,2},{3,4},{5,6},{7,8},{9,10},{11,12},{13,14},{15,16},{17,18},{19... | collective-permute-start | bytes 1572872 | tf_op jit(solution)/shard_map/ppermute | solution.py:21
  119.5 6.7 %collective-permute-done.4 = f32[2,128,512]{2,1,0:T(8,128)S(1)} collective-permute-done((f32[2,128,512]{2,1,0:T(8,128)S(1)}, f32[2,128,512]{2,1,0:T(8,128)S(1)}, u32[]{:S(2)}, u32[]{:S(2)}) %collective-permute-start.4) | collective-permute-done | bytes 524320 | tf_op jit(solution)/shard_map/ppermute | solution.py:21
  126.3 2.2 fusion.262
  128.5 2.2 fusion.329
  130.8 1.6 fusion.273
  133.8 5.1 %collective-permute-start.6 = (f32[2,128,512]{2,1,0:T(8,128)S(1)}, f32[2,128,512]{2,1,0:T(8,128)S(1)}, u32[]{:S(2)}, u32[]{:S(2)}) collective-permute-start(f32[2,128,512]{2,1,0:T(8,128)S(1)} %fusion.28), channel_id=1, source_target_pairs={{1,2},{3,4},{5,6},{7,8},{9,10},{11,12},{13,14},{15,16},{17,18},{19... | collective-permute-start | bytes 1572872 | tf_op jit(solution)/shard_map/ppermute | solution.py:21
  139.1 7.3 %collective-permute-done.6 = f32[2,128,512]{2,1,0:T(8,128)S(1)} collective-permute-done((f32[2,128,512]{2,1,0:T(8,128)S(1)}, f32[2,128,512]{2,1,0:T(8,128)S(1)}, u32[]{:S(2)}, u32[]{:S(2)}) %collective-permute-start.6) | collective-permute-done | bytes 524320 | tf_op jit(solution)/shard_map/ppermute | solution.py:21
  146.5 2.1 fusion.258
  148.7 2.4 fusion.324
  151.1 1.7 fusion.276
  154.2 5.1 %collective-permute-start.8 = (f32[2,128,512]{2,1,0:T(8,128)S(1)}, f32[2,128,512]{2,1,0:T(8,128)S(1)}, u32[]{:S(2)}, u32[]{:S(2)}) collective-permute-start(f32[2,128,512]{2,1,0:T(8,128)S(1)} %fusion.38), channel_id=1, source_target_pairs={{1,2},{3,4},{5,6},{7,8},{9,10},{11,12},{13,14},{15,16},{17,18},{19... | collective-permute-start | bytes 1572872 | tf_op jit(solution)/shard_map/ppermute | solution.py:21
  160.1 6.7 %collective-permute-done.8 = f32[2,128,512]{2,1,0:T(8,128)S(1)} collective-permute-done((f32[2,128,512]{2,1,0:T(8,128)S(1)}, f32[2,128,512]{2,1,0:T(8,128)S(1)}, u32[]{:S(2)}, u32[]{:S(2)}) %collective-permute-start.8) | collective-permute-done | bytes 524320 | tf_op jit(solution)/shard_map/ppermute | solution.py:21
  166.9 2.3 fusion.254
  169.3 2.3 fusion.319
  171.5 1.6 fusion.279
  174.6 5.1 %collective-permute-start.10 = (f32[2,128,512]{2,1,0:T(8,128)S(1)}, f32[2,128,512]{2,1,0:T(8,128)S(1)}, u32[]{:S(2)}, u32[]{:S(2)}) collective-permute-start(f32[2,128,512]{2,1,0:T(8,128)S(1)} %fusion.48), channel_id=1, source_target_pairs={{1,2},{3,4},{5,6},{7,8},{9,10},{11,12},{13,14},{15,16},{17,18},{19... | collective-permute-start | bytes 1572872 | tf_op jit(solution)/shard_map/ppermute | solution.py:21
  180.2 7.1 %collective-permute-done.10 = f32[2,128,512]{2,1,0:T(8,128)S(1)} collective-permute-done((f32[2,128,512]{2,1,0:T(8,128)S(1)}, f32[2,128,512]{2,1,0:T(8,128)S(1)}, u32[]{:S(2)}, u32[]{:S(2)}) %collective-permute-start.10) | collective-permute-done | bytes 524320 | tf_op jit(solution)/shard_map/ppermute | solution.py:21
  187.4 2.2 fusion.250
  189.6 2.3 fusion.314
  191.9 1.7 fusion.282
  195.0 5.1 %collective-permute-start.12 = (f32[2,128,512]{2,1,0:T(8,128)S(1)}, f32[2,128,512]{2,1,0:T(8,128)S(1)}, u32[]{:S(2)}, u32[]{:S(2)}) collective-permute-start(f32[2,128,512]{2,1,0:T(8,128)S(1)} %fusion.58), channel_id=1, source_target_pairs={{1,2},{3,4},{5,6},{7,8},{9,10},{11,12},{13,14},{15,16},{17,18},{19... | collective-permute-start | bytes 1572872 | tf_op jit(solution)/shard_map/ppermute | solution.py:21
  200.9 6.7 %collective-permute-done.12 = f32[2,128,512]{2,1,0:T(8,128)S(1)} collective-permute-done((f32[2,128,512]{2,1,0:T(8,128)S(1)}, f32[2,128,512]{2,1,0:T(8,128)S(1)}, u32[]{:S(2)}, u32[]{:S(2)}) %collective-permute-start.12) | collective-permute-done | bytes 524320 | tf_op jit(solution)/shard_map/ppermute | solution.py:21
  207.8 2.2 fusion.246
  210.0 2.4 fusion.309
  215.4 5.1 %collective-permute-start.14 = (f32[2,128,512]{2,1,0:T(8,128)S(1)}, f32[2,128,512]{2,1,0:T(8,128)S(1)}, u32[]{:S(2)}, u32[]{:S(2)}) collective-permute-start(f32[2,128,512]{2,1,0:T(8,128)S(1)} %fusion.68), channel_id=1, source_target_pairs={{1,2},{3,4},{5,6},{7,8},{9,10},{11,12},{13,14},{15,16},{17,18},{19... | collective-permute-start | bytes 1572872 | tf_op jit(solution)/shard_map/ppermute | solution.py:21
  220.7 7.3 %collective-permute-done.14 = f32[2,128,512]{2,1,0:T(8,128)S(1)} collective-permute-done((f32[2,128,512]{2,1,0:T(8,128)S(1)}, f32[2,128,512]{2,1,0:T(8,128)S(1)}, u32[]{:S(2)}, u32[]{:S(2)}) %collective-permute-start.14) | collective-permute-done | bytes 524320 | tf_op jit(solution)/shard_map/ppermute | solution.py:21
  228.2 2.2 fusion.242
  230.4 2.3 fusion.304
  232.8 1.7 fusion.288
  234.9 1.7 fusion.78
  236.6 5.1 %collective-permute-start.16 = (f32[2,128,512]{2,1,0:T(8,128)}, f32[2,128,512]{2,1,0:T(8,128)}, u32[]{:S(2)}, u32[]{:S(2)}) collective-permute-start(f32[2,128,512]{2,1,0:T(8,128)} %fusion.78), channel_id=1, source_target_pairs={{1,2},{3,4},{5,6},{7,8},{9,10},{11,12},{13,14},{15,16},{17,18},{19... | collective-permute-start | bytes 1572872 | tf_op jit(solution)/shard_map/ppermute | solution.py:21
  246.9 2.5 collective-permute-done.16
  250.8 4.8 %fusion.299 = f32[1,2,128,512]{3,2,1,0:T(8,128)} fusion(f32[2,128,512]{2,1,0:T(8,128)} %fusion.78, f32[2,128,512]{2,1,0:T(8,128)S(1)} %get-tuple-element.38, f32[2,128,512]{2,1,0:T(8,128)S(1)} %get-tuple-element.37, f32[4,128,512]{2,1,0:T(8,128)} %copy-done.6, f32[4,128,512]{2,1,0:T(8,128)} %copy-done.4, f32[4,128,512]{2,1,0:T(8,128)S(1)} %copy-done.3, ...), kind=kLoop, calls=%fused_computation.346 | loop fusion | flops 2359296 | bytes 5767188 | tf_op jit(solution)/shard_map/broadcast_in_dim | solution.py:110
  (184 shorter events, 30.6 us)
Async XLA Ops:
  6.5 25.9 %copy-start.47 = (s32[2]{0:T(128)S(1)}, s32[2]{0:T(128)}, u32[]{:S(2)}) copy-start(s32[2]{0:T(128)} %param.13) | copy-start | bytes 28
  6.5 82.0 %all-gather.2.cloned.1.call-start = ((), (), s32[]{:S(2)}) async-start(), calls=%async_computation | async-start | bytes 4718592 | tf_op jit(solution)/shard_map/all_gather | solution.py:65
  9.2 48.1 %collective-permute-start = (f32[1,128,512]{2,1,0:T(8,128)}, f32[1,128,512]{2,1,0:T(8,128)}, u32[]{:S(2)}, u32[]{:S(2)}) collective-permute-start(f32[1,128,512]{2,1,0:T(8,128)} %get-tuple-element.55), channel_id=1, source_target_pairs={{0,1},{2,3},{4,5},{6,7},{8,9},{10,11},{12,13},{14,15},{16,17},{18,... | collective-permute-start | bytes 786440 | tf_op jit(solution)/shard_map/ppermute | solution.py:20
  9.2 48.1 %collective-permute-start.1 = (f32[1,128,512]{2,1,0:T(8,128)}, f32[1,128,512]{2,1,0:T(8,128)}, u32[]{:S(2)}, u32[]{:S(2)}) collective-permute-start(f32[1,128,512]{2,1,0:T(8,128)} %get-tuple-element.56), channel_id=1, source_target_pairs={{1,2},{3,4},{5,6},{7,8},{9,10},{11,12},{13,14},{15,16},{17,18},{19... | collective-permute-start | bytes 786440 | tf_op jit(solution)/shard_map/ppermute | solution.py:21
  33.6 9.4 %copy-start.43 = (f32[8,3]{0,1:T(4,128)S(1)}, f32[8,3]{0,1:T(4,128)}, u32[]{:S(2)}) copy-start(f32[8,3]{0,1:T(4,128)} %param.11) | copy-start | bytes 292
  50.1 4.2 %copy-start.24 = (f32[1,2,128,144]{2,0,3,1:T(1,128)}, f32[1,2,128,144]{2,0,3,1:T(1,128)S(1)}, u32[]{:S(2)}) copy-start(f32[1,2,128,144]{2,0,3,1:T(1,128)S(1)} %get-tuple-element.27) | copy-start | bytes 442372
  52.6 4.0 %copy-start.42 = (f32[8]{0:T(128)S(1)}, f32[8]{0:T(128)}, u32[]{:S(2)}) copy-start(f32[8]{0:T(128)} %param.9) | copy-start | bytes 100
  54.3 4.0 %copy-start.5 = (f32[2,128,512]{2,1,0:T(8,128)S(1)}, f32[2,128,512]{2,1,0:T(8,128)}, u32[]{:S(2)}) copy-start(f32[2,128,512]{2,1,0:T(8,128)} %param.7) | copy-start | bytes 1572868
  55.9 42.1 %copy-start.22 = (f32[1,2,128,144]{2,0,3,1:T(1,128)}, f32[1,2,128,144]{2,0,3,1:T(1,128)S(1)}, u32[]{:S(2)}) copy-start(f32[1,2,128,144]{2,0,3,1:T(1,128)S(1)} %get-tuple-element.11) | copy-start | bytes 442372
  55.9 83.2 %copy-start.17 = (f32[1,2,128,144]{2,0,3,1:T(1,128)}, f32[1,2,128,144]{2,0,3,1:T(1,128)S(1)}, u32[]{:S(2)}) copy-start(f32[1,2,128,144]{2,0,3,1:T(1,128)S(1)} %get-tuple-element.9) | copy-start | bytes 442372
  55.9 32.7 %copy-start.25 = (f32[1,2,128,144]{2,0,3,1:T(1,128)S(1)}, f32[1,2,128,144]{2,0,3,1:T(1,128)}, u32[]{:S(2)}) copy-start(f32[1,2,128,144]{2,0,3,1:T(1,128)} %copy-done.24) | copy-start | bytes 442372
  55.9 32.7 %copy-start.40 = (f32[2,128,136]{1,2,0:T(8,128)S(1)}, f32[2,128,136]{1,2,0:T(8,128)}, u32[]{:S(2)}) copy-start(f32[2,128,136]{1,2,0:T(8,128)} %get-tuple-element.87) | copy-start | bytes 417796
  55.9 32.7 %copy-start.41 = (f32[2,128,136]{1,2,0:T(8,128)S(1)}, f32[2,128,136]{1,2,0:T(8,128)}, u32[]{:S(2)}) copy-start(f32[2,128,136]{1,2,0:T(8,128)} %get-tuple-element.88) | copy-start | bytes 417796
  91.5 6.4 %copy-start.21 = (f32[1,2,128,144]{2,0,3,1:T(1,128)S(1)}, f32[1,2,128,144]{2,0,3,1:T(1,128)}, u32[]{:S(2)}) copy-start(f32[1,2,128,144]{2,0,3,1:T(1,128)} %get-tuple-element.26) | copy-start | bytes 442372
  92.5 12.6 %collective-permute-start.2 = (f32[2,128,512]{2,1,0:T(8,128)S(1)}, f32[2,128,512]{2,1,0:T(8,128)S(1)}, u32[]{:S(2)}, u32[]{:S(2)}) collective-permute-start(f32[2,128,512]{2,1,0:T(8,128)S(1)} %fusion.8), channel_id=1, source_target_pairs={{1,2},{3,4},{5,6},{7,8},{9,10},{11,12},{13,14},{15,16},{17,18},{19... | collective-permute-start | bytes 1572872 | tf_op jit(solution)/shard_map/ppermute | solution.py:21
  97.7 7.5 %collective-permute-start.3 = (f32[2,128,512]{2,1,0:T(8,128)S(1)}, f32[2,128,512]{2,1,0:T(8,128)S(1)}, u32[]{:S(2)}, u32[]{:S(2)}) collective-permute-start(f32[2,128,512]{2,1,0:T(8,128)S(1)} %fusion.8), channel_id=1, source_target_pairs={{0,1},{2,3},{4,5},{6,7},{8,9},{10,11},{12,13},{14,15},{16,17},{18,... | collective-permute-start | bytes 1572872 | tf_op jit(solution)/shard_map/ppermute | solution.py:20
  105.3 5.2 %copy-start.46 = (f32[8,2,128,512]{3,2,1,0:T(8,128)S(1)}, f32[8,2,128,512]{3,2,1,0:T(8,128)}, u32[]{:S(2)}) copy-start(f32[8,2,128,512]{3,2,1,0:T(8,128)} %all-gather.2.cloned.1.call-done) | copy-start | bytes 12582916
  112.6 6.3 %copy-start.44 = (f32[1,3]{0,1:T(4,128)S(1)}, f32[1,3]{0,1:T(4,128)}, u32[]{:S(2)}) copy-start(f32[1,3]{0,1:T(4,128)} %get-tuple-element.98) | copy-start | bytes 40
  112.6 6.3 %copy-start.45 = (f32[1,3]{0,1:T(4,128)S(1)}, f32[1,3]{0,1:T(4,128)}, u32[]{:S(2)}) copy-start(f32[1,3]{0,1:T(4,128)} %get-tuple-element.99) | copy-start | bytes 40
  112.6 6.9 %copy-start.19 = (f32[1,2,128,144]{2,0,3,1:T(1,128)S(1)}, f32[1,2,128,144]{2,0,3,1:T(1,128)}, u32[]{:S(2)}) copy-start(f32[1,2,128,144]{2,0,3,1:T(1,128)} %get-tuple-element.25) | copy-start | bytes 442372
  112.6 6.9 %copy-start.20 = (f32[1,2,128,144]{2,0,3,1:T(1,128)S(1)}, f32[1,2,128,144]{2,0,3,1:T(1,128)}, u32[]{:S(2)}) copy-start(f32[1,2,128,144]{2,0,3,1:T(1,128)} %get-tuple-element.10) | copy-start | bytes 442372
  113.6 12.6 %collective-permute-start.4 = (f32[2,128,512]{2,1,0:T(8,128)S(1)}, f32[2,128,512]{2,1,0:T(8,128)S(1)}, u32[]{:S(2)}, u32[]{:S(2)}) collective-permute-start(f32[2,128,512]{2,1,0:T(8,128)S(1)} %fusion.18), channel_id=1, source_target_pairs={{1,2},{3,4},{5,6},{7,8},{9,10},{11,12},{13,14},{15,16},{17,18},{19... | collective-permute-start | bytes 1572872 | tf_op jit(solution)/shard_map/ppermute | solution.py:21
  118.7 7.5 %collective-permute-start.5 = (f32[2,128,512]{2,1,0:T(8,128)S(1)}, f32[2,128,512]{2,1,0:T(8,128)S(1)}, u32[]{:S(2)}, u32[]{:S(2)}) collective-permute-start(f32[2,128,512]{2,1,0:T(8,128)S(1)} %fusion.18), channel_id=1, source_target_pairs={{0,1},{2,3},{4,5},{6,7},{8,9},{10,11},{12,13},{14,15},{16,17},{18,... | collective-permute-start | bytes 1572872 | tf_op jit(solution)/shard_map/ppermute | solution.py:20
  132.8 6.2 %copy-start.16 = (f32[1,2,128,144]{2,0,3,1:T(1,128)S(1)}, f32[1,2,128,144]{2,0,3,1:T(1,128)}, u32[]{:S(2)}) copy-start(f32[1,2,128,144]{2,0,3,1:T(1,128)} %get-tuple-element.24) | copy-start | bytes 442372
  133.8 12.6 %collective-permute-start.6 = (f32[2,128,512]{2,1,0:T(8,128)S(1)}, f32[2,128,512]{2,1,0:T(8,128)S(1)}, u32[]{:S(2)}, u32[]{:S(2)}) collective-permute-start(f32[2,128,512]{2,1,0:T(8,128)S(1)} %fusion.28), channel_id=1, source_target_pairs={{1,2},{3,4},{5,6},{7,8},{9,10},{11,12},{13,14},{15,16},{17,18},{19... | collective-permute-start | bytes 1572872 | tf_op jit(solution)/shard_map/ppermute | solution.py:21
  139.0 7.5 %collective-permute-start.7 = (f32[2,128,512]{2,1,0:T(8,128)S(1)}, f32[2,128,512]{2,1,0:T(8,128)S(1)}, u32[]{:S(2)}, u32[]{:S(2)}) collective-permute-start(f32[2,128,512]{2,1,0:T(8,128)S(1)} %fusion.28), channel_id=1, source_target_pairs={{0,1},{2,3},{4,5},{6,7},{8,9},{10,11},{12,13},{14,15},{16,17},{18,... | collective-permute-start | bytes 1572872 | tf_op jit(solution)/shard_map/ppermute | solution.py:20
  153.2 6.9 %copy-start.14 = (f32[1,2,128,144]{2,0,3,1:T(1,128)S(1)}, f32[1,2,128,144]{2,0,3,1:T(1,128)}, u32[]{:S(2)}) copy-start(f32[1,2,128,144]{2,0,3,1:T(1,128)} %get-tuple-element.23) | copy-start | bytes 442372
  153.2 6.9 %copy-start.15 = (f32[1,2,128,144]{2,0,3,1:T(1,128)S(1)}, f32[1,2,128,144]{2,0,3,1:T(1,128)}, u32[]{:S(2)}) copy-start(f32[1,2,128,144]{2,0,3,1:T(1,128)} %get-tuple-element.8) | copy-start | bytes 442372
  154.2 12.6 %collective-permute-start.8 = (f32[2,128,512]{2,1,0:T(8,128)S(1)}, f32[2,128,512]{2,1,0:T(8,128)S(1)}, u32[]{:S(2)}, u32[]{:S(2)}) collective-permute-start(f32[2,128,512]{2,1,0:T(8,128)S(1)} %fusion.38), channel_id=1, source_target_pairs={{1,2},{3,4},{5,6},{7,8},{9,10},{11,12},{13,14},{15,16},{17,18},{19... | collective-permute-start | bytes 1572872 | tf_op jit(solution)/shard_map/ppermute | solution.py:21
  159.4 7.5 %collective-permute-start.9 = (f32[2,128,512]{2,1,0:T(8,128)S(1)}, f32[2,128,512]{2,1,0:T(8,128)S(1)}, u32[]{:S(2)}, u32[]{:S(2)}) collective-permute-start(f32[2,128,512]{2,1,0:T(8,128)S(1)} %fusion.38), channel_id=1, source_target_pairs={{0,1},{2,3},{4,5},{6,7},{8,9},{10,11},{12,13},{14,15},{16,17},{18,... | collective-permute-start | bytes 1572872 | tf_op jit(solution)/shard_map/ppermute | solution.py:20
  169.2 18.1 %copy-start = (f32[4,128,512]{2,1,0:T(8,128)}, f32[4,128,512]{2,1,0:T(8,128)S(1)}, u32[]{:S(2)}) copy-start(f32[4,128,512]{2,1,0:T(8,128)S(1)} %fusion.254) | copy-start | bytes 3145732
  173.6 6.5 %copy-start.12 = (f32[1,2,128,144]{2,0,3,1:T(1,128)S(1)}, f32[1,2,128,144]{2,0,3,1:T(1,128)}, u32[]{:S(2)}) copy-start(f32[1,2,128,144]{2,0,3,1:T(1,128)} %get-tuple-element.22) | copy-start | bytes 442372
  173.6 6.5 %copy-start.13 = (f32[1,2,128,144]{2,0,3,1:T(1,128)S(1)}, f32[1,2,128,144]{2,0,3,1:T(1,128)}, u32[]{:S(2)}) copy-start(f32[1,2,128,144]{2,0,3,1:T(1,128)} %get-tuple-element.7) | copy-start | bytes 442372
  174.6 12.6 %collective-permute-start.10 = (f32[2,128,512]{2,1,0:T(8,128)S(1)}, f32[2,128,512]{2,1,0:T(8,128)S(1)}, u32[]{:S(2)}, u32[]{:S(2)}) collective-permute-start(f32[2,128,512]{2,1,0:T(8,128)S(1)} %fusion.48), channel_id=1, source_target_pairs={{1,2},{3,4},{5,6},{7,8},{9,10},{11,12},{13,14},{15,16},{17,18},{19... | collective-permute-start | bytes 1572872 | tf_op jit(solution)/shard_map/ppermute | solution.py:21
  179.8 7.5 %collective-permute-start.11 = (f32[2,128,512]{2,1,0:T(8,128)S(1)}, f32[2,128,512]{2,1,0:T(8,128)S(1)}, u32[]{:S(2)}, u32[]{:S(2)}) collective-permute-start(f32[2,128,512]{2,1,0:T(8,128)S(1)} %fusion.48), channel_id=1, source_target_pairs={{0,1},{2,3},{4,5},{6,7},{8,9},{10,11},{12,13},{14,15},{16,17},{18,... | collective-permute-start | bytes 1572872 | tf_op jit(solution)/shard_map/ppermute | solution.py:20
  189.5 18.2 %copy-start.2 = (f32[4,128,512]{2,1,0:T(8,128)}, f32[4,128,512]{2,1,0:T(8,128)S(1)}, u32[]{:S(2)}) copy-start(f32[4,128,512]{2,1,0:T(8,128)S(1)} %fusion.250) | copy-start | bytes 3145732
  194.0 6.8 %copy-start.10 = (f32[1,2,128,144]{2,0,3,1:T(1,128)S(1)}, f32[1,2,128,144]{2,0,3,1:T(1,128)}, u32[]{:S(2)}) copy-start(f32[1,2,128,144]{2,0,3,1:T(1,128)} %get-tuple-element.28) | copy-start | bytes 442372
  194.0 6.9 %copy-start.11 = (f32[1,2,128,144]{2,0,3,1:T(1,128)S(1)}, f32[1,2,128,144]{2,0,3,1:T(1,128)}, u32[]{:S(2)}) copy-start(f32[1,2,128,144]{2,0,3,1:T(1,128)} %get-tuple-element.6) | copy-start | bytes 442372
  195.0 12.6 %collective-permute-start.12 = (f32[2,128,512]{2,1,0:T(8,128)S(1)}, f32[2,128,512]{2,1,0:T(8,128)S(1)}, u32[]{:S(2)}, u32[]{:S(2)}) collective-permute-start(f32[2,128,512]{2,1,0:T(8,128)S(1)} %fusion.58), channel_id=1, source_target_pairs={{1,2},{3,4},{5,6},{7,8},{9,10},{11,12},{13,14},{15,16},{17,18},{19... | collective-permute-start | bytes 1572872 | tf_op jit(solution)/shard_map/ppermute | solution.py:21
  200.2 7.5 %collective-permute-start.13 = (f32[2,128,512]{2,1,0:T(8,128)S(1)}, f32[2,128,512]{2,1,0:T(8,128)S(1)}, u32[]{:S(2)}, u32[]{:S(2)}) collective-permute-start(f32[2,128,512]{2,1,0:T(8,128)S(1)} %fusion.58), channel_id=1, source_target_pairs={{0,1},{2,3},{4,5},{6,7},{8,9},{10,11},{12,13},{14,15},{16,17},{18,... | collective-permute-start | bytes 1572872 | tf_op jit(solution)/shard_map/ppermute | solution.py:20
  210.0 18.2 %copy-start.4 = (f32[4,128,512]{2,1,0:T(8,128)}, f32[4,128,512]{2,1,0:T(8,128)S(1)}, u32[]{:S(2)}) copy-start(f32[4,128,512]{2,1,0:T(8,128)S(1)} %fusion.246) | copy-start | bytes 3145732
  214.4 6.2 %copy-start.8 = (f32[1,2,128,144]{2,0,3,1:T(1,128)S(1)}, f32[1,2,128,144]{2,0,3,1:T(1,128)}, u32[]{:S(2)}) copy-start(f32[1,2,128,144]{2,0,3,1:T(1,128)} %get-tuple-element.21) | copy-start | bytes 442372
  214.4 6.3 %copy-start.9 = (f32[1,2,128,144]{2,0,3,1:T(1,128)S(1)}, f32[1,2,128,144]{2,0,3,1:T(1,128)}, u32[]{:S(2)}) copy-start(f32[1,2,128,144]{2,0,3,1:T(1,128)} %get-tuple-element.5) | copy-start | bytes 442372
  215.4 12.6 %collective-permute-start.14 = (f32[2,128,512]{2,1,0:T(8,128)S(1)}, f32[2,128,512]{2,1,0:T(8,128)S(1)}, u32[]{:S(2)}, u32[]{:S(2)}) collective-permute-start(f32[2,128,512]{2,1,0:T(8,128)S(1)} %fusion.68), channel_id=1, source_target_pairs={{1,2},{3,4},{5,6},{7,8},{9,10},{11,12},{13,14},{15,16},{17,18},{19... | collective-permute-start | bytes 1572872 | tf_op jit(solution)/shard_map/ppermute | solution.py:21
  220.6 7.5 %collective-permute-start.15 = (f32[2,128,512]{2,1,0:T(8,128)S(1)}, f32[2,128,512]{2,1,0:T(8,128)S(1)}, u32[]{:S(2)}, u32[]{:S(2)}) collective-permute-start(f32[2,128,512]{2,1,0:T(8,128)S(1)} %fusion.68), channel_id=1, source_target_pairs={{0,1},{2,3},{4,5},{6,7},{8,9},{10,11},{12,13},{14,15},{16,17},{18,... | collective-permute-start | bytes 1572872 | tf_op jit(solution)/shard_map/ppermute | solution.py:20
  230.4 4.1 %copy-start.6 = (f32[4,128,512]{2,1,0:T(8,128)}, f32[4,128,512]{2,1,0:T(8,128)S(1)}, u32[]{:S(2)}) copy-start(f32[4,128,512]{2,1,0:T(8,128)S(1)} %fusion.242) | copy-start | bytes 3145732
  236.6 12.9 %collective-permute-start.16 = (f32[2,128,512]{2,1,0:T(8,128)}, f32[2,128,512]{2,1,0:T(8,128)}, u32[]{:S(2)}, u32[]{:S(2)}) collective-permute-start(f32[2,128,512]{2,1,0:T(8,128)} %fusion.78), channel_id=1, source_target_pairs={{1,2},{3,4},{5,6},{7,8},{9,10},{11,12},{13,14},{15,16},{17,18},{19... | collective-permute-start | bytes 1572872 | tf_op jit(solution)/shard_map/ppermute | solution.py:21
  241.7 7.8 %collective-permute-start.17 = (f32[2,128,512]{2,1,0:T(8,128)}, f32[2,128,512]{2,1,0:T(8,128)}, u32[]{:S(2)}, u32[]{:S(2)}) collective-permute-start(f32[2,128,512]{2,1,0:T(8,128)} %fusion.78), channel_id=1, source_target_pairs={{0,1},{2,3},{4,5},{6,7},{8,9},{10,11},{12,13},{14,15},{16,17},{18,... | collective-permute-start | bytes 1572872 | tf_op jit(solution)/shard_map/ppermute | solution.py:20
  (19 other events, 43.4 us)
Sparse Core Ops, SparseCore 0:
  10.0 78.4 all-gather.1

commit v7 on v6

--- a/solution.py
+++ b/solution.py
@@ -107,6 +107,7 @@
             corr = corr + kz[k] * gp[2 - k : 2 - k + count + 2]
         padded = padded * corr
         results = jnp.where(my_view == view_id, padded[RZ:-RZ], results)
+        padded, results = lax.optimization_barrier((padded, results))
     return results[None]
 
 

time: 264 us -> 281 us (1.064)
  matrix products: 50.3 us -> 59.5 us
  other arithmetic: 28.5 us -> 32.8 us
  local copies, waits for them, and re-layouts: 18.5 us -> 21.7 us
    mul x7 -> x8, other arithmetic: 16 us -> 23.9 us  [per_device(): padded = padded * corr]
    dot_general x8, matrix products: 14.1 us -> 21.1 us  [per_device(): jnp.einsum('lix,lax->lia', t, bx_all[position], precision=blur_mode)]
    broadcast_in_dim x1 -> x0, other arithmetic: 4.82 us -> none  [per_device(): return results[None]]
where the time goes in v7:
time: 281 us; the launch traced here: 279 us
  waiting for transfers between devices  80 us (28%)
  matrix products  59.5 us (21%)
  starting transfers between devices  50.1 us (18%)
  between operations  34.7 us (12%)
  other arithmetic  32.8 us (12%)
  local copies, waits for them, and re-layouts  21.7 us (8%)
    ppermute x9, waiting for transfers between devices, halo(): outer_got = lax.ppermute(jnp.where(odd, top, bottom), axis, outer)  52 us
    ppermute x9, starting transfers between devices, halo(): outer_got = lax.ppermute(jnp.where(odd, top, bottom), axis, outer)  49 us
    all_gather x1, waiting for transfers between devices, per_device(): data_all = lax.all_gather(view_data[0], 'view', axis=0)  27.3 us
    mul x8, other arithmetic, per_device(): padded = padded * corr  23.9 us
    dot_general x8, matrix products, per_device(): jnp.einsum('lix,lax->lia', t, bx_all[position], precision=blur_mode)  21.1 us
    dot_general x8, matrix products, per_device(): t = jnp.einsum('lij,ljx->lix', by, c, precision=blur_mode)  18.7 us
    dot_general x8, matrix products, per_device(): g = jnp.einsum('lix,lax->lia', u, bxr_all[position], precision=blur_mode)  10.5 us
    slice x1, local copies, waits for them, and re-layouts, per_device(): bx_all = [band_matrix(mats[2][p], nx, reach) for p in range(view_count)]  6.94 us
  transfers between devices with their start and end apart: 19, of which 9 were waited for; matrix products, arithmetic and copies ran while one was open for 12% of the time, Pallas kernels for 0%

profile of v7, /device:TPU:2, one launch (start us, length us, event | category | flops | bytes accessed | tf_op | source)
XLA Modules:
  0.0 278.9 jit_solution(14217057621155554274)
XLA Ops:
  7.3 1.9 slice_select_fusion.9
  9.2 7.8 %collective-permute-start.1 = (f32[1,128,512]{2,1,0:T(8,128)}, f32[1,128,512]{2,1,0:T(8,128)}, u32[]{:S(2)}, u32[]{:S(2)}) collective-permute-start(f32[1,128,512]{2,1,0:T(8,128)} %get-tuple-element.86), channel_id=1, source_target_pairs={{1,2},{3,4},{5,6},{7,8},{9,10},{11,12},{13,14},{15,16},{17,18},{19... | collective-permute-start | bytes 786440 | tf_op jit(solution)/shard_map/ppermute | solution.py:21
  33.2 1.8 fusion.209
  43.1 6.9 %fusion.455 = (f32[1,2,128,144]{2,0,3,1:T(1,128)}, f32[1,2,128,144]{2,0,3,1:T(1,128)}, f32[1,2,128,144]{2,0,3,1:T(1,128)}, f32[1,2,128,144]{2,0,3,1:T(1,128)}, f...) fusion(f32[8,2,128,144]{2,0,3,1:T(8,128)} %fusion.209), kind=kLoop, calls=%fused_computation.546 | loop fusion | bytes 2359296 | tf_op jit(solution)/shard_map/slice | solution.py:86
  50.8 1.7 fusion.456
  52.5 1.7 fusion.454
  59.0 2.2 fusion.301
  61.2 27.3 %all-gather.2.cloned.1.call-done = f32[8,2,128,512]{3,2,1,0:T(8,128)} async-done(((f32[1,2,128,512]{3,2,1,0:T(8,128)}), f32[8,2,128,512]{3,2,1,0:T(8,128)}) %all-gather.2.cloned.1.call-update) | async-done | bytes 4194320 | tf_op jit(solution)/shard_map/all_gather | solution.py:65
  88.7 2.6 fusion.271
  92.8 5.1 %collective-permute-start.2 = (f32[2,128,512]{2,1,0:T(8,128)S(1)}, f32[2,128,512]{2,1,0:T(8,128)S(1)}, u32[]{:S(2)}, u32[]{:S(2)}) collective-permute-start(f32[2,128,512]{2,1,0:T(8,128)S(1)} %fusion.8), channel_id=1, source_target_pairs={{1,2},{3,4},{5,6},{7,8},{9,10},{11,12},{13,14},{15,16},{17,18},{19... | collective-permute-start | bytes 1572872 | tf_op jit(solution)/shard_map/ppermute | solution.py:21
  99.0 6.5 %collective-permute-done.2 = f32[2,128,512]{2,1,0:T(8,128)S(1)} collective-permute-done((f32[2,128,512]{2,1,0:T(8,128)S(1)}, f32[2,128,512]{2,1,0:T(8,128)S(1)}, u32[]{:S(2)}, u32[]{:S(2)}) %collective-permute-start.2) | collective-permute-done | bytes 524320 | tf_op jit(solution)/shard_map/ppermute | solution.py:21
  105.6 2.2 fusion.270
  107.8 2.3 fusion.362
  110.2 2.6 fusion.274
  114.9 5.1 %collective-permute-start.4 = (f32[2,128,512]{2,1,0:T(8,128)}, f32[2,128,512]{2,1,0:T(8,128)S(1)}, u32[]{:S(2)}, u32[]{:S(2)}) collective-permute-start(f32[2,128,512]{2,1,0:T(8,128)} %fusion.18), channel_id=1, source_target_pairs={{1,2},{3,4},{5,6},{7,8},{9,10},{11,12},{13,14},{15,16},{17,18},{19... | collective-permute-start | bytes 1572872 | tf_op jit(solution)/shard_map/ppermute | solution.py:21
  121.5 6.2 %collective-permute-done.4 = f32[2,128,512]{2,1,0:T(8,128)S(1)} collective-permute-done((f32[2,128,512]{2,1,0:T(8,128)}, f32[2,128,512]{2,1,0:T(8,128)S(1)}, u32[]{:S(2)}, u32[]{:S(2)}) %collective-permute-start.4) | collective-permute-done | bytes 524320 | tf_op jit(solution)/shard_map/ppermute | solution.py:21
  128.9 3.8 %fusion.266 = f32[4,128,512]{2,1,0:T(8,128)S(1)} fusion(f32[4,128,512]{2,1,0:T(8,128)S(1)} %fusion.270, f32[2,128,512]{2,1,0:T(8,128)S(1)} %get-tuple-element.80, f32[2,128,512]{2,1,0:T(8,128)} %fusion.18, f32[2,128,512]{2,1,0:T(8,128)S(1)} %get-tuple-element.79, f32[]{:T(128)} %bitcast.30, f32[]{:T(128)} %bitcast.29, f32[]{:T(128)} %bitcast.25), kind=kLoop, calls=%fused_computation.313 | loop fusion | flops 2621440 | bytes 3670028 | tf_op jit(solution)/shard_map/mul | solution.py:108
  132.8 2.5 fusion.353
  135.4 2.6 fusion.277
  139.4 5.1 %collective-permute-start.6 = (f32[2,128,512]{2,1,0:T(8,128)S(1)}, f32[2,128,512]{2,1,0:T(8,128)S(1)}, u32[]{:S(2)}, u32[]{:S(2)}) collective-permute-start(f32[2,128,512]{2,1,0:T(8,128)S(1)} %fusion.28), channel_id=1, source_target_pairs={{1,2},{3,4},{5,6},{7,8},{9,10},{11,12},{13,14},{15,16},{17,18},{19... | collective-permute-start | bytes 1572872 | tf_op jit(solution)/shard_map/ppermute | solution.py:21
  145.3 6.7 %collective-permute-done.6 = f32[2,128,512]{2,1,0:T(8,128)S(1)} collective-permute-done((f32[2,128,512]{2,1,0:T(8,128)S(1)}, f32[2,128,512]{2,1,0:T(8,128)S(1)}, u32[]{:S(2)}, u32[]{:S(2)}) %collective-permute-start.6) | collective-permute-done | bytes 524320 | tf_op jit(solution)/shard_map/ppermute | solution.py:21
  153.1 2.3 fusion.262
  155.6 2.3 fusion.344
  157.9 2.6 fusion.280
  162.6 5.1 %collective-permute-start.8 = (f32[2,128,512]{2,1,0:T(8,128)}, f32[2,128,512]{2,1,0:T(8,128)S(1)}, u32[]{:S(2)}, u32[]{:S(2)}) collective-permute-start(f32[2,128,512]{2,1,0:T(8,128)} %fusion.38), channel_id=1, source_target_pairs={{1,2},{3,4},{5,6},{7,8},{9,10},{11,12},{13,14},{15,16},{17,18},{19... | collective-permute-start | bytes 1572872 | tf_op jit(solution)/shard_map/ppermute | solution.py:21
  169.2 6.3 %collective-permute-done.8 = f32[2,128,512]{2,1,0:T(8,128)S(1)} collective-permute-done((f32[2,128,512]{2,1,0:T(8,128)}, f32[2,128,512]{2,1,0:T(8,128)S(1)}, u32[]{:S(2)}, u32[]{:S(2)}) %collective-permute-start.8) | collective-permute-done | bytes 524320 | tf_op jit(solution)/shard_map/ppermute | solution.py:21
  175.6 3.7 %fusion.258 = f32[4,128,512]{2,1,0:T(8,128)S(1)} fusion(f32[4,128,512]{2,1,0:T(8,128)S(1)} %fusion.262, f32[2,128,512]{2,1,0:T(8,128)S(1)} %get-tuple-element.76, f32[2,128,512]{2,1,0:T(8,128)} %fusion.38, f32[2,128,512]{2,1,0:T(8,128)S(1)} %get-tuple-element.75, f32[]{:T(128)} %bitcast.50, f32[]{:T(128)} %bitcast.49, f32[]{:T(128)} %bitcast.45), kind=kLoop, calls=%fused_computation.301 | loop fusion | flops 2621440 | bytes 3670028 | tf_op jit(solution)/shard_map/mul | solution.py:108
  179.4 2.3 fusion.335
  181.8 2.7 fusion.283
  186.0 5.1 %collective-permute-start.10 = (f32[2,128,512]{2,1,0:T(8,128)S(1)}, f32[2,128,512]{2,1,0:T(8,128)S(1)}, u32[]{:S(2)}, u32[]{:S(2)}) collective-permute-start(f32[2,128,512]{2,1,0:T(8,128)S(1)} %fusion.48), channel_id=1, source_target_pairs={{1,2},{3,4},{5,6},{7,8},{9,10},{11,12},{13,14},{15,16},{17,18},{19... | collective-permute-start | bytes 1572872 | tf_op jit(solution)/shard_map/ppermute | solution.py:21
  192.1 6.4 %collective-permute-done.10 = f32[2,128,512]{2,1,0:T(8,128)S(1)} collective-permute-done((f32[2,128,512]{2,1,0:T(8,128)S(1)}, f32[2,128,512]{2,1,0:T(8,128)S(1)}, u32[]{:S(2)}, u32[]{:S(2)}) %collective-permute-start.10) | collective-permute-done | bytes 524320 | tf_op jit(solution)/shard_map/ppermute | solution.py:21
  199.6 2.2 fusion.254
  201.9 2.2 fusion.326
  204.2 2.7 fusion.286
  207.3 1.7 fusion.58
  209.0 5.1 %collective-permute-start.12 = (f32[2,128,512]{2,1,0:T(8,128)}, f32[2,128,512]{2,1,0:T(8,128)S(1)}, u32[]{:S(2)}, u32[]{:S(2)}) collective-permute-start(f32[2,128,512]{2,1,0:T(8,128)} %fusion.58), channel_id=1, source_target_pairs={{1,2},{3,4},{5,6},{7,8},{9,10},{11,12},{13,14},{15,16},{17,18},{19... | collective-permute-start | bytes 1572872 | tf_op jit(solution)/shard_map/ppermute | solution.py:21
  215.6 6.2 %collective-permute-done.12 = f32[2,128,512]{2,1,0:T(8,128)S(1)} collective-permute-done((f32[2,128,512]{2,1,0:T(8,128)}, f32[2,128,512]{2,1,0:T(8,128)S(1)}, u32[]{:S(2)}, u32[]{:S(2)}) %collective-permute-start.12) | collective-permute-done | bytes 524320 | tf_op jit(solution)/shard_map/ppermute | solution.py:21
  222.0 3.7 %fusion.250 = f32[4,128,512]{2,1,0:T(8,128)S(1)} fusion(f32[4,128,512]{2,1,0:T(8,128)S(1)} %fusion.254, f32[2,128,512]{2,1,0:T(8,128)S(1)} %get-tuple-element.72, f32[2,128,512]{2,1,0:T(8,128)} %fusion.58, f32[2,128,512]{2,1,0:T(8,128)S(1)} %get-tuple-element.71, f32[]{:T(128)} %bitcast.70, f32[]{:T(128)} %bitcast.69, f32[]{:T(128)} %bitcast.65), kind=kLoop, calls=%fused_computation.289 | loop fusion | flops 2621440 | bytes 3670028 | tf_op jit(solution)/shard_map/mul | solution.py:108
  225.7 2.4 fusion.317
  228.2 2.6 fusion.289
  232.9 5.1 %collective-permute-start.14 = (f32[2,128,512]{2,1,0:T(8,128)}, f32[2,128,512]{2,1,0:T(8,128)S(1)}, u32[]{:S(2)}, u32[]{:S(2)}) collective-permute-start(f32[2,128,512]{2,1,0:T(8,128)} %fusion.68), channel_id=1, source_target_pairs={{1,2},{3,4},{5,6},{7,8},{9,10},{11,12},{13,14},{15,16},{17,18},{19... | collective-permute-start | bytes 1572872 | tf_op jit(solution)/shard_map/ppermute | solution.py:21
  238.8 6.9 %collective-permute-done.14 = f32[2,128,512]{2,1,0:T(8,128)S(1)} collective-permute-done((f32[2,128,512]{2,1,0:T(8,128)}, f32[2,128,512]{2,1,0:T(8,128)S(1)}, u32[]{:S(2)}, u32[]{:S(2)}) %collective-permute-start.14) | collective-permute-done | bytes 524320 | tf_op jit(solution)/shard_map/ppermute | solution.py:21
  245.8 3.8 %fusion.246 = f32[4,128,512]{2,1,0:T(8,128)S(1)} fusion(f32[4,128,512]{2,1,0:T(8,128)S(1)} %fusion.250, f32[2,128,512]{2,1,0:T(8,128)S(1)} %get-tuple-element.70, f32[2,128,512]{2,1,0:T(8,128)} %fusion.68, f32[2,128,512]{2,1,0:T(8,128)S(1)} %get-tuple-element.69, f32[]{:T(128)} %bitcast.80, f32[]{:T(128)} %bitcast.79, f32[]{:T(128)} %bitcast.75), kind=kLoop, calls=%fused_computation.283 | loop fusion | flops 2621440 | bytes 3670028 | tf_op jit(solution)/shard_map/mul | solution.py:108
  249.8 2.3 fusion.308
  252.1 2.7 fusion.292
  256.2 5.1 %collective-permute-start.16 = (f32[2,128,512]{2,1,0:T(8,128)S(1)}, f32[2,128,512]{2,1,0:T(8,128)S(1)}, u32[]{:S(2)}, u32[]{:S(2)}) collective-permute-start(f32[2,128,512]{2,1,0:T(8,128)S(1)} %fusion.78), channel_id=1, source_target_pairs={{1,2},{3,4},{5,6},{7,8},{9,10},{11,12},{13,14},{15,16},{17,18},{19... | collective-permute-start | bytes 1572872 | tf_op jit(solution)/shard_map/ppermute | solution.py:21
  262.1 6.8 %collective-permute-done.16 = f32[2,128,512]{2,1,0:T(8,128)S(1)} collective-permute-done((f32[2,128,512]{2,1,0:T(8,128)S(1)}, f32[2,128,512]{2,1,0:T(8,128)S(1)}, u32[]{:S(2)}, u32[]{:S(2)}) %collective-permute-start.16) | collective-permute-done | bytes 524320 | tf_op jit(solution)/shard_map/ppermute | solution.py:21
  269.0 2.2 fusion.242
  (242 shorter events, 36.5 us)
Async XLA Ops:
  6.5 25.5 %copy-start.72 = (s32[2]{0:T(128)S(1)}, s32[2]{0:T(128)}, u32[]{:S(2)}) copy-start(s32[2]{0:T(128)} %param.13) | copy-start | bytes 28
  6.5 82.0 %all-gather.2.cloned.1.call-start = ((), (), s32[]{:S(2)}) async-start(), calls=%async_computation | async-start | bytes 4718592 | tf_op jit(solution)/shard_map/all_gather | solution.py:65
  9.2 48.7 %collective-permute-start = (f32[1,128,512]{2,1,0:T(8,128)}, f32[1,128,512]{2,1,0:T(8,128)}, u32[]{:S(2)}, u32[]{:S(2)}) collective-permute-start(f32[1,128,512]{2,1,0:T(8,128)} %get-tuple-element.85), channel_id=1, source_target_pairs={{0,1},{2,3},{4,5},{6,7},{8,9},{10,11},{12,13},{14,15},{16,17},{18,... | collective-permute-start | bytes 786440 | tf_op jit(solution)/shard_map/ppermute | solution.py:20
  9.2 48.7 %collective-permute-start.1 = (f32[1,128,512]{2,1,0:T(8,128)}, f32[1,128,512]{2,1,0:T(8,128)}, u32[]{:S(2)}, u32[]{:S(2)}) collective-permute-start(f32[1,128,512]{2,1,0:T(8,128)} %get-tuple-element.86), channel_id=1, source_target_pairs={{1,2},{3,4},{5,6},{7,8},{9,10},{11,12},{13,14},{15,16},{17,18},{19... | collective-permute-start | bytes 786440 | tf_op jit(solution)/shard_map/ppermute | solution.py:21
  33.1 9.2 %copy-start.69 = (f32[8,3]{0,1:T(4,128)S(1)}, f32[8,3]{0,1:T(4,128)}, u32[]{:S(2)}) copy-start(f32[8,3]{0,1:T(4,128)} %param.11) | copy-start | bytes 292
  50.0 4.2 %copy-start.19 = (f32[1,2,128,144]{2,0,3,1:T(1,128)}, f32[1,2,128,144]{2,0,3,1:T(1,128)S(1)}, u32[]{:S(2)}) copy-start(f32[1,2,128,144]{2,0,3,1:T(1,128)S(1)} %get-tuple-element.57) | copy-start | bytes 442372
  54.2 4.8 %copy-start = (f32[2,128,512]{2,1,0:T(8,128)S(1)}, f32[2,128,512]{2,1,0:T(8,128)}, u32[]{:S(2)}) copy-start(f32[2,128,512]{2,1,0:T(8,128)} %param.7) | copy-start | bytes 1572868
  55.8 43.1 %copy-start.17 = (f32[1,2,128,144]{2,0,3,1:T(1,128)}, f32[1,2,128,144]{2,0,3,1:T(1,128)S(1)}, u32[]{:S(2)}) copy-start(f32[1,2,128,144]{2,0,3,1:T(1,128)S(1)} %get-tuple-element.41) | copy-start | bytes 442372
  55.8 65.7 %copy-start.14 = (f32[1,2,128,144]{2,0,3,1:T(1,128)}, f32[1,2,128,144]{2,0,3,1:T(1,128)S(1)}, u32[]{:S(2)}) copy-start(f32[1,2,128,144]{2,0,3,1:T(1,128)S(1)} %get-tuple-element.40) | copy-start | bytes 442372
  55.8 32.8 %copy-start.20 = (f32[1,2,128,144]{2,0,3,1:T(1,128)S(1)}, f32[1,2,128,144]{2,0,3,1:T(1,128)}, u32[]{:S(2)}) copy-start(f32[1,2,128,144]{2,0,3,1:T(1,128)} %copy-done.19) | copy-start | bytes 442372
  55.8 32.8 %copy-start.48 = (f32[2,128,136]{1,2,0:T(8,128)S(1)}, f32[2,128,136]{1,2,0:T(8,128)}, u32[]{:S(2)}) copy-start(f32[2,128,136]{1,2,0:T(8,128)} %get-tuple-element.117) | copy-start | bytes 417796
  55.8 32.8 %copy-start.49 = (f32[2,128,136]{1,2,0:T(8,128)S(1)}, f32[2,128,136]{1,2,0:T(8,128)}, u32[]{:S(2)}) copy-start(f32[2,128,136]{1,2,0:T(8,128)} %get-tuple-element.118) | copy-start | bytes 417796
  91.8 7.1 %copy-start.16 = (f32[1,2,128,144]{2,0,3,1:T(1,128)S(1)}, f32[1,2,128,144]{2,0,3,1:T(1,128)}, u32[]{:S(2)}) copy-start(f32[1,2,128,144]{2,0,3,1:T(1,128)} %get-tuple-element.56) | copy-start | bytes 442372
  92.8 12.6 %collective-permute-start.2 = (f32[2,128,512]{2,1,0:T(8,128)S(1)}, f32[2,128,512]{2,1,0:T(8,128)S(1)}, u32[]{:S(2)}, u32[]{:S(2)}) collective-permute-start(f32[2,128,512]{2,1,0:T(8,128)S(1)} %fusion.8), channel_id=1, source_target_pairs={{1,2},{3,4},{5,6},{7,8},{9,10},{11,12},{13,14},{15,16},{17,18},{19... | collective-permute-start | bytes 1572872 | tf_op jit(solution)/shard_map/ppermute | solution.py:21
  98.0 7.5 %collective-permute-start.3 = (f32[2,128,512]{2,1,0:T(8,128)S(1)}, f32[2,128,512]{2,1,0:T(8,128)S(1)}, u32[]{:S(2)}, u32[]{:S(2)}) collective-permute-start(f32[2,128,512]{2,1,0:T(8,128)S(1)} %fusion.8), channel_id=1, source_target_pairs={{0,1},{2,3},{4,5},{6,7},{8,9},{10,11},{12,13},{14,15},{16,17},{18,... | collective-permute-start | bytes 1572872 | tf_op jit(solution)/shard_map/ppermute | solution.py:20
  105.6 4.6 %copy-start.41 = (f32[2,128,256]{1,2,0:T(8,128)S(1)}, f32[2,128,256]{1,2,0:T(8,128)}, u32[]{:S(2)}) copy-start(f32[2,128,256]{1,2,0:T(8,128)} %copy-done.40) | copy-start | bytes 786436
  105.6 4.6 %copy-start.53 = (f32[2,128,128]{1,2,0:T(8,128)S(1)}, f32[2,128,128]{1,2,0:T(8,128)}, u32[]{:S(2)}) copy-start(f32[2,128,128]{1,2,0:T(8,128)} %copy-done.52) | copy-start | bytes 393220
  105.6 4.6 %copy-start.61 = (f32[2,128,120]{1,2,0:T(8,128)S(1)}, f32[2,128,120]{1,2,0:T(8,128)}, u32[]{:S(2)}) copy-start(f32[2,128,120]{1,2,0:T(8,128)} %copy-done.60) | copy-start | bytes 368644
  113.3 6.9 %copy-start.70 = (f32[1,3]{0,1:T(4,128)S(1)}, f32[1,3]{0,1:T(4,128)}, u32[]{:S(2)}) copy-start(f32[1,3]{0,1:T(4,128)} %get-tuple-element.128) | copy-start | bytes 40
  113.3 6.9 %copy-start.71 = (f32[1,3]{0,1:T(4,128)S(1)}, f32[1,3]{0,1:T(4,128)}, u32[]{:S(2)}) copy-start(f32[1,3]{0,1:T(4,128)} %get-tuple-element.129) | copy-start | bytes 40
  113.3 8.2 %copy-start.13 = (f32[1,2,128,144]{2,0,3,1:T(1,128)S(1)}, f32[1,2,128,144]{2,0,3,1:T(1,128)}, u32[]{:S(2)}) copy-start(f32[1,2,128,144]{2,0,3,1:T(1,128)} %get-tuple-element.55) | copy-start | bytes 442372
  114.9 12.8 %collective-permute-start.4 = (f32[2,128,512]{2,1,0:T(8,128)}, f32[2,128,512]{2,1,0:T(8,128)S(1)}, u32[]{:S(2)}, u32[]{:S(2)}) collective-permute-start(f32[2,128,512]{2,1,0:T(8,128)} %fusion.18), channel_id=1, source_target_pairs={{1,2},{3,4},{5,6},{7,8},{9,10},{11,12},{13,14},{15,16},{17,18},{19... | collective-permute-start | bytes 1572872 | tf_op jit(solution)/shard_map/ppermute | solution.py:21
  120.1 7.7 %collective-permute-start.5 = (f32[2,128,512]{2,1,0:T(8,128)}, f32[2,128,512]{2,1,0:T(8,128)}, u32[]{:S(2)}, u32[]{:S(2)}) collective-permute-start(f32[2,128,512]{2,1,0:T(8,128)} %fusion.18), channel_id=1, source_target_pairs={{0,1},{2,3},{4,5},{6,7},{8,9},{10,11},{12,13},{14,15},{16,17},{18,... | collective-permute-start | bytes 1572872 | tf_op jit(solution)/shard_map/ppermute | solution.py:20
  138.5 6.8 %copy-start.11 = (f32[1,2,128,144]{2,0,3,1:T(1,128)S(1)}, f32[1,2,128,144]{2,0,3,1:T(1,128)}, u32[]{:S(2)}) copy-start(f32[1,2,128,144]{2,0,3,1:T(1,128)} %get-tuple-element.54) | copy-start | bytes 442372
  138.5 6.8 %copy-start.12 = (f32[1,2,128,144]{2,0,3,1:T(1,128)S(1)}, f32[1,2,128,144]{2,0,3,1:T(1,128)}, u32[]{:S(2)}) copy-start(f32[1,2,128,144]{2,0,3,1:T(1,128)} %get-tuple-element.39) | copy-start | bytes 442372
  139.4 12.6 %copy-start.36 = (f32[2,128,512]{2,1,0:T(8,128)}, f32[2,128,512]{2,1,0:T(8,128)S(1)}, u32[]{:S(2)}) copy-start(f32[2,128,512]{2,1,0:T(8,128)S(1)} %fusion.28) | copy-start | bytes 1572868
  139.4 12.6 %collective-permute-start.6 = (f32[2,128,512]{2,1,0:T(8,128)S(1)}, f32[2,128,512]{2,1,0:T(8,128)S(1)}, u32[]{:S(2)}, u32[]{:S(2)}) collective-permute-start(f32[2,128,512]{2,1,0:T(8,128)S(1)} %fusion.28), channel_id=1, source_target_pairs={{1,2},{3,4},{5,6},{7,8},{9,10},{11,12},{13,14},{15,16},{17,18},{19... | collective-permute-start | bytes 1572872 | tf_op jit(solution)/shard_map/ppermute | solution.py:21
  144.6 7.5 %collective-permute-start.7 = (f32[2,128,512]{2,1,0:T(8,128)S(1)}, f32[2,128,512]{2,1,0:T(8,128)S(1)}, u32[]{:S(2)}, u32[]{:S(2)}) collective-permute-start(f32[2,128,512]{2,1,0:T(8,128)S(1)} %fusion.28), channel_id=1, source_target_pairs={{0,1},{2,3},{4,5},{6,7},{8,9},{10,11},{12,13},{14,15},{16,17},{18,... | collective-permute-start | bytes 1572872 | tf_op jit(solution)/shard_map/ppermute | solution.py:20
  161.0 8.1 %copy-start.8 = (f32[1,2,128,144]{2,0,3,1:T(1,128)S(1)}, f32[1,2,128,144]{2,0,3,1:T(1,128)}, u32[]{:S(2)}) copy-start(f32[1,2,128,144]{2,0,3,1:T(1,128)} %get-tuple-element.53) | copy-start | bytes 442372
  161.0 8.1 %copy-start.9 = (f32[1,2,128,144]{2,0,3,1:T(1,128)S(1)}, f32[1,2,128,144]{2,0,3,1:T(1,128)}, u32[]{:S(2)}) copy-start(f32[1,2,128,144]{2,0,3,1:T(1,128)} %get-tuple-element.38) | copy-start | bytes 442372
  162.6 12.8 %collective-permute-start.8 = (f32[2,128,512]{2,1,0:T(8,128)}, f32[2,128,512]{2,1,0:T(8,128)S(1)}, u32[]{:S(2)}, u32[]{:S(2)}) collective-permute-start(f32[2,128,512]{2,1,0:T(8,128)} %fusion.38), channel_id=1, source_target_pairs={{1,2},{3,4},{5,6},{7,8},{9,10},{11,12},{13,14},{15,16},{17,18},{19... | collective-permute-start | bytes 1572872 | tf_op jit(solution)/shard_map/ppermute | solution.py:21
  167.8 7.7 %collective-permute-start.9 = (f32[2,128,512]{2,1,0:T(8,128)}, f32[2,128,512]{2,1,0:T(8,128)S(1)}, u32[]{:S(2)}, u32[]{:S(2)}) collective-permute-start(f32[2,128,512]{2,1,0:T(8,128)} %fusion.38), channel_id=1, source_target_pairs={{0,1},{2,3},{4,5},{6,7},{8,9},{10,11},{12,13},{14,15},{16,17},{18,... | collective-permute-start | bytes 1572872 | tf_op jit(solution)/shard_map/ppermute | solution.py:20
  184.9 7.1 %copy-start.6 = (f32[1,2,128,144]{2,0,3,1:T(1,128)S(1)}, f32[1,2,128,144]{2,0,3,1:T(1,128)}, u32[]{:S(2)}) copy-start(f32[1,2,128,144]{2,0,3,1:T(1,128)} %get-tuple-element.52) | copy-start | bytes 442372
  185.0 7.2 %copy-start.7 = (f32[1,2,128,144]{2,0,3,1:T(1,128)S(1)}, f32[1,2,128,144]{2,0,3,1:T(1,128)}, u32[]{:S(2)}) copy-start(f32[1,2,128,144]{2,0,3,1:T(1,128)} %get-tuple-element.37) | copy-start | bytes 442372
  185.9 12.6 %copy-start.38 = (f32[2,128,512]{2,1,0:T(8,128)}, f32[2,128,512]{2,1,0:T(8,128)S(1)}, u32[]{:S(2)}) copy-start(f32[2,128,512]{2,1,0:T(8,128)S(1)} %fusion.48) | copy-start | bytes 1572868
  186.0 12.6 %collective-permute-start.10 = (f32[2,128,512]{2,1,0:T(8,128)S(1)}, f32[2,128,512]{2,1,0:T(8,128)S(1)}, u32[]{:S(2)}, u32[]{:S(2)}) collective-permute-start(f32[2,128,512]{2,1,0:T(8,128)S(1)} %fusion.48), channel_id=1, source_target_pairs={{1,2},{3,4},{5,6},{7,8},{9,10},{11,12},{13,14},{15,16},{17,18},{19... | collective-permute-start | bytes 1572872 | tf_op jit(solution)/shard_map/ppermute | solution.py:21
  191.1 7.5 %collective-permute-start.11 = (f32[2,128,512]{2,1,0:T(8,128)S(1)}, f32[2,128,512]{2,1,0:T(8,128)S(1)}, u32[]{:S(2)}, u32[]{:S(2)}) collective-permute-start(f32[2,128,512]{2,1,0:T(8,128)S(1)} %fusion.48), channel_id=1, source_target_pairs={{0,1},{2,3},{4,5},{6,7},{8,9},{10,11},{12,13},{14,15},{16,17},{18,... | collective-permute-start | bytes 1572872 | tf_op jit(solution)/shard_map/ppermute | solution.py:20
  207.3 8.2 %copy-start.4 = (f32[1,2,128,144]{2,0,3,1:T(1,128)S(1)}, f32[1,2,128,144]{2,0,3,1:T(1,128)}, u32[]{:S(2)}) copy-start(f32[1,2,128,144]{2,0,3,1:T(1,128)} %get-tuple-element.58) | copy-start | bytes 442372
  207.3 8.2 %copy-start.5 = (f32[1,2,128,144]{2,0,3,1:T(1,128)S(1)}, f32[1,2,128,144]{2,0,3,1:T(1,128)}, u32[]{:S(2)}) copy-start(f32[1,2,128,144]{2,0,3,1:T(1,128)} %get-tuple-element.36) | copy-start | bytes 442372
  209.0 12.8 %collective-permute-start.12 = (f32[2,128,512]{2,1,0:T(8,128)}, f32[2,128,512]{2,1,0:T(8,128)S(1)}, u32[]{:S(2)}, u32[]{:S(2)}) collective-permute-start(f32[2,128,512]{2,1,0:T(8,128)} %fusion.58), channel_id=1, source_target_pairs={{1,2},{3,4},{5,6},{7,8},{9,10},{11,12},{13,14},{15,16},{17,18},{19... | collective-permute-start | bytes 1572872 | tf_op jit(solution)/shard_map/ppermute | solution.py:21
  214.2 7.7 %collective-permute-start.13 = (f32[2,128,512]{2,1,0:T(8,128)}, f32[2,128,512]{2,1,0:T(8,128)S(1)}, u32[]{:S(2)}, u32[]{:S(2)}) collective-permute-start(f32[2,128,512]{2,1,0:T(8,128)} %fusion.58), channel_id=1, source_target_pairs={{0,1},{2,3},{4,5},{6,7},{8,9},{10,11},{12,13},{14,15},{16,17},{18,... | collective-permute-start | bytes 1572872 | tf_op jit(solution)/shard_map/ppermute | solution.py:20
  231.2 7.5 %copy-start.2 = (f32[1,2,128,144]{2,0,3,1:T(1,128)S(1)}, f32[1,2,128,144]{2,0,3,1:T(1,128)}, u32[]{:S(2)}) copy-start(f32[1,2,128,144]{2,0,3,1:T(1,128)} %get-tuple-element.51) | copy-start | bytes 442372
  231.2 7.6 %copy-start.3 = (f32[1,2,128,144]{2,0,3,1:T(1,128)S(1)}, f32[1,2,128,144]{2,0,3,1:T(1,128)}, u32[]{:S(2)}) copy-start(f32[1,2,128,144]{2,0,3,1:T(1,128)} %get-tuple-element.35) | copy-start | bytes 442372
  232.9 12.8 %collective-permute-start.14 = (f32[2,128,512]{2,1,0:T(8,128)}, f32[2,128,512]{2,1,0:T(8,128)S(1)}, u32[]{:S(2)}, u32[]{:S(2)}) collective-permute-start(f32[2,128,512]{2,1,0:T(8,128)} %fusion.68), channel_id=1, source_target_pairs={{1,2},{3,4},{5,6},{7,8},{9,10},{11,12},{13,14},{15,16},{17,18},{19... | collective-permute-start | bytes 1572872 | tf_op jit(solution)/shard_map/ppermute | solution.py:21
  238.0 7.7 %collective-permute-start.15 = (f32[2,128,512]{2,1,0:T(8,128)}, f32[2,128,512]{2,1,0:T(8,128)S(1)}, u32[]{:S(2)}, u32[]{:S(2)}) collective-permute-start(f32[2,128,512]{2,1,0:T(8,128)} %fusion.68), channel_id=1, source_target_pairs={{0,1},{2,3},{4,5},{6,7},{8,9},{10,11},{12,13},{14,15},{16,17},{18,... | collective-permute-start | bytes 1572872 | tf_op jit(solution)/shard_map/ppermute | solution.py:20
  245.8 4.0 %copy-start.22 = (f32[1,2,128,144]{2,0,3,1:T(1,128)S(1)}, f32[1,2,128,144]{2,0,3,1:T(1,128)}, u32[]{:S(2)}) copy-start(f32[1,2,128,144]{2,0,3,1:T(1,128)} %get-tuple-element.59) | copy-start | bytes 442372
  256.2 12.6 %collective-permute-start.16 = (f32[2,128,512]{2,1,0:T(8,128)S(1)}, f32[2,128,512]{2,1,0:T(8,128)S(1)}, u32[]{:S(2)}, u32[]{:S(2)}) collective-permute-start(f32[2,128,512]{2,1,0:T(8,128)S(1)} %fusion.78), channel_id=1, source_target_pairs={{1,2},{3,4},{5,6},{7,8},{9,10},{11,12},{13,14},{15,16},{17,18},{19... | collective-permute-start | bytes 1572872 | tf_op jit(solution)/shard_map/ppermute | solution.py:21
  261.4 7.5 %collective-permute-start.17 = (f32[2,128,512]{2,1,0:T(8,128)S(1)}, f32[2,128,512]{2,1,0:T(8,128)S(1)}, u32[]{:S(2)}, u32[]{:S(2)}) collective-permute-start(f32[2,128,512]{2,1,0:T(8,128)S(1)} %fusion.78), channel_id=1, source_target_pairs={{0,1},{2,3},{4,5},{6,7},{8,9},{10,11},{12,13},{14,15},{16,17},{18,... | collective-permute-start | bytes 1572872 | tf_op jit(solution)/shard_map/ppermute | solution.py:20
  (44 other events, 120.6 us)
Sparse Core Ops, SparseCore 0:
  10.0 78.4 all-gather.1

commit v8 on v6

--- a/solution.py
+++ b/solution.py
@@ -96,6 +96,7 @@
         c = kz[0] * padded[0:count]
         for k in range(1, 3):
             c = c + kz[k] * padded[k : k + count]
+        c = lax.optimization_barrier(c)
         t = jnp.einsum("lij,ljx->lix", by, c, precision=blur_mode)
         blurred = jnp.einsum("lix,lax->lia", t, bx_all[position], precision=blur_mode)
         quotient = data / (blurred + offset)

time: 264 us -> 265 us (level)
  other arithmetic: 28.5 us -> 44.4 us
  matrix products: 50.3 us -> 35.1 us
    add x0 -> x8, other arithmetic: none -> 15.8 us  [per_device(): c = c + kz[k] * padded[k:k + count]]
    dot_general x8, matrix products: 18.5 us -> 3.34 us  [per_device(): t = jnp.einsum('lij,ljx->lix', by, c, precision=blur_mode)]
where the time goes in v8:
time: 265 us; the launch traced here: 263 us
  waiting for transfers between devices  79.6 us (30%)
  starting transfers between devices  50.2 us (19%)
  other arithmetic  44.4 us (17%)
  between operations  35.2 us (13%)
  matrix products  35.1 us (13%)
  local copies, waits for them, and re-layouts  18.5 us (7%)
    ppermute x9, waiting for transfers between devices, halo(): outer_got = lax.ppermute(jnp.where(odd, top, bottom), axis, outer)  51.3 us
    ppermute x9, starting transfers between devices, halo(): outer_got = lax.ppermute(jnp.where(odd, top, bottom), axis, outer)  49 us
    all_gather x1, waiting for transfers between devices, per_device(): data_all = lax.all_gather(view_data[0], 'view', axis=0)  27.6 us
    mul x7, other arithmetic, per_device(): padded = padded * corr  16.1 us
    add x8, other arithmetic, per_device(): c = c + kz[k] * padded[k:k + count]  15.8 us
    dot_general x8, matrix products, per_device(): jnp.einsum('lix,lax->lia', t, bx_all[position], precision=blur_mode)  14.1 us
    dot_general x8, matrix products, per_device(): g = jnp.einsum('lix,lax->lia', u, bxr_all[position], precision=blur_mode)  8.43 us
    slice x1, local copies, waits for them, and re-layouts, per_device(): bx_all = [band_matrix(mats[2][p], nx, reach) for p in range(view_count)]  6.37 us
  transfers between devices with their start and end apart: 19, of which 9 were waited for; matrix products, arithmetic and copies ran while one was open for 12% of the time, Pallas kernels for 0%

profile of v8, /device:TPU:2, one launch (start us, length us, event | category | flops | bytes accessed | tf_op | source)
XLA Modules:
  0.0 263.1 jit_solution(9368600855704168924)
XLA Ops:
  7.3 1.9 slice_select_fusion.1
  9.2 7.8 %collective-permute-start.1 = (f32[1,128,512]{2,1,0:T(8,128)}, f32[1,128,512]{2,1,0:T(8,128)}, u32[]{:S(2)}, u32[]{:S(2)}) collective-permute-start(f32[1,128,512]{2,1,0:T(8,128)} %get-tuple-element.56), channel_id=1, source_target_pairs={{1,2},{3,4},{5,6},{7,8},{9,10},{11,12},{13,14},{15,16},{17,18},{19... | collective-permute-start | bytes 786440 | tf_op jit(solution)/shard_map/ppermute | solution.py:21
  33.6 1.8 fusion.209
  36.3 1.6 fusion.207
  43.7 6.4 %fusion.387 = (f32[1,2,128,144]{2,0,3,1:T(1,128)}, f32[1,2,128,144]{2,0,3,1:T(1,128)}, f32[1,2,128,144]{2,0,3,1:T(1,128)}, f32[1,2,128,144]{2,0,3,1:T(1,128)}, f...) fusion(f32[8,2,128,144]{2,0,3,1:T(8,128)} %fusion.209), kind=kLoop, calls=%fused_computation.486 | loop fusion | bytes 2359296 | tf_op jit(solution)/shard_map/slice | solution.py:86
  50.8 1.7 fusion.388
  52.6 1.7 fusion.386
  58.5 2.0 fusion.318
  61.0 27.6 %all-gather.2.cloned.1.call-done = f32[8,2,128,512]{3,2,1,0:T(8,128)} async-done(((f32[1,2,128,512]{3,2,1,0:T(8,128)}), f32[8,2,128,512]{3,2,1,0:T(8,128)}) %all-gather.2.cloned.1.call-update) | async-done | bytes 4194320 | tf_op jit(solution)/shard_map/all_gather | solution.py:65
  88.6 2.5 fusion.267
  92.5 5.1 %collective-permute-start.2 = (f32[2,128,512]{2,1,0:T(8,128)S(1)}, f32[2,128,512]{2,1,0:T(8,128)S(1)}, u32[]{:S(2)}, u32[]{:S(2)}) collective-permute-start(f32[2,128,512]{2,1,0:T(8,128)S(1)} %fusion.8), channel_id=1, source_target_pairs={{1,2},{3,4},{5,6},{7,8},{9,10},{11,12},{13,14},{15,16},{17,18},{19... | collective-permute-start | bytes 1572872 | tf_op jit(solution)/shard_map/ppermute | solution.py:21
  98.0 7.1 %collective-permute-done.2 = f32[2,128,512]{2,1,0:T(8,128)S(1)} collective-permute-done((f32[2,128,512]{2,1,0:T(8,128)S(1)}, f32[2,128,512]{2,1,0:T(8,128)S(1)}, u32[]{:S(2)}, u32[]{:S(2)}) %collective-permute-start.2) | collective-permute-done | bytes 524320 | tf_op jit(solution)/shard_map/ppermute | solution.py:21
  105.3 2.8 %fusion.266 = f32[4,128,512]{2,1,0:T(8,128)S(1)} fusion(f32[2,128,512]{2,1,0:T(8,128)S(1)} %get-tuple-element.52, f32[2,128,512]{2,1,0:T(8,128)S(1)} %fusion.8, f32[2,128,512]{2,1,0:T(8,128)S(1)} %get-tuple-element.51, f32[1,128,512]{2,1,0:T(8,128)S(1)} %get-tuple-element.54, f32[2,128,512]{2,1,0:T(8,128)S(1)} %copy-done.6, ...), kind=kLoop, calls=%fused_computation.313 | loop fusion | flops 3145728 | bytes 3670028 | tf_op jit(solution)/shard_map/mul | solution.py:109
  108.1 2.0 fusion.315
  110.6 1.6 fusion.270
  113.7 5.1 %collective-permute-start.4 = (f32[2,128,512]{2,1,0:T(8,128)S(1)}, f32[2,128,512]{2,1,0:T(8,128)S(1)}, u32[]{:S(2)}, u32[]{:S(2)}) collective-permute-start(f32[2,128,512]{2,1,0:T(8,128)S(1)} %fusion.18), channel_id=1, source_target_pairs={{1,2},{3,4},{5,6},{7,8},{9,10},{11,12},{13,14},{15,16},{17,18},{19... | collective-permute-start | bytes 1572872 | tf_op jit(solution)/shard_map/ppermute | solution.py:21
  119.6 6.7 %collective-permute-done.4 = f32[2,128,512]{2,1,0:T(8,128)S(1)} collective-permute-done((f32[2,128,512]{2,1,0:T(8,128)S(1)}, f32[2,128,512]{2,1,0:T(8,128)S(1)}, u32[]{:S(2)}, u32[]{:S(2)}) %collective-permute-start.4) | collective-permute-done | bytes 524320 | tf_op jit(solution)/shard_map/ppermute | solution.py:21
  126.4 2.2 fusion.262
  128.6 1.9 fusion.313
  130.9 1.6 fusion.273
  134.0 5.1 %collective-permute-start.6 = (f32[2,128,512]{2,1,0:T(8,128)S(1)}, f32[2,128,512]{2,1,0:T(8,128)S(1)}, u32[]{:S(2)}, u32[]{:S(2)}) collective-permute-start(f32[2,128,512]{2,1,0:T(8,128)S(1)} %fusion.28), channel_id=1, source_target_pairs={{1,2},{3,4},{5,6},{7,8},{9,10},{11,12},{13,14},{15,16},{17,18},{19... | collective-permute-start | bytes 1572872 | tf_op jit(solution)/shard_map/ppermute | solution.py:21
  139.3 7.3 %collective-permute-done.6 = f32[2,128,512]{2,1,0:T(8,128)S(1)} collective-permute-done((f32[2,128,512]{2,1,0:T(8,128)S(1)}, f32[2,128,512]{2,1,0:T(8,128)S(1)}, u32[]{:S(2)}, u32[]{:S(2)}) %collective-permute-start.6) | collective-permute-done | bytes 524320 | tf_op jit(solution)/shard_map/ppermute | solution.py:21
  146.7 2.1 fusion.258
  148.8 2.1 fusion.311
  151.4 1.7 fusion.276
  154.5 5.1 %collective-permute-start.8 = (f32[2,128,512]{2,1,0:T(8,128)S(1)}, f32[2,128,512]{2,1,0:T(8,128)S(1)}, u32[]{:S(2)}, u32[]{:S(2)}) collective-permute-start(f32[2,128,512]{2,1,0:T(8,128)S(1)} %fusion.38), channel_id=1, source_target_pairs={{1,2},{3,4},{5,6},{7,8},{9,10},{11,12},{13,14},{15,16},{17,18},{19... | collective-permute-start | bytes 1572872 | tf_op jit(solution)/shard_map/ppermute | solution.py:21
  160.4 6.7 %collective-permute-done.8 = f32[2,128,512]{2,1,0:T(8,128)S(1)} collective-permute-done((f32[2,128,512]{2,1,0:T(8,128)S(1)}, f32[2,128,512]{2,1,0:T(8,128)S(1)}, u32[]{:S(2)}, u32[]{:S(2)}) %collective-permute-start.8) | collective-permute-done | bytes 524320 | tf_op jit(solution)/shard_map/ppermute | solution.py:21
  167.2 2.3 fusion.254
  169.5 1.9 fusion.309
  171.9 1.6 fusion.279
  175.0 5.1 %collective-permute-start.10 = (f32[2,128,512]{2,1,0:T(8,128)S(1)}, f32[2,128,512]{2,1,0:T(8,128)S(1)}, u32[]{:S(2)}, u32[]{:S(2)}) collective-permute-start(f32[2,128,512]{2,1,0:T(8,128)S(1)} %fusion.48), channel_id=1, source_target_pairs={{1,2},{3,4},{5,6},{7,8},{9,10},{11,12},{13,14},{15,16},{17,18},{19... | collective-permute-start | bytes 1572872 | tf_op jit(solution)/shard_map/ppermute | solution.py:21
  180.5 7.1 %collective-permute-done.10 = f32[2,128,512]{2,1,0:T(8,128)S(1)} collective-permute-done((f32[2,128,512]{2,1,0:T(8,128)S(1)}, f32[2,128,512]{2,1,0:T(8,128)S(1)}, u32[]{:S(2)}, u32[]{:S(2)}) %collective-permute-start.10) | collective-permute-done | bytes 524320 | tf_op jit(solution)/shard_map/ppermute | solution.py:21
  187.7 2.2 fusion.250
  189.9 2.0 fusion.307
  192.3 1.7 fusion.282
  195.4 5.1 %collective-permute-start.12 = (f32[2,128,512]{2,1,0:T(8,128)S(1)}, f32[2,128,512]{2,1,0:T(8,128)S(1)}, u32[]{:S(2)}, u32[]{:S(2)}) collective-permute-start(f32[2,128,512]{2,1,0:T(8,128)S(1)} %fusion.58), channel_id=1, source_target_pairs={{1,2},{3,4},{5,6},{7,8},{9,10},{11,12},{13,14},{15,16},{17,18},{19... | collective-permute-start | bytes 1572872 | tf_op jit(solution)/shard_map/ppermute | solution.py:21
  201.3 6.7 %collective-permute-done.12 = f32[2,128,512]{2,1,0:T(8,128)S(1)} collective-permute-done((f32[2,128,512]{2,1,0:T(8,128)S(1)}, f32[2,128,512]{2,1,0:T(8,128)S(1)}, u32[]{:S(2)}, u32[]{:S(2)}) %collective-permute-start.12) | collective-permute-done | bytes 524320 | tf_op jit(solution)/shard_map/ppermute | solution.py:21
  208.2 2.2 fusion.246
  210.4 2.0 fusion.305
  215.9 5.1 %collective-permute-start.14 = (f32[2,128,512]{2,1,0:T(8,128)S(1)}, f32[2,128,512]{2,1,0:T(8,128)S(1)}, u32[]{:S(2)}, u32[]{:S(2)}) collective-permute-start(f32[2,128,512]{2,1,0:T(8,128)S(1)} %fusion.68), channel_id=1, source_target_pairs={{1,2},{3,4},{5,6},{7,8},{9,10},{11,12},{13,14},{15,16},{17,18},{19... | collective-permute-start | bytes 1572872 | tf_op jit(solution)/shard_map/ppermute | solution.py:21
  221.2 7.3 %collective-permute-done.14 = f32[2,128,512]{2,1,0:T(8,128)S(1)} collective-permute-done((f32[2,128,512]{2,1,0:T(8,128)S(1)}, f32[2,128,512]{2,1,0:T(8,128)S(1)}, u32[]{:S(2)}, u32[]{:S(2)}) %collective-permute-start.14) | collective-permute-done | bytes 524320 | tf_op jit(solution)/shard_map/ppermute | solution.py:21
  228.7 2.2 fusion.242
  230.9 2.0 fusion.303
  233.3 1.7 fusion.288
  235.5 1.7 fusion.78
  237.1 5.1 %collective-permute-start.16 = (f32[2,128,512]{2,1,0:T(8,128)}, f32[2,128,512]{2,1,0:T(8,128)}, u32[]{:S(2)}, u32[]{:S(2)}) collective-permute-start(f32[2,128,512]{2,1,0:T(8,128)} %fusion.78), channel_id=1, source_target_pairs={{1,2},{3,4},{5,6},{7,8},{9,10},{11,12},{13,14},{15,16},{17,18},{19... | collective-permute-start | bytes 1572872 | tf_op jit(solution)/shard_map/ppermute | solution.py:21
  247.5 2.5 collective-permute-done.16
  251.4 4.8 %fusion.299 = f32[1,2,128,512]{3,2,1,0:T(8,128)} fusion(f32[2,128,512]{2,1,0:T(8,128)} %fusion.78, f32[2,128,512]{2,1,0:T(8,128)S(1)} %get-tuple-element.38, f32[2,128,512]{2,1,0:T(8,128)S(1)} %get-tuple-element.37, f32[4,128,512]{2,1,0:T(8,128)} %copy-done.5, f32[4,128,512]{2,1,0:T(8,128)} %copy-done.4, f32[4,128,512]{2,1,0:T(8,128)S(1)} %copy-done.3, ...), kind=kLoop, calls=%fused_computation.346 | loop fusion | flops 2359296 | bytes 5767188 | tf_op jit(solution)/shard_map/broadcast_in_dim | solution.py:111
  (192 shorter events, 34.0 us)
Async XLA Ops:
  6.5 25.9 %copy-start.47 = (s32[2]{0:T(128)S(1)}, s32[2]{0:T(128)}, u32[]{:S(2)}) copy-start(s32[2]{0:T(128)} %param.13) | copy-start | bytes 28
  6.5 82.0 %all-gather.2.cloned.1.call-start = ((), (), s32[]{:S(2)}) async-start(), calls=%async_computation | async-start | bytes 4718592 | tf_op jit(solution)/shard_map/all_gather | solution.py:65
  9.2 48.2 %collective-permute-start = (f32[1,128,512]{2,1,0:T(8,128)}, f32[1,128,512]{2,1,0:T(8,128)}, u32[]{:S(2)}, u32[]{:S(2)}) collective-permute-start(f32[1,128,512]{2,1,0:T(8,128)} %get-tuple-element.55), channel_id=1, source_target_pairs={{0,1},{2,3},{4,5},{6,7},{8,9},{10,11},{12,13},{14,15},{16,17},{18,... | collective-permute-start | bytes 786440 | tf_op jit(solution)/shard_map/ppermute | solution.py:20
  9.2 48.2 %collective-permute-start.1 = (f32[1,128,512]{2,1,0:T(8,128)}, f32[1,128,512]{2,1,0:T(8,128)}, u32[]{:S(2)}, u32[]{:S(2)}) collective-permute-start(f32[1,128,512]{2,1,0:T(8,128)} %get-tuple-element.56), channel_id=1, source_target_pairs={{1,2},{3,4},{5,6},{7,8},{9,10},{11,12},{13,14},{15,16},{17,18},{19... | collective-permute-start | bytes 786440 | tf_op jit(solution)/shard_map/ppermute | solution.py:21
  33.6 9.4 %copy-start.43 = (f32[8,3]{0,1:T(4,128)S(1)}, f32[8,3]{0,1:T(4,128)}, u32[]{:S(2)}) copy-start(f32[8,3]{0,1:T(4,128)} %param.11) | copy-start | bytes 292
  55.9 42.1 %copy-start.22 = (f32[1,2,128,144]{2,0,3,1:T(1,128)}, f32[1,2,128,144]{2,0,3,1:T(1,128)S(1)}, u32[]{:S(2)}) copy-start(f32[1,2,128,144]{2,0,3,1:T(1,128)S(1)} %get-tuple-element.11) | copy-start | bytes 442372
  55.9 83.4 %copy-start.17 = (f32[1,2,128,144]{2,0,3,1:T(1,128)}, f32[1,2,128,144]{2,0,3,1:T(1,128)S(1)}, u32[]{:S(2)}) copy-start(f32[1,2,128,144]{2,0,3,1:T(1,128)S(1)} %get-tuple-element.9) | copy-start | bytes 442372
  57.3 31.3 %copy-start.25 = (f32[1,2,128,144]{2,0,3,1:T(1,128)S(1)}, f32[1,2,128,144]{2,0,3,1:T(1,128)}, u32[]{:S(2)}) copy-start(f32[1,2,128,144]{2,0,3,1:T(1,128)} %copy-done.24) | copy-start | bytes 442372
  57.3 31.3 %copy-start.40 = (f32[2,128,136]{1,2,0:T(8,128)S(1)}, f32[2,128,136]{1,2,0:T(8,128)}, u32[]{:S(2)}) copy-start(f32[2,128,136]{1,2,0:T(8,128)} %get-tuple-element.87) | copy-start | bytes 417796
  57.3 31.3 %copy-start.41 = (f32[2,128,136]{1,2,0:T(8,128)S(1)}, f32[2,128,136]{1,2,0:T(8,128)}, u32[]{:S(2)}) copy-start(f32[2,128,136]{1,2,0:T(8,128)} %get-tuple-element.88) | copy-start | bytes 417796
  91.5 6.4 %copy-start.21 = (f32[1,2,128,144]{2,0,3,1:T(1,128)S(1)}, f32[1,2,128,144]{2,0,3,1:T(1,128)}, u32[]{:S(2)}) copy-start(f32[1,2,128,144]{2,0,3,1:T(1,128)} %get-tuple-element.26) | copy-start | bytes 442372
  92.5 12.6 %collective-permute-start.2 = (f32[2,128,512]{2,1,0:T(8,128)S(1)}, f32[2,128,512]{2,1,0:T(8,128)S(1)}, u32[]{:S(2)}, u32[]{:S(2)}) collective-permute-start(f32[2,128,512]{2,1,0:T(8,128)S(1)} %fusion.8), channel_id=1, source_target_pairs={{1,2},{3,4},{5,6},{7,8},{9,10},{11,12},{13,14},{15,16},{17,18},{19... | collective-permute-start | bytes 1572872 | tf_op jit(solution)/shard_map/ppermute | solution.py:21
  97.7 7.5 %collective-permute-start.3 = (f32[2,128,512]{2,1,0:T(8,128)S(1)}, f32[2,128,512]{2,1,0:T(8,128)S(1)}, u32[]{:S(2)}, u32[]{:S(2)}) collective-permute-start(f32[2,128,512]{2,1,0:T(8,128)S(1)} %fusion.8), channel_id=1, source_target_pairs={{0,1},{2,3},{4,5},{6,7},{8,9},{10,11},{12,13},{14,15},{16,17},{18,... | collective-permute-start | bytes 1572872 | tf_op jit(solution)/shard_map/ppermute | solution.py:20
  105.3 4.8 %copy-start.39 = (f32[1,2,128,144]{2,0,3,1:T(1,128)S(1)}, f32[1,2,128,144]{2,0,3,1:T(1,128)}, u32[]{:S(2)}) copy-start(f32[1,2,128,144]{2,0,3,1:T(1,128)} %get-tuple-element.35) | copy-start | bytes 442372
  105.3 5.3 %copy-start.46 = (f32[8,2,128,512]{3,2,1,0:T(8,128)S(1)}, f32[8,2,128,512]{3,2,1,0:T(8,128)}, u32[]{:S(2)}) copy-start(f32[8,2,128,512]{3,2,1,0:T(8,128)} %all-gather.2.cloned.1.call-done) | copy-start | bytes 12582916
  112.7 6.3 %copy-start.44 = (f32[1,3]{0,1:T(4,128)S(1)}, f32[1,3]{0,1:T(4,128)}, u32[]{:S(2)}) copy-start(f32[1,3]{0,1:T(4,128)} %get-tuple-element.98) | copy-start | bytes 40
  112.7 6.3 %copy-start.45 = (f32[1,3]{0,1:T(4,128)S(1)}, f32[1,3]{0,1:T(4,128)}, u32[]{:S(2)}) copy-start(f32[1,3]{0,1:T(4,128)} %get-tuple-element.99) | copy-start | bytes 40
  112.7 6.9 %copy-start.19 = (f32[1,2,128,144]{2,0,3,1:T(1,128)S(1)}, f32[1,2,128,144]{2,0,3,1:T(1,128)}, u32[]{:S(2)}) copy-start(f32[1,2,128,144]{2,0,3,1:T(1,128)} %get-tuple-element.25) | copy-start | bytes 442372
  112.7 6.9 %copy-start.20 = (f32[1,2,128,144]{2,0,3,1:T(1,128)S(1)}, f32[1,2,128,144]{2,0,3,1:T(1,128)}, u32[]{:S(2)}) copy-start(f32[1,2,128,144]{2,0,3,1:T(1,128)} %get-tuple-element.10) | copy-start | bytes 442372
  113.7 12.6 %collective-permute-start.4 = (f32[2,128,512]{2,1,0:T(8,128)S(1)}, f32[2,128,512]{2,1,0:T(8,128)S(1)}, u32[]{:S(2)}, u32[]{:S(2)}) collective-permute-start(f32[2,128,512]{2,1,0:T(8,128)S(1)} %fusion.18), channel_id=1, source_target_pairs={{1,2},{3,4},{5,6},{7,8},{9,10},{11,12},{13,14},{15,16},{17,18},{19... | collective-permute-start | bytes 1572872 | tf_op jit(solution)/shard_map/ppermute | solution.py:21
  118.8 7.5 %collective-permute-start.5 = (f32[2,128,512]{2,1,0:T(8,128)S(1)}, f32[2,128,512]{2,1,0:T(8,128)S(1)}, u32[]{:S(2)}, u32[]{:S(2)}) collective-permute-start(f32[2,128,512]{2,1,0:T(8,128)S(1)} %fusion.18), channel_id=1, source_target_pairs={{0,1},{2,3},{4,5},{6,7},{8,9},{10,11},{12,13},{14,15},{16,17},{18,... | collective-permute-start | bytes 1572872 | tf_op jit(solution)/shard_map/ppermute | solution.py:20
  133.0 6.2 %copy-start.16 = (f32[1,2,128,144]{2,0,3,1:T(1,128)S(1)}, f32[1,2,128,144]{2,0,3,1:T(1,128)}, u32[]{:S(2)}) copy-start(f32[1,2,128,144]{2,0,3,1:T(1,128)} %get-tuple-element.24) | copy-start | bytes 442372
  134.0 12.6 %collective-permute-start.6 = (f32[2,128,512]{2,1,0:T(8,128)S(1)}, f32[2,128,512]{2,1,0:T(8,128)S(1)}, u32[]{:S(2)}, u32[]{:S(2)}) collective-permute-start(f32[2,128,512]{2,1,0:T(8,128)S(1)} %fusion.28), channel_id=1, source_target_pairs={{1,2},{3,4},{5,6},{7,8},{9,10},{11,12},{13,14},{15,16},{17,18},{19... | collective-permute-start | bytes 1572872 | tf_op jit(solution)/shard_map/ppermute | solution.py:21
  139.1 7.5 %collective-permute-start.7 = (f32[2,128,512]{2,1,0:T(8,128)S(1)}, f32[2,128,512]{2,1,0:T(8,128)S(1)}, u32[]{:S(2)}, u32[]{:S(2)}) collective-permute-start(f32[2,128,512]{2,1,0:T(8,128)S(1)} %fusion.28), channel_id=1, source_target_pairs={{0,1},{2,3},{4,5},{6,7},{8,9},{10,11},{12,13},{14,15},{16,17},{18,... | collective-permute-start | bytes 1572872 | tf_op jit(solution)/shard_map/ppermute | solution.py:20
  153.5 6.9 %copy-start.14 = (f32[1,2,128,144]{2,0,3,1:T(1,128)S(1)}, f32[1,2,128,144]{2,0,3,1:T(1,128)}, u32[]{:S(2)}) copy-start(f32[1,2,128,144]{2,0,3,1:T(1,128)} %get-tuple-element.23) | copy-start | bytes 442372
  153.5 6.9 %copy-start.15 = (f32[1,2,128,144]{2,0,3,1:T(1,128)S(1)}, f32[1,2,128,144]{2,0,3,1:T(1,128)}, u32[]{:S(2)}) copy-start(f32[1,2,128,144]{2,0,3,1:T(1,128)} %get-tuple-element.8) | copy-start | bytes 442372
  154.5 12.6 %collective-permute-start.8 = (f32[2,128,512]{2,1,0:T(8,128)S(1)}, f32[2,128,512]{2,1,0:T(8,128)S(1)}, u32[]{:S(2)}, u32[]{:S(2)}) collective-permute-start(f32[2,128,512]{2,1,0:T(8,128)S(1)} %fusion.38), channel_id=1, source_target_pairs={{1,2},{3,4},{5,6},{7,8},{9,10},{11,12},{13,14},{15,16},{17,18},{19... | collective-permute-start | bytes 1572872 | tf_op jit(solution)/shard_map/ppermute | solution.py:21
  159.6 7.5 %collective-permute-start.9 = (f32[2,128,512]{2,1,0:T(8,128)S(1)}, f32[2,128,512]{2,1,0:T(8,128)S(1)}, u32[]{:S(2)}, u32[]{:S(2)}) collective-permute-start(f32[2,128,512]{2,1,0:T(8,128)S(1)} %fusion.38), channel_id=1, source_target_pairs={{0,1},{2,3},{4,5},{6,7},{8,9},{10,11},{12,13},{14,15},{16,17},{18,... | collective-permute-start | bytes 1572872 | tf_op jit(solution)/shard_map/ppermute | solution.py:20
  167.2 4.3 %copy-start.33 = (f32[1,2,128,144]{2,0,3,1:T(1,128)S(1)}, f32[1,2,128,144]{2,0,3,1:T(1,128)}, u32[]{:S(2)}) copy-start(f32[1,2,128,144]{2,0,3,1:T(1,128)} %get-tuple-element.32) | copy-start | bytes 442372
  169.5 18.2 %copy-start = (f32[4,128,512]{2,1,0:T(8,128)}, f32[4,128,512]{2,1,0:T(8,128)S(1)}, u32[]{:S(2)}) copy-start(f32[4,128,512]{2,1,0:T(8,128)S(1)} %fusion.254) | copy-start | bytes 3145732
  174.0 6.5 %copy-start.12 = (f32[1,2,128,144]{2,0,3,1:T(1,128)S(1)}, f32[1,2,128,144]{2,0,3,1:T(1,128)}, u32[]{:S(2)}) copy-start(f32[1,2,128,144]{2,0,3,1:T(1,128)} %get-tuple-element.22) | copy-start | bytes 442372
  174.0 6.5 %copy-start.13 = (f32[1,2,128,144]{2,0,3,1:T(1,128)S(1)}, f32[1,2,128,144]{2,0,3,1:T(1,128)}, u32[]{:S(2)}) copy-start(f32[1,2,128,144]{2,0,3,1:T(1,128)} %get-tuple-element.7) | copy-start | bytes 442372
  175.0 12.6 %collective-permute-start.10 = (f32[2,128,512]{2,1,0:T(8,128)S(1)}, f32[2,128,512]{2,1,0:T(8,128)S(1)}, u32[]{:S(2)}, u32[]{:S(2)}) collective-permute-start(f32[2,128,512]{2,1,0:T(8,128)S(1)} %fusion.48), channel_id=1, source_target_pairs={{1,2},{3,4},{5,6},{7,8},{9,10},{11,12},{13,14},{15,16},{17,18},{19... | collective-permute-start | bytes 1572872 | tf_op jit(solution)/shard_map/ppermute | solution.py:21
  180.1 7.5 %collective-permute-start.11 = (f32[2,128,512]{2,1,0:T(8,128)S(1)}, f32[2,128,512]{2,1,0:T(8,128)S(1)}, u32[]{:S(2)}, u32[]{:S(2)}) collective-permute-start(f32[2,128,512]{2,1,0:T(8,128)S(1)} %fusion.48), channel_id=1, source_target_pairs={{0,1},{2,3},{4,5},{6,7},{8,9},{10,11},{12,13},{14,15},{16,17},{18,... | collective-permute-start | bytes 1572872 | tf_op jit(solution)/shard_map/ppermute | solution.py:20
  189.9 18.3 %copy-start.2 = (f32[4,128,512]{2,1,0:T(8,128)}, f32[4,128,512]{2,1,0:T(8,128)S(1)}, u32[]{:S(2)}) copy-start(f32[4,128,512]{2,1,0:T(8,128)S(1)} %fusion.250) | copy-start | bytes 3145732
  194.4 6.8 %copy-start.10 = (f32[1,2,128,144]{2,0,3,1:T(1,128)S(1)}, f32[1,2,128,144]{2,0,3,1:T(1,128)}, u32[]{:S(2)}) copy-start(f32[1,2,128,144]{2,0,3,1:T(1,128)} %get-tuple-element.28) | copy-start | bytes 442372
  194.5 6.9 %copy-start.11 = (f32[1,2,128,144]{2,0,3,1:T(1,128)S(1)}, f32[1,2,128,144]{2,0,3,1:T(1,128)}, u32[]{:S(2)}) copy-start(f32[1,2,128,144]{2,0,3,1:T(1,128)} %get-tuple-element.6) | copy-start | bytes 442372
  195.4 12.6 %collective-permute-start.12 = (f32[2,128,512]{2,1,0:T(8,128)S(1)}, f32[2,128,512]{2,1,0:T(8,128)S(1)}, u32[]{:S(2)}, u32[]{:S(2)}) collective-permute-start(f32[2,128,512]{2,1,0:T(8,128)S(1)} %fusion.58), channel_id=1, source_target_pairs={{1,2},{3,4},{5,6},{7,8},{9,10},{11,12},{13,14},{15,16},{17,18},{19... | collective-permute-start | bytes 1572872 | tf_op jit(solution)/shard_map/ppermute | solution.py:21
  200.6 7.5 %collective-permute-start.13 = (f32[2,128,512]{2,1,0:T(8,128)S(1)}, f32[2,128,512]{2,1,0:T(8,128)S(1)}, u32[]{:S(2)}, u32[]{:S(2)}) collective-permute-start(f32[2,128,512]{2,1,0:T(8,128)S(1)} %fusion.58), channel_id=1, source_target_pairs={{0,1},{2,3},{4,5},{6,7},{8,9},{10,11},{12,13},{14,15},{16,17},{18,... | collective-permute-start | bytes 1572872 | tf_op jit(solution)/shard_map/ppermute | solution.py:20
  208.2 4.2 %copy-start.29 = (f32[1,2,128,144]{2,0,3,1:T(1,128)S(1)}, f32[1,2,128,144]{2,0,3,1:T(1,128)}, u32[]{:S(2)}) copy-start(f32[1,2,128,144]{2,0,3,1:T(1,128)} %get-tuple-element.30) | copy-start | bytes 442372
  210.4 18.3 %copy-start.4 = (f32[4,128,512]{2,1,0:T(8,128)}, f32[4,128,512]{2,1,0:T(8,128)S(1)}, u32[]{:S(2)}) copy-start(f32[4,128,512]{2,1,0:T(8,128)S(1)} %fusion.246) | copy-start | bytes 3145732
  214.9 6.2 %copy-start.8 = (f32[1,2,128,144]{2,0,3,1:T(1,128)S(1)}, f32[1,2,128,144]{2,0,3,1:T(1,128)}, u32[]{:S(2)}) copy-start(f32[1,2,128,144]{2,0,3,1:T(1,128)} %get-tuple-element.21) | copy-start | bytes 442372
  214.9 6.3 %copy-start.9 = (f32[1,2,128,144]{2,0,3,1:T(1,128)S(1)}, f32[1,2,128,144]{2,0,3,1:T(1,128)}, u32[]{:S(2)}) copy-start(f32[1,2,128,144]{2,0,3,1:T(1,128)} %get-tuple-element.5) | copy-start | bytes 442372
  215.9 12.6 %collective-permute-start.14 = (f32[2,128,512]{2,1,0:T(8,128)S(1)}, f32[2,128,512]{2,1,0:T(8,128)S(1)}, u32[]{:S(2)}, u32[]{:S(2)}) collective-permute-start(f32[2,128,512]{2,1,0:T(8,128)S(1)} %fusion.68), channel_id=1, source_target_pairs={{1,2},{3,4},{5,6},{7,8},{9,10},{11,12},{13,14},{15,16},{17,18},{19... | collective-permute-start | bytes 1572872 | tf_op jit(solution)/shard_map/ppermute | solution.py:21
  221.1 7.5 %collective-permute-start.15 = (f32[2,128,512]{2,1,0:T(8,128)S(1)}, f32[2,128,512]{2,1,0:T(8,128)S(1)}, u32[]{:S(2)}, u32[]{:S(2)}) collective-permute-start(f32[2,128,512]{2,1,0:T(8,128)S(1)} %fusion.68), channel_id=1, source_target_pairs={{0,1},{2,3},{4,5},{6,7},{8,9},{10,11},{12,13},{14,15},{16,17},{18,... | collective-permute-start | bytes 1572872 | tf_op jit(solution)/shard_map/ppermute | solution.py:20
  228.6 4.2 %copy-start.27 = (f32[1,2,128,144]{2,0,3,1:T(1,128)S(1)}, f32[1,2,128,144]{2,0,3,1:T(1,128)}, u32[]{:S(2)}) copy-start(f32[1,2,128,144]{2,0,3,1:T(1,128)} %get-tuple-element.29) | copy-start | bytes 442372
  237.1 12.9 %collective-permute-start.16 = (f32[2,128,512]{2,1,0:T(8,128)}, f32[2,128,512]{2,1,0:T(8,128)}, u32[]{:S(2)}, u32[]{:S(2)}) collective-permute-start(f32[2,128,512]{2,1,0:T(8,128)} %fusion.78), channel_id=1, source_target_pairs={{1,2},{3,4},{5,6},{7,8},{9,10},{11,12},{13,14},{15,16},{17,18},{19... | collective-permute-start | bytes 1572872 | tf_op jit(solution)/shard_map/ppermute | solution.py:21
  242.3 7.8 %collective-permute-start.17 = (f32[2,128,512]{2,1,0:T(8,128)}, f32[2,128,512]{2,1,0:T(8,128)}, u32[]{:S(2)}, u32[]{:S(2)}) collective-permute-start(f32[2,128,512]{2,1,0:T(8,128)} %fusion.78), channel_id=1, source_target_pairs={{0,1},{2,3},{4,5},{6,7},{8,9},{10,11},{12,13},{14,15},{16,17},{18,... | collective-permute-start | bytes 1572872 | tf_op jit(solution)/shard_map/ppermute | solution.py:20
  (19 other events, 56.2 us)
Sparse Core Ops, SparseCore 0:
  10.0 78.4 all-gather.1

commit v9 on v6

--- a/solution.py
+++ b/solution.py
@@ -86,7 +86,7 @@
     bx_all = [band_matrix(mats[2][p], nx, reach) for p in range(view_count)]
     bxr_all = [band_matrix(mats[3][p], nx, reach) for p in range(view_count)]
     padded = halo(estimate, "slab", RZ)
-    results = jnp.zeros_like(estimate)
+    history = []
     for position in range(view_count):
         view_id = view_order[position]
         by = by_all[position]
@@ -106,8 +106,9 @@
         for k in range(1, 3):
             corr = corr + kz[k] * gp[2 - k : 2 - k + count + 2]
         padded = padded * corr
-        results = jnp.where(my_view == view_id, padded[RZ:-RZ], results)
-    return results[None]
+        history.append(padded[RZ:-RZ])
+    mine = (my_view - view_order[0]) % view_count
+    return lax.dynamic_index_in_dim(jnp.stack(history, axis=0), mine, 0, keepdims=True)
 
 
 def solution(mesh):

time: 264 us -> 267 us (1.011)
  starting transfers between devices: 50.2 us -> 55.4 us
  local copies, waits for them, and re-layouts: 18.5 us -> 22.8 us
  between operations: 35.2 us -> 31.2 us
    ppermute x9, starting transfers between devices: 49 us -> 54.8 us  [halo(): outer_got = lax.ppermute(jnp.where(odd, top, bottom), axis, outer)]
    slice x1, local copies, waits for them, and re-layouts: 1.6 us -> 6.48 us  [per_device(): bxr_all = [band_matrix(mats[3][p], nx, reach) for p in range(view_count)]]
    broadcast_in_dim x1 -> x0, other arithmetic: 4.82 us -> none  [per_device(): return results[None]]
    slice x1, local copies, waits for them, and re-layouts: 6.37 us -> 1.71 us  [per_device(): bx_all = [band_matrix(mats[2][p], nx, reach) for p in range(view_count)]]
    slice x16, local copies, waits for them, and re-layouts: 1.06 us -> 4.28 us  [band_matrix(): diagonal = mats[..., reach:reach + block]]
    ppermute x9, waiting for transfers between devices: 51.3 us -> 48.1 us  [halo(): outer_got = lax.ppermute(jnp.where(odd, top, bottom), axis, outer)]
  transfers between devices with their start and end apart: 19 -> 19, of which waited for: 9 -> 9; matrix products, arithmetic and copies ran while one was open for 12% -> 13% of each run, Pallas kernels for 0% -> 0%
where the time goes in v9:
time: 267 us; the launch traced here: 265 us
  waiting for transfers between devices  77.6 us (29%)
  starting transfers between devices  55.4 us (21%)
  matrix products  51.4 us (19%)
  between operations  31.2 us (12%)
  other arithmetic  27.1 us (10%)
  local copies, waits for them, and re-layouts  22.8 us (9%)
    ppermute x9, starting transfers between devices, halo(): outer_got = lax.ppermute(jnp.where(odd, top, bottom), axis, outer)  54.8 us
    ppermute x9, waiting for transfers between devices, halo(): outer_got = lax.ppermute(jnp.where(odd, top, bottom), axis, outer)  48.1 us
    all_gather x1, waiting for transfers between devices, per_device(): data_all = lax.all_gather(view_data[0], 'view', axis=0)  28.7 us
    dot_general x8, matrix products, per_device(): t = jnp.einsum('lij,ljx->lix', by, c, precision=blur_mode)  18.4 us
    mul x7, other arithmetic, per_device(): padded = padded * corr  17.4 us
    dot_general x8, matrix products, per_device(): jnp.einsum('lix,lax->lia', t, bx_all[position], precision=blur_mode)  16.2 us
    dot_general x8, matrix products, per_device(): g = jnp.einsum('lix,lax->lia', u, bxr_all[position], precision=blur_mode)  8.43 us
    slice x1, local copies, waits for them, and re-layouts, per_device(): bxr_all = [band_matrix(mats[3][p], nx, reach) for p in range(view_count)]  6.48 us
  transfers between devices with their start and end apart: 19, of which 9 were waited for; matrix products, arithmetic and copies ran while one was open for 13% of the time, Pallas kernels for 0%

profile of v9, /device:TPU:2, one launch (start us, length us, event | category | flops | bytes accessed | tf_op | source)
XLA Modules:
  0.0 265.5 jit_solution(5158578913119478861)
XLA Ops:
  7.3 1.9 slice_select_fusion.1
  9.2 7.8 %collective-permute-start.1 = (f32[1,128,512]{2,1,0:T(8,128)}, f32[1,128,512]{2,1,0:T(8,128)}, u32[]{:S(2)}, u32[]{:S(2)}) collective-permute-start(f32[1,128,512]{2,1,0:T(8,128)} %get-tuple-element.56), channel_id=1, source_target_pairs={{1,2},{3,4},{5,6},{7,8},{9,10},{11,12},{13,14},{15,16},{17,18},{19... | collective-permute-start | bytes 786440 | tf_op jit(solution)/shard_map/ppermute | solution.py:21
  17.0 1.6 fusion.473
  33.1 1.8 fusion.207
  43.0 6.5 %fusion.443 = (f32[1,2,128,144]{2,0,3,1:T(1,128)}, f32[1,2,128,144]{2,0,3,1:T(1,128)}, f32[1,2,128,144]{2,0,3,1:T(1,128)}, f32[1,2,128,144]{2,0,3,1:T(1,128)}, f...) fusion(f32[8,2,128,144]{2,0,3,1:T(8,128)} %fusion.207), kind=kLoop, calls=%fused_computation.534 | loop fusion | bytes 2359296 | tf_op jit(solution)/shard_map/slice | solution.py:87
  50.3 1.7 fusion.445
  52.0 1.6 fusion.446
  57.6 2.2 fusion.340
  59.8 28.7 %all-gather.2.cloned.1.call-done = f32[8,2,128,512]{3,2,1,0:T(8,128)} async-done(((f32[1,2,128,512]{3,2,1,0:T(8,128)}), f32[8,2,128,512]{3,2,1,0:T(8,128)}) %all-gather.2.cloned.1.call-update) | async-done | bytes 4194320 | tf_op jit(solution)/shard_map/all_gather | solution.py:65
  88.7 2.8 %fusion.267 = f32[2,128,512]{2,1,0:T(8,128)S(1)} fusion(f32[2,128,512]{2,1,0:T(8,128)S(1)} %fusion.340, f32[2,128,256]{1,2,0:T(8,128)S(1)} %broadcast.21, f32[2,128,120]{1,2,0:T(8,128)S(1)} %broadcast.20, f32[2,128,128]{1,2,0:T(8,128)S(1)} %broadcast.22, f32[2,128,136]{1,2,0:T(8,128)S(1)} %get-tuple-element.88, f32[2,128,144]{1,2,0:T(8,128)S(1)} %bitcast.229, ...), kind=kOutput, calls=%fused_computation.329 | convolution fusion | flops 409731072 | bytes 2514952 | tf_op jit(solution)/shard_map/lix,lax->lia/dot_general | solution.py:100
  93.0 6.4 %collective-permute-start.2 = (f32[2,128,512]{2,1,0:T(8,128)S(1)}, f32[2,128,512]{2,1,0:T(8,128)S(1)}, u32[]{:S(2)}, u32[]{:S(2)}) collective-permute-start(f32[2,128,512]{2,1,0:T(8,128)S(1)} %fusion.8), channel_id=1, source_target_pairs={{1,2},{3,4},{5,6},{7,8},{9,10},{11,12},{13,14},{15,16},{17,18},{19... | collective-permute-start | bytes 1572872 | tf_op jit(solution)/shard_map/ppermute | solution.py:21
  100.2 5.8 %collective-permute-done.2 = f32[2,128,512]{2,1,0:T(8,128)S(1)} collective-permute-done((f32[2,128,512]{2,1,0:T(8,128)S(1)}, f32[2,128,512]{2,1,0:T(8,128)S(1)}, u32[]{:S(2)}, u32[]{:S(2)}) %collective-permute-start.2) | collective-permute-done | bytes 524320 | tf_op jit(solution)/shard_map/ppermute | solution.py:21
  106.2 2.3 fusion.266
  108.5 2.3 fusion.334
  110.9 1.6 fusion.270
  114.0 5.8 %collective-permute-start.4 = (f32[2,128,512]{2,1,0:T(8,128)S(1)}, f32[2,128,512]{2,1,0:T(8,128)S(1)}, u32[]{:S(2)}, u32[]{:S(2)}) collective-permute-start(f32[2,128,512]{2,1,0:T(8,128)S(1)} %fusion.18), channel_id=1, source_target_pairs={{1,2},{3,4},{5,6},{7,8},{9,10},{11,12},{13,14},{15,16},{17,18},{19... | collective-permute-start | bytes 1572872 | tf_op jit(solution)/shard_map/ppermute | solution.py:21
  120.5 6.2 %collective-permute-done.4 = f32[2,128,512]{2,1,0:T(8,128)S(1)} collective-permute-done((f32[2,128,512]{2,1,0:T(8,128)S(1)}, f32[2,128,512]{2,1,0:T(8,128)S(1)}, u32[]{:S(2)}, u32[]{:S(2)}) %collective-permute-start.4) | collective-permute-done | bytes 524320 | tf_op jit(solution)/shard_map/ppermute | solution.py:21
  126.7 2.2 fusion.262
  129.0 2.3 fusion.329
  131.3 1.6 fusion.273
  134.5 5.7 %collective-permute-start.6 = (f32[2,128,512]{2,1,0:T(8,128)S(1)}, f32[2,128,512]{2,1,0:T(8,128)S(1)}, u32[]{:S(2)}, u32[]{:S(2)}) collective-permute-start(f32[2,128,512]{2,1,0:T(8,128)S(1)} %fusion.28), channel_id=1, source_target_pairs={{1,2},{3,4},{5,6},{7,8},{9,10},{11,12},{13,14},{15,16},{17,18},{19... | collective-permute-start | bytes 1572872 | tf_op jit(solution)/shard_map/ppermute | solution.py:21
  141.0 6.0 %collective-permute-done.6 = f32[2,128,512]{2,1,0:T(8,128)S(1)} collective-permute-done((f32[2,128,512]{2,1,0:T(8,128)S(1)}, f32[2,128,512]{2,1,0:T(8,128)S(1)}, u32[]{:S(2)}, u32[]{:S(2)}) %collective-permute-start.6) | collective-permute-done | bytes 524320 | tf_op jit(solution)/shard_map/ppermute | solution.py:21
  147.2 2.3 fusion.258
  149.5 2.3 fusion.324
  154.9 5.8 %collective-permute-start.8 = (f32[2,128,512]{2,1,0:T(8,128)S(1)}, f32[2,128,512]{2,1,0:T(8,128)S(1)}, u32[]{:S(2)}, u32[]{:S(2)}) collective-permute-start(f32[2,128,512]{2,1,0:T(8,128)S(1)} %fusion.38), channel_id=1, source_target_pairs={{1,2},{3,4},{5,6},{7,8},{9,10},{11,12},{13,14},{15,16},{17,18},{19... | collective-permute-start | bytes 1572872 | tf_op jit(solution)/shard_map/ppermute | solution.py:21
  161.3 6.2 %collective-permute-done.8 = f32[2,128,512]{2,1,0:T(8,128)S(1)} collective-permute-done((f32[2,128,512]{2,1,0:T(8,128)S(1)}, f32[2,128,512]{2,1,0:T(8,128)S(1)}, u32[]{:S(2)}, u32[]{:S(2)}) %collective-permute-start.8) | collective-permute-done | bytes 524320 | tf_op jit(solution)/shard_map/ppermute | solution.py:21
  167.6 2.2 fusion.254
  169.8 2.3 fusion.319
  172.1 1.6 fusion.279
  175.3 6.0 %collective-permute-start.10 = (f32[2,128,512]{2,1,0:T(8,128)S(1)}, f32[2,128,512]{2,1,0:T(8,128)S(1)}, u32[]{:S(2)}, u32[]{:S(2)}) collective-permute-start(f32[2,128,512]{2,1,0:T(8,128)S(1)} %fusion.48), channel_id=1, source_target_pairs={{1,2},{3,4},{5,6},{7,8},{9,10},{11,12},{13,14},{15,16},{17,18},{19... | collective-permute-start | bytes 1572872 | tf_op jit(solution)/shard_map/ppermute | solution.py:21
  182.1 5.8 %collective-permute-done.10 = f32[2,128,512]{2,1,0:T(8,128)S(1)} collective-permute-done((f32[2,128,512]{2,1,0:T(8,128)S(1)}, f32[2,128,512]{2,1,0:T(8,128)S(1)}, u32[]{:S(2)}, u32[]{:S(2)}) %collective-permute-start.10) | collective-permute-done | bytes 524320 | tf_op jit(solution)/shard_map/ppermute | solution.py:21
  188.0 2.2 fusion.250
  190.2 2.3 fusion.314
  192.5 1.7 fusion.282
  194.7 1.7 fusion.58
  196.4 5.7 %collective-permute-start.12 = (f32[2,128,512]{2,1,0:T(8,128)}, f32[2,128,512]{2,1,0:T(8,128)}, u32[]{:S(2)}, u32[]{:S(2)}) collective-permute-start(f32[2,128,512]{2,1,0:T(8,128)} %fusion.58), channel_id=1, source_target_pairs={{1,2},{3,4},{5,6},{7,8},{9,10},{11,12},{13,14},{15,16},{17,18},{19... | collective-permute-start | bytes 1572872 | tf_op jit(solution)/shard_map/ppermute | solution.py:21
  204.6 4.7 %collective-permute-done.12 = f32[2,128,512]{2,1,0:T(8,128)} collective-permute-done((f32[2,128,512]{2,1,0:T(8,128)}, f32[2,128,512]{2,1,0:T(8,128)}, u32[]{:S(2)}, u32[]{:S(2)}) %collective-permute-start.12) | collective-permute-done | bytes 524320 | tf_op jit(solution)/shard_map/ppermute | solution.py:21
  210.6 3.9 %fusion.246 = f32[4,128,512]{2,1,0:T(8,128)S(1)} fusion(f32[4,128,512]{2,1,0:T(8,128)S(1)} %copy-done.1, f32[2,128,512]{2,1,0:T(8,128)S(1)} %get-tuple-element.42, f32[2,128,512]{2,1,0:T(8,128)} %fusion.58, f32[2,128,512]{2,1,0:T(8,128)S(1)} %get-tuple-element.41, f32[]{:T(128)} %bitcast.75, f32[]{:T(128)} %bitcast.74, f32[]{:T(128)} %bitcast.70), kind=kLoop, calls=%fused_computation.283 | loop fusion | flops 2621440 | bytes 3670028 | tf_op jit(solution)/shard_map/mul | solution.py:108
  214.6 2.4 fusion.309
  217.1 2.6 fusion.285
  221.3 5.9 %collective-permute-start.14 = (f32[2,128,512]{2,1,0:T(8,128)S(1)}, f32[2,128,512]{2,1,0:T(8,128)S(1)}, u32[]{:S(2)}, u32[]{:S(2)}) collective-permute-start(f32[2,128,512]{2,1,0:T(8,128)S(1)} %fusion.68), channel_id=1, source_target_pairs={{1,2},{3,4},{5,6},{7,8},{9,10},{11,12},{13,14},{15,16},{17,18},{19... | collective-permute-start | bytes 1572872 | tf_op jit(solution)/shard_map/ppermute | solution.py:21
  227.3 6.7 %collective-permute-done.14 = f32[2,128,512]{2,1,0:T(8,128)S(1)} collective-permute-done((f32[2,128,512]{2,1,0:T(8,128)S(1)}, f32[2,128,512]{2,1,0:T(8,128)S(1)}, u32[]{:S(2)}, u32[]{:S(2)}) %collective-permute-start.14) | collective-permute-done | bytes 524320 | tf_op jit(solution)/shard_map/ppermute | solution.py:21
  234.1 2.3 fusion.242
  236.4 2.3 fusion.304
  238.9 2.6 fusion.288
  243.0 5.7 %collective-permute-start.16 = (f32[2,128,512]{2,1,0:T(8,128)S(1)}, f32[2,128,512]{2,1,0:T(8,128)S(1)}, u32[]{:S(2)}, u32[]{:S(2)}) collective-permute-start(f32[2,128,512]{2,1,0:T(8,128)S(1)} %fusion.78), channel_id=1, source_target_pairs={{1,2},{3,4},{5,6},{7,8},{9,10},{11,12},{13,14},{15,16},{17,18},{19... | collective-permute-start | bytes 1572872 | tf_op jit(solution)/shard_map/ppermute | solution.py:21
  248.9 6.7 %collective-permute-done.16 = f32[2,128,512]{2,1,0:T(8,128)S(1)} collective-permute-done((f32[2,128,512]{2,1,0:T(8,128)S(1)}, f32[2,128,512]{2,1,0:T(8,128)S(1)}, u32[]{:S(2)}, u32[]{:S(2)}) %collective-permute-start.16) | collective-permute-done | bytes 524320 | tf_op jit(solution)/shard_map/ppermute | solution.py:21
  255.7 2.1 fusion.299
  (202 shorter events, 33.5 us)
Async XLA Ops:
  6.5 26.1 %copy-start.52 = (s32[2]{0:T(128)S(1)}, s32[2]{0:T(128)}, u32[]{:S(2)}) copy-start(s32[2]{0:T(128)} %param.13) | copy-start | bytes 28
  6.5 82.0 %all-gather.2.cloned.1.call-start = ((), (), s32[]{:S(2)}) async-start(), calls=%async_computation | async-start | bytes 4718592 | tf_op jit(solution)/shard_map/all_gather | solution.py:65
  9.2 47.3 %collective-permute-start = (f32[1,128,512]{2,1,0:T(8,128)}, f32[1,128,512]{2,1,0:T(8,128)}, u32[]{:S(2)}, u32[]{:S(2)}) collective-permute-start(f32[1,128,512]{2,1,0:T(8,128)} %get-tuple-element.55), channel_id=1, source_target_pairs={{0,1},{2,3},{4,5},{6,7},{8,9},{10,11},{12,13},{14,15},{16,17},{18,... | collective-permute-start | bytes 786440 | tf_op jit(solution)/shard_map/ppermute | solution.py:20
  9.2 47.4 %collective-permute-start.1 = (f32[1,128,512]{2,1,0:T(8,128)}, f32[1,128,512]{2,1,0:T(8,128)}, u32[]{:S(2)}, u32[]{:S(2)}) collective-permute-start(f32[1,128,512]{2,1,0:T(8,128)} %get-tuple-element.56), channel_id=1, source_target_pairs={{1,2},{3,4},{5,6},{7,8},{9,10},{11,12},{13,14},{15,16},{17,18},{19... | collective-permute-start | bytes 786440 | tf_op jit(solution)/shard_map/ppermute | solution.py:21
  34.9 7.4 %copy-start.48 = (f32[8,3]{0,1:T(4,128)S(1)}, f32[8,3]{0,1:T(4,128)}, u32[]{:S(2)}) copy-start(f32[8,3]{0,1:T(4,128)} %param.11) | copy-start | bytes 292
  56.5 32.1 %copy-start.23 = (f32[1,2,128,144]{2,0,3,1:T(1,128)S(1)}, f32[1,2,128,144]{2,0,3,1:T(1,128)}, u32[]{:S(2)}) copy-start(f32[1,2,128,144]{2,0,3,1:T(1,128)} %copy-done.22) | copy-start | bytes 442372
  88.5 106.1 %copy-start.45 = (f32[2,128,120]{1,2,0:T(8,128)}, f32[2,128,120]{1,2,0:T(8,128)S(1)}, u32[]{:S(2)}) copy-start(f32[2,128,120]{1,2,0:T(8,128)S(1)} %broadcast.20) | copy-start | bytes 368644
  88.6 106.1 %copy-start.43 = (f32[2,128,128]{1,2,0:T(8,128)}, f32[2,128,128]{1,2,0:T(8,128)S(1)}, u32[]{:S(2)}) copy-start(f32[2,128,128]{1,2,0:T(8,128)S(1)} %broadcast.22) | copy-start | bytes 393220
  88.6 106.1 %copy-start.33 = (f32[2,128,256]{1,2,0:T(8,128)}, f32[2,128,256]{1,2,0:T(8,128)S(1)}, u32[]{:S(2)}) copy-start(f32[2,128,256]{1,2,0:T(8,128)S(1)} %broadcast.21) | copy-start | bytes 786436
  91.9 7.5 %copy-start.7 = (f32[1,2,128,144]{2,0,3,1:T(1,128)S(1)}, f32[1,2,128,144]{2,0,3,1:T(1,128)}, u32[]{:S(2)}) copy-start(f32[1,2,128,144]{2,0,3,1:T(1,128)} %get-tuple-element.6) | copy-start | bytes 442372
  91.9 8.2 %copy-start.18 = (f32[1,2,128,144]{2,0,3,1:T(1,128)S(1)}, f32[1,2,128,144]{2,0,3,1:T(1,128)}, u32[]{:S(2)}) copy-start(f32[1,2,128,144]{2,0,3,1:T(1,128)} %get-tuple-element.11) | copy-start | bytes 442372
  91.9 8.3 %copy-start.19 = (f32[1,2,128,144]{2,0,3,1:T(1,128)S(1)}, f32[1,2,128,144]{2,0,3,1:T(1,128)}, u32[]{:S(2)}) copy-start(f32[1,2,128,144]{2,0,3,1:T(1,128)} %get-tuple-element.26) | copy-start | bytes 442372
  92.9 7.3 %collective-permute-start.3 = (f32[2,128,512]{2,1,0:T(8,128)S(1)}, f32[2,128,512]{2,1,0:T(8,128)S(1)}, u32[]{:S(2)}, u32[]{:S(2)}) collective-permute-start(f32[2,128,512]{2,1,0:T(8,128)S(1)} %fusion.8), channel_id=1, source_target_pairs={{0,1},{2,3},{4,5},{6,7},{8,9},{10,11},{12,13},{14,15},{16,17},{18,... | collective-permute-start | bytes 1572872 | tf_op jit(solution)/shard_map/ppermute | solution.py:20
  93.0 13.1 %collective-permute-start.2 = (f32[2,128,512]{2,1,0:T(8,128)S(1)}, f32[2,128,512]{2,1,0:T(8,128)S(1)}, u32[]{:S(2)}, u32[]{:S(2)}) collective-permute-start(f32[2,128,512]{2,1,0:T(8,128)S(1)} %fusion.8), channel_id=1, source_target_pairs={{1,2},{3,4},{5,6},{7,8},{9,10},{11,12},{13,14},{15,16},{17,18},{19... | collective-permute-start | bytes 1572872 | tf_op jit(solution)/shard_map/ppermute | solution.py:21
  112.9 6.9 %copy-start.49 = (f32[1,3]{0,1:T(4,128)S(1)}, f32[1,3]{0,1:T(4,128)}, u32[]{:S(2)}) copy-start(f32[1,3]{0,1:T(4,128)} %get-tuple-element.98) | copy-start | bytes 40
  112.9 6.9 %copy-start.50 = (f32[1,3]{0,1:T(4,128)S(1)}, f32[1,3]{0,1:T(4,128)}, u32[]{:S(2)}) copy-start(f32[1,3]{0,1:T(4,128)} %get-tuple-element.99) | copy-start | bytes 40
  112.9 7.5 %copy-start.16 = (f32[1,2,128,144]{2,0,3,1:T(1,128)S(1)}, f32[1,2,128,144]{2,0,3,1:T(1,128)}, u32[]{:S(2)}) copy-start(f32[1,2,128,144]{2,0,3,1:T(1,128)} %get-tuple-element.10) | copy-start | bytes 442372
  112.9 7.5 %copy-start.17 = (f32[1,2,128,144]{2,0,3,1:T(1,128)S(1)}, f32[1,2,128,144]{2,0,3,1:T(1,128)}, u32[]{:S(2)}) copy-start(f32[1,2,128,144]{2,0,3,1:T(1,128)} %get-tuple-element.25) | copy-start | bytes 442372
  113.9 6.5 %collective-permute-start.5 = (f32[2,128,512]{2,1,0:T(8,128)S(1)}, f32[2,128,512]{2,1,0:T(8,128)S(1)}, u32[]{:S(2)}, u32[]{:S(2)}) collective-permute-start(f32[2,128,512]{2,1,0:T(8,128)S(1)} %fusion.18), channel_id=1, source_target_pairs={{0,1},{2,3},{4,5},{6,7},{8,9},{10,11},{12,13},{14,15},{16,17},{18,... | collective-permute-start | bytes 1572872 | tf_op jit(solution)/shard_map/ppermute | solution.py:20
  114.0 12.6 %collective-permute-start.4 = (f32[2,128,512]{2,1,0:T(8,128)S(1)}, f32[2,128,512]{2,1,0:T(8,128)S(1)}, u32[]{:S(2)}, u32[]{:S(2)}) collective-permute-start(f32[2,128,512]{2,1,0:T(8,128)S(1)} %fusion.18), channel_id=1, source_target_pairs={{1,2},{3,4},{5,6},{7,8},{9,10},{11,12},{13,14},{15,16},{17,18},{19... | collective-permute-start | bytes 1572872 | tf_op jit(solution)/shard_map/ppermute | solution.py:21
  133.4 6.9 %copy-start.5 = (f32[1,2,128,144]{2,0,3,1:T(1,128)S(1)}, f32[1,2,128,144]{2,0,3,1:T(1,128)}, u32[]{:S(2)}) copy-start(f32[1,2,128,144]{2,0,3,1:T(1,128)} %get-tuple-element.5) | copy-start | bytes 442372
  133.4 7.6 %copy-start.14 = (f32[1,2,128,144]{2,0,3,1:T(1,128)S(1)}, f32[1,2,128,144]{2,0,3,1:T(1,128)}, u32[]{:S(2)}) copy-start(f32[1,2,128,144]{2,0,3,1:T(1,128)} %get-tuple-element.9) | copy-start | bytes 442372
  133.4 7.6 %copy-start.15 = (f32[1,2,128,144]{2,0,3,1:T(1,128)S(1)}, f32[1,2,128,144]{2,0,3,1:T(1,128)}, u32[]{:S(2)}) copy-start(f32[1,2,128,144]{2,0,3,1:T(1,128)} %get-tuple-element.24) | copy-start | bytes 442372
  134.4 6.7 %collective-permute-start.7 = (f32[2,128,512]{2,1,0:T(8,128)S(1)}, f32[2,128,512]{2,1,0:T(8,128)S(1)}, u32[]{:S(2)}, u32[]{:S(2)}) collective-permute-start(f32[2,128,512]{2,1,0:T(8,128)S(1)} %fusion.28), channel_id=1, source_target_pairs={{0,1},{2,3},{4,5},{6,7},{8,9},{10,11},{12,13},{14,15},{16,17},{18,... | collective-permute-start | bytes 1572872 | tf_op jit(solution)/shard_map/ppermute | solution.py:20
  134.5 12.6 %collective-permute-start.6 = (f32[2,128,512]{2,1,0:T(8,128)S(1)}, f32[2,128,512]{2,1,0:T(8,128)S(1)}, u32[]{:S(2)}, u32[]{:S(2)}) collective-permute-start(f32[2,128,512]{2,1,0:T(8,128)S(1)} %fusion.28), channel_id=1, source_target_pairs={{1,2},{3,4},{5,6},{7,8},{9,10},{11,12},{13,14},{15,16},{17,18},{19... | collective-permute-start | bytes 1572872 | tf_op jit(solution)/shard_map/ppermute | solution.py:21
  153.8 7.5 %copy-start.12 = (f32[1,2,128,144]{2,0,3,1:T(1,128)S(1)}, f32[1,2,128,144]{2,0,3,1:T(1,128)}, u32[]{:S(2)}) copy-start(f32[1,2,128,144]{2,0,3,1:T(1,128)} %get-tuple-element.8) | copy-start | bytes 442372
  153.8 7.5 %copy-start.13 = (f32[1,2,128,144]{2,0,3,1:T(1,128)S(1)}, f32[1,2,128,144]{2,0,3,1:T(1,128)}, u32[]{:S(2)}) copy-start(f32[1,2,128,144]{2,0,3,1:T(1,128)} %get-tuple-element.23) | copy-start | bytes 442372
  154.8 6.5 %collective-permute-start.9 = (f32[2,128,512]{2,1,0:T(8,128)S(1)}, f32[2,128,512]{2,1,0:T(8,128)S(1)}, u32[]{:S(2)}, u32[]{:S(2)}) collective-permute-start(f32[2,128,512]{2,1,0:T(8,128)S(1)} %fusion.38), channel_id=1, source_target_pairs={{0,1},{2,3},{4,5},{6,7},{8,9},{10,11},{12,13},{14,15},{16,17},{18,... | collective-permute-start | bytes 1572872 | tf_op jit(solution)/shard_map/ppermute | solution.py:20
  154.9 12.6 %collective-permute-start.8 = (f32[2,128,512]{2,1,0:T(8,128)S(1)}, f32[2,128,512]{2,1,0:T(8,128)S(1)}, u32[]{:S(2)}, u32[]{:S(2)}) collective-permute-start(f32[2,128,512]{2,1,0:T(8,128)S(1)} %fusion.38), channel_id=1, source_target_pairs={{1,2},{3,4},{5,6},{7,8},{9,10},{11,12},{13,14},{15,16},{17,18},{19... | collective-permute-start | bytes 1572872 | tf_op jit(solution)/shard_map/ppermute | solution.py:21
  169.8 18.2 %copy-start.2 = (f32[4,128,512]{2,1,0:T(8,128)}, f32[4,128,512]{2,1,0:T(8,128)S(1)}, u32[]{:S(2)}) copy-start(f32[4,128,512]{2,1,0:T(8,128)S(1)} %fusion.254) | copy-start | bytes 3145732
  174.2 7.1 %copy-start.10 = (f32[1,2,128,144]{2,0,3,1:T(1,128)S(1)}, f32[1,2,128,144]{2,0,3,1:T(1,128)}, u32[]{:S(2)}) copy-start(f32[1,2,128,144]{2,0,3,1:T(1,128)} %get-tuple-element.7) | copy-start | bytes 442372
  174.2 7.1 %copy-start.11 = (f32[1,2,128,144]{2,0,3,1:T(1,128)S(1)}, f32[1,2,128,144]{2,0,3,1:T(1,128)}, u32[]{:S(2)}) copy-start(f32[1,2,128,144]{2,0,3,1:T(1,128)} %get-tuple-element.22) | copy-start | bytes 442372
  174.2 7.1 %copy-start.6 = (f32[1,2,128,144]{2,0,3,1:T(1,128)S(1)}, f32[1,2,128,144]{2,0,3,1:T(1,128)}, u32[]{:S(2)}) copy-start(f32[1,2,128,144]{2,0,3,1:T(1,128)} %get-tuple-element.21) | copy-start | bytes 442372
  175.2 6.9 %collective-permute-start.11 = (f32[2,128,512]{2,1,0:T(8,128)S(1)}, f32[2,128,512]{2,1,0:T(8,128)S(1)}, u32[]{:S(2)}, u32[]{:S(2)}) collective-permute-start(f32[2,128,512]{2,1,0:T(8,128)S(1)} %fusion.48), channel_id=1, source_target_pairs={{0,1},{2,3},{4,5},{6,7},{8,9},{10,11},{12,13},{14,15},{16,17},{18,... | collective-permute-start | bytes 1572872 | tf_op jit(solution)/shard_map/ppermute | solution.py:20
  175.3 12.6 %collective-permute-start.10 = (f32[2,128,512]{2,1,0:T(8,128)S(1)}, f32[2,128,512]{2,1,0:T(8,128)S(1)}, u32[]{:S(2)}, u32[]{:S(2)}) collective-permute-start(f32[2,128,512]{2,1,0:T(8,128)S(1)} %fusion.48), channel_id=1, source_target_pairs={{1,2},{3,4},{5,6},{7,8},{9,10},{11,12},{13,14},{15,16},{17,18},{19... | collective-permute-start | bytes 1572872 | tf_op jit(solution)/shard_map/ppermute | solution.py:21
  196.4 8.2 %collective-permute-start.13 = (f32[2,128,512]{2,1,0:T(8,128)}, f32[2,128,512]{2,1,0:T(8,128)}, u32[]{:S(2)}, u32[]{:S(2)}) collective-permute-start(f32[2,128,512]{2,1,0:T(8,128)} %fusion.58), channel_id=1, source_target_pairs={{0,1},{2,3},{4,5},{6,7},{8,9},{10,11},{12,13},{14,15},{16,17},{18,... | collective-permute-start | bytes 1572872 | tf_op jit(solution)/shard_map/ppermute | solution.py:20
  196.4 12.9 %collective-permute-start.12 = (f32[2,128,512]{2,1,0:T(8,128)}, f32[2,128,512]{2,1,0:T(8,128)}, u32[]{:S(2)}, u32[]{:S(2)}) collective-permute-start(f32[2,128,512]{2,1,0:T(8,128)} %fusion.58), channel_id=1, source_target_pairs={{1,2},{3,4},{5,6},{7,8},{9,10},{11,12},{13,14},{15,16},{17,18},{19... | collective-permute-start | bytes 1572872 | tf_op jit(solution)/shard_map/ppermute | solution.py:21
  203.4 7.2 %copy-start.1 = (f32[4,128,512]{2,1,0:T(8,128)S(1)}, f32[4,128,512]{2,1,0:T(8,128)}, u32[]{:S(2)}) copy-start(f32[4,128,512]{2,1,0:T(8,128)} %copy-done) | copy-start | bytes 3145732
  210.6 6.4 %copy-start.9 = (f32[1,2,128,144]{2,0,3,1:T(1,128)S(1)}, f32[1,2,128,144]{2,0,3,1:T(1,128)}, u32[]{:S(2)}) copy-start(f32[1,2,128,144]{2,0,3,1:T(1,128)} %get-tuple-element.28) | copy-start | bytes 442372
  210.6 6.4 %copy-start.34 = (f32[2,128,256]{1,2,0:T(8,128)S(1)}, f32[2,128,256]{1,2,0:T(8,128)}, u32[]{:S(2)}) copy-start(f32[2,128,256]{1,2,0:T(8,128)} %copy-done.33) | copy-start | bytes 786436
  210.6 6.4 %copy-start.44 = (f32[2,128,128]{1,2,0:T(8,128)S(1)}, f32[2,128,128]{1,2,0:T(8,128)}, u32[]{:S(2)}) copy-start(f32[2,128,128]{1,2,0:T(8,128)} %copy-done.43) | copy-start | bytes 393220
  210.6 6.4 %copy-start.46 = (f32[2,128,120]{1,2,0:T(8,128)S(1)}, f32[2,128,120]{1,2,0:T(8,128)}, u32[]{:S(2)}) copy-start(f32[2,128,120]{1,2,0:T(8,128)} %copy-done.45) | copy-start | bytes 368644
  221.1 6.1 %copy-start.3 = (f32[4,128,512]{2,1,0:T(8,128)S(1)}, f32[4,128,512]{2,1,0:T(8,128)}, u32[]{:S(2)}) copy-start(f32[4,128,512]{2,1,0:T(8,128)} %copy-done.2) | copy-start | bytes 3145732
  221.2 6.1 %collective-permute-start.15 = (f32[2,128,512]{2,1,0:T(8,128)S(1)}, f32[2,128,512]{2,1,0:T(8,128)S(1)}, u32[]{:S(2)}, u32[]{:S(2)}) collective-permute-start(f32[2,128,512]{2,1,0:T(8,128)S(1)} %fusion.68), channel_id=1, source_target_pairs={{0,1},{2,3},{4,5},{6,7},{8,9},{10,11},{12,13},{14,15},{16,17},{18,... | collective-permute-start | bytes 1572872 | tf_op jit(solution)/shard_map/ppermute | solution.py:20
  221.3 12.7 %collective-permute-start.14 = (f32[2,128,512]{2,1,0:T(8,128)S(1)}, f32[2,128,512]{2,1,0:T(8,128)S(1)}, u32[]{:S(2)}, u32[]{:S(2)}) collective-permute-start(f32[2,128,512]{2,1,0:T(8,128)S(1)} %fusion.68), channel_id=1, source_target_pairs={{1,2},{3,4},{5,6},{7,8},{9,10},{11,12},{13,14},{15,16},{17,18},{19... | collective-permute-start | bytes 1572872 | tf_op jit(solution)/shard_map/ppermute | solution.py:21
  234.1 4.7 %copy-start.39 = (f32[2,128,136]{1,2,0:T(8,128)S(1)}, f32[2,128,136]{1,2,0:T(8,128)}, u32[]{:S(2)}) copy-start(f32[2,128,136]{1,2,0:T(8,128)} %get-tuple-element.59) | copy-start | bytes 417796
  242.9 6.0 %collective-permute-start.17 = (f32[2,128,512]{2,1,0:T(8,128)S(1)}, f32[2,128,512]{2,1,0:T(8,128)S(1)}, u32[]{:S(2)}, u32[]{:S(2)}) collective-permute-start(f32[2,128,512]{2,1,0:T(8,128)S(1)} %fusion.78), channel_id=1, source_target_pairs={{0,1},{2,3},{4,5},{6,7},{8,9},{10,11},{12,13},{14,15},{16,17},{18,... | collective-permute-start | bytes 1572872 | tf_op jit(solution)/shard_map/ppermute | solution.py:20
  243.0 12.6 %collective-permute-start.16 = (f32[2,128,512]{2,1,0:T(8,128)S(1)}, f32[2,128,512]{2,1,0:T(8,128)S(1)}, u32[]{:S(2)}, u32[]{:S(2)}) collective-permute-start(f32[2,128,512]{2,1,0:T(8,128)S(1)} %fusion.78), channel_id=1, source_target_pairs={{1,2},{3,4},{5,6},{7,8},{9,10},{11,12},{13,14},{15,16},{17,18},{19... | collective-permute-start | bytes 1572872 | tf_op jit(solution)/shard_map/ppermute | solution.py:21
  (24 other events, 76.2 us)
Sparse Core Ops, SparseCore 0:
  10.0 78.4 all-gather.1
